TPU v7x, 512 devices: a whole 4x8x8 slice. The times are simulated.
512 devices in a mesh: ctx: 64 (over y, x, core), head: 8 (over z).
Axes of the slice: x: 4, y: 8, z: 8, core: 2. Of those that a mesh axis runs over, the one named last changes fastest.
Arguments:
- tokens: bfloat16 [65536, 2048], P('ctx', 'head'), may hold values from -6 to 6
- w_qkv: bfloat16 [3, 2048, 2048], P(None, 'ctx', 'head'), may hold values from -0.125 to 0.125
- out_gain: float32 [2048], P('head'), may hold values from 0.25 to 1.75
- seg_ids: int32 [65536], P('ctx'), may hold values from 0 to 15, never falling along the last dimension, each value on 1 to 16384 neighbouring positions
Outputs:
- attended: bfloat16 [65536, 2048], P('ctx', 'head')
Inputs may be any that keep to these rules, and one draw needn't show every extreme that they name: `seg_ids`: segment numbers never fall along the stream; each segment covers 1 to 16384 consecutive tokens, and one covers exactly 16384.
All inputs are finite; a program needn't handle non-finite values.
Results may differ from a plain program's by a relative error of at most 0.012.
Values may be sent and summed in bfloat16 or wider, within the bound.
No kernel may reach another device: no remote copies, remote signals or barrier semaphores. Data moves between devices by JAX's collectives and lax.ppermute only.
A program may use at most 64 MiB of HBM per device.

v0:
```python
import jax
import jax.numpy as jnp
from jax import lax
from jax.sharding import PartitionSpec as P

HEAD_DIM = 128


def passed_along(value, axis, steps):
    count = lax.axis_size(axis)
    leading, last = (max(0, -steps), min(count, count - steps))
    return lax.ppermute(value, axis, [(source, source + steps) for source in range(leading, last)])


def feature_map(values):
    return (jax.nn.elu(values.astype(jnp.float32)) + 1.0).astype(jnp.bfloat16)


def combine(earlier, later):
    first_state, first_tail = earlier
    later_state, later_tail = later
    linked = (first_tail == later_tail) | (later_tail < 0.0)
    return (
        later_state + jnp.where(linked, first_state, 0.0),
        jnp.where(later_tail < 0.0, first_tail, later_tail),
    )


def prepare(projected, segment):
    row_count = segment.shape[0]
    head_count = projected.shape[2] // HEAD_DIM
    queries = feature_map(projected[0]).reshape(row_count, head_count, HEAD_DIM)
    key_map = feature_map(projected[1]).reshape(row_count, head_count, HEAD_DIM)
    values = projected[2].reshape(row_count, head_count, HEAD_DIM)
    seg_float = segment.astype(jnp.float32)
    tail_id = seg_float[-1]
    key_tail = jnp.where((seg_float == tail_id)[:, None, None], key_map, jnp.zeros_like(key_map))
    kv_state = jnp.einsum("thd,the->hde", key_tail, values, preferred_element_type=jnp.float32)
    return (queries, key_map, values, seg_float, kv_state, tail_id)


def complete(queries, key_map, values, seg_float, state_in, tail_in, out_gain):
    row_count, head_count = (queries.shape[0], queries.shape[1])
    state_low = state_in.astype(jnp.bfloat16)
    prefix = jnp.einsum("thd,hde->the", queries, state_low, preferred_element_type=jnp.float32)
    prefix = jnp.where((seg_float == tail_in)[:, None, None], prefix, 0.0)
    block_rows = min(512, row_count)
    positions = jnp.arange(row_count, dtype=jnp.int32)

    def one_block(blk_no):
        first_row = blk_no * block_rows
        query_blk = lax.dynamic_slice_in_dim(queries, first_row, block_rows, 0)
        query_pos = first_row + jnp.arange(block_rows, dtype=jnp.int32)
        query_seg = lax.dynamic_slice_in_dim(seg_float, first_row, block_rows, 0)
        scores = jnp.einsum("bhd,shd->hbs", query_blk, key_map, preferred_element_type=jnp.float32)
        visible = (positions[None, :] <= query_pos[:, None]) & (
            seg_float[None, :] == query_seg[:, None]
        )
        weights = jnp.where(visible[None], scores, 0.0).astype(jnp.bfloat16)
        return jnp.einsum("hbs,she->bhe", weights, values, preferred_element_type=jnp.float32)

    local_part = lax.map(one_block, jnp.arange(row_count // block_rows, dtype=jnp.int32))
    numerator = local_part.reshape(row_count, head_count, HEAD_DIM) + prefix
    inv_norm = lax.rsqrt(jnp.mean(numerator * numerator, axis=-1, keepdims=True) + 1e-05)
    result = numerator * inv_norm * out_gain.reshape(head_count, HEAD_DIM)
    return result.astype(jnp.bfloat16).reshape(row_count, head_count * HEAD_DIM)


def per_device(tokens, w_qkv, out_gain, seg_ids):
    whole = lax.all_gather(tokens, "head", axis=1, tiled=True)
    projected = jnp.einsum(
        "tr,grc->gtc",
        whole,
        lax.all_gather(w_qkv, "ctx", axis=1, tiled=True),
        preferred_element_type=jnp.float32,
    ).astype(jnp.bfloat16)
    queries, key_map, values, seg_float, kv_state, tail_id = prepare(projected, seg_ids)
    empty_state = jnp.zeros_like(kv_state)
    own_pair = (kv_state, tail_id)

    def hand_round(turn_no, carried):
        running, _ = carried
        incoming = (
            passed_along(running[0].astype(jnp.bfloat16), "ctx", 1).astype(jnp.float32),
            passed_along(running[1].astype(jnp.bfloat16), "ctx", 1).astype(jnp.float32),
        )
        return (combine(incoming, own_pair), incoming)

    start_pair = (empty_state, jnp.array(-1.0, jnp.float32))
    _, arrived = lax.fori_loop(0, lax.axis_size("ctx") - 1, hand_round, (own_pair, start_pair))
    state_in, tail_in = arrived
    return complete(queries, key_map, values, seg_float, state_in, tail_in, out_gain)


def solution(mesh):
    placed = (P("ctx", "head"), P(None, "ctx", "head"), P("head"), P("ctx"))
    return jax.shard_map(
        per_device, mesh=mesh, in_specs=placed, out_specs=P("ctx", "head"), check_vma=False
    )
```

profile of v0, /device:TPU:32, one launch (start us, length us, event | category | flops | bytes accessed | tf_op | source)
XLA Modules:
  0.0 1084.5 jit_solution(1804793181118891656)
XLA Ops:
  12.1 84.4 %all-gather.3.cloned.1.call-done = bf16[3,2048,256]{2,1,0:T(8,128)(2,1)} async-done(((bf16[3,32,256]{2,1,0:T(8,128)(2,1)}), bf16[3,2048,256]{2,1,0:T(8,128)(2,1)}) %all-gather.3.cloned.1.call-update) | async-done | bytes 3145744 | tf_op jit(solution)/shard_map/all_gather | solution.py:74
  96.5 67.6 %all-gather.5.cloned.1.call-done = bf16[1024,2048]{1,0:T(8,128)(2,1)} async-done(((bf16[1024,256]{1,0:T(8,128)(2,1)}), bf16[1024,2048]{1,0:T(8,128)(2,1)}) %all-gather.5.cloned.1.call-update) | async-done | bytes 4194320 | tf_op jit(solution)/shard_map/all_gather | solution.py:70
  164.0 6.6 fusion.15
  176.5 877.2 %while.28 = (s32[]{:T(128)}, bf16[2,128,128]{2,1,0:T(8,128)(2,1)S(1)}, bf16[]{:T(256)}, bf16[2,128,128]{2,1,0:T(8,128)(2,1)}, f32[]{:T(128)}, /*index=5*/f32[]{:...) while((s32[]{:T(128)}, bf16[2,128,128]{2,1,0:T(8,128)(2,1)S(1)}, bf16[]{:T(256)}, ...), condition=%wide.region_3.4_spmd, body=%wide.region_2.3_spmd.sunk | while | flops 163846 | bytes 590031 | solution.py:90
  195.3 5.4 collective-permute-done
  209.2 5.4 collective-permute-done
  223.1 5.4 collective-permute-done
  264.9 5.4 collective-permute-done
  278.8 5.4 collective-permute-done
  292.7 5.4 collective-permute-done
  306.6 5.4 collective-permute-done
  320.6 5.4 collective-permute-done
  334.5 5.4 collective-permute-done
  348.4 5.4 collective-permute-done
  362.3 5.4 collective-permute-done
  404.1 5.4 collective-permute-done
  418.0 5.4 collective-permute-done
  432.0 5.4 collective-permute-done
  445.9 5.4 collective-permute-done
  459.8 5.4 collective-permute-done
  473.7 5.4 collective-permute-done
  487.6 5.4 collective-permute-done
  529.4 5.4 collective-permute-done
  543.3 5.4 collective-permute-done
  557.3 5.4 collective-permute-done
  571.2 5.4 collective-permute-done
  585.1 5.4 collective-permute-done
  599.0 5.4 collective-permute-done
  613.0 5.4 collective-permute-done
  626.9 5.4 collective-permute-done
  668.6 5.4 collective-permute-done
  1056.0 19.2 %while.29 = (s32[]{:T(128)}, f32[2,512,2,128]{1,0,3,2:T(2,128)S(1)}, s32[2]{0:T(128)S(1)}, f32[1024]{0:T(1024)S(1)}, bf16[1024,2,128]{2,1,0:T(2,128)(2,1)S(1)}, ...) while((s32[]{:T(128)}, ...), condition=%wide.region_1.2_spmd.clone, body=%wide.region_0.1_spmd.clone.sunk | while | flops 540541440 | bytes 5519551 | solution.py:62
  (335 shorter events, 568.7 us)
Async XLA Ops:
  6.5 89.9 %all-gather.3.cloned.1.call-start = ((), (), s32[]{:S(2)}) async-start(), calls=%async_computation | async-start | bytes 3194880 | tf_op jit(solution)/shard_map/all_gather | solution.py:74
  7.3 156.8 %all-gather.5.cloned.1.call-start = ((), (), s32[]{:S(2)}) async-start(), calls=%async_computation.1 | async-start | bytes 4718592 | tf_op jit(solution)/shard_map/all_gather | solution.py:70
  176.5 13.3 %collective-permute-start.1 = (bf16[2,128,128]{2,1,0:T(8,128)(2,1)S(1)}, bf16[2,128,128]{2,1,0:T(8,128)(2,1)S(1)}, u32[]{:S(2)}, u32[]{:S(2)}) collective-permute-start(bf16[2,128,128]{2,1,0:T(8,128)(2,1)S(1)} %get-tuple-element.318), channel_id=1, source_target_pairs={{0,8},{8,16},{16,24},{24,32},{32,40},{40,48},{48,56},{56,64},{64,7... | collective-permute-start | bytes 196616 | tf_op jit(solution)/shard_map/while/body/eval_jaxpr/ppermute | solution.py:12
  190.5 13.3 %collective-permute-start.1 = (bf16[2,128,128]{2,1,0:T(8,128)(2,1)S(1)}, bf16[2,128,128]{2,1,0:T(8,128)(2,1)S(1)}, u32[]{:S(2)}, u32[]{:S(2)}) collective-permute-start(bf16[2,128,128]{2,1,0:T(8,128)(2,1)S(1)} %get-tuple-element.318), channel_id=1, source_target_pairs={{0,8},{8,16},{16,24},{24,32},{32,40},{40,48},{48,56},{56,64},{64,7... | collective-permute-start | bytes 196616 | tf_op jit(solution)/shard_map/while/body/eval_jaxpr/ppermute | solution.py:12
  204.4 13.3 %collective-permute-start.1 = (bf16[2,128,128]{2,1,0:T(8,128)(2,1)S(1)}, bf16[2,128,128]{2,1,0:T(8,128)(2,1)S(1)}, u32[]{:S(2)}, u32[]{:S(2)}) collective-permute-start(bf16[2,128,128]{2,1,0:T(8,128)(2,1)S(1)} %get-tuple-element.318), channel_id=1, source_target_pairs={{0,8},{8,16},{16,24},{24,32},{32,40},{40,48},{48,56},{56,64},{64,7... | collective-permute-start | bytes 196616 | tf_op jit(solution)/shard_map/while/body/eval_jaxpr/ppermute | solution.py:12
  218.3 13.3 %collective-permute-start.1 = (bf16[2,128,128]{2,1,0:T(8,128)(2,1)S(1)}, bf16[2,128,128]{2,1,0:T(8,128)(2,1)S(1)}, u32[]{:S(2)}, u32[]{:S(2)}) collective-permute-start(bf16[2,128,128]{2,1,0:T(8,128)(2,1)S(1)} %get-tuple-element.318), channel_id=1, source_target_pairs={{0,8},{8,16},{16,24},{24,32},{32,40},{40,48},{48,56},{56,64},{64,7... | collective-permute-start | bytes 196616 | tf_op jit(solution)/shard_map/while/body/eval_jaxpr/ppermute | solution.py:12
  287.9 13.3 %collective-permute-start.1 = (bf16[2,128,128]{2,1,0:T(8,128)(2,1)S(1)}, bf16[2,128,128]{2,1,0:T(8,128)(2,1)S(1)}, u32[]{:S(2)}, u32[]{:S(2)}) collective-permute-start(bf16[2,128,128]{2,1,0:T(8,128)(2,1)S(1)} %get-tuple-element.318), channel_id=1, source_target_pairs={{0,8},{8,16},{16,24},{24,32},{32,40},{40,48},{48,56},{56,64},{64,7... | collective-permute-start | bytes 196616 | tf_op jit(solution)/shard_map/while/body/eval_jaxpr/ppermute | solution.py:12
  301.9 13.3 %collective-permute-start.1 = (bf16[2,128,128]{2,1,0:T(8,128)(2,1)S(1)}, bf16[2,128,128]{2,1,0:T(8,128)(2,1)S(1)}, u32[]{:S(2)}, u32[]{:S(2)}) collective-permute-start(bf16[2,128,128]{2,1,0:T(8,128)(2,1)S(1)} %get-tuple-element.318), channel_id=1, source_target_pairs={{0,8},{8,16},{16,24},{24,32},{32,40},{40,48},{48,56},{56,64},{64,7... | collective-permute-start | bytes 196616 | tf_op jit(solution)/shard_map/while/body/eval_jaxpr/ppermute | solution.py:12
  315.8 13.3 %collective-permute-start.1 = (bf16[2,128,128]{2,1,0:T(8,128)(2,1)S(1)}, bf16[2,128,128]{2,1,0:T(8,128)(2,1)S(1)}, u32[]{:S(2)}, u32[]{:S(2)}) collective-permute-start(bf16[2,128,128]{2,1,0:T(8,128)(2,1)S(1)} %get-tuple-element.318), channel_id=1, source_target_pairs={{0,8},{8,16},{16,24},{24,32},{32,40},{40,48},{48,56},{56,64},{64,7... | collective-permute-start | bytes 196616 | tf_op jit(solution)/shard_map/while/body/eval_jaxpr/ppermute | solution.py:12
  329.7 13.3 %collective-permute-start.1 = (bf16[2,128,128]{2,1,0:T(8,128)(2,1)S(1)}, bf16[2,128,128]{2,1,0:T(8,128)(2,1)S(1)}, u32[]{:S(2)}, u32[]{:S(2)}) collective-permute-start(bf16[2,128,128]{2,1,0:T(8,128)(2,1)S(1)} %get-tuple-element.318), channel_id=1, source_target_pairs={{0,8},{8,16},{16,24},{24,32},{32,40},{40,48},{48,56},{56,64},{64,7... | collective-permute-start | bytes 196616 | tf_op jit(solution)/shard_map/while/body/eval_jaxpr/ppermute | solution.py:12
  343.6 13.3 %collective-permute-start.1 = (bf16[2,128,128]{2,1,0:T(8,128)(2,1)S(1)}, bf16[2,128,128]{2,1,0:T(8,128)(2,1)S(1)}, u32[]{:S(2)}, u32[]{:S(2)}) collective-permute-start(bf16[2,128,128]{2,1,0:T(8,128)(2,1)S(1)} %get-tuple-element.318), channel_id=1, source_target_pairs={{0,8},{8,16},{16,24},{24,32},{32,40},{40,48},{48,56},{56,64},{64,7... | collective-permute-start | bytes 196616 | tf_op jit(solution)/shard_map/while/body/eval_jaxpr/ppermute | solution.py:12
  413.3 13.3 %collective-permute-start.1 = (bf16[2,128,128]{2,1,0:T(8,128)(2,1)S(1)}, bf16[2,128,128]{2,1,0:T(8,128)(2,1)S(1)}, u32[]{:S(2)}, u32[]{:S(2)}) collective-permute-start(bf16[2,128,128]{2,1,0:T(8,128)(2,1)S(1)} %get-tuple-element.318), channel_id=1, source_target_pairs={{0,8},{8,16},{16,24},{24,32},{32,40},{40,48},{48,56},{56,64},{64,7... | collective-permute-start | bytes 196616 | tf_op jit(solution)/shard_map/while/body/eval_jaxpr/ppermute | solution.py:12
  427.2 13.3 %collective-permute-start.1 = (bf16[2,128,128]{2,1,0:T(8,128)(2,1)S(1)}, bf16[2,128,128]{2,1,0:T(8,128)(2,1)S(1)}, u32[]{:S(2)}, u32[]{:S(2)}) collective-permute-start(bf16[2,128,128]{2,1,0:T(8,128)(2,1)S(1)} %get-tuple-element.318), channel_id=1, source_target_pairs={{0,8},{8,16},{16,24},{24,32},{32,40},{40,48},{48,56},{56,64},{64,7... | collective-permute-start | bytes 196616 | tf_op jit(solution)/shard_map/while/body/eval_jaxpr/ppermute | solution.py:12
  441.1 13.3 %collective-permute-start.1 = (bf16[2,128,128]{2,1,0:T(8,128)(2,1)S(1)}, bf16[2,128,128]{2,1,0:T(8,128)(2,1)S(1)}, u32[]{:S(2)}, u32[]{:S(2)}) collective-permute-start(bf16[2,128,128]{2,1,0:T(8,128)(2,1)S(1)} %get-tuple-element.318), channel_id=1, source_target_pairs={{0,8},{8,16},{16,24},{24,32},{32,40},{40,48},{48,56},{56,64},{64,7... | collective-permute-start | bytes 196616 | tf_op jit(solution)/shard_map/while/body/eval_jaxpr/ppermute | solution.py:12
  455.0 13.3 %collective-permute-start.1 = (bf16[2,128,128]{2,1,0:T(8,128)(2,1)S(1)}, bf16[2,128,128]{2,1,0:T(8,128)(2,1)S(1)}, u32[]{:S(2)}, u32[]{:S(2)}) collective-permute-start(bf16[2,128,128]{2,1,0:T(8,128)(2,1)S(1)} %get-tuple-element.318), channel_id=1, source_target_pairs={{0,8},{8,16},{16,24},{24,32},{32,40},{40,48},{48,56},{56,64},{64,7... | collective-permute-start | bytes 196616 | tf_op jit(solution)/shard_map/while/body/eval_jaxpr/ppermute | solution.py:12
  468.9 13.3 %collective-permute-start.1 = (bf16[2,128,128]{2,1,0:T(8,128)(2,1)S(1)}, bf16[2,128,128]{2,1,0:T(8,128)(2,1)S(1)}, u32[]{:S(2)}, u32[]{:S(2)}) collective-permute-start(bf16[2,128,128]{2,1,0:T(8,128)(2,1)S(1)} %get-tuple-element.318), channel_id=1, source_target_pairs={{0,8},{8,16},{16,24},{24,32},{32,40},{40,48},{48,56},{56,64},{64,7... | collective-permute-start | bytes 196616 | tf_op jit(solution)/shard_map/while/body/eval_jaxpr/ppermute | solution.py:12
  482.9 13.3 %collective-permute-start.1 = (bf16[2,128,128]{2,1,0:T(8,128)(2,1)S(1)}, bf16[2,128,128]{2,1,0:T(8,128)(2,1)S(1)}, u32[]{:S(2)}, u32[]{:S(2)}) collective-permute-start(bf16[2,128,128]{2,1,0:T(8,128)(2,1)S(1)} %get-tuple-element.318), channel_id=1, source_target_pairs={{0,8},{8,16},{16,24},{24,32},{32,40},{40,48},{48,56},{56,64},{64,7... | collective-permute-start | bytes 196616 | tf_op jit(solution)/shard_map/while/body/eval_jaxpr/ppermute | solution.py:12
  552.5 13.3 %collective-permute-start.1 = (bf16[2,128,128]{2,1,0:T(8,128)(2,1)S(1)}, bf16[2,128,128]{2,1,0:T(8,128)(2,1)S(1)}, u32[]{:S(2)}, u32[]{:S(2)}) collective-permute-start(bf16[2,128,128]{2,1,0:T(8,128)(2,1)S(1)} %get-tuple-element.318), channel_id=1, source_target_pairs={{0,8},{8,16},{16,24},{24,32},{32,40},{40,48},{48,56},{56,64},{64,7... | collective-permute-start | bytes 196616 | tf_op jit(solution)/shard_map/while/body/eval_jaxpr/ppermute | solution.py:12
  566.4 13.3 %collective-permute-start.1 = (bf16[2,128,128]{2,1,0:T(8,128)(2,1)S(1)}, bf16[2,128,128]{2,1,0:T(8,128)(2,1)S(1)}, u32[]{:S(2)}, u32[]{:S(2)}) collective-permute-start(bf16[2,128,128]{2,1,0:T(8,128)(2,1)S(1)} %get-tuple-element.318), channel_id=1, source_target_pairs={{0,8},{8,16},{16,24},{24,32},{32,40},{40,48},{48,56},{56,64},{64,7... | collective-permute-start | bytes 196616 | tf_op jit(solution)/shard_map/while/body/eval_jaxpr/ppermute | solution.py:12
  580.3 13.3 %collective-permute-start.1 = (bf16[2,128,128]{2,1,0:T(8,128)(2,1)S(1)}, bf16[2,128,128]{2,1,0:T(8,128)(2,1)S(1)}, u32[]{:S(2)}, u32[]{:S(2)}) collective-permute-start(bf16[2,128,128]{2,1,0:T(8,128)(2,1)S(1)} %get-tuple-element.318), channel_id=1, source_target_pairs={{0,8},{8,16},{16,24},{24,32},{32,40},{40,48},{48,56},{56,64},{64,7... | collective-permute-start | bytes 196616 | tf_op jit(solution)/shard_map/while/body/eval_jaxpr/ppermute | solution.py:12
  594.3 13.3 %collective-permute-start.1 = (bf16[2,128,128]{2,1,0:T(8,128)(2,1)S(1)}, bf16[2,128,128]{2,1,0:T(8,128)(2,1)S(1)}, u32[]{:S(2)}, u32[]{:S(2)}) collective-permute-start(bf16[2,128,128]{2,1,0:T(8,128)(2,1)S(1)} %get-tuple-element.318), channel_id=1, source_target_pairs={{0,8},{8,16},{16,24},{24,32},{32,40},{40,48},{48,56},{56,64},{64,7... | collective-permute-start | bytes 196616 | tf_op jit(solution)/shard_map/while/body/eval_jaxpr/ppermute | solution.py:12
  608.2 13.3 %collective-permute-start.1 = (bf16[2,128,128]{2,1,0:T(8,128)(2,1)S(1)}, bf16[2,128,128]{2,1,0:T(8,128)(2,1)S(1)}, u32[]{:S(2)}, u32[]{:S(2)}) collective-permute-start(bf16[2,128,128]{2,1,0:T(8,128)(2,1)S(1)} %get-tuple-element.318), channel_id=1, source_target_pairs={{0,8},{8,16},{16,24},{24,32},{32,40},{40,48},{48,56},{56,64},{64,7... | collective-permute-start | bytes 196616 | tf_op jit(solution)/shard_map/while/body/eval_jaxpr/ppermute | solution.py:12
  677.8 13.3 %collective-permute-start.1 = (bf16[2,128,128]{2,1,0:T(8,128)(2,1)S(1)}, bf16[2,128,128]{2,1,0:T(8,128)(2,1)S(1)}, u32[]{:S(2)}, u32[]{:S(2)}) collective-permute-start(bf16[2,128,128]{2,1,0:T(8,128)(2,1)S(1)} %get-tuple-element.318), channel_id=1, source_target_pairs={{0,8},{8,16},{16,24},{24,32},{32,40},{40,48},{48,56},{56,64},{64,7... | collective-permute-start | bytes 196616 | tf_op jit(solution)/shard_map/while/body/eval_jaxpr/ppermute | solution.py:12
  691.7 13.3 %collective-permute-start.1 = (bf16[2,128,128]{2,1,0:T(8,128)(2,1)S(1)}, bf16[2,128,128]{2,1,0:T(8,128)(2,1)S(1)}, u32[]{:S(2)}, u32[]{:S(2)}) collective-permute-start(bf16[2,128,128]{2,1,0:T(8,128)(2,1)S(1)} %get-tuple-element.318), channel_id=1, source_target_pairs={{0,8},{8,16},{16,24},{24,32},{32,40},{40,48},{48,56},{56,64},{64,7... | collective-permute-start | bytes 196616 | tf_op jit(solution)/shard_map/while/body/eval_jaxpr/ppermute | solution.py:12
  705.6 13.3 %collective-permute-start.1 = (bf16[2,128,128]{2,1,0:T(8,128)(2,1)S(1)}, bf16[2,128,128]{2,1,0:T(8,128)(2,1)S(1)}, u32[]{:S(2)}, u32[]{:S(2)}) collective-permute-start(bf16[2,128,128]{2,1,0:T(8,128)(2,1)S(1)} %get-tuple-element.318), channel_id=1, source_target_pairs={{0,8},{8,16},{16,24},{24,32},{32,40},{40,48},{48,56},{56,64},{64,7... | collective-permute-start | bytes 196616 | tf_op jit(solution)/shard_map/while/body/eval_jaxpr/ppermute | solution.py:12
  719.6 13.3 %collective-permute-start.1 = (bf16[2,128,128]{2,1,0:T(8,128)(2,1)S(1)}, bf16[2,128,128]{2,1,0:T(8,128)(2,1)S(1)}, u32[]{:S(2)}, u32[]{:S(2)}) collective-permute-start(bf16[2,128,128]{2,1,0:T(8,128)(2,1)S(1)} %get-tuple-element.318), channel_id=1, source_target_pairs={{0,8},{8,16},{16,24},{24,32},{32,40},{40,48},{48,56},{56,64},{64,7... | collective-permute-start | bytes 196616 | tf_op jit(solution)/shard_map/while/body/eval_jaxpr/ppermute | solution.py:12
  733.5 13.3 %collective-permute-start.1 = (bf16[2,128,128]{2,1,0:T(8,128)(2,1)S(1)}, bf16[2,128,128]{2,1,0:T(8,128)(2,1)S(1)}, u32[]{:S(2)}, u32[]{:S(2)}) collective-permute-start(bf16[2,128,128]{2,1,0:T(8,128)(2,1)S(1)} %get-tuple-element.318), channel_id=1, source_target_pairs={{0,8},{8,16},{16,24},{24,32},{32,40},{40,48},{48,56},{56,64},{64,7... | collective-permute-start | bytes 196616 | tf_op jit(solution)/shard_map/while/body/eval_jaxpr/ppermute | solution.py:12
  747.4 13.3 %collective-permute-start.1 = (bf16[2,128,128]{2,1,0:T(8,128)(2,1)S(1)}, bf16[2,128,128]{2,1,0:T(8,128)(2,1)S(1)}, u32[]{:S(2)}, u32[]{:S(2)}) collective-permute-start(bf16[2,128,128]{2,1,0:T(8,128)(2,1)S(1)} %get-tuple-element.318), channel_id=1, source_target_pairs={{0,8},{8,16},{16,24},{24,32},{32,40},{40,48},{48,56},{56,64},{64,7... | collective-permute-start | bytes 196616 | tf_op jit(solution)/shard_map/while/body/eval_jaxpr/ppermute | solution.py:12
  817.0 13.3 %collective-permute-start.1 = (bf16[2,128,128]{2,1,0:T(8,128)(2,1)S(1)}, bf16[2,128,128]{2,1,0:T(8,128)(2,1)S(1)}, u32[]{:S(2)}, u32[]{:S(2)}) collective-permute-start(bf16[2,128,128]{2,1,0:T(8,128)(2,1)S(1)} %get-tuple-element.318), channel_id=1, source_target_pairs={{0,8},{8,16},{16,24},{24,32},{32,40},{40,48},{48,56},{56,64},{64,7... | collective-permute-start | bytes 196616 | tf_op jit(solution)/shard_map/while/body/eval_jaxpr/ppermute | solution.py:12
  830.9 13.3 %collective-permute-start.1 = (bf16[2,128,128]{2,1,0:T(8,128)(2,1)S(1)}, bf16[2,128,128]{2,1,0:T(8,128)(2,1)S(1)}, u32[]{:S(2)}, u32[]{:S(2)}) collective-permute-start(bf16[2,128,128]{2,1,0:T(8,128)(2,1)S(1)} %get-tuple-element.318), channel_id=1, source_target_pairs={{0,8},{8,16},{16,24},{24,32},{32,40},{40,48},{48,56},{56,64},{64,7... | collective-permute-start | bytes 196616 | tf_op jit(solution)/shard_map/while/body/eval_jaxpr/ppermute | solution.py:12
  844.9 13.3 %collective-permute-start.1 = (bf16[2,128,128]{2,1,0:T(8,128)(2,1)S(1)}, bf16[2,128,128]{2,1,0:T(8,128)(2,1)S(1)}, u32[]{:S(2)}, u32[]{:S(2)}) collective-permute-start(bf16[2,128,128]{2,1,0:T(8,128)(2,1)S(1)} %get-tuple-element.318), channel_id=1, source_target_pairs={{0,8},{8,16},{16,24},{24,32},{32,40},{40,48},{48,56},{56,64},{64,7... | collective-permute-start | bytes 196616 | tf_op jit(solution)/shard_map/while/body/eval_jaxpr/ppermute | solution.py:12
  858.8 13.3 %collective-permute-start.1 = (bf16[2,128,128]{2,1,0:T(8,128)(2,1)S(1)}, bf16[2,128,128]{2,1,0:T(8,128)(2,1)S(1)}, u32[]{:S(2)}, u32[]{:S(2)}) collective-permute-start(bf16[2,128,128]{2,1,0:T(8,128)(2,1)S(1)} %get-tuple-element.318), channel_id=1, source_target_pairs={{0,8},{8,16},{16,24},{24,32},{32,40},{40,48},{48,56},{56,64},{64,7... | collective-permute-start | bytes 196616 | tf_op jit(solution)/shard_map/while/body/eval_jaxpr/ppermute | solution.py:12
  (100 other events, 2743.7 us)
Sparse Core Ops, SparseCore 0:
  10.8 85.6 all-gather.2
  98.5 65.5 all-gather.4
where the time goes:
time: 1090 us; the launch traced here: 1080 us
  waiting for transfers between devices  494 us (45%)
  starting transfers between devices  302 us (28%)
  loops' own time  196 us (18%)
  other arithmetic  50.1 us (5%)
  local copies, waits for them, and re-layouts  16.1 us (1%)
  between operations  14.9 us (1%)
  matrix products  11.9 us (1%)
    ppermute x126, waiting for transfers between devices, passed_along(): lax.ppermute(value, axis, [(source, source + steps) for source in range(l...  340 us
    ppermute x126, starting transfers between devices, passed_along(): lax.ppermute(value, axis, [(source, source + steps) for source in range(l...  302 us
    another operation x1, loops' own time, per_device(): lax.fori_loop(0, lax.axis_size('ctx') - 1, hand_round, (own_pair, start_p...  194 us
    all_gather x1, waiting for transfers between devices, per_device(): lax.all_gather(w_qkv, 'ctx', axis=1, tiled=True)  84.4 us
    all_gather x1, waiting for transfers between devices, per_device(): whole = lax.all_gather(tokens, 'head', axis=1, tiled=True)  67.6 us
    add x63, other arithmetic, combine(): later_state + jnp.where(linked, first_state, 0.0)  40.5 us
  transfers between devices with their start and end apart: 128, of which 65 were waited for; matrix products, arithmetic and copies ran while one was open for 0% of the time, Pallas kernels for 0%

commit v1 on v0

v1 whole, which is shorter than its diff:
```python
import jax
import jax.numpy as jnp
from jax import lax
from jax.sharding import PartitionSpec as P

HEAD_DIM = 128
SPAN = 16384


def shifted(value, axis, steps):
    count = lax.axis_size(axis)
    return lax.ppermute(value, axis, [(source, source + steps) for source in range(count - steps)])


def feature_map(values):
    return (jax.nn.elu(values.astype(jnp.float32)) + 1.0).astype(jnp.bfloat16)


def state_scan(kv_state, tail_id, row_count):
    head_count = kv_state.shape[0]
    flat = kv_state.reshape(head_count * HEAD_DIM, HEAD_DIM)
    tail_rows = jnp.full((8, HEAD_DIM), tail_id, jnp.float32)
    packed = jnp.concatenate([flat, tail_rows], axis=0)
    state_rows = head_count * HEAD_DIM
    is_state = (jnp.arange(packed.shape[0]) < state_rows)[:, None]
    count = lax.axis_size("ctx")
    window = min(count - 1, 1 + (SPAN - 1) // row_count)
    running = shifted(packed, "ctx", 1)
    step = 1
    while step < window:
        incoming = shifted(running, "ctx", step)
        linked = incoming[state_rows, 0] == running[state_rows, 0]
        running = running + jnp.where(is_state & linked, incoming, 0.0)
        step *= 2
    state_in = running[:state_rows].reshape(head_count, HEAD_DIM, HEAD_DIM)
    return state_in, running[state_rows, 0]


def per_device(tokens, w_qkv, out_gain, seg_ids):
    whole = lax.all_gather(tokens, "head", axis=1, tiled=True)
    projected = jnp.einsum(
        "tr,grc->gtc",
        whole,
        lax.all_gather(w_qkv, "ctx", axis=1, tiled=True),
        preferred_element_type=jnp.float32,
    ).astype(jnp.bfloat16)
    row_count = seg_ids.shape[0]
    head_count = projected.shape[2] // HEAD_DIM
    queries = feature_map(projected[0]).reshape(row_count, head_count, HEAD_DIM)
    key_map = feature_map(projected[1]).reshape(row_count, head_count, HEAD_DIM)
    values = projected[2].reshape(row_count, head_count, HEAD_DIM)
    seg_float = seg_ids.astype(jnp.float32)
    tail_id = seg_float[-1]
    key_tail = jnp.where((seg_float == tail_id)[:, None, None], key_map, jnp.zeros_like(key_map))
    kv_state = jnp.einsum("thd,the->hde", key_tail, values, preferred_element_type=jnp.float32)

    state_in, tail_in = state_scan(kv_state, tail_id, row_count)

    block_rows = min(512, row_count)
    pieces = []
    for blk_no in range(row_count // block_rows):
        first_row = blk_no * block_rows
        key_end = first_row + block_rows
        query_blk = queries[first_row:key_end]
        query_pos = first_row + jnp.arange(block_rows, dtype=jnp.int32)
        query_seg = seg_float[first_row:key_end]
        scores = jnp.einsum(
            "bhd,shd->hbs", query_blk, key_map[:key_end], preferred_element_type=jnp.float32
        )
        visible = (jnp.arange(key_end, dtype=jnp.int32)[None, :] <= query_pos[:, None]) & (
            seg_float[None, :key_end] == query_seg[:, None]
        )
        weights = jnp.where(visible[None], scores, 0.0).astype(jnp.bfloat16)
        pieces.append(
            jnp.einsum("hbs,she->bhe", weights, values[:key_end], preferred_element_type=jnp.float32)
        )
    local_part = jnp.concatenate(pieces, axis=0)

    state_low = state_in.astype(jnp.bfloat16)
    prefix = jnp.einsum("thd,hde->the", queries, state_low, preferred_element_type=jnp.float32)
    prefix = jnp.where((seg_float == tail_in)[:, None, None], prefix, 0.0)
    numerator = local_part + prefix
    inv_norm = lax.rsqrt(jnp.mean(numerator * numerator, axis=-1, keepdims=True) + 1e-05)
    result = numerator * inv_norm * out_gain.reshape(head_count, HEAD_DIM)
    return result.astype(jnp.bfloat16).reshape(row_count, head_count * HEAD_DIM)


def solution(mesh):
    placed = (P("ctx", "head"), P(None, "ctx", "head"), P("head"), P("ctx"))
    return jax.shard_map(
        per_device, mesh=mesh, in_specs=placed, out_specs=P("ctx", "head"), check_vma=False
    )
```

time: 1090 us -> 245 us (0.22)
  waiting for transfers between devices: 494 us -> 180 us
  starting transfers between devices: 302 us -> 9.63 us
  loops' own time: 196 us -> 0 us
  other arithmetic: 50.1 us -> 7.82 us
    ppermute x126 -> x5, waiting for transfers between devices: 340 us -> 27.2 us  [shifted(): lax.ppermute(value, axis, [(source, source + steps) for source in range(c...]
    ppermute x126 -> x5, starting transfers between devices: 302 us -> 9.59 us  [shifted(): lax.ppermute(value, axis, [(source, source + steps) for source in range(c...]
    another operation x2 -> x0, loops' own time: 196 us -> none  [the longest x1 194 us: per_device(): lax.fori_loop(0, lax.axis_size('ctx') - 1, hand_round, (own_pair, start_p...]
    add x65 -> x5, other arithmetic: 40.5 us -> 1.32 us  [the longest x4 1.32 us: state_scan(): running = running + jnp.where(is_state & linked, incoming, 0.0)]
  transfers between devices with their start and end apart: 128 -> 7, of which waited for: 65 -> 7; matrix products, arithmetic and copies ran while one was open for 0% -> 6% of each run, Pallas kernels for 0% -> 0%
where the time goes in v1:
time: 245 us
  waiting for transfers between devices  180 us (73%)
  between operations  18.7 us (8%)
  matrix products  17 us (7%)
  local copies, waits for them, and re-layouts  11.1 us (5%)
  starting transfers between devices  9.63 us (4%)
  other arithmetic  7.82 us (3%)
    all_gather x1, waiting for transfers between devices, per_device(): lax.all_gather(w_qkv, 'ctx', axis=1, tiled=True)  84.3 us
    all_gather x1, waiting for transfers between devices, per_device(): whole = lax.all_gather(tokens, 'head', axis=1, tiled=True)  67.6 us
    ppermute x5, waiting for transfers between devices, shifted(): lax.ppermute(value, axis, [(source, source + steps) for source in range(c...  27.2 us
    ppermute x5, starting transfers between devices, shifted(): lax.ppermute(value, axis, [(source, source + steps) for source in range(c...  9.59 us
    dot_general x1, matrix products, per_device(): jnp.einsum('tr,grc->gtc', whole, lax.all_gather(w_qkv, 'ctx', axis=1, til...  6.6 us
    dot_general x2, matrix products, per_device(): jnp.einsum('hbs,she->bhe', weights, values[:key_end], preferred_element_t...  6.48 us
    slice x8, local copies, waits for them, and re-layouts, state_scan(): linked = incoming[state_rows, 0] == running[state_rows, 0]  5.04 us
  transfers between devices with their start and end apart: 7, of which 7 were waited for; matrix products, arithmetic and copies ran while one was open for 6% of the time, Pallas kernels for 0%

profile of v1, /device:TPU:32, one launch (start us, length us, event | category | flops | bytes accessed | tf_op | source)
XLA Modules:
  0.0 244.8 jit_solution(2544516807584703272)
XLA Ops:
  6.5 0.7 all-gather.3.cloned.1.call-update
  7.3 0.7 all-gather.5.cloned.1.call-update
  8.0 0.7 convert_element_type.60
  8.7 0.6 slice.88
  9.3 1.3 broadcast_compare_fusion.1
  10.9 1.3 fusion.2
  12.2 84.3 %all-gather.3.cloned.1.call-done = bf16[3,2048,256]{2,1,0:T(8,128)(2,1)} async-done(((bf16[3,32,256]{2,1,0:T(8,128)(2,1)}), bf16[3,2048,256]{2,1,0:T(8,128)(2,1)}) %all-gather.3.cloned.1.call-update) | async-done | bytes 3145744 | tf_op jit(solution)/shard_map/all_gather | solution.py:44
  96.5 67.6 %all-gather.5.cloned.1.call-done = bf16[1024,2048]{1,0:T(8,128)(2,1)} async-done(((bf16[1024,256]{1,0:T(8,128)(2,1)}), bf16[1024,2048]{1,0:T(8,128)(2,1)}) %all-gather.5.cloned.1.call-update) | async-done | bytes 4194320 | tf_op jit(solution)/shard_map/all_gather | solution.py:40
  164.0 6.6 %fusion.7 = bf16[3,1024,256]{1,2,0:T(8,128)(2,1)S(1)} fusion(bf16[3,2048,256]{2,1,0:T(8,128)(2,1)} %all-gather.3.cloned.1.call-done, bf16[1024,2048]{1,0:T(8,128)(2,1)} %all-gather.5.cloned.1.call-done), kind=kOutput, calls=%fused_computation.16 | convolution fusion | flops 3222011904 | bytes 8912896 | tf_op jit(solution)/shard_map/tr,grc->gtc/dot_general | solution.py:41
  170.7 1.5 slice_convert_fusion.1
  172.2 1.3 copy.14
  173.5 2.1 fusion.31
  175.6 0.7 concatenate.7
  176.2 1.9 collective-permute-start
  178.6 7.2 %collective-permute-done = f32[264,128]{1,0:T(8,128)S(1)} collective-permute-done((f32[264,128]{1,0:T(8,128)S(1)}, f32[264,128]{1,0:T(8,128)S(1)}, u32[]{:S(2)}, u32[]{:S(2)}) %collective-permute-start) | collective-permute-done | bytes 135200 | tf_op jit(solution)/shard_map/ppermute | solution.py:12
  185.9 1.9 collective-permute-start.1
  187.8 0.8 fusion.50
  189.2 6.3 %collective-permute-done.1 = f32[264,128]{1,0:T(8,128)S(1)} collective-permute-done((f32[264,128]{1,0:T(8,128)S(1)}, f32[264,128]{1,0:T(8,128)S(1)}, u32[]{:S(2)}, u32[]{:S(2)}) %collective-permute-start.1) | collective-permute-done | bytes 135200 | tf_op jit(solution)/shard_map/ppermute | solution.py:12
  197.4 1.9 collective-permute-start.2
  199.3 3.9 %fusion.13 = f32[512,2,128]{0,2,1:T(8,128)} fusion(bf16[1024,2,128]{0,2,1:T(8,128)(2,1)S(1)} %bitcast.50, bf16[512,2,128]{0,2,1:T(8,128)(2,1)} %bitcast.54, pred[512,1024]{1,0:T(8,128)(4,1)} %fusion.2, f32[1024,2,128]{2,0,1:T(8,128)} %copy.14), kind=kOutput, calls=%fused_computation.21 | convolution fusion | flops 540278784 | bytes 2883584 | tf_op jit(solution)/shard_map/hbs,she->bhe/dot_general | solution.py:75
  203.2 0.7 slice.99
  204.8 2.9 %collective-permute-done.2 = f32[264,128]{1,0:T(8,128)} collective-permute-done((f32[264,128]{1,0:T(8,128)S(1)}, f32[264,128]{1,0:T(8,128)}, u32[]{:S(2)}, u32[]{:S(2)}) %collective-permute-start.2) | collective-permute-done | bytes 135200 | tf_op jit(solution)/shard_map/ppermute | solution.py:12
  207.7 1.2 slice.108
  210.2 1.0 select_add_fusion.2
  211.2 1.9 collective-permute-start.3
  213.9 7.8 %collective-permute-done.3 = f32[264,128]{1,0:T(8,128)S(1)} collective-permute-done((f32[264,128]{1,0:T(8,128)S(1)}, f32[264,128]{1,0:T(8,128)S(1)}, u32[]{:S(2)}, u32[]{:S(2)}) %collective-permute-start.3) | collective-permute-done | bytes 135200 | tf_op jit(solution)/shard_map/ppermute | solution.py:12
  223.7 1.9 collective-permute-start.4
  225.6 2.6 %fusion.14 = f32[512,2,128]{0,2,1:T(8,128)} fusion(bf16[512,2,128]{0,2,1:T(8,128)(2,1)} %bitcast.52, bf16[512,2,128]{0,2,1:T(8,128)(2,1)} %bitcast.53, bf16[512,2,128]{0,2,1:T(8,128)(2,1)S(1)} %bitcast.51, pred[512,512]{1,0:T(8,128)(4,1)S(1)} %fusion.25), kind=kOutput, calls=%fused_computation.22 | convolution fusion | flops 269484032 | bytes 1572864 | tf_op jit(solution)/shard_map/hbs,she->bhe/dot_general | solution.py:75
  228.8 3.0 %collective-permute-done.4 = f32[264,128]{1,0:T(8,128)S(1)} collective-permute-done((f32[264,128]{1,0:T(8,128)S(1)}, f32[264,128]{1,0:T(8,128)S(1)}, u32[]{:S(2)}, u32[]{:S(2)}) %collective-permute-start.4) | collective-permute-done | bytes 135200 | tf_op jit(solution)/shard_map/ppermute | solution.py:12
  234.3 0.6 broadcast_compare_fusion
  234.9 1.8 multiply_reduce_fusion
  236.9 1.0 copy.23
  (36 shorter events, 6.2 us)
Async XLA Ops:
  6.5 89.9 %all-gather.3.cloned.1.call-start = ((), (), s32[]{:S(2)}) async-start(), calls=%async_computation | async-start | bytes 3194880 | tf_op jit(solution)/shard_map/all_gather | solution.py:44
  7.3 156.8 %all-gather.5.cloned.1.call-start = ((), (), s32[]{:S(2)}) async-start(), calls=%async_computation.1 | async-start | bytes 4718592 | tf_op jit(solution)/shard_map/all_gather | solution.py:40
  170.7 1.5 copy-start
  173.5 4.7 %copy-start.1 = (bf16[3,1024,256]{1,2,0:T(8,128)(2,1)S(1)}, bf16[3,1024,256]{1,2,0:T(8,128)(2,1)}, u32[]{:S(2)}) copy-start(bf16[3,1024,256]{1,2,0:T(8,128)(2,1)} %copy-done) | copy-start | bytes 4718596
  176.2 9.7 %collective-permute-start = (f32[264,128]{1,0:T(8,128)S(1)}, f32[264,128]{1,0:T(8,128)S(1)}, u32[]{:S(2)}, u32[]{:S(2)}) collective-permute-start(f32[264,128]{1,0:T(8,128)S(1)} %concatenate.7), channel_id=1, source_target_pairs={{0,8},{8,16},{16,24},{24,32},{32,40},{40,48},{48,56},{56,64},{64,7... | collective-permute-start | bytes 405512 | tf_op jit(solution)/shard_map/ppermute | solution.py:12
  185.9 9.6 %collective-permute-start.1 = (f32[264,128]{1,0:T(8,128)S(1)}, f32[264,128]{1,0:T(8,128)S(1)}, u32[]{:S(2)}, u32[]{:S(2)}) collective-permute-start(f32[264,128]{1,0:T(8,128)S(1)} %collective-permute-done), channel_id=1, source_target_pairs={{0,8},{8,16},{16,24},{24,32},{32,40},{40,48},{48,56},{56,64},{64,7... | collective-permute-start | bytes 405512 | tf_op jit(solution)/shard_map/ppermute | solution.py:12
  197.4 10.3 %collective-permute-start.2 = (f32[264,128]{1,0:T(8,128)S(1)}, f32[264,128]{1,0:T(8,128)}, u32[]{:S(2)}, u32[]{:S(2)}) collective-permute-start(f32[264,128]{1,0:T(8,128)S(1)} %select_add_fusion.3), channel_id=1, source_target_pairs={{0,16},{8,24},{16,32},{24,40},{32,48},{40,56},{48,64},{56,72},{64,... | collective-permute-start | bytes 405512 | tf_op jit(solution)/shard_map/ppermute | solution.py:12
  203.9 9.2 %copy-start.2 = (f32[1024,256]{0,1:T(8,128)S(1)}, f32[1024,256]{0,1:T(8,128)}, u32[]{:S(2)}) copy-start(f32[1024,256]{0,1:T(8,128)} %get-tuple-element.6) | copy-start | bytes 3145732
  211.2 23.1 %copy-start.3 = (s32[1024]{0:T(1024)S(1)}, s32[1024]{0:T(1024)}, u32[]{:S(2)}) copy-start(s32[1024]{0:T(1024)} %param.7) | copy-start | bytes 12292
  211.2 10.5 %collective-permute-start.3 = (f32[264,128]{1,0:T(8,128)S(1)}, f32[264,128]{1,0:T(8,128)S(1)}, u32[]{:S(2)}, u32[]{:S(2)}) collective-permute-start(f32[264,128]{1,0:T(8,128)S(1)} %select_add_fusion.2), channel_id=1, source_target_pairs={{0,32},{8,40},{16,48},{24,56},{32,64},{40,72},{48,80},{56,88},{64,... | collective-permute-start | bytes 405512 | tf_op jit(solution)/shard_map/ppermute | solution.py:12
  223.7 8.1 %collective-permute-start.4 = (f32[264,128]{1,0:T(8,128)S(1)}, f32[264,128]{1,0:T(8,128)S(1)}, u32[]{:S(2)}, u32[]{:S(2)}) collective-permute-start(f32[264,128]{1,0:T(8,128)S(1)} %select_add_fusion.1), channel_id=1, source_target_pairs={{0,64},{8,72},{16,80},{24,88},{32,96},{40,104},{48,112},{56,120},{... | collective-permute-start | bytes 405512 | tf_op jit(solution)/shard_map/ppermute | solution.py:12
  233.6 3.2 %copy-start.4 = (f32[256]{0:T(256)S(1)}, f32[256]{0:T(256)}, u32[]{:S(2)}) copy-start(f32[256]{0:T(256)} %param.6) | copy-start | bytes 3076
Sparse Core Ops, SparseCore 0:
  10.8 85.6 all-gather.2
  98.5 65.5 all-gather.4

commit v2 on v1

--- a/solution.py
+++ b/solution.py
@@ -1,15 +1,37 @@
 import jax
 import jax.numpy as jnp
 from jax import lax
+from jax.sharding import Mesh
 from jax.sharding import PartitionSpec as P
 
 HEAD_DIM = 128
 SPAN = 16384
 
 
-def shifted(value, axis, steps):
-    count = lax.axis_size(axis)
+CTX = ("y", "x", "core")
+
+
+def shifted(value, axis, steps, count):
     return lax.ppermute(value, axis, [(source, source + steps) for source in range(count - steps)])
+
+
+def ring_gather(value, axis, count, dim):
+    by_offset = {0: value}
+    ahead = value
+    behind = value
+    for step in range(1, count // 2 + 1):
+        ahead = lax.ppermute(ahead, axis, [(j, (j + 1) % count) for j in range(count)])
+        by_offset[-step] = ahead
+        if step < count - count // 2:
+            behind = lax.ppermute(behind, axis, [(j, (j - 1) % count) for j in range(count)])
+            by_offset[step] = behind
+    low = -(count // 2)
+    stacked = jnp.stack([by_offset[off] for off in range(low, low + count)], axis=0)
+    ordered = jnp.roll(stacked, lax.axis_index(axis) + low, axis=0)
+    moved = jnp.moveaxis(ordered, 0, dim)
+    shape = list(value.shape)
+    shape[dim] *= count
+    return moved.reshape(shape)
 
 
 def feature_map(values):
@@ -23,12 +45,12 @@
     packed = jnp.concatenate([flat, tail_rows], axis=0)
     state_rows = head_count * HEAD_DIM
     is_state = (jnp.arange(packed.shape[0]) < state_rows)[:, None]
-    count = lax.axis_size("ctx")
+    count = lax.axis_size(CTX)
     window = min(count - 1, 1 + (SPAN - 1) // row_count)
-    running = shifted(packed, "ctx", 1)
+    running = shifted(packed, CTX, 1, count)
     step = 1
     while step < window:
-        incoming = shifted(running, "ctx", step)
+        incoming = shifted(running, CTX, step, count)
         linked = incoming[state_rows, 0] == running[state_rows, 0]
         running = running + jnp.where(is_state & linked, incoming, 0.0)
         step *= 2
@@ -38,11 +60,11 @@
 
 def per_device(tokens, w_qkv, out_gain, seg_ids):
     whole = lax.all_gather(tokens, "head", axis=1, tiled=True)
+    w_rows = lax.all_gather(w_qkv, "core", axis=1, tiled=True)
+    w_rows = ring_gather(w_rows, "x", lax.axis_size("x"), 1)
+    w_rows = ring_gather(w_rows, "y", lax.axis_size("y"), 1)
     projected = jnp.einsum(
-        "tr,grc->gtc",
-        whole,
-        lax.all_gather(w_qkv, "ctx", axis=1, tiled=True),
-        preferred_element_type=jnp.float32,
+        "tr,grc->gtc", whole, w_rows, preferred_element_type=jnp.float32
     ).astype(jnp.bfloat16)
     row_count = seg_ids.shape[0]
     head_count = projected.shape[2] // HEAD_DIM
@@ -86,7 +108,10 @@
 
 
 def solution(mesh):
-    placed = (P("ctx", "head"), P(None, "ctx", "head"), P("head"), P("ctx"))
+    shape = dict(zip(mesh.axis_names, mesh.devices.shape))
+    head = shape["head"]
+    fine = Mesh(mesh.devices.reshape(-1, 4, 2, head), (*CTX, "head"))
+    placed = (P(CTX, "head"), P(None, CTX, "head"), P("head"), P(CTX))
     return jax.shard_map(
-        per_device, mesh=mesh, in_specs=placed, out_specs=P("ctx", "head"), check_vma=False
+        per_device, mesh=fine, in_specs=placed, out_specs=P(CTX, "head"), check_vma=False
     )

time: 245 us -> 173 us (0.71)
  waiting for transfers between devices: 180 us -> 61.4 us
  starting transfers between devices: 9.63 us -> 44.2 us
  local copies, waits for them, and re-layouts: 11.1 us -> 21.3 us
    all_gather x1 -> x0, waiting for transfers between devices: 84.3 us -> none  [per_device(): lax.all_gather(w_qkv, 'ctx', axis=1, tiled=True)]
    all_gather x1, waiting for transfers between devices: 67.6 us -> 7.65 us  [per_device(): whole = lax.all_gather(tokens, 'head', axis=1, tiled=True)]
    ppermute x0 -> x10, starting transfers between devices: none -> 34.6 us  [the longest x4 20.7 us: ring_gather(): lax.ppermute(behind, axis, [(j, (j - 1) % count) for j in range(count)])]
    ppermute x0 -> x10, waiting for transfers between devices: none -> 27.6 us  [the longest x6 22.1 us: ring_gather(): lax.ppermute(ahead, axis, [(j, (j + 1) % count) for j in range(count)])]
    reshape x0 -> x1, local copies, waits for them, and re-layouts: none -> 4.22 us  [ring_gather(): return moved.reshape(shape)]
    transpose x0 -> x2, local copies, waits for them, and re-layouts: none -> 3.64 us  [ring_gather(): moved = jnp.moveaxis(ordered, 0, dim)]
  transfers between devices with their start and end apart: 7 -> 16, of which waited for: 7 -> 15; matrix products, arithmetic and copies ran while one was open for 6% -> 15% of each run, Pallas kernels for 0% -> 0%
where the time goes in v2:
time: 173 us; the launch traced here: 172 us
  waiting for transfers between devices  61.4 us (35%)
  starting transfers between devices  44.2 us (26%)
  local copies, waits for them, and re-layouts  21.3 us (12%)
  between operations  19 us (11%)
  matrix products  15.2 us (9%)
  other arithmetic  8.43 us (5%)
  blocking collectives  2.24 us (1%)
    ppermute x5, waiting for transfers between devices, shifted(): lax.ppermute(value, axis, [(source, source + steps) for source in range(c...  26.1 us
    ppermute x6, waiting for transfers between devices, ring_gather(): lax.ppermute(ahead, axis, [(j, (j + 1) % count) for j in range(count)])  22.1 us
    ppermute x4, starting transfers between devices, ring_gather(): lax.ppermute(behind, axis, [(j, (j - 1) % count) for j in range(count)])  20.7 us
    ppermute x6, starting transfers between devices, ring_gather(): lax.ppermute(ahead, axis, [(j, (j + 1) % count) for j in range(count)])  13.9 us
    ppermute x5, starting transfers between devices, shifted(): lax.ppermute(value, axis, [(source, source + steps) for source in range(c...  9.59 us
    all_gather x1, waiting for transfers between devices, per_device(): whole = lax.all_gather(tokens, 'head', axis=1, tiled=True)  7.65 us
    dot_general x2, matrix products, per_device(): jnp.einsum('hbs,she->bhe', weights, values[:key_end], preferred_element_t...  5.78 us
    dot_general x1, matrix products, per_device(): jnp.einsum('tr,grc->gtc', whole, w_rows, preferred_element_type=jnp.float32)  5.63 us
  transfers between devices with their start and end apart: 16, of which 15 were waited for; matrix products, arithmetic and copies ran while one was open for 15% of the time, Pallas kernels for 0%

profile of v2, /device:TPU:32, one launch (start us, length us, event | category | flops | bytes accessed | tf_op | source)
XLA Modules:
  0.0 171.7 jit_solution(18071429680948909619)
XLA Ops:
  6.5 2.2 %all_gather.6 = bf16[3,64,256]{2,1,0:T(8,128)(2,1)S(1)} all-gather(bf16[3,32,256]{2,1,0:T(8,128)(2,1)} %param.5), channel_id=1, replica_groups=mesh['y'=8,'x'=4,'core'=2,'head'=8] {'core'}, dimensions={1}, use_global_device_ids=true | all-gather | bytes 147456 | tf_op jit(solution)/shard_map/all_gather | solution.py:63
  8.8 3.4 %collective-permute-start = (bf16[3,64,256]{2,1,0:T(8,128)(2,1)S(1)}, bf16[3,64,256]{2,1,0:T(8,128)(2,1)S(1)}, u32[]{:S(2)}, u32[]{:S(2)}) collective-permute-start(bf16[3,64,256]{2,1,0:T(8,128)(2,1)S(1)} %all_gather.6), channel_id=1, source_target_pairs={{0,16},{16,32},{32,48},{48,0},{1,17},{17,33},{33,49},{49,1},{2,18}... | collective-permute-start | bytes 294920 | tf_op jit(solution)/shard_map/ppermute | solution.py:23
  12.2 4.6 %collective-permute-done = bf16[3,64,256]{2,1,0:T(8,128)(2,1)S(1)} collective-permute-done((bf16[3,64,256]{2,1,0:T(8,128)(2,1)S(1)}, bf16[3,64,256]{2,1,0:T(8,128)(2,1)S(1)}, u32[]{:S(2)}, u32[]{:S(2)}) %collective-permute-start) | collective-permute-done | bytes 98336 | tf_op jit(solution)/shard_map/ppermute | solution.py:23
  16.7 2.2 %collective-permute-start.1 = (bf16[3,64,256]{2,1,0:T(8,128)(2,1)S(1)}, bf16[3,64,256]{2,1,0:T(8,128)(2,1)S(1)}, u32[]{:S(2)}, u32[]{:S(2)}) collective-permute-start(bf16[3,64,256]{2,1,0:T(8,128)(2,1)S(1)} %collective-permute-done), channel_id=1, source_target_pairs={{0,16},{16,32},{32,48},{48,0},{1,17},{17,33},{33,49},{49,1},{2,18}... | collective-permute-start | bytes 294920 | tf_op jit(solution)/shard_map/ppermute | solution.py:23
  18.9 4.9 %collective-permute-start.2 = (bf16[3,64,256]{2,1,0:T(8,128)(2,1)S(1)}, bf16[3,64,256]{2,1,0:T(8,128)(2,1)S(1)}, u32[]{:S(2)}, u32[]{:S(2)}) collective-permute-start(bf16[3,64,256]{2,1,0:T(8,128)(2,1)S(1)} %all_gather.6), channel_id=1, source_target_pairs={{0,48},{16,0},{32,16},{48,32},{1,49},{17,1},{33,17},{49,33},{2,50}... | collective-permute-start | bytes 294920 | tf_op jit(solution)/shard_map/ppermute | solution.py:26
  26.1 2.6 %collective-permute-start.3 = (bf16[3,256,256]{2,1,0:T(8,128)(2,1)S(1)}, bf16[3,256,256]{2,1,0:T(8,128)(2,1)S(1)}, u32[]{:S(2)}, u32[]{:S(2)}) collective-permute-start(bf16[3,256,256]{2,1,0:T(8,128)(2,1)S(1)} %bitcast.101), channel_id=1, source_target_pairs={{0,64},{64,128},{128,192},{192,256},{256,320},{320,384},{384,448},... | collective-permute-start | bytes 1179656 | tf_op jit(solution)/shard_map/ppermute | solution.py:23
  28.7 9.7 %collective-permute-done.3 = bf16[3,256,256]{2,1,0:T(8,128)(2,1)S(1)} collective-permute-done((bf16[3,256,256]{2,1,0:T(8,128)(2,1)S(1)}, bf16[3,256,256]{2,1,0:T(8,128)(2,1)S(1)}, u32[]{:S(2)}, u32[]{:S(2)}) %collective-permute-start.3) | collective-permute-done | bytes 393248 | tf_op jit(solution)/shard_map/ppermute | solution.py:23
  38.4 1.9 %collective-permute-start.4 = (bf16[3,256,256]{2,1,0:T(8,128)(2,1)S(1)}, bf16[3,256,256]{2,1,0:T(8,128)(2,1)S(1)}, u32[]{:S(2)}, u32[]{:S(2)}) collective-permute-start(bf16[3,256,256]{2,1,0:T(8,128)(2,1)S(1)} %collective-permute-done.3), channel_id=1, source_target_pairs={{0,64},{64,128},{128,192},{192,256},{256,320},{320,384},{384,448},... | collective-permute-start | bytes 1179656 | tf_op jit(solution)/shard_map/ppermute | solution.py:23
  41.6 5.1 %collective-permute-start.7 = (bf16[3,256,256]{2,1,0:T(8,128)(2,1)S(1)}, bf16[3,256,256]{2,1,0:T(8,128)(2,1)S(1)}, u32[]{:S(2)}, u32[]{:S(2)}) collective-permute-start(bf16[3,256,256]{2,1,0:T(8,128)(2,1)S(1)} %bitcast.102), channel_id=1, source_target_pairs={{0,448},{64,0},{128,64},{192,128},{256,192},{320,256},{384,320},{4... | collective-permute-start | bytes 1179656 | tf_op jit(solution)/shard_map/ppermute | solution.py:26
  46.7 3.1 %collective-permute-done.4 = bf16[3,256,256]{2,1,0:T(8,128)(2,1)S(1)} collective-permute-done((bf16[3,256,256]{2,1,0:T(8,128)(2,1)S(1)}, bf16[3,256,256]{2,1,0:T(8,128)(2,1)S(1)}, u32[]{:S(2)}, u32[]{:S(2)}) %collective-permute-start.4) | collective-permute-done | bytes 393248 | tf_op jit(solution)/shard_map/ppermute | solution.py:23
  49.8 1.9 %collective-permute-start.5 = (bf16[3,256,256]{2,1,0:T(8,128)(2,1)S(1)}, bf16[3,256,256]{2,1,0:T(8,128)(2,1)S(1)}, u32[]{:S(2)}, u32[]{:S(2)}) collective-permute-start(bf16[3,256,256]{2,1,0:T(8,128)(2,1)S(1)} %collective-permute-done.4), channel_id=1, source_target_pairs={{0,64},{64,128},{128,192},{192,256},{256,320},{320,384},{384,448},... | collective-permute-start | bytes 1179656 | tf_op jit(solution)/shard_map/ppermute | solution.py:23
  52.2 5.6 %collective-permute-start.8 = (bf16[3,256,256]{2,1,0:T(8,128)(2,1)S(1)}, bf16[3,256,256]{2,1,0:T(8,128)(2,1)S(1)}, u32[]{:S(2)}, u32[]{:S(2)}) collective-permute-start(bf16[3,256,256]{2,1,0:T(8,128)(2,1)S(1)} %collective-permute-done.7), channel_id=1, source_target_pairs={{0,448},{64,0},{128,64},{192,128},{256,192},{320,256},{384,320},{4... | collective-permute-start | bytes 1179656 | tf_op jit(solution)/shard_map/ppermute | solution.py:26
  57.8 2.9 %collective-permute-done.5 = bf16[3,256,256]{2,1,0:T(8,128)(2,1)S(1)} collective-permute-done((bf16[3,256,256]{2,1,0:T(8,128)(2,1)S(1)}, bf16[3,256,256]{2,1,0:T(8,128)(2,1)S(1)}, u32[]{:S(2)}, u32[]{:S(2)}) %collective-permute-start.5) | collective-permute-done | bytes 393248 | tf_op jit(solution)/shard_map/ppermute | solution.py:23
  60.7 1.9 %collective-permute-start.6 = (bf16[3,256,256]{2,1,0:T(8,128)(2,1)S(1)}, bf16[3,256,256]{2,1,0:T(8,128)(2,1)S(1)}, u32[]{:S(2)}, u32[]{:S(2)}) collective-permute-start(bf16[3,256,256]{2,1,0:T(8,128)(2,1)S(1)} %collective-permute-done.5), channel_id=1, source_target_pairs={{0,64},{64,128},{128,192},{192,256},{256,320},{320,384},{384,448},... | collective-permute-start | bytes 1179656 | tf_op jit(solution)/shard_map/ppermute | solution.py:23
  65.1 5.1 %collective-permute-start.9 = (bf16[3,256,256]{2,1,0:T(8,128)(2,1)S(1)}, bf16[3,256,256]{2,1,0:T(8,128)(2,1)S(1)}, u32[]{:S(2)}, u32[]{:S(2)}) collective-permute-start(bf16[3,256,256]{2,1,0:T(8,128)(2,1)S(1)} %collective-permute-done.8), channel_id=1, source_target_pairs={{0,448},{64,0},{128,64},{192,128},{256,192},{320,256},{384,320},{4... | collective-permute-start | bytes 1179656 | tf_op jit(solution)/shard_map/ppermute | solution.py:26
  71.8 3.7 %collective-permute-done.9 = bf16[3,256,256]{2,1,0:T(8,128)(2,1)S(1)} collective-permute-done((bf16[3,256,256]{2,1,0:T(8,128)(2,1)S(1)}, bf16[3,256,256]{2,1,0:T(8,128)(2,1)S(1)}, u32[]{:S(2)}, u32[]{:S(2)}) %collective-permute-start.9) | collective-permute-done | bytes 393248 | tf_op jit(solution)/shard_map/ppermute | solution.py:26
  76.1 3.4 %copy.32 = bf16[3,8,256,256]{2,1,3,0:T(8,128)(2,1)} copy(bf16[3,8,256,256]{3,2,0,1:T(8,128)(2,1)S(1)} %dynamic-slice_bitcast_fusion) | data formatting | bytes 6291456 | tf_op jit(solution)/shard_map/transpose | solution.py:31
  79.5 4.2 %reshape.155 = bf16[3,2048,256]{1,2,0:T(8,128)(2,1)S(1)} reshape(bf16[3,8,256,256]{2,1,3,0:T(8,128)(2,1)} %copy.32) | data formatting | bytes 6291456 | tf_op jit(solution)/shard_map/reshape | solution.py:34
  83.7 7.7 %all-gather.2.cloned.1.call-done = bf16[1024,2048]{1,0:T(8,128)(2,1)} async-done(((bf16[1024,256]{1,0:T(8,128)(2,1)}), bf16[1024,2048]{1,0:T(8,128)(2,1)}) %all-gather.2.cloned.1.call-update) | async-done | bytes 4194320 | tf_op jit(solution)/shard_map/all_gather | solution.py:62
  91.4 5.6 %fusion.7 = bf16[3,1024,256]{1,2,0:T(8,128)(2,1)S(1)} fusion(bf16[3,2048,256]{1,2,0:T(8,128)(2,1)S(1)} %reshape.155, bf16[1024,2048]{1,0:T(8,128)(2,1)} %all-gather.2.cloned.1.call-done), kind=kOutput, calls=%fused_computation.17 | convolution fusion | flops 3222011904 | bytes 8912896 | tf_op jit(solution)/shard_map/tr,grc->gtc/dot_general | solution.py:66
  100.6 2.1 %fusion.31 = f32[2,128,128]{2,1,0:T(8,128)S(1)} fusion(bf16[1024,2,128]{0,2,1:T(8,128)(2,1)} %bitcast.106, pred[1024]{0:T(1024)(128)(4,1)S(1)} %broadcast_compare_fusion.1, f32[1024,2,128]{2,0,1:T(8,128)} %copy.33), kind=kOutput, calls=%fused_computation.44 | convolution fusion | flops 68681728 | bytes 1704960 | tf_op jit(solution)/shard_map/thd,the->hde/dot_general | solution.py:77
  103.3 1.9 %collective-permute-start.10 = (f32[264,128]{1,0:T(8,128)S(1)}, f32[264,128]{1,0:T(8,128)S(1)}, u32[]{:S(2)}, u32[]{:S(2)}) collective-permute-start(f32[264,128]{1,0:T(8,128)S(1)} %concatenate.19), channel_id=1, source_target_pairs={{0,8},{8,16},{16,24},{24,32},{32,40},{40,48},{48,56},{56,64},{64,7... | collective-permute-start | bytes 405512 | tf_op jit(solution)/shard_map/ppermute | solution.py:15
  106.7 6.2 %collective-permute-done.10 = f32[264,128]{1,0:T(8,128)S(1)} collective-permute-done((f32[264,128]{1,0:T(8,128)S(1)}, f32[264,128]{1,0:T(8,128)S(1)}, u32[]{:S(2)}, u32[]{:S(2)}) %collective-permute-start.10) | collective-permute-done | bytes 135200 | tf_op jit(solution)/shard_map/ppermute | solution.py:15
  113.0 1.9 %collective-permute-start.11 = (f32[264,128]{1,0:T(8,128)S(1)}, f32[264,128]{1,0:T(8,128)S(1)}, u32[]{:S(2)}, u32[]{:S(2)}) collective-permute-start(f32[264,128]{1,0:T(8,128)S(1)} %collective-permute-done.10), channel_id=1, source_target_pairs={{0,8},{8,16},{16,24},{24,32},{32,40},{40,48},{48,56},{56,64},{64,7... | collective-permute-start | bytes 405512 | tf_op jit(solution)/shard_map/ppermute | solution.py:15
  116.2 6.4 %collective-permute-done.11 = f32[264,128]{1,0:T(8,128)S(1)} collective-permute-done((f32[264,128]{1,0:T(8,128)S(1)}, f32[264,128]{1,0:T(8,128)S(1)}, u32[]{:S(2)}, u32[]{:S(2)}) %collective-permute-start.11) | collective-permute-done | bytes 135200 | tf_op jit(solution)/shard_map/ppermute | solution.py:15
  124.5 1.9 %collective-permute-start.12 = (f32[264,128]{1,0:T(8,128)S(1)}, f32[264,128]{1,0:T(8,128)}, u32[]{:S(2)}, u32[]{:S(2)}) collective-permute-start(f32[264,128]{1,0:T(8,128)S(1)} %select_add_fusion.3), channel_id=1, source_target_pairs={{0,16},{8,24},{16,32},{24,40},{32,48},{40,56},{48,64},{56,72},{64,... | collective-permute-start | bytes 405512 | tf_op jit(solution)/shard_map/ppermute | solution.py:15
  126.4 4.0 %fusion.13 = f32[512,2,128]{0,2,1:T(8,128)} fusion(bf16[1024,2,128]{0,2,1:T(8,128)(2,1)} %bitcast.107, bf16[512,2,128]{0,2,1:T(8,128)(2,1)S(1)} %bitcast.111, pred[512,1024]{1,0:T(8,128)(4,1)} %fusion.2, f32[1024,2,128]{2,0,1:T(8,128)} %copy.33), kind=kOutput, calls=%fused_computation.22 | convolution fusion | flops 540278784 | bytes 2883584 | tf_op jit(solution)/shard_map/hbs,she->bhe/dot_general | solution.py:97
  133.0 1.8 %collective-permute-done.12 = f32[264,128]{1,0:T(8,128)} collective-permute-done((f32[264,128]{1,0:T(8,128)S(1)}, f32[264,128]{1,0:T(8,128)}, u32[]{:S(2)}, u32[]{:S(2)}) %collective-permute-start.12) | collective-permute-done | bytes 135200 | tf_op jit(solution)/shard_map/ppermute | solution.py:15
  138.3 1.9 %collective-permute-start.13 = (f32[264,128]{1,0:T(8,128)S(1)}, f32[264,128]{1,0:T(8,128)S(1)}, u32[]{:S(2)}, u32[]{:S(2)}) collective-permute-start(f32[264,128]{1,0:T(8,128)S(1)} %select_add_fusion.2), channel_id=1, source_target_pairs={{0,32},{8,40},{16,48},{24,56},{32,64},{40,72},{48,80},{56,88},{64,... | collective-permute-start | bytes 405512 | tf_op jit(solution)/shard_map/ppermute | solution.py:15
  141.1 7.8 %collective-permute-done.13 = f32[264,128]{1,0:T(8,128)S(1)} collective-permute-done((f32[264,128]{1,0:T(8,128)S(1)}, f32[264,128]{1,0:T(8,128)S(1)}, u32[]{:S(2)}, u32[]{:S(2)}) %collective-permute-start.13) | collective-permute-done | bytes 135200 | tf_op jit(solution)/shard_map/ppermute | solution.py:15
  150.8 1.9 %collective-permute-start.14 = (f32[264,128]{1,0:T(8,128)S(1)}, f32[264,128]{1,0:T(8,128)S(1)}, u32[]{:S(2)}, u32[]{:S(2)}) collective-permute-start(f32[264,128]{1,0:T(8,128)S(1)} %select_add_fusion.1), channel_id=1, source_target_pairs={{0,64},{8,72},{16,80},{24,88},{32,96},{40,104},{48,112},{56,120},{... | collective-permute-start | bytes 405512 | tf_op jit(solution)/shard_map/ppermute | solution.py:15
  155.1 3.8 %collective-permute-done.14 = f32[264,128]{1,0:T(8,128)S(1)} collective-permute-done((f32[264,128]{1,0:T(8,128)S(1)}, f32[264,128]{1,0:T(8,128)S(1)}, u32[]{:S(2)}, u32[]{:S(2)}) %collective-permute-start.14) | collective-permute-done | bytes 135200 | tf_op jit(solution)/shard_map/ppermute | solution.py:15
  (78 shorter events, 29.3 us)
Async XLA Ops:
  6.5 84.9 %all-gather.2.cloned.1.call-start = ((), (), s32[]{:S(2)}) async-start(), calls=%async_computation | async-start | bytes 4718592 | tf_op jit(solution)/shard_map/all_gather | solution.py:62
  8.8 8.0 %collective-permute-start = (bf16[3,64,256]{2,1,0:T(8,128)(2,1)S(1)}, bf16[3,64,256]{2,1,0:T(8,128)(2,1)S(1)}, u32[]{:S(2)}, u32[]{:S(2)}) collective-permute-start(bf16[3,64,256]{2,1,0:T(8,128)(2,1)S(1)} %all_gather.6), channel_id=1, source_target_pairs={{0,16},{16,32},{32,48},{48,0},{1,17},{17,33},{33,49},{49,1},{2,18}... | collective-permute-start | bytes 294920 | tf_op jit(solution)/shard_map/ppermute | solution.py:23
  16.7 7.7 %collective-permute-start.1 = (bf16[3,64,256]{2,1,0:T(8,128)(2,1)S(1)}, bf16[3,64,256]{2,1,0:T(8,128)(2,1)S(1)}, u32[]{:S(2)}, u32[]{:S(2)}) collective-permute-start(bf16[3,64,256]{2,1,0:T(8,128)(2,1)S(1)} %collective-permute-done), channel_id=1, source_target_pairs={{0,16},{16,32},{32,48},{48,0},{1,17},{17,33},{33,49},{49,1},{2,18}... | collective-permute-start | bytes 294920 | tf_op jit(solution)/shard_map/ppermute | solution.py:23
  18.9 7.1 %collective-permute-start.2 = (bf16[3,64,256]{2,1,0:T(8,128)(2,1)S(1)}, bf16[3,64,256]{2,1,0:T(8,128)(2,1)S(1)}, u32[]{:S(2)}, u32[]{:S(2)}) collective-permute-start(bf16[3,64,256]{2,1,0:T(8,128)(2,1)S(1)} %all_gather.6), channel_id=1, source_target_pairs={{0,48},{16,0},{32,16},{48,32},{1,49},{17,1},{33,17},{49,33},{2,50}... | collective-permute-start | bytes 294920 | tf_op jit(solution)/shard_map/ppermute | solution.py:26
  26.1 12.3 %collective-permute-start.3 = (bf16[3,256,256]{2,1,0:T(8,128)(2,1)S(1)}, bf16[3,256,256]{2,1,0:T(8,128)(2,1)S(1)}, u32[]{:S(2)}, u32[]{:S(2)}) collective-permute-start(bf16[3,256,256]{2,1,0:T(8,128)(2,1)S(1)} %bitcast.101), channel_id=1, source_target_pairs={{0,64},{64,128},{128,192},{192,256},{256,320},{320,384},{384,448},... | collective-permute-start | bytes 1179656 | tf_op jit(solution)/shard_map/ppermute | solution.py:23
  38.4 11.4 %collective-permute-start.4 = (bf16[3,256,256]{2,1,0:T(8,128)(2,1)S(1)}, bf16[3,256,256]{2,1,0:T(8,128)(2,1)S(1)}, u32[]{:S(2)}, u32[]{:S(2)}) collective-permute-start(bf16[3,256,256]{2,1,0:T(8,128)(2,1)S(1)} %collective-permute-done.3), channel_id=1, source_target_pairs={{0,64},{64,128},{128,192},{192,256},{256,320},{320,384},{384,448},... | collective-permute-start | bytes 1179656 | tf_op jit(solution)/shard_map/ppermute | solution.py:23
  41.6 10.6 %collective-permute-start.7 = (bf16[3,256,256]{2,1,0:T(8,128)(2,1)S(1)}, bf16[3,256,256]{2,1,0:T(8,128)(2,1)S(1)}, u32[]{:S(2)}, u32[]{:S(2)}) collective-permute-start(bf16[3,256,256]{2,1,0:T(8,128)(2,1)S(1)} %bitcast.102), channel_id=1, source_target_pairs={{0,448},{64,0},{128,64},{192,128},{256,192},{320,256},{384,320},{4... | collective-permute-start | bytes 1179656 | tf_op jit(solution)/shard_map/ppermute | solution.py:26
  49.8 10.9 %collective-permute-start.5 = (bf16[3,256,256]{2,1,0:T(8,128)(2,1)S(1)}, bf16[3,256,256]{2,1,0:T(8,128)(2,1)S(1)}, u32[]{:S(2)}, u32[]{:S(2)}) collective-permute-start(bf16[3,256,256]{2,1,0:T(8,128)(2,1)S(1)} %collective-permute-done.4), channel_id=1, source_target_pairs={{0,64},{64,128},{128,192},{192,256},{256,320},{320,384},{384,448},... | collective-permute-start | bytes 1179656 | tf_op jit(solution)/shard_map/ppermute | solution.py:23
  52.2 12.9 %collective-permute-start.8 = (bf16[3,256,256]{2,1,0:T(8,128)(2,1)S(1)}, bf16[3,256,256]{2,1,0:T(8,128)(2,1)S(1)}, u32[]{:S(2)}, u32[]{:S(2)}) collective-permute-start(bf16[3,256,256]{2,1,0:T(8,128)(2,1)S(1)} %collective-permute-done.7), channel_id=1, source_target_pairs={{0,448},{64,0},{128,64},{192,128},{256,192},{320,256},{384,320},{4... | collective-permute-start | bytes 1179656 | tf_op jit(solution)/shard_map/ppermute | solution.py:26
  60.7 10.9 %collective-permute-start.6 = (bf16[3,256,256]{2,1,0:T(8,128)(2,1)S(1)}, bf16[3,256,256]{2,1,0:T(8,128)(2,1)S(1)}, u32[]{:S(2)}, u32[]{:S(2)}) collective-permute-start(bf16[3,256,256]{2,1,0:T(8,128)(2,1)S(1)} %collective-permute-done.5), channel_id=1, source_target_pairs={{0,64},{64,128},{128,192},{192,256},{256,320},{320,384},{384,448},... | collective-permute-start | bytes 1179656 | tf_op jit(solution)/shard_map/ppermute | solution.py:23
  65.1 10.4 %collective-permute-start.9 = (bf16[3,256,256]{2,1,0:T(8,128)(2,1)S(1)}, bf16[3,256,256]{2,1,0:T(8,128)(2,1)S(1)}, u32[]{:S(2)}, u32[]{:S(2)}) collective-permute-start(bf16[3,256,256]{2,1,0:T(8,128)(2,1)S(1)} %collective-permute-done.8), channel_id=1, source_target_pairs={{0,448},{64,0},{128,64},{192,128},{256,192},{320,256},{384,320},{4... | collective-permute-start | bytes 1179656 | tf_op jit(solution)/shard_map/ppermute | solution.py:26
  97.0 1.2 copy-start
  103.3 9.7 %collective-permute-start.10 = (f32[264,128]{1,0:T(8,128)S(1)}, f32[264,128]{1,0:T(8,128)S(1)}, u32[]{:S(2)}, u32[]{:S(2)}) collective-permute-start(f32[264,128]{1,0:T(8,128)S(1)} %concatenate.19), channel_id=1, source_target_pairs={{0,8},{8,16},{16,24},{24,32},{32,40},{40,48},{48,56},{56,64},{64,7... | collective-permute-start | bytes 405512 | tf_op jit(solution)/shard_map/ppermute | solution.py:15
  113.0 9.6 %collective-permute-start.11 = (f32[264,128]{1,0:T(8,128)S(1)}, f32[264,128]{1,0:T(8,128)S(1)}, u32[]{:S(2)}, u32[]{:S(2)}) collective-permute-start(f32[264,128]{1,0:T(8,128)S(1)} %collective-permute-done.10), channel_id=1, source_target_pairs={{0,8},{8,16},{16,24},{24,32},{32,40},{40,48},{48,56},{56,64},{64,7... | collective-permute-start | bytes 405512 | tf_op jit(solution)/shard_map/ppermute | solution.py:15
  124.5 10.3 %collective-permute-start.12 = (f32[264,128]{1,0:T(8,128)S(1)}, f32[264,128]{1,0:T(8,128)}, u32[]{:S(2)}, u32[]{:S(2)}) collective-permute-start(f32[264,128]{1,0:T(8,128)S(1)} %select_add_fusion.3), channel_id=1, source_target_pairs={{0,16},{8,24},{16,32},{24,40},{32,48},{40,56},{48,64},{56,72},{64,... | collective-permute-start | bytes 405512 | tf_op jit(solution)/shard_map/ppermute | solution.py:15
  126.4 34.9 %copy-start.1 = (s32[1024]{0:T(1024)S(1)}, s32[1024]{0:T(1024)}, u32[]{:S(2)}) copy-start(s32[1024]{0:T(1024)} %param.7) | copy-start | bytes 12292
  130.4 33.3 %copy-start.2 = (f32[256]{0:T(256)S(1)}, f32[256]{0:T(256)}, u32[]{:S(2)}) copy-start(f32[256]{0:T(256)} %param.6) | copy-start | bytes 3076
  138.3 10.5 %collective-permute-start.13 = (f32[264,128]{1,0:T(8,128)S(1)}, f32[264,128]{1,0:T(8,128)S(1)}, u32[]{:S(2)}, u32[]{:S(2)}) collective-permute-start(f32[264,128]{1,0:T(8,128)S(1)} %select_add_fusion.2), channel_id=1, source_target_pairs={{0,32},{8,40},{16,48},{24,56},{32,64},{40,72},{48,80},{56,88},{64,... | collective-permute-start | bytes 405512 | tf_op jit(solution)/shard_map/ppermute | solution.py:15
  150.8 8.1 %collective-permute-start.14 = (f32[264,128]{1,0:T(8,128)S(1)}, f32[264,128]{1,0:T(8,128)S(1)}, u32[]{:S(2)}, u32[]{:S(2)}) collective-permute-start(f32[264,128]{1,0:T(8,128)S(1)} %select_add_fusion.1), channel_id=1, source_target_pairs={{0,64},{8,72},{16,80},{24,88},{32,96},{40,104},{48,112},{56,120},{... | collective-permute-start | bytes 405512 | tf_op jit(solution)/shard_map/ppermute | solution.py:15
Sparse Core Ops, SparseCore 0:
  23.9 67.4 all-gather.1

commit v3 on v2

--- a/solution.py
+++ b/solution.py
@@ -34,6 +34,23 @@
     return moved.reshape(shape)
 
 
+def gather_weights(w_local):
+    half = w_local.shape[2] // 2
+    core = lax.axis_index("core")
+    partner = lax.ppermute(w_local, "core", [(0, 1), (1, 0)])
+    low_rows = jnp.where(core == 0, w_local[:, :, :half], partner[:, :, half:])
+    high_rows = jnp.where(core == 0, partner[:, :, :half], w_local[:, :, half:])
+    rows = jnp.concatenate([low_rows, high_rows], axis=1)
+    rows = ring_gather(rows, "x", lax.axis_size("x"), 1)
+    rows = ring_gather(rows, "y", lax.axis_size("y"), 1)
+    other = lax.ppermute(rows, "core", [(0, 1), (1, 0)])
+    return jnp.where(
+        core == 0,
+        jnp.concatenate([rows, other], axis=2),
+        jnp.concatenate([other, rows], axis=2),
+    )
+
+
 def feature_map(values):
     return (jax.nn.elu(values.astype(jnp.float32)) + 1.0).astype(jnp.bfloat16)
 
@@ -60,9 +77,7 @@
 
 def per_device(tokens, w_qkv, out_gain, seg_ids):
     whole = lax.all_gather(tokens, "head", axis=1, tiled=True)
-    w_rows = lax.all_gather(w_qkv, "core", axis=1, tiled=True)
-    w_rows = ring_gather(w_rows, "x", lax.axis_size("x"), 1)
-    w_rows = ring_gather(w_rows, "y", lax.axis_size("y"), 1)
+    w_rows = gather_weights(w_qkv)
     projected = jnp.einsum(
         "tr,grc->gtc", whole, w_rows, preferred_element_type=jnp.float32
     ).astype(jnp.bfloat16)

time: 173 us -> 173 us (level)
  local copies, waits for them, and re-layouts: 21.3 us -> 12.3 us
  waiting for transfers between devices: 61.4 us -> 69.4 us
  starting transfers between devices: 44.2 us -> 47.6 us
  blocking collectives: 2.24 us -> 0 us
    all_gather x1, waiting for transfers between devices: 7.65 us -> 20.5 us  [per_device(): whole = lax.all_gather(tokens, 'head', axis=1, tiled=True)]
    ppermute x6, waiting for transfers between devices: 22.1 us -> 15.1 us  [ring_gather(): lax.ppermute(ahead, axis, [(j, (j + 1) % count) for j in range(count)])]
    reshape x1 -> x0, local copies, waits for them, and re-layouts: 4.22 us -> none  [ring_gather(): return moved.reshape(shape)]
    ppermute x0 -> x2, starting transfers between devices: none -> 3.83 us  [the longest x1 1.92 us: gather_weights(): other = lax.ppermute(rows, 'core', [(0, 1), (1, 0)])]
    transpose x2, local copies, waits for them, and re-layouts: 3.64 us -> 0.3 us  [ring_gather(): moved = jnp.moveaxis(ordered, 0, dim)]
    ppermute x5, waiting for transfers between devices: 26.1 us -> 28.8 us  [shifted(): lax.ppermute(value, axis, [(source, source + steps) for source in range(c...]
    ppermute x4, waiting for transfers between devices: 5.51 us -> 2.89 us  [ring_gather(): lax.ppermute(behind, axis, [(j, (j - 1) % count) for j in range(count)])]
    all_gather x1 -> x0, blocking collectives: 2.24 us -> none  [per_device(): w_rows = lax.all_gather(w_qkv, 'core', axis=1, tiled=True)]
  transfers between devices with their start and end apart: 16 -> 18, of which waited for: 15 -> 16; matrix products, arithmetic and copies ran while one was open for 15% -> 8% of each run, Pallas kernels for 0% -> 0%
where the time goes in v3:
time: 173 us; the launch traced here: 172 us
  waiting for transfers between devices  69.4 us (40%)
  starting transfers between devices  47.6 us (28%)
  between operations  19.1 us (11%)
  matrix products  15.1 us (9%)
  local copies, waits for them, and re-layouts  12.3 us (7%)
  other arithmetic  8.11 us (5%)
    ppermute x5, waiting for transfers between devices, shifted(): lax.ppermute(value, axis, [(source, source + steps) for source in range(c...  28.8 us
    all_gather x1, waiting for transfers between devices, per_device(): whole = lax.all_gather(tokens, 'head', axis=1, tiled=True)  20.5 us
    ppermute x4, starting transfers between devices, ring_gather(): lax.ppermute(behind, axis, [(j, (j - 1) % count) for j in range(count)])  20.3 us
    ppermute x6, waiting for transfers between devices, ring_gather(): lax.ppermute(ahead, axis, [(j, (j + 1) % count) for j in range(count)])  15.1 us
    ppermute x6, starting transfers between devices, ring_gather(): lax.ppermute(ahead, axis, [(j, (j + 1) % count) for j in range(count)])  13.9 us
    ppermute x5, starting transfers between devices, shifted(): lax.ppermute(value, axis, [(source, source + steps) for source in range(c...  9.59 us
    dot_general x1, matrix products, per_device(): jnp.einsum('tr,grc->gtc', whole, w_rows, preferred_element_type=jnp.float32)  6.6 us
    slice x8, local copies, waits for them, and re-layouts, state_scan(): linked = incoming[state_rows, 0] == running[state_rows, 0]  4.96 us
  transfers between devices with their start and end apart: 18, of which 16 were waited for; matrix products, arithmetic and copies ran while one was open for 8% of the time, Pallas kernels for 0%

profile of v3, /device:TPU:32, one launch (start us, length us, event | category | flops | bytes accessed | tf_op | source)
XLA Modules:
  0.0 171.6 jit_solution(10349362654001061485)
XLA Ops:
  6.5 1.9 %collective-permute-start = (bf16[3,32,256]{2,1,0:T(8,128)(2,1)}, bf16[3,32,256]{2,1,0:T(8,128)(2,1)S(1)}, u32[]{:S(2)}, u32[]{:S(2)}) collective-permute-start(bf16[3,32,256]{2,1,0:T(8,128)(2,1)} %param.5), channel_id=1, source_target_pairs={{0,8},{8,0},{1,9},{9,1},{2,10},{10,2},{3,11},{11,3},{4,12},{12,4},... | collective-permute-start | bytes 147464 | tf_op jit(solution)/shard_map/ppermute | solution.py:40
  10.6 3.4 %collective-permute-start.1 = (bf16[3,64,128]{2,1,0:T(8,128)(2,1)S(1)}, bf16[3,64,128]{2,1,0:T(8,128)(2,1)S(1)}, u32[]{:S(2)}, u32[]{:S(2)}) collective-permute-start(bf16[3,64,128]{2,1,0:T(8,128)(2,1)S(1)} %pad_maximum_fusion), channel_id=1, source_target_pairs={{0,16},{16,32},{32,48},{48,0},{1,17},{17,33},{33,49},{49,1},{2,18}... | collective-permute-start | bytes 147464 | tf_op jit(solution)/shard_map/ppermute | solution.py:23
  14.0 3.8 %collective-permute-done.1 = bf16[3,64,128]{2,1,0:T(8,128)(2,1)S(1)} collective-permute-done((bf16[3,64,128]{2,1,0:T(8,128)(2,1)S(1)}, bf16[3,64,128]{2,1,0:T(8,128)(2,1)S(1)}, u32[]{:S(2)}, u32[]{:S(2)}) %collective-permute-start.1) | collective-permute-done | bytes 49184 | tf_op jit(solution)/shard_map/ppermute | solution.py:23
  17.8 2.2 %collective-permute-start.2 = (bf16[3,64,128]{2,1,0:T(8,128)(2,1)S(1)}, bf16[3,64,128]{2,1,0:T(8,128)(2,1)S(1)}, u32[]{:S(2)}, u32[]{:S(2)}) collective-permute-start(bf16[3,64,128]{2,1,0:T(8,128)(2,1)S(1)} %collective-permute-done.1), channel_id=1, source_target_pairs={{0,16},{16,32},{32,48},{48,0},{1,17},{17,33},{33,49},{49,1},{2,18}... | collective-permute-start | bytes 147464 | tf_op jit(solution)/shard_map/ppermute | solution.py:23
  20.1 4.9 %collective-permute-start.3 = (bf16[3,64,128]{2,1,0:T(8,128)(2,1)S(1)}, bf16[3,64,128]{2,1,0:T(8,128)(2,1)S(1)}, u32[]{:S(2)}, u32[]{:S(2)}) collective-permute-start(bf16[3,64,128]{2,1,0:T(8,128)(2,1)S(1)} %pad_maximum_fusion), channel_id=1, source_target_pairs={{0,48},{16,0},{32,16},{48,32},{1,49},{17,1},{33,17},{49,33},{2,50}... | collective-permute-start | bytes 147464 | tf_op jit(solution)/shard_map/ppermute | solution.py:26
  26.8 2.6 %collective-permute-start.4 = (bf16[3,256,128]{2,1,0:T(8,128)(2,1)S(1)}, bf16[3,256,128]{2,1,0:T(8,128)(2,1)S(1)}, u32[]{:S(2)}, u32[]{:S(2)}) collective-permute-start(bf16[3,256,128]{2,1,0:T(8,128)(2,1)S(1)} %bitcast.98), channel_id=1, source_target_pairs={{0,64},{64,128},{128,192},{192,256},{256,320},{320,384},{384,448},... | collective-permute-start | bytes 589832 | tf_op jit(solution)/shard_map/ppermute | solution.py:23
  29.4 6.2 %collective-permute-done.4 = bf16[3,256,128]{2,1,0:T(8,128)(2,1)S(1)} collective-permute-done((bf16[3,256,128]{2,1,0:T(8,128)(2,1)S(1)}, bf16[3,256,128]{2,1,0:T(8,128)(2,1)S(1)}, u32[]{:S(2)}, u32[]{:S(2)}) %collective-permute-start.4) | collective-permute-done | bytes 196640 | tf_op jit(solution)/shard_map/ppermute | solution.py:23
  35.6 1.9 %collective-permute-start.5 = (bf16[3,256,128]{2,1,0:T(8,128)(2,1)S(1)}, bf16[3,256,128]{2,1,0:T(8,128)(2,1)S(1)}, u32[]{:S(2)}, u32[]{:S(2)}) collective-permute-start(bf16[3,256,128]{2,1,0:T(8,128)(2,1)S(1)} %collective-permute-done.4), channel_id=1, source_target_pairs={{0,64},{64,128},{128,192},{192,256},{256,320},{320,384},{384,448},... | collective-permute-start | bytes 589832 | tf_op jit(solution)/shard_map/ppermute | solution.py:23
  37.5 5.1 %collective-permute-start.8 = (bf16[3,256,128]{2,1,0:T(8,128)(2,1)S(1)}, bf16[3,256,128]{2,1,0:T(8,128)(2,1)S(1)}, u32[]{:S(2)}, u32[]{:S(2)}) collective-permute-start(bf16[3,256,128]{2,1,0:T(8,128)(2,1)S(1)} %bitcast.99), channel_id=1, source_target_pairs={{0,448},{64,0},{128,64},{192,128},{256,192},{320,256},{384,320},{4... | collective-permute-start | bytes 589832 | tf_op jit(solution)/shard_map/ppermute | solution.py:26
  42.6 1.7 collective-permute-done.5
  44.3 1.9 %collective-permute-start.6 = (bf16[3,256,128]{2,1,0:T(8,128)(2,1)S(1)}, bf16[3,256,128]{2,1,0:T(8,128)(2,1)S(1)}, u32[]{:S(2)}, u32[]{:S(2)}) collective-permute-start(bf16[3,256,128]{2,1,0:T(8,128)(2,1)S(1)} %collective-permute-done.5), channel_id=1, source_target_pairs={{0,64},{64,128},{128,192},{192,256},{256,320},{320,384},{384,448},... | collective-permute-start | bytes 589832 | tf_op jit(solution)/shard_map/ppermute | solution.py:23
  46.2 5.1 %collective-permute-start.9 = (bf16[3,256,128]{2,1,0:T(8,128)(2,1)S(1)}, bf16[3,256,128]{2,1,0:T(8,128)(2,1)S(1)}, u32[]{:S(2)}, u32[]{:S(2)}) collective-permute-start(bf16[3,256,128]{2,1,0:T(8,128)(2,1)S(1)} %collective-permute-done.8), channel_id=1, source_target_pairs={{0,448},{64,0},{128,64},{192,128},{256,192},{320,256},{384,320},{4... | collective-permute-start | bytes 589832 | tf_op jit(solution)/shard_map/ppermute | solution.py:26
  51.4 1.7 collective-permute-done.6
  53.1 1.9 %collective-permute-start.7 = (bf16[3,256,128]{2,1,0:T(8,128)(2,1)S(1)}, bf16[3,256,128]{2,1,0:T(8,128)(2,1)S(1)}, u32[]{:S(2)}, u32[]{:S(2)}) collective-permute-start(bf16[3,256,128]{2,1,0:T(8,128)(2,1)S(1)} %collective-permute-done.6), channel_id=1, source_target_pairs={{0,64},{64,128},{128,192},{192,256},{256,320},{320,384},{384,448},... | collective-permute-start | bytes 589832 | tf_op jit(solution)/shard_map/ppermute | solution.py:23
  55.0 5.1 %collective-permute-start.10 = (bf16[3,256,128]{2,1,0:T(8,128)(2,1)S(1)}, bf16[3,256,128]{2,1,0:T(8,128)(2,1)S(1)}, u32[]{:S(2)}, u32[]{:S(2)}) collective-permute-start(bf16[3,256,128]{2,1,0:T(8,128)(2,1)S(1)} %collective-permute-done.9), channel_id=1, source_target_pairs={{0,448},{64,0},{128,64},{192,128},{256,192},{320,256},{384,320},{4... | collective-permute-start | bytes 589832 | tf_op jit(solution)/shard_map/ppermute | solution.py:26
  60.2 1.7 collective-permute-done.7
  64.0 1.9 %collective-permute-start.11 = (bf16[3,2048,128]{2,1,0:T(8,128)(2,1)S(1)}, bf16[3,2048,128]{2,1,0:T(8,128)(2,1)}, u32[]{:S(2)}, u32[]{:S(2)}) collective-permute-start(bf16[3,2048,128]{2,1,0:T(8,128)(2,1)S(1)} %bitcast.102), channel_id=1, source_target_pairs={{0,8},{8,0},{1,9},{9,1},{2,10},{10,2},{3,11},{11,3},{4,12},{12,4},... | collective-permute-start | bytes 4718600 | tf_op jit(solution)/shard_map/ppermute | solution.py:46
  69.4 20.5 %all-gather.2.cloned.1.call-done = bf16[1024,2048]{1,0:T(8,128)(2,1)} async-done(((bf16[1024,256]{1,0:T(8,128)(2,1)}), bf16[1024,2048]{1,0:T(8,128)(2,1)}) %all-gather.2.cloned.1.call-update) | async-done | bytes 4194320 | tf_op jit(solution)/shard_map/all_gather | solution.py:79
  90.0 6.6 %fusion.13 = bf16[3,1024,256]{1,2,0:T(8,128)(2,1)S(1)} fusion(bf16[1024,2048]{1,0:T(8,128)(2,1)} %all-gather.2.cloned.1.call-done, bf16[3,2048,128]{2,1,0:T(8,128)(2,1)} %collective-permute-done.11, bf16[3,2048,128]{2,1,0:T(8,128)(2,1)S(1)} %bitcast.103, pred[]{:T(512)S(6)} %eq.80), kind=kOutput, calls=%fused_computation.24 | convolution fusion | flops 3236167680 | bytes 8912897 | tf_op jit(solution)/shard_map/tr,grc->gtc/dot_general | solution.py:81
  100.4 2.1 %fusion.37 = f32[2,128,128]{2,1,0:T(8,128)S(1)} fusion(bf16[1024,2,128]{0,2,1:T(8,128)(2,1)S(1)} %bitcast.104, pred[1024]{0:T(1024)(128)(4,1)S(1)} %broadcast_compare_fusion.1, f32[1024,2,128]{2,0,1:T(8,128)} %copy.52), kind=kOutput, calls=%fused_computation.51 | convolution fusion | flops 68681728 | bytes 1704960 | tf_op jit(solution)/shard_map/thd,the->hde/dot_general | solution.py:92
  103.2 1.9 %collective-permute-start.12 = (f32[264,128]{1,0:T(8,128)S(1)}, f32[264,128]{1,0:T(8,128)S(1)}, u32[]{:S(2)}, u32[]{:S(2)}) collective-permute-start(f32[264,128]{1,0:T(8,128)S(1)} %concatenate.31), channel_id=1, source_target_pairs={{0,8},{8,16},{16,24},{24,32},{32,40},{40,48},{48,56},{56,64},{64,7... | collective-permute-start | bytes 405512 | tf_op jit(solution)/shard_map/ppermute | solution.py:15
  105.6 7.2 %collective-permute-done.12 = f32[264,128]{1,0:T(8,128)S(1)} collective-permute-done((f32[264,128]{1,0:T(8,128)S(1)}, f32[264,128]{1,0:T(8,128)S(1)}, u32[]{:S(2)}, u32[]{:S(2)}) %collective-permute-start.12) | collective-permute-done | bytes 135200 | tf_op jit(solution)/shard_map/ppermute | solution.py:15
  112.8 1.9 %collective-permute-start.13 = (f32[264,128]{1,0:T(8,128)S(1)}, f32[264,128]{1,0:T(8,128)S(1)}, u32[]{:S(2)}, u32[]{:S(2)}) collective-permute-start(f32[264,128]{1,0:T(8,128)S(1)} %collective-permute-done.12), channel_id=1, source_target_pairs={{0,8},{8,16},{16,24},{24,32},{32,40},{40,48},{48,56},{56,64},{64,7... | collective-permute-start | bytes 405512 | tf_op jit(solution)/shard_map/ppermute | solution.py:15
  116.2 6.3 %collective-permute-done.13 = f32[264,128]{1,0:T(8,128)S(1)} collective-permute-done((f32[264,128]{1,0:T(8,128)S(1)}, f32[264,128]{1,0:T(8,128)S(1)}, u32[]{:S(2)}, u32[]{:S(2)}) %collective-permute-start.13) | collective-permute-done | bytes 135200 | tf_op jit(solution)/shard_map/ppermute | solution.py:15
  124.5 1.9 %collective-permute-start.14 = (f32[264,128]{1,0:T(8,128)S(1)}, f32[264,128]{1,0:T(8,128)}, u32[]{:S(2)}, u32[]{:S(2)}) collective-permute-start(f32[264,128]{1,0:T(8,128)S(1)} %select_add_fusion.3), channel_id=1, source_target_pairs={{0,16},{8,24},{16,32},{24,40},{32,48},{40,56},{48,64},{56,72},{64,... | collective-permute-start | bytes 405512 | tf_op jit(solution)/shard_map/ppermute | solution.py:15
  126.4 3.9 %fusion.19 = f32[512,2,128]{0,2,1:T(8,128)} fusion(bf16[1024,2,128]{0,2,1:T(8,128)(2,1)S(1)} %bitcast.105, bf16[512,2,128]{0,2,1:T(8,128)(2,1)} %bitcast.109, pred[512,1024]{1,0:T(8,128)(4,1)} %fusion.8, f32[1024,2,128]{2,0,1:T(8,128)} %copy.52), kind=kOutput, calls=%fused_computation.29 | convolution fusion | flops 540278784 | bytes 2883584 | tf_op jit(solution)/shard_map/hbs,she->bhe/dot_general | solution.py:112
  131.2 3.6 %collective-permute-done.14 = f32[264,128]{1,0:T(8,128)} collective-permute-done((f32[264,128]{1,0:T(8,128)S(1)}, f32[264,128]{1,0:T(8,128)}, u32[]{:S(2)}, u32[]{:S(2)}) %collective-permute-start.14) | collective-permute-done | bytes 135200 | tf_op jit(solution)/shard_map/ppermute | solution.py:15
  138.3 1.9 %collective-permute-start.15 = (f32[264,128]{1,0:T(8,128)S(1)}, f32[264,128]{1,0:T(8,128)S(1)}, u32[]{:S(2)}, u32[]{:S(2)}) collective-permute-start(f32[264,128]{1,0:T(8,128)S(1)} %select_add_fusion.2), channel_id=1, source_target_pairs={{0,32},{8,40},{16,48},{24,56},{32,64},{40,72},{48,80},{56,88},{64,... | collective-permute-start | bytes 405512 | tf_op jit(solution)/shard_map/ppermute | solution.py:15
  142.0 6.8 %collective-permute-done.15 = f32[264,128]{1,0:T(8,128)S(1)} collective-permute-done((f32[264,128]{1,0:T(8,128)S(1)}, f32[264,128]{1,0:T(8,128)S(1)}, u32[]{:S(2)}, u32[]{:S(2)}) %collective-permute-start.15) | collective-permute-done | bytes 135200 | tf_op jit(solution)/shard_map/ppermute | solution.py:15
  150.6 1.9 %collective-permute-start.16 = (f32[264,128]{1,0:T(8,128)S(1)}, f32[264,128]{1,0:T(8,128)S(1)}, u32[]{:S(2)}, u32[]{:S(2)}) collective-permute-start(f32[264,128]{1,0:T(8,128)S(1)} %select_add_fusion.1), channel_id=1, source_target_pairs={{0,64},{8,72},{16,80},{24,88},{32,96},{40,104},{48,112},{56,120},{... | collective-permute-start | bytes 405512 | tf_op jit(solution)/shard_map/ppermute | solution.py:15
  154.0 4.8 %collective-permute-done.16 = f32[264,128]{1,0:T(8,128)S(1)} collective-permute-done((f32[264,128]{1,0:T(8,128)S(1)}, f32[264,128]{1,0:T(8,128)S(1)}, u32[]{:S(2)}, u32[]{:S(2)}) %collective-permute-start.16) | collective-permute-done | bytes 135200 | tf_op jit(solution)/shard_map/ppermute | solution.py:15
  161.9 1.7 multiply_reduce_fusion
  (86 shorter events, 26.2 us)
Async XLA Ops:
  6.5 83.4 %all-gather.2.cloned.1.call-start = ((), (), s32[]{:S(2)}) async-start(), calls=%async_computation | async-start | bytes 4718592 | tf_op jit(solution)/shard_map/all_gather | solution.py:79
  6.5 3.3 %collective-permute-start = (bf16[3,32,256]{2,1,0:T(8,128)(2,1)}, bf16[3,32,256]{2,1,0:T(8,128)(2,1)S(1)}, u32[]{:S(2)}, u32[]{:S(2)}) collective-permute-start(bf16[3,32,256]{2,1,0:T(8,128)(2,1)} %param.5), channel_id=1, source_target_pairs={{0,8},{8,0},{1,9},{9,1},{2,10},{10,2},{3,11},{11,3},{4,12},{12,4},... | collective-permute-start | bytes 147464 | tf_op jit(solution)/shard_map/ppermute | solution.py:40
  10.6 7.2 %collective-permute-start.1 = (bf16[3,64,128]{2,1,0:T(8,128)(2,1)S(1)}, bf16[3,64,128]{2,1,0:T(8,128)(2,1)S(1)}, u32[]{:S(2)}, u32[]{:S(2)}) collective-permute-start(bf16[3,64,128]{2,1,0:T(8,128)(2,1)S(1)} %pad_maximum_fusion), channel_id=1, source_target_pairs={{0,16},{16,32},{32,48},{48,0},{1,17},{17,33},{33,49},{49,1},{2,18}... | collective-permute-start | bytes 147464 | tf_op jit(solution)/shard_map/ppermute | solution.py:23
  17.8 7.2 %collective-permute-start.2 = (bf16[3,64,128]{2,1,0:T(8,128)(2,1)S(1)}, bf16[3,64,128]{2,1,0:T(8,128)(2,1)S(1)}, u32[]{:S(2)}, u32[]{:S(2)}) collective-permute-start(bf16[3,64,128]{2,1,0:T(8,128)(2,1)S(1)} %collective-permute-done.1), channel_id=1, source_target_pairs={{0,16},{16,32},{32,48},{48,0},{1,17},{17,33},{33,49},{49,1},{2,18}... | collective-permute-start | bytes 147464 | tf_op jit(solution)/shard_map/ppermute | solution.py:23
  20.1 6.6 %collective-permute-start.3 = (bf16[3,64,128]{2,1,0:T(8,128)(2,1)S(1)}, bf16[3,64,128]{2,1,0:T(8,128)(2,1)S(1)}, u32[]{:S(2)}, u32[]{:S(2)}) collective-permute-start(bf16[3,64,128]{2,1,0:T(8,128)(2,1)S(1)} %pad_maximum_fusion), channel_id=1, source_target_pairs={{0,48},{16,0},{32,16},{48,32},{1,49},{17,1},{33,17},{49,33},{2,50}... | collective-permute-start | bytes 147464 | tf_op jit(solution)/shard_map/ppermute | solution.py:26
  26.8 8.8 %collective-permute-start.4 = (bf16[3,256,128]{2,1,0:T(8,128)(2,1)S(1)}, bf16[3,256,128]{2,1,0:T(8,128)(2,1)S(1)}, u32[]{:S(2)}, u32[]{:S(2)}) collective-permute-start(bf16[3,256,128]{2,1,0:T(8,128)(2,1)S(1)} %bitcast.98), channel_id=1, source_target_pairs={{0,64},{64,128},{128,192},{192,256},{256,320},{320,384},{384,448},... | collective-permute-start | bytes 589832 | tf_op jit(solution)/shard_map/ppermute | solution.py:23
  35.6 8.8 %collective-permute-start.5 = (bf16[3,256,128]{2,1,0:T(8,128)(2,1)S(1)}, bf16[3,256,128]{2,1,0:T(8,128)(2,1)S(1)}, u32[]{:S(2)}, u32[]{:S(2)}) collective-permute-start(bf16[3,256,128]{2,1,0:T(8,128)(2,1)S(1)} %collective-permute-done.4), channel_id=1, source_target_pairs={{0,64},{64,128},{128,192},{192,256},{256,320},{320,384},{384,448},... | collective-permute-start | bytes 589832 | tf_op jit(solution)/shard_map/ppermute | solution.py:23
  37.5 8.8 %collective-permute-start.8 = (bf16[3,256,128]{2,1,0:T(8,128)(2,1)S(1)}, bf16[3,256,128]{2,1,0:T(8,128)(2,1)S(1)}, u32[]{:S(2)}, u32[]{:S(2)}) collective-permute-start(bf16[3,256,128]{2,1,0:T(8,128)(2,1)S(1)} %bitcast.99), channel_id=1, source_target_pairs={{0,448},{64,0},{128,64},{192,128},{256,192},{320,256},{384,320},{4... | collective-permute-start | bytes 589832 | tf_op jit(solution)/shard_map/ppermute | solution.py:26
  44.3 8.8 %collective-permute-start.6 = (bf16[3,256,128]{2,1,0:T(8,128)(2,1)S(1)}, bf16[3,256,128]{2,1,0:T(8,128)(2,1)S(1)}, u32[]{:S(2)}, u32[]{:S(2)}) collective-permute-start(bf16[3,256,128]{2,1,0:T(8,128)(2,1)S(1)} %collective-permute-done.5), channel_id=1, source_target_pairs={{0,64},{64,128},{128,192},{192,256},{256,320},{320,384},{384,448},... | collective-permute-start | bytes 589832 | tf_op jit(solution)/shard_map/ppermute | solution.py:23
  46.2 8.8 %collective-permute-start.9 = (bf16[3,256,128]{2,1,0:T(8,128)(2,1)S(1)}, bf16[3,256,128]{2,1,0:T(8,128)(2,1)S(1)}, u32[]{:S(2)}, u32[]{:S(2)}) collective-permute-start(bf16[3,256,128]{2,1,0:T(8,128)(2,1)S(1)} %collective-permute-done.8), channel_id=1, source_target_pairs={{0,448},{64,0},{128,64},{192,128},{256,192},{320,256},{384,320},{4... | collective-permute-start | bytes 589832 | tf_op jit(solution)/shard_map/ppermute | solution.py:26
  53.1 8.8 %collective-permute-start.7 = (bf16[3,256,128]{2,1,0:T(8,128)(2,1)S(1)}, bf16[3,256,128]{2,1,0:T(8,128)(2,1)S(1)}, u32[]{:S(2)}, u32[]{:S(2)}) collective-permute-start(bf16[3,256,128]{2,1,0:T(8,128)(2,1)S(1)} %collective-permute-done.6), channel_id=1, source_target_pairs={{0,64},{64,128},{128,192},{192,256},{256,320},{320,384},{384,448},... | collective-permute-start | bytes 589832 | tf_op jit(solution)/shard_map/ppermute | solution.py:23
  55.0 8.3 %collective-permute-start.10 = (bf16[3,256,128]{2,1,0:T(8,128)(2,1)S(1)}, bf16[3,256,128]{2,1,0:T(8,128)(2,1)S(1)}, u32[]{:S(2)}, u32[]{:S(2)}) collective-permute-start(bf16[3,256,128]{2,1,0:T(8,128)(2,1)S(1)} %collective-permute-done.9), channel_id=1, source_target_pairs={{0,448},{64,0},{128,64},{192,128},{256,192},{320,256},{384,320},{4... | collective-permute-start | bytes 589832 | tf_op jit(solution)/shard_map/ppermute | solution.py:26
  63.7 2.3 %copy-start.3 = (s32[1024]{0:T(1024)S(1)}, s32[1024]{0:T(1024)}, u32[]{:S(2)}) copy-start(s32[1024]{0:T(1024)} %param.7) | copy-start | bytes 12292
  64.0 5.4 %collective-permute-start.11 = (bf16[3,2048,128]{2,1,0:T(8,128)(2,1)S(1)}, bf16[3,2048,128]{2,1,0:T(8,128)(2,1)}, u32[]{:S(2)}, u32[]{:S(2)}) collective-permute-start(bf16[3,2048,128]{2,1,0:T(8,128)(2,1)S(1)} %bitcast.102), channel_id=1, source_target_pairs={{0,8},{8,0},{1,9},{9,1},{2,10},{10,2},{3,11},{11,3},{4,12},{12,4},... | collective-permute-start | bytes 4718600 | tf_op jit(solution)/shard_map/ppermute | solution.py:46
  96.6 1.2 copy-start
  100.4 4.7 %copy-start.1 = (bf16[3,1024,256]{1,2,0:T(8,128)(2,1)S(1)}, bf16[3,1024,256]{1,2,0:T(8,128)(2,1)}, u32[]{:S(2)}) copy-start(bf16[3,1024,256]{1,2,0:T(8,128)(2,1)} %copy-done) | copy-start | bytes 4718596
  103.2 9.7 %collective-permute-start.12 = (f32[264,128]{1,0:T(8,128)S(1)}, f32[264,128]{1,0:T(8,128)S(1)}, u32[]{:S(2)}, u32[]{:S(2)}) collective-permute-start(f32[264,128]{1,0:T(8,128)S(1)} %concatenate.31), channel_id=1, source_target_pairs={{0,8},{8,16},{16,24},{24,32},{32,40},{40,48},{48,56},{56,64},{64,7... | collective-permute-start | bytes 405512 | tf_op jit(solution)/shard_map/ppermute | solution.py:15
  112.8 9.6 %collective-permute-start.13 = (f32[264,128]{1,0:T(8,128)S(1)}, f32[264,128]{1,0:T(8,128)S(1)}, u32[]{:S(2)}, u32[]{:S(2)}) collective-permute-start(f32[264,128]{1,0:T(8,128)S(1)} %collective-permute-done.12), channel_id=1, source_target_pairs={{0,8},{8,16},{16,24},{24,32},{32,40},{40,48},{48,56},{56,64},{64,7... | collective-permute-start | bytes 405512 | tf_op jit(solution)/shard_map/ppermute | solution.py:15
  124.5 10.3 %collective-permute-start.14 = (f32[264,128]{1,0:T(8,128)S(1)}, f32[264,128]{1,0:T(8,128)}, u32[]{:S(2)}, u32[]{:S(2)}) collective-permute-start(f32[264,128]{1,0:T(8,128)S(1)} %select_add_fusion.3), channel_id=1, source_target_pairs={{0,16},{8,24},{16,32},{24,40},{32,48},{40,56},{48,64},{56,72},{64,... | collective-permute-start | bytes 405512 | tf_op jit(solution)/shard_map/ppermute | solution.py:15
  130.3 22.2 %copy-start.2 = (bf16[512,256]{0,1:T(8,128)(2,1)S(1)}, bf16[512,256]{0,1:T(8,128)(2,1)}, u32[]{:S(2)}) copy-start(bf16[512,256]{0,1:T(8,128)(2,1)} %get-tuple-element.9) | copy-start | bytes 786436
  138.3 10.5 %collective-permute-start.15 = (f32[264,128]{1,0:T(8,128)S(1)}, f32[264,128]{1,0:T(8,128)S(1)}, u32[]{:S(2)}, u32[]{:S(2)}) collective-permute-start(f32[264,128]{1,0:T(8,128)S(1)} %select_add_fusion.2), channel_id=1, source_target_pairs={{0,32},{8,40},{16,48},{24,56},{32,64},{40,72},{48,80},{56,88},{64,... | collective-permute-start | bytes 405512 | tf_op jit(solution)/shard_map/ppermute | solution.py:15
  150.6 8.1 %collective-permute-start.16 = (f32[264,128]{1,0:T(8,128)S(1)}, f32[264,128]{1,0:T(8,128)S(1)}, u32[]{:S(2)}, u32[]{:S(2)}) collective-permute-start(f32[264,128]{1,0:T(8,128)S(1)} %select_add_fusion.1), channel_id=1, source_target_pairs={{0,64},{8,72},{16,80},{24,88},{32,96},{40,104},{48,112},{56,120},{... | collective-permute-start | bytes 405512 | tf_op jit(solution)/shard_map/ppermute | solution.py:15
  152.6 11.0 %copy-start.4 = (f32[256]{0:T(256)S(1)}, f32[256]{0:T(256)}, u32[]{:S(2)}) copy-start(f32[256]{0:T(256)} %param.6) | copy-start | bytes 3076
Sparse Core Ops, SparseCore 0:
  20.2 69.7 all-gather.1

commit v4 on v3

--- a/solution.py
+++ b/solution.py
@@ -57,22 +57,32 @@
 
 def state_scan(kv_state, tail_id, row_count):
     head_count = kv_state.shape[0]
-    flat = kv_state.reshape(head_count * HEAD_DIM, HEAD_DIM)
-    tail_rows = jnp.full((8, HEAD_DIM), tail_id, jnp.float32)
-    packed = jnp.concatenate([flat, tail_rows], axis=0)
     state_rows = head_count * HEAD_DIM
-    is_state = (jnp.arange(packed.shape[0]) < state_rows)[:, None]
-    count = lax.axis_size(CTX)
-    window = min(count - 1, 1 + (SPAN - 1) // row_count)
-    running = shifted(packed, CTX, 1, count)
-    step = 1
-    while step < window:
-        incoming = shifted(running, CTX, step, count)
-        linked = incoming[state_rows, 0] == running[state_rows, 0]
-        running = running + jnp.where(is_state & linked, incoming, 0.0)
-        step *= 2
-    state_in = running[:state_rows].reshape(head_count, HEAD_DIM, HEAD_DIM)
-    return state_in, running[state_rows, 0]
+    flat = kv_state.reshape(state_rows, HEAD_DIM)
+    packed = jnp.concatenate([flat, jnp.full((8, HEAD_DIM), tail_id, jnp.float32)], axis=0)
+    row_len = lax.axis_size("x") * lax.axis_size("core")
+    window = min(lax.axis_size(CTX) - 1, 1 + (SPAN - 1) // row_count)
+    assert window <= 2 * row_len
+    row = lax.all_gather(packed, ("x", "core"), axis=0, tiled=False)
+    states = row[:, :state_rows]
+    tails = row[:, state_rows, 0]
+    pos = lax.axis_index("x") * lax.axis_size("core") + lax.axis_index("core")
+    places = jnp.arange(row_len)
+    last_tail = tails[row_len - 1]
+    in_tail = tails == last_tail
+    row_total = jnp.sum(jnp.where(in_tail[:, None, None], states, 0.0), axis=0)
+    row_rest = jnp.sum(jnp.where((in_tail & (places >= pos))[:, None, None], states, 0.0), axis=0)
+    tail_block = jnp.full((8, HEAD_DIM), last_tail, jnp.float32)
+    y_count = lax.axis_size("y")
+    one_back = shifted(jnp.concatenate([row_total, tail_block], axis=0), "y", 1, y_count)
+    two_back = shifted(jnp.concatenate([row_rest, tail_block], axis=0), "y", 2, y_count)
+    prev_tail = jnp.where(pos > 0, tails[jnp.maximum(pos - 1, 0)], one_back[state_rows, 0])
+    before = (places < pos) & (tails == prev_tail)
+    state = jnp.sum(jnp.where(before[:, None, None], states, 0.0), axis=0)
+    state = state + jnp.where(one_back[state_rows, 0] == prev_tail, one_back[:state_rows], 0.0)
+    if window > row_len:
+        state = state + jnp.where(two_back[state_rows, 0] == prev_tail, two_back[:state_rows], 0.0)
+    return state.reshape(head_count, HEAD_DIM, HEAD_DIM), prev_tail
 
 
 def per_device(tokens, w_qkv, out_gain, seg_ids):

time: 173 us -> 172 us (level)
  starting transfers between devices: 47.6 us -> 42.4 us
  waiting for transfers between devices: 69.4 us -> 73.5 us
  between operations: 19.1 us -> 16.3 us
  other arithmetic: 8.11 us -> 10.9 us
    all_gather x0 -> x1, waiting for transfers between devices: none -> 17.2 us  [state_scan(): row = lax.all_gather(packed, ('x', 'core'), axis=0, tiled=False)]
    ppermute x5 -> x2, waiting for transfers between devices: 28.8 us -> 14 us  [shifted(): lax.ppermute(value, axis, [(source, source + steps) for source in range(c...]
    ppermute x5 -> x2, starting transfers between devices: 9.59 us -> 4.39 us  [shifted(): lax.ppermute(value, axis, [(source, source + steps) for source in range(c...]
    slice x10 -> x4, local copies, waits for them, and re-layouts: 5.49 us -> 2.31 us  [the longest x1 1.28 us: state_scan(): last_tail = tails[row_len - 1]]
    concatenate x1 -> x3, local copies, waits for them, and re-layouts: 0.65 us -> 2.49 us  [the longest x1 1.35 us: state_scan(): jnp.concatenate([flat, jnp.full((8, HEAD_DIM), tail_id, jnp.float32)], ax...]
  transfers between devices with their start and end apart: 18 -> 16, of which waited for: 16 -> 13; matrix products, arithmetic and copies ran while one was open for 8% -> 8% of each run, Pallas kernels for 0% -> 0%
where the time goes in v4:
time: 172 us; the launch traced here: 171 us
  waiting for transfers between devices  73.5 us (43%)
  starting transfers between devices  42.4 us (25%)
  between operations  16.3 us (9%)
  matrix products  16.1 us (9%)
  local copies, waits for them, and re-layouts  12.3 us (7%)
  other arithmetic  10.9 us (6%)
    all_gather x1, waiting for transfers between devices, per_device(): whole = lax.all_gather(tokens, 'head', axis=1, tiled=True)  20.5 us
    ppermute x4, starting transfers between devices, ring_gather(): lax.ppermute(behind, axis, [(j, (j - 1) % count) for j in range(count)])  20.3 us
    all_gather x1, waiting for transfers between devices, state_scan(): row = lax.all_gather(packed, ('x', 'core'), axis=0, tiled=False)  17.2 us
    ppermute x6, waiting for transfers between devices, ring_gather(): lax.ppermute(ahead, axis, [(j, (j + 1) % count) for j in range(count)])  15.1 us
    ppermute x2, waiting for transfers between devices, shifted(): lax.ppermute(value, axis, [(source, source + steps) for source in range(c...  14 us
    ppermute x6, starting transfers between devices, ring_gather(): lax.ppermute(ahead, axis, [(j, (j + 1) % count) for j in range(count)])  13.9 us
    dot_general x1, matrix products, per_device(): jnp.einsum('tr,grc->gtc', whole, w_rows, preferred_element_type=jnp.float32)  6.62 us
    dot_general x2, matrix products, per_device(): jnp.einsum('hbs,she->bhe', weights, values[:key_end], preferred_element_t...  5.51 us
  transfers between devices with their start and end apart: 16, of which 13 were waited for; matrix products, arithmetic and copies ran while one was open for 8% of the time, Pallas kernels for 0%

profile of v4, /device:TPU:32, one launch (start us, length us, event | category | flops | bytes accessed | tf_op | source)
XLA Modules:
  0.0 171.5 jit_solution(11996731560615904269)
XLA Ops:
  6.5 1.9 %collective-permute-start = (bf16[3,32,256]{2,1,0:T(8,128)(2,1)}, bf16[3,32,256]{2,1,0:T(8,128)(2,1)S(1)}, u32[]{:S(2)}, u32[]{:S(2)}) collective-permute-start(bf16[3,32,256]{2,1,0:T(8,128)(2,1)} %param.5), channel_id=1, source_target_pairs={{0,8},{8,0},{1,9},{9,1},{2,10},{10,2},{3,11},{11,3},{4,12},{12,4},... | collective-permute-start | bytes 147464 | tf_op jit(solution)/shard_map/ppermute | solution.py:40
  8.5 1.4 collective-permute-done
  10.6 3.4 %collective-permute-start.1 = (bf16[3,64,128]{2,1,0:T(8,128)(2,1)S(1)}, bf16[3,64,128]{2,1,0:T(8,128)(2,1)S(1)}, u32[]{:S(2)}, u32[]{:S(2)}) collective-permute-start(bf16[3,64,128]{2,1,0:T(8,128)(2,1)S(1)} %pad_maximum_fusion), channel_id=1, source_target_pairs={{0,16},{16,32},{32,48},{48,0},{1,17},{17,33},{33,49},{49,1},{2,18}... | collective-permute-start | bytes 147464 | tf_op jit(solution)/shard_map/ppermute | solution.py:23
  14.0 3.8 %collective-permute-done.1 = bf16[3,64,128]{2,1,0:T(8,128)(2,1)S(1)} collective-permute-done((bf16[3,64,128]{2,1,0:T(8,128)(2,1)S(1)}, bf16[3,64,128]{2,1,0:T(8,128)(2,1)S(1)}, u32[]{:S(2)}, u32[]{:S(2)}) %collective-permute-start.1) | collective-permute-done | bytes 49184 | tf_op jit(solution)/shard_map/ppermute | solution.py:23
  17.8 2.2 %collective-permute-start.2 = (bf16[3,64,128]{2,1,0:T(8,128)(2,1)S(1)}, bf16[3,64,128]{2,1,0:T(8,128)(2,1)S(1)}, u32[]{:S(2)}, u32[]{:S(2)}) collective-permute-start(bf16[3,64,128]{2,1,0:T(8,128)(2,1)S(1)} %collective-permute-done.1), channel_id=1, source_target_pairs={{0,16},{16,32},{32,48},{48,0},{1,17},{17,33},{33,49},{49,1},{2,18}... | collective-permute-start | bytes 147464 | tf_op jit(solution)/shard_map/ppermute | solution.py:23
  20.1 4.9 %collective-permute-start.3 = (bf16[3,64,128]{2,1,0:T(8,128)(2,1)S(1)}, bf16[3,64,128]{2,1,0:T(8,128)(2,1)S(1)}, u32[]{:S(2)}, u32[]{:S(2)}) collective-permute-start(bf16[3,64,128]{2,1,0:T(8,128)(2,1)S(1)} %pad_maximum_fusion), channel_id=1, source_target_pairs={{0,48},{16,0},{32,16},{48,32},{1,49},{17,1},{33,17},{49,33},{2,50}... | collective-permute-start | bytes 147464 | tf_op jit(solution)/shard_map/ppermute | solution.py:26
  25.0 1.7 collective-permute-done.3
  26.8 2.6 %collective-permute-start.4 = (bf16[3,256,128]{2,1,0:T(8,128)(2,1)S(1)}, bf16[3,256,128]{2,1,0:T(8,128)(2,1)S(1)}, u32[]{:S(2)}, u32[]{:S(2)}) collective-permute-start(bf16[3,256,128]{2,1,0:T(8,128)(2,1)S(1)} %bitcast.104), channel_id=1, source_target_pairs={{0,64},{64,128},{128,192},{192,256},{256,320},{320,384},{384,448},... | collective-permute-start | bytes 589832 | tf_op jit(solution)/shard_map/ppermute | solution.py:23
  29.4 6.2 %collective-permute-done.4 = bf16[3,256,128]{2,1,0:T(8,128)(2,1)S(1)} collective-permute-done((bf16[3,256,128]{2,1,0:T(8,128)(2,1)S(1)}, bf16[3,256,128]{2,1,0:T(8,128)(2,1)S(1)}, u32[]{:S(2)}, u32[]{:S(2)}) %collective-permute-start.4) | collective-permute-done | bytes 196640 | tf_op jit(solution)/shard_map/ppermute | solution.py:23
  35.6 1.9 %collective-permute-start.5 = (bf16[3,256,128]{2,1,0:T(8,128)(2,1)S(1)}, bf16[3,256,128]{2,1,0:T(8,128)(2,1)S(1)}, u32[]{:S(2)}, u32[]{:S(2)}) collective-permute-start(bf16[3,256,128]{2,1,0:T(8,128)(2,1)S(1)} %collective-permute-done.4), channel_id=1, source_target_pairs={{0,64},{64,128},{128,192},{192,256},{256,320},{320,384},{384,448},... | collective-permute-start | bytes 589832 | tf_op jit(solution)/shard_map/ppermute | solution.py:23
  37.5 5.1 %collective-permute-start.8 = (bf16[3,256,128]{2,1,0:T(8,128)(2,1)S(1)}, bf16[3,256,128]{2,1,0:T(8,128)(2,1)S(1)}, u32[]{:S(2)}, u32[]{:S(2)}) collective-permute-start(bf16[3,256,128]{2,1,0:T(8,128)(2,1)S(1)} %bitcast.105), channel_id=1, source_target_pairs={{0,448},{64,0},{128,64},{192,128},{256,192},{320,256},{384,320},{4... | collective-permute-start | bytes 589832 | tf_op jit(solution)/shard_map/ppermute | solution.py:26
  42.7 1.7 collective-permute-done.5
  44.4 1.9 %collective-permute-start.6 = (bf16[3,256,128]{2,1,0:T(8,128)(2,1)S(1)}, bf16[3,256,128]{2,1,0:T(8,128)(2,1)S(1)}, u32[]{:S(2)}, u32[]{:S(2)}) collective-permute-start(bf16[3,256,128]{2,1,0:T(8,128)(2,1)S(1)} %collective-permute-done.5), channel_id=1, source_target_pairs={{0,64},{64,128},{128,192},{192,256},{256,320},{320,384},{384,448},... | collective-permute-start | bytes 589832 | tf_op jit(solution)/shard_map/ppermute | solution.py:23
  46.3 5.1 %collective-permute-start.9 = (bf16[3,256,128]{2,1,0:T(8,128)(2,1)S(1)}, bf16[3,256,128]{2,1,0:T(8,128)(2,1)S(1)}, u32[]{:S(2)}, u32[]{:S(2)}) collective-permute-start(bf16[3,256,128]{2,1,0:T(8,128)(2,1)S(1)} %collective-permute-done.8), channel_id=1, source_target_pairs={{0,448},{64,0},{128,64},{192,128},{256,192},{320,256},{384,320},{4... | collective-permute-start | bytes 589832 | tf_op jit(solution)/shard_map/ppermute | solution.py:26
  51.4 1.7 collective-permute-done.6
  53.1 1.9 %collective-permute-start.7 = (bf16[3,256,128]{2,1,0:T(8,128)(2,1)S(1)}, bf16[3,256,128]{2,1,0:T(8,128)(2,1)S(1)}, u32[]{:S(2)}, u32[]{:S(2)}) collective-permute-start(bf16[3,256,128]{2,1,0:T(8,128)(2,1)S(1)} %collective-permute-done.6), channel_id=1, source_target_pairs={{0,64},{64,128},{128,192},{192,256},{256,320},{320,384},{384,448},... | collective-permute-start | bytes 589832 | tf_op jit(solution)/shard_map/ppermute | solution.py:23
  55.1 5.1 %collective-permute-start.10 = (bf16[3,256,128]{2,1,0:T(8,128)(2,1)S(1)}, bf16[3,256,128]{2,1,0:T(8,128)(2,1)S(1)}, u32[]{:S(2)}, u32[]{:S(2)}) collective-permute-start(bf16[3,256,128]{2,1,0:T(8,128)(2,1)S(1)} %collective-permute-done.9), channel_id=1, source_target_pairs={{0,448},{64,0},{128,64},{192,128},{256,192},{320,256},{384,320},{4... | collective-permute-start | bytes 589832 | tf_op jit(solution)/shard_map/ppermute | solution.py:26
  60.2 1.7 collective-permute-done.7
  64.0 1.9 %collective-permute-start.11 = (bf16[3,2048,128]{2,1,0:T(8,128)(2,1)S(1)}, bf16[3,2048,128]{2,1,0:T(8,128)(2,1)}, u32[]{:S(2)}, u32[]{:S(2)}) collective-permute-start(bf16[3,2048,128]{2,1,0:T(8,128)(2,1)S(1)} %bitcast.108), channel_id=1, source_target_pairs={{0,8},{8,0},{1,9},{9,1},{2,10},{10,2},{3,11},{11,3},{4,12},{12,4},... | collective-permute-start | bytes 4718600 | tf_op jit(solution)/shard_map/ppermute | solution.py:46
  67.2 2.2 %collective-permute-done.11 = bf16[3,2048,128]{2,1,0:T(8,128)(2,1)} collective-permute-done((bf16[3,2048,128]{2,1,0:T(8,128)(2,1)S(1)}, bf16[3,2048,128]{2,1,0:T(8,128)(2,1)}, u32[]{:S(2)}, u32[]{:S(2)}) %collective-permute-start.11) | collective-permute-done | bytes 1572896 | tf_op jit(solution)/shard_map/ppermute | solution.py:46
  69.4 20.5 %all-gather.4.cloned.1.call-done = bf16[1024,2048]{1,0:T(8,128)(2,1)} async-done(((bf16[1024,256]{1,0:T(8,128)(2,1)}), bf16[1024,2048]{1,0:T(8,128)(2,1)}) %all-gather.4.cloned.1.call-update) | async-done | bytes 4194320 | tf_op jit(solution)/shard_map/all_gather | solution.py:89
  90.0 6.6 %fusion.13 = bf16[3,1024,256]{1,2,0:T(8,128)(2,1)S(1)} fusion(bf16[1024,2048]{1,0:T(8,128)(2,1)} %all-gather.4.cloned.1.call-done, bf16[3,2048,128]{2,1,0:T(8,128)(2,1)} %collective-permute-done.11, bf16[3,2048,128]{2,1,0:T(8,128)(2,1)S(1)} %bitcast.109, pred[]{:T(512)S(6)} %eq.77), kind=kOutput, calls=%fused_computation.24 | convolution fusion | flops 3236167680 | bytes 8912897 | tf_op jit(solution)/shard_map/tr,grc->gtc/dot_general | solution.py:91
  100.3 2.1 %fusion.37 = f32[2,128,128]{2,1,0:T(8,128)S(1)} fusion(bf16[1024,2,128]{0,2,1:T(8,128)(2,1)S(1)} %bitcast.110, pred[1024]{0:T(1024)(128)(4,1)S(1)} %broadcast_compare_fusion.1, f32[1024,2,128]{2,0,1:T(8,128)} %copy.52), kind=kOutput, calls=%fused_computation.54 | convolution fusion | flops 68681728 | bytes 1704960 | tf_op jit(solution)/shard_map/thd,the->hde/dot_general | solution.py:102
  109.9 3.9 %fusion.19 = f32[512,2,128]{0,2,1:T(8,128)} fusion(bf16[1024,2,128]{0,2,1:T(8,128)(2,1)S(1)} %bitcast.111, bf16[512,2,128]{0,2,1:T(8,128)(2,1)S(1)} %bitcast.115, pred[512,1024]{1,0:T(8,128)(4,1)} %fusion.8, f32[1024,2,128]{2,0,1:T(8,128)} %copy.52), kind=kOutput, calls=%fused_computation.29 | convolution fusion | flops 540278784 | bytes 2883584 | tf_op jit(solution)/shard_map/hbs,she->bhe/dot_general | solution.py:122
  113.8 17.2 %all-gather.6.cloned.1.call-done = f32[2112,128]{1,0:T(8,128)} async-done(((f32[264,128]{1,0:T(8,128)}), f32[2112,128]{1,0:T(8,128)}) %all-gather.6.cloned.1.call-update) | async-done | bytes 1081360 | tf_op jit(solution)/shard_map/all_gather | solution.py:66
  132.3 1.6 compare_reduce_fusion
  135.9 2.5 %collective-permute-start.12 = (f32[264,128]{1,0:T(8,128)S(1)}, f32[264,128]{1,0:T(8,128)S(1)}, u32[]{:S(2)}, u32[]{:S(2)}) collective-permute-start(f32[264,128]{1,0:T(8,128)S(1)} %concatenate.38), channel_id=1, source_target_pairs={{0,64},{64,128},{128,192},{192,256},{256,320},{320,384},{384,448},... | collective-permute-start | bytes 405512 | tf_op jit(solution)/shard_map/ppermute | solution.py:15
  138.4 1.6 fusion.20
  140.5 4.2 %collective-permute-done.12 = f32[264,128]{1,0:T(8,128)S(1)} collective-permute-done((f32[264,128]{1,0:T(8,128)S(1)}, f32[264,128]{1,0:T(8,128)S(1)}, u32[]{:S(2)}, u32[]{:S(2)}) %collective-permute-start.12) | collective-permute-done | bytes 135200 | tf_op jit(solution)/shard_map/ppermute | solution.py:15
  148.7 1.9 %collective-permute-start.13 = (f32[264,128]{1,0:T(8,128)S(1)}, f32[264,128]{1,0:T(8,128)S(1)}, u32[]{:S(2)}, u32[]{:S(2)}) collective-permute-start(f32[264,128]{1,0:T(8,128)S(1)} %concatenate.39), channel_id=1, source_target_pairs={{0,128},{64,192},{128,256},{192,320},{256,384},{320,448},{1,129},{... | collective-permute-start | bytes 405512 | tf_op jit(solution)/shard_map/ppermute | solution.py:15
  150.7 9.8 %collective-permute-done.13 = f32[264,128]{1,0:T(8,128)S(1)} collective-permute-done((f32[264,128]{1,0:T(8,128)S(1)}, f32[264,128]{1,0:T(8,128)S(1)}, u32[]{:S(2)}, u32[]{:S(2)}) %collective-permute-start.13) | collective-permute-done | bytes 135200 | tf_op jit(solution)/shard_map/ppermute | solution.py:15
  161.6 1.8 %multiply_reduce_fusion = (f32[1024,2]{0,1:T(2,128)S(1)}, f32[1024,2,128]{0,2,1:T(8,128)S(1)}) fusion(bf16[2,128,128]{2,1,0:T(8,128)(2,1)S(1)} %bitcast.117, f32[1024,2,128]{2,0,1:T(8,128)S(1)} %copy-done.3, pred[1024]{0:T(1024)(128)(4,1)S(1)} %broadcast_compare_fusion, f32[512,2,128]{0,2,1:T(8,128)} %fusion.19, f32[512,2,128]{0,2,1:T(8,128)} %fusion.20), kind=kOutput, calls=%fused_computation.41 | convolution fusion | flops 69728256 | bytes 3220480 | tf_op jit(solution)/shard_map/thd,hde->the/dot_general | solution.py:127
  (83 shorter events, 23.0 us)
Async XLA Ops:
  6.5 83.4 %all-gather.4.cloned.1.call-start = ((), (), s32[]{:S(2)}) async-start(), calls=%async_computation | async-start | bytes 4718592 | tf_op jit(solution)/shard_map/all_gather | solution.py:89
  6.5 3.3 %collective-permute-start = (bf16[3,32,256]{2,1,0:T(8,128)(2,1)}, bf16[3,32,256]{2,1,0:T(8,128)(2,1)S(1)}, u32[]{:S(2)}, u32[]{:S(2)}) collective-permute-start(bf16[3,32,256]{2,1,0:T(8,128)(2,1)} %param.5), channel_id=1, source_target_pairs={{0,8},{8,0},{1,9},{9,1},{2,10},{10,2},{3,11},{11,3},{4,12},{12,4},... | collective-permute-start | bytes 147464 | tf_op jit(solution)/shard_map/ppermute | solution.py:40
  10.6 7.2 %collective-permute-start.1 = (bf16[3,64,128]{2,1,0:T(8,128)(2,1)S(1)}, bf16[3,64,128]{2,1,0:T(8,128)(2,1)S(1)}, u32[]{:S(2)}, u32[]{:S(2)}) collective-permute-start(bf16[3,64,128]{2,1,0:T(8,128)(2,1)S(1)} %pad_maximum_fusion), channel_id=1, source_target_pairs={{0,16},{16,32},{32,48},{48,0},{1,17},{17,33},{33,49},{49,1},{2,18}... | collective-permute-start | bytes 147464 | tf_op jit(solution)/shard_map/ppermute | solution.py:23
  17.8 7.2 %collective-permute-start.2 = (bf16[3,64,128]{2,1,0:T(8,128)(2,1)S(1)}, bf16[3,64,128]{2,1,0:T(8,128)(2,1)S(1)}, u32[]{:S(2)}, u32[]{:S(2)}) collective-permute-start(bf16[3,64,128]{2,1,0:T(8,128)(2,1)S(1)} %collective-permute-done.1), channel_id=1, source_target_pairs={{0,16},{16,32},{32,48},{48,0},{1,17},{17,33},{33,49},{49,1},{2,18}... | collective-permute-start | bytes 147464 | tf_op jit(solution)/shard_map/ppermute | solution.py:23
  20.0 111.0 %all-gather.6.cloned.1.call-start = ((), (), s32[]{:S(2)}) async-start(), calls=%async_computation.1 | async-start | bytes 1216512 | tf_op jit(solution)/shard_map/all_gather | solution.py:66
  20.1 6.6 %collective-permute-start.3 = (bf16[3,64,128]{2,1,0:T(8,128)(2,1)S(1)}, bf16[3,64,128]{2,1,0:T(8,128)(2,1)S(1)}, u32[]{:S(2)}, u32[]{:S(2)}) collective-permute-start(bf16[3,64,128]{2,1,0:T(8,128)(2,1)S(1)} %pad_maximum_fusion), channel_id=1, source_target_pairs={{0,48},{16,0},{32,16},{48,32},{1,49},{17,1},{33,17},{49,33},{2,50}... | collective-permute-start | bytes 147464 | tf_op jit(solution)/shard_map/ppermute | solution.py:26
  26.8 8.8 %collective-permute-start.4 = (bf16[3,256,128]{2,1,0:T(8,128)(2,1)S(1)}, bf16[3,256,128]{2,1,0:T(8,128)(2,1)S(1)}, u32[]{:S(2)}, u32[]{:S(2)}) collective-permute-start(bf16[3,256,128]{2,1,0:T(8,128)(2,1)S(1)} %bitcast.104), channel_id=1, source_target_pairs={{0,64},{64,128},{128,192},{192,256},{256,320},{320,384},{384,448},... | collective-permute-start | bytes 589832 | tf_op jit(solution)/shard_map/ppermute | solution.py:23
  35.6 8.8 %collective-permute-start.5 = (bf16[3,256,128]{2,1,0:T(8,128)(2,1)S(1)}, bf16[3,256,128]{2,1,0:T(8,128)(2,1)S(1)}, u32[]{:S(2)}, u32[]{:S(2)}) collective-permute-start(bf16[3,256,128]{2,1,0:T(8,128)(2,1)S(1)} %collective-permute-done.4), channel_id=1, source_target_pairs={{0,64},{64,128},{128,192},{192,256},{256,320},{320,384},{384,448},... | collective-permute-start | bytes 589832 | tf_op jit(solution)/shard_map/ppermute | solution.py:23
  37.5 8.8 %collective-permute-start.8 = (bf16[3,256,128]{2,1,0:T(8,128)(2,1)S(1)}, bf16[3,256,128]{2,1,0:T(8,128)(2,1)S(1)}, u32[]{:S(2)}, u32[]{:S(2)}) collective-permute-start(bf16[3,256,128]{2,1,0:T(8,128)(2,1)S(1)} %bitcast.105), channel_id=1, source_target_pairs={{0,448},{64,0},{128,64},{192,128},{256,192},{320,256},{384,320},{4... | collective-permute-start | bytes 589832 | tf_op jit(solution)/shard_map/ppermute | solution.py:26
  44.4 8.8 %collective-permute-start.6 = (bf16[3,256,128]{2,1,0:T(8,128)(2,1)S(1)}, bf16[3,256,128]{2,1,0:T(8,128)(2,1)S(1)}, u32[]{:S(2)}, u32[]{:S(2)}) collective-permute-start(bf16[3,256,128]{2,1,0:T(8,128)(2,1)S(1)} %collective-permute-done.5), channel_id=1, source_target_pairs={{0,64},{64,128},{128,192},{192,256},{256,320},{320,384},{384,448},... | collective-permute-start | bytes 589832 | tf_op jit(solution)/shard_map/ppermute | solution.py:23
  46.3 8.8 %collective-permute-start.9 = (bf16[3,256,128]{2,1,0:T(8,128)(2,1)S(1)}, bf16[3,256,128]{2,1,0:T(8,128)(2,1)S(1)}, u32[]{:S(2)}, u32[]{:S(2)}) collective-permute-start(bf16[3,256,128]{2,1,0:T(8,128)(2,1)S(1)} %collective-permute-done.8), channel_id=1, source_target_pairs={{0,448},{64,0},{128,64},{192,128},{256,192},{320,256},{384,320},{4... | collective-permute-start | bytes 589832 | tf_op jit(solution)/shard_map/ppermute | solution.py:26
  53.1 8.8 %collective-permute-start.7 = (bf16[3,256,128]{2,1,0:T(8,128)(2,1)S(1)}, bf16[3,256,128]{2,1,0:T(8,128)(2,1)S(1)}, u32[]{:S(2)}, u32[]{:S(2)}) collective-permute-start(bf16[3,256,128]{2,1,0:T(8,128)(2,1)S(1)} %collective-permute-done.6), channel_id=1, source_target_pairs={{0,64},{64,128},{128,192},{192,256},{256,320},{320,384},{384,448},... | collective-permute-start | bytes 589832 | tf_op jit(solution)/shard_map/ppermute | solution.py:23
  55.1 8.3 %collective-permute-start.10 = (bf16[3,256,128]{2,1,0:T(8,128)(2,1)S(1)}, bf16[3,256,128]{2,1,0:T(8,128)(2,1)S(1)}, u32[]{:S(2)}, u32[]{:S(2)}) collective-permute-start(bf16[3,256,128]{2,1,0:T(8,128)(2,1)S(1)} %collective-permute-done.9), channel_id=1, source_target_pairs={{0,448},{64,0},{128,64},{192,128},{256,192},{320,256},{384,320},{4... | collective-permute-start | bytes 589832 | tf_op jit(solution)/shard_map/ppermute | solution.py:26
  63.7 2.2 %copy-start.6 = (s32[1024]{0:T(1024)S(1)}, s32[1024]{0:T(1024)}, u32[]{:S(2)}) copy-start(s32[1024]{0:T(1024)} %param.7) | copy-start | bytes 12292
  64.0 5.4 %collective-permute-start.11 = (bf16[3,2048,128]{2,1,0:T(8,128)(2,1)S(1)}, bf16[3,2048,128]{2,1,0:T(8,128)(2,1)}, u32[]{:S(2)}, u32[]{:S(2)}) collective-permute-start(bf16[3,2048,128]{2,1,0:T(8,128)(2,1)S(1)} %bitcast.108), channel_id=1, source_target_pairs={{0,8},{8,0},{1,9},{9,1},{2,10},{10,2},{3,11},{11,3},{4,12},{12,4},... | collective-permute-start | bytes 4718600 | tf_op jit(solution)/shard_map/ppermute | solution.py:46
  96.6 1.2 copy-start.1
  100.3 5.7 %copy-start.2 = (bf16[3,1024,256]{1,2,0:T(8,128)(2,1)S(1)}, bf16[3,1024,256]{1,2,0:T(8,128)(2,1)}, u32[]{:S(2)}) copy-start(bf16[3,1024,256]{1,2,0:T(8,128)(2,1)} %copy-done.1) | copy-start | bytes 4718596
  109.9 28.4 %copy-start.4 = (pred[512,512]{1,0:T(8,128)(4,1)S(1)}, pred[512,512]{1,0:T(8,128)(4,1)}, u32[]{:S(2)}) copy-start(pred[512,512]{1,0:T(8,128)(4,1)} %fusion.31) | copy-start | bytes 786436
  109.9 28.4 %copy-start.5 = (bf16[1,512,256]{1,2,0:T(8,128)(2,1)S(1)}, bf16[1,512,256]{1,2,0:T(8,128)(2,1)}, u32[]{:S(2)}) copy-start(bf16[1,512,256]{1,2,0:T(8,128)(2,1)} %slice.107) | copy-start | bytes 786436
  113.8 47.8 %copy-start.3 = (f32[1024,2,128]{2,0,1:T(8,128)S(1)}, f32[1024,2,128]{2,0,1:T(8,128)}, u32[]{:S(2)}) copy-start(f32[1024,2,128]{2,0,1:T(8,128)} %copy.58) | copy-start | bytes 3145732
  131.1 8.9 %copy-start = (f32[2112,128]{1,0:T(8,128)S(1)}, f32[2112,128]{1,0:T(8,128)}, u32[]{:S(2)}) copy-start(f32[2112,128]{1,0:T(8,128)} %all-gather.6.cloned.1.call-done) | copy-start | bytes 3244036
  135.9 8.9 %collective-permute-start.12 = (f32[264,128]{1,0:T(8,128)S(1)}, f32[264,128]{1,0:T(8,128)S(1)}, u32[]{:S(2)}, u32[]{:S(2)}) collective-permute-start(f32[264,128]{1,0:T(8,128)S(1)} %concatenate.38), channel_id=1, source_target_pairs={{0,64},{64,128},{128,192},{192,256},{256,320},{320,384},{384,448},... | collective-permute-start | bytes 405512 | tf_op jit(solution)/shard_map/ppermute | solution.py:15
  140.0 23.5 %copy-start.7 = (f32[256]{0:T(256)S(1)}, f32[256]{0:T(256)}, u32[]{:S(2)}) copy-start(f32[256]{0:T(256)} %param.6) | copy-start | bytes 3076
  148.7 11.7 %collective-permute-start.13 = (f32[264,128]{1,0:T(8,128)S(1)}, f32[264,128]{1,0:T(8,128)S(1)}, u32[]{:S(2)}, u32[]{:S(2)}) collective-permute-start(f32[264,128]{1,0:T(8,128)S(1)} %concatenate.39), channel_id=1, source_target_pairs={{0,128},{64,192},{128,256},{192,320},{256,384},{320,448},{1,129},{... | collective-permute-start | bytes 405512 | tf_op jit(solution)/shard_map/ppermute | solution.py:15
Sparse Core Ops, SparseCore 0:
  20.2 69.7 all-gather.3
  103.9 27.0 all-gather.5

commit v5 on v3

--- a/solution.py
+++ b/solution.py
@@ -57,22 +57,29 @@
 
 def state_scan(kv_state, tail_id, row_count):
     head_count = kv_state.shape[0]
-    flat = kv_state.reshape(head_count * HEAD_DIM, HEAD_DIM)
-    tail_rows = jnp.full((8, HEAD_DIM), tail_id, jnp.float32)
-    packed = jnp.concatenate([flat, tail_rows], axis=0)
     state_rows = head_count * HEAD_DIM
-    is_state = (jnp.arange(packed.shape[0]) < state_rows)[:, None]
+    flat = kv_state.reshape(state_rows, HEAD_DIM)
     count = lax.axis_size(CTX)
     window = min(count - 1, 1 + (SPAN - 1) // row_count)
-    running = shifted(packed, CTX, 1, count)
-    step = 1
-    while step < window:
-        incoming = shifted(running, CTX, step, count)
-        linked = incoming[state_rows, 0] == running[state_rows, 0]
-        running = running + jnp.where(is_state & linked, incoming, 0.0)
-        step *= 2
-    state_in = running[:state_rows].reshape(head_count, HEAD_DIM, HEAD_DIM)
-    return state_in, running[state_rows, 0]
+    packed = jnp.concatenate([flat, jnp.full((8, HEAD_DIM), tail_id, jnp.float32)], axis=0)
+    radix = 4
+    span = 1
+    running = None
+    while span < window:
+        got = [shifted(packed if running is None else running, CTX, span * k, count)
+               for k in range(1, radix + (running is None))]
+        if running is None:
+            prev_tail = got[0][state_rows, 0]
+            total = sum(jnp.where(g[state_rows, 0] == prev_tail, g[:state_rows], 0.0) for g in got)
+            running = jnp.concatenate([total, jnp.full((8, HEAD_DIM), prev_tail, jnp.float32)], axis=0)
+            span = radix
+        else:
+            total = running[:state_rows] + sum(
+                jnp.where(g[state_rows, 0] == prev_tail, g[:state_rows], 0.0) for g in got
+            )
+            running = jnp.concatenate([total, running[state_rows:]], axis=0)
+            span *= radix
+    return running[:state_rows].reshape(head_count, HEAD_DIM, HEAD_DIM), prev_tail
 
 
 def per_device(tokens, w_qkv, out_gain, seg_ids):

time: 173 us -> 168 us (0.971)
  the two profiles are of different devices: /device:TPU:32 before, /device:TPU:24 now
where the time goes in v5:
time: 168 us; the launch traced here: 167 us
  starting transfers between devices  66.7 us (40%)
  waiting for transfers between devices  41.7 us (25%)
  between operations  23 us (14%)
  local copies, waits for them, and re-layouts  14.7 us (9%)
  matrix products  13.3 us (8%)
  other arithmetic  7.55 us (4%)
    ppermute x6, starting transfers between devices, ring_gather(): lax.ppermute(ahead, axis, [(j, (j + 1) % count) for j in range(count)])  27 us
    ppermute x7, starting transfers between devices, shifted(): lax.ppermute(value, axis, [(source, source + steps) for source in range(c...  25.3 us
    all_gather x1, waiting for transfers between devices, per_device(): whole = lax.all_gather(tokens, 'head', axis=1, tiled=True)  17.4 us
    ppermute x6, waiting for transfers between devices, ring_gather(): lax.ppermute(ahead, axis, [(j, (j + 1) % count) for j in range(count)])  10.7 us
    ppermute x4, starting transfers between devices, ring_gather(): lax.ppermute(behind, axis, [(j, (j - 1) % count) for j in range(count)])  10.6 us
    ppermute x4, waiting for transfers between devices, ring_gather(): lax.ppermute(behind, axis, [(j, (j - 1) % count) for j in range(count)])  7.04 us
    dot_general x1, matrix products, per_device(): jnp.einsum('tr,grc->gtc', whole, w_rows, preferred_element_type=jnp.float32)  5.67 us
    slice x6, local copies, waits for them, and re-layouts, state_scan(): g[state_rows, 0] == prev_tail  5.25 us
  transfers between devices with their start and end apart: 20, of which 11 were waited for; matrix products, arithmetic and copies ran while one was open for 10% of the time, Pallas kernels for 0%

profile of v5, /device:TPU:24, one launch (start us, length us, event | category | flops | bytes accessed | tf_op | source)
XLA Modules:
  0.0 167.0 jit_solution(8781600548025541768)
XLA Ops:
  6.5 1.9 %collective-permute-start = (bf16[3,32,256]{2,1,0:T(8,128)(2,1)}, bf16[3,32,256]{2,1,0:T(8,128)(2,1)S(1)}, u32[]{:S(2)}, u32[]{:S(2)}) collective-permute-start(bf16[3,32,256]{2,1,0:T(8,128)(2,1)} %param.5), channel_id=1, source_target_pairs={{0,8},{8,0},{1,9},{9,1},{2,10},{10,2},{3,11},{11,3},{4,12},{12,4},... | collective-permute-start | bytes 147464 | tf_op jit(solution)/shard_map/ppermute | solution.py:40
  8.5 1.4 collective-permute-done
  10.6 3.4 %collective-permute-start.1 = (bf16[3,64,128]{2,1,0:T(8,128)(2,1)S(1)}, bf16[3,64,128]{2,1,0:T(8,128)(2,1)S(1)}, u32[]{:S(2)}, u32[]{:S(2)}) collective-permute-start(bf16[3,64,128]{2,1,0:T(8,128)(2,1)S(1)} %pad_maximum_fusion), channel_id=1, source_target_pairs={{0,16},{16,32},{32,48},{48,0},{1,17},{17,33},{33,49},{49,1},{2,18}... | collective-permute-start | bytes 147464 | tf_op jit(solution)/shard_map/ppermute | solution.py:23
  14.0 3.8 %collective-permute-done.1 = bf16[3,64,128]{2,1,0:T(8,128)(2,1)S(1)} collective-permute-done((bf16[3,64,128]{2,1,0:T(8,128)(2,1)S(1)}, bf16[3,64,128]{2,1,0:T(8,128)(2,1)S(1)}, u32[]{:S(2)}, u32[]{:S(2)}) %collective-permute-start.1) | collective-permute-done | bytes 49184 | tf_op jit(solution)/shard_map/ppermute | solution.py:23
  17.8 2.2 %collective-permute-start.2 = (bf16[3,64,128]{2,1,0:T(8,128)(2,1)S(1)}, bf16[3,64,128]{2,1,0:T(8,128)(2,1)S(1)}, u32[]{:S(2)}, u32[]{:S(2)}) collective-permute-start(bf16[3,64,128]{2,1,0:T(8,128)(2,1)S(1)} %collective-permute-done.1), channel_id=1, source_target_pairs={{0,16},{16,32},{32,48},{48,0},{1,17},{17,33},{33,49},{49,1},{2,18}... | collective-permute-start | bytes 147464 | tf_op jit(solution)/shard_map/ppermute | solution.py:23
  20.1 4.9 %collective-permute-start.3 = (bf16[3,64,128]{2,1,0:T(8,128)(2,1)S(1)}, bf16[3,64,128]{2,1,0:T(8,128)(2,1)S(1)}, u32[]{:S(2)}, u32[]{:S(2)}) collective-permute-start(bf16[3,64,128]{2,1,0:T(8,128)(2,1)S(1)} %pad_maximum_fusion), channel_id=1, source_target_pairs={{0,48},{16,0},{32,16},{48,32},{1,49},{17,1},{33,17},{49,33},{2,50}... | collective-permute-start | bytes 147464 | tf_op jit(solution)/shard_map/ppermute | solution.py:26
  25.0 1.6 collective-permute-done.3
  26.8 4.7 %collective-permute-start.4 = (bf16[3,256,128]{2,1,0:T(8,128)(2,1)S(1)}, bf16[3,256,128]{2,1,0:T(8,128)(2,1)S(1)}, u32[]{:S(2)}, u32[]{:S(2)}) collective-permute-start(bf16[3,256,128]{2,1,0:T(8,128)(2,1)S(1)} %bitcast.102), channel_id=1, source_target_pairs={{0,64},{64,128},{128,192},{192,256},{256,320},{320,384},{384,448},... | collective-permute-start | bytes 589832 | tf_op jit(solution)/shard_map/ppermute | solution.py:23
  31.5 3.2 %collective-permute-done.4 = bf16[3,256,128]{2,1,0:T(8,128)(2,1)S(1)} collective-permute-done((bf16[3,256,128]{2,1,0:T(8,128)(2,1)S(1)}, bf16[3,256,128]{2,1,0:T(8,128)(2,1)S(1)}, u32[]{:S(2)}, u32[]{:S(2)}) %collective-permute-start.4) | collective-permute-done | bytes 196640 | tf_op jit(solution)/shard_map/ppermute | solution.py:23
  34.6 5.6 %collective-permute-start.5 = (bf16[3,256,128]{2,1,0:T(8,128)(2,1)S(1)}, bf16[3,256,128]{2,1,0:T(8,128)(2,1)S(1)}, u32[]{:S(2)}, u32[]{:S(2)}) collective-permute-start(bf16[3,256,128]{2,1,0:T(8,128)(2,1)S(1)} %collective-permute-done.4), channel_id=1, source_target_pairs={{0,64},{64,128},{128,192},{192,256},{256,320},{320,384},{384,448},... | collective-permute-start | bytes 589832 | tf_op jit(solution)/shard_map/ppermute | solution.py:23
  40.2 1.9 %collective-permute-start.8 = (bf16[3,256,128]{2,1,0:T(8,128)(2,1)S(1)}, bf16[3,256,128]{2,1,0:T(8,128)(2,1)S(1)}, u32[]{:S(2)}, u32[]{:S(2)}) collective-permute-start(bf16[3,256,128]{2,1,0:T(8,128)(2,1)S(1)} %bitcast.103), channel_id=1, source_target_pairs={{0,448},{64,0},{128,64},{192,128},{256,192},{320,256},{384,320},{4... | collective-permute-start | bytes 589832 | tf_op jit(solution)/shard_map/ppermute | solution.py:26
  43.4 5.6 %collective-permute-start.6 = (bf16[3,256,128]{2,1,0:T(8,128)(2,1)S(1)}, bf16[3,256,128]{2,1,0:T(8,128)(2,1)S(1)}, u32[]{:S(2)}, u32[]{:S(2)}) collective-permute-start(bf16[3,256,128]{2,1,0:T(8,128)(2,1)S(1)} %collective-permute-done.5), channel_id=1, source_target_pairs={{0,64},{64,128},{128,192},{192,256},{256,320},{320,384},{384,448},... | collective-permute-start | bytes 589832 | tf_op jit(solution)/shard_map/ppermute | solution.py:23
  49.0 1.9 %collective-permute-start.9 = (bf16[3,256,128]{2,1,0:T(8,128)(2,1)S(1)}, bf16[3,256,128]{2,1,0:T(8,128)(2,1)S(1)}, u32[]{:S(2)}, u32[]{:S(2)}) collective-permute-start(bf16[3,256,128]{2,1,0:T(8,128)(2,1)S(1)} %collective-permute-done.8), channel_id=1, source_target_pairs={{0,448},{64,0},{128,64},{192,128},{256,192},{320,256},{384,320},{4... | collective-permute-start | bytes 589832 | tf_op jit(solution)/shard_map/ppermute | solution.py:26
  52.2 5.6 %collective-permute-start.7 = (bf16[3,256,128]{2,1,0:T(8,128)(2,1)S(1)}, bf16[3,256,128]{2,1,0:T(8,128)(2,1)S(1)}, u32[]{:S(2)}, u32[]{:S(2)}) collective-permute-start(bf16[3,256,128]{2,1,0:T(8,128)(2,1)S(1)} %collective-permute-done.6), channel_id=1, source_target_pairs={{0,64},{64,128},{128,192},{192,256},{256,320},{320,384},{384,448},... | collective-permute-start | bytes 589832 | tf_op jit(solution)/shard_map/ppermute | solution.py:23
  57.8 1.9 %collective-permute-start.10 = (bf16[3,256,128]{2,1,0:T(8,128)(2,1)S(1)}, bf16[3,256,128]{2,1,0:T(8,128)(2,1)S(1)}, u32[]{:S(2)}, u32[]{:S(2)}) collective-permute-start(bf16[3,256,128]{2,1,0:T(8,128)(2,1)S(1)} %collective-permute-done.9), channel_id=1, source_target_pairs={{0,448},{64,0},{128,64},{192,128},{256,192},{320,256},{384,320},{4... | collective-permute-start | bytes 589832 | tf_op jit(solution)/shard_map/ppermute | solution.py:26
  61.2 5.4 %collective-permute-done.10 = bf16[3,256,128]{2,1,0:T(8,128)(2,1)S(1)} collective-permute-done((bf16[3,256,128]{2,1,0:T(8,128)(2,1)S(1)}, bf16[3,256,128]{2,1,0:T(8,128)(2,1)S(1)}, u32[]{:S(2)}, u32[]{:S(2)}) %collective-permute-start.10) | collective-permute-done | bytes 196640 | tf_op jit(solution)/shard_map/ppermute | solution.py:26
  67.2 1.9 %collective-permute-start.11 = (bf16[3,2048,128]{2,1,0:T(8,128)(2,1)S(1)}, bf16[3,2048,128]{2,1,0:T(8,128)(2,1)S(1)}, u32[]{:S(2)}, u32[]{:S(2)}) collective-permute-start(bf16[3,2048,128]{2,1,0:T(8,128)(2,1)S(1)} %bitcast.106), channel_id=1, source_target_pairs={{0,8},{8,0},{1,9},{9,1},{2,10},{10,2},{3,11},{11,3},{4,12},{12,4},... | collective-permute-start | bytes 4718600 | tf_op jit(solution)/shard_map/ppermute | solution.py:46
  71.4 1.3 fusion.8
  72.7 17.4 %all-gather.2.cloned.1.call-done = bf16[1024,2048]{1,0:T(8,128)(2,1)} async-done(((bf16[1024,256]{1,0:T(8,128)(2,1)}), bf16[1024,2048]{1,0:T(8,128)(2,1)}) %all-gather.2.cloned.1.call-update) | async-done | bytes 4194320 | tf_op jit(solution)/shard_map/all_gather | solution.py:86
  90.1 5.7 %fusion.13 = bf16[3,1024,256]{1,2,0:T(8,128)(2,1)S(1)} fusion(bf16[1024,2048]{1,0:T(8,128)(2,1)} %all-gather.2.cloned.1.call-done, bf16[3,2048,128]{2,1,0:T(8,128)(2,1)S(1)} %collective-permute-done.11, bf16[3,2048,128]{2,1,0:T(8,128)(2,1)S(1)} %bitcast.107, pred[]{:T(512)S(6)} %eq.77), kind=kOutput, calls=%fused_computation.24 | convolution fusion | flops 3236167680 | bytes 8912897 | tf_op jit(solution)/shard_map/tr,grc->gtc/dot_general | solution.py:88
  98.0 1.3 copy.52
  99.4 2.2 %fusion.36 = f32[2,128,128]{2,1,0:T(8,128)S(1)} fusion(bf16[1024,2,128]{0,2,1:T(8,128)(2,1)} %bitcast.108, pred[1024]{0:T(1024)(128)(4,1)S(1)} %broadcast_compare_fusion.1, f32[1024,2,128]{2,0,1:T(8,128)} %copy.52), kind=kOutput, calls=%fused_computation.50 | convolution fusion | flops 68681728 | bytes 1704960 | tf_op jit(solution)/shard_map/thd,the->hde/dot_general | solution.py:99
  102.4 1.9 %collective-permute-start.12 = (f32[264,128]{1,0:T(8,128)S(1)}, f32[264,128]{1,0:T(8,128)}, u32[]{:S(2)}, u32[]{:S(2)}) collective-permute-start(f32[264,128]{1,0:T(8,128)S(1)} %concatenate.34), channel_id=1, source_target_pairs={{0,8},{8,16},{16,24},{24,32},{32,40},{40,48},{48,56},{56,64},{64,7... | collective-permute-start | bytes 405512 | tf_op jit(solution)/shard_map/ppermute | solution.py:15
  104.3 3.4 %collective-permute-start.13 = (f32[264,128]{1,0:T(8,128)S(1)}, f32[264,128]{1,0:T(8,128)}, u32[]{:S(2)}, u32[]{:S(2)}) collective-permute-start(f32[264,128]{1,0:T(8,128)S(1)} %concatenate.34), channel_id=1, source_target_pairs={{0,16},{8,24},{16,32},{24,40},{32,48},{40,56},{48,64},{56,72},{64,... | collective-permute-start | bytes 405512 | tf_op jit(solution)/shard_map/ppermute | solution.py:15
  107.7 4.0 %collective-permute-start.14 = (f32[264,128]{1,0:T(8,128)S(1)}, f32[264,128]{1,0:T(8,128)}, u32[]{:S(2)}, u32[]{:S(2)}) collective-permute-start(f32[264,128]{1,0:T(8,128)S(1)} %concatenate.34), channel_id=1, source_target_pairs={{0,24},{8,32},{16,40},{24,48},{32,56},{40,64},{48,72},{56,80},{64,... | collective-permute-start | bytes 405512 | tf_op jit(solution)/shard_map/ppermute | solution.py:15
  111.7 6.1 %collective-permute-start.15 = (f32[264,128]{1,0:T(8,128)S(1)}, f32[264,128]{1,0:T(8,128)}, u32[]{:S(2)}, u32[]{:S(2)}) collective-permute-start(f32[264,128]{1,0:T(8,128)S(1)} %concatenate.34), channel_id=1, source_target_pairs={{0,32},{8,40},{16,48},{24,56},{32,64},{40,72},{48,80},{56,88},{64,... | collective-permute-start | bytes 405512 | tf_op jit(solution)/shard_map/ppermute | solution.py:15
  120.3 2.9 %fusion.17 = f32[512,2,128]{0,2,1:T(8,128)S(1)} fusion(bf16[1024,2,128]{0,2,1:T(8,128)(2,1)} %bitcast.109, bf16[512,2,128]{0,2,1:T(8,128)(2,1)} %bitcast.113, pred[512,1024]{1,0:T(8,128)(4,1)} %fusion.8, f32[1024,2,128]{2,0,1:T(8,128)S(1)} %copy-done.2), kind=kOutput, calls=%fused_computation.26 | convolution fusion | flops 540278784 | bytes 2883584 | tf_op jit(solution)/shard_map/hbs,she->bhe/dot_general | solution.py:119
  123.3 1.9 %fusion.18 = f32[512,2,128]{0,2,1:T(8,128)S(1)} fusion(bf16[512,2,128]{0,2,1:T(8,128)(2,1)} %bitcast.111, bf16[512,2,128]{0,2,1:T(8,128)(2,1)} %bitcast.112, bf16[512,2,128]{0,2,1:T(8,128)(2,1)S(1)} %bitcast.110, pred[512,512]{1,0:T(8,128)(4,1)} %fusion.29), kind=kOutput, calls=%fused_computation.27 | convolution fusion | flops 269484032 | bytes 1572864 | tf_op jit(solution)/shard_map/hbs,she->bhe/dot_general | solution.py:119
  137.0 3.4 %collective-permute-start.16 = (f32[264,128]{1,0:T(8,128)S(1)}, f32[264,128]{1,0:T(8,128)S(1)}, u32[]{:S(2)}, u32[]{:S(2)}) collective-permute-start(f32[264,128]{1,0:T(8,128)S(1)} %concatenate.35), channel_id=1, source_target_pairs={{0,32},{8,40},{16,48},{24,56},{32,64},{40,72},{48,80},{56,88},{64,... | collective-permute-start | bytes 405512 | tf_op jit(solution)/shard_map/ppermute | solution.py:15
  140.4 2.5 %collective-permute-start.17 = (f32[264,128]{1,0:T(8,128)S(1)}, f32[264,128]{1,0:T(8,128)S(1)}, u32[]{:S(2)}, u32[]{:S(2)}) collective-permute-start(f32[264,128]{1,0:T(8,128)S(1)} %concatenate.35), channel_id=1, source_target_pairs={{0,64},{8,72},{16,80},{24,88},{32,96},{40,104},{48,112},{56,120},{... | collective-permute-start | bytes 405512 | tf_op jit(solution)/shard_map/ppermute | solution.py:15
  142.9 4.0 %collective-permute-start.18 = (f32[264,128]{1,0:T(8,128)S(1)}, f32[264,128]{1,0:T(8,128)S(1)}, u32[]{:S(2)}, u32[]{:S(2)}) collective-permute-start(f32[264,128]{1,0:T(8,128)S(1)} %concatenate.35), channel_id=1, source_target_pairs={{0,96},{8,104},{16,112},{24,120},{32,128},{40,136},{48,144},{56,15... | collective-permute-start | bytes 405512 | tf_op jit(solution)/shard_map/ppermute | solution.py:15
  151.2 5.1 %collective-permute-done.18 = f32[264,128]{1,0:T(8,128)S(1)} collective-permute-done((f32[264,128]{1,0:T(8,128)S(1)}, f32[264,128]{1,0:T(8,128)S(1)}, u32[]{:S(2)}, u32[]{:S(2)}) %collective-permute-start.18) | collective-permute-done | bytes 135200 | tf_op jit(solution)/shard_map/ppermute | solution.py:15
  (82 shorter events, 24.0 us)
Async XLA Ops:
  6.5 83.5 %all-gather.2.cloned.1.call-start = ((), (), s32[]{:S(2)}) async-start(), calls=%async_computation | async-start | bytes 4718592 | tf_op jit(solution)/shard_map/all_gather | solution.py:86
  6.5 3.3 %collective-permute-start = (bf16[3,32,256]{2,1,0:T(8,128)(2,1)}, bf16[3,32,256]{2,1,0:T(8,128)(2,1)S(1)}, u32[]{:S(2)}, u32[]{:S(2)}) collective-permute-start(bf16[3,32,256]{2,1,0:T(8,128)(2,1)} %param.5), channel_id=1, source_target_pairs={{0,8},{8,0},{1,9},{9,1},{2,10},{10,2},{3,11},{11,3},{4,12},{12,4},... | collective-permute-start | bytes 147464 | tf_op jit(solution)/shard_map/ppermute | solution.py:40
  10.6 7.2 %collective-permute-start.1 = (bf16[3,64,128]{2,1,0:T(8,128)(2,1)S(1)}, bf16[3,64,128]{2,1,0:T(8,128)(2,1)S(1)}, u32[]{:S(2)}, u32[]{:S(2)}) collective-permute-start(bf16[3,64,128]{2,1,0:T(8,128)(2,1)S(1)} %pad_maximum_fusion), channel_id=1, source_target_pairs={{0,16},{16,32},{32,48},{48,0},{1,17},{17,33},{33,49},{49,1},{2,18}... | collective-permute-start | bytes 147464 | tf_op jit(solution)/shard_map/ppermute | solution.py:23
  17.8 7.2 %collective-permute-start.2 = (bf16[3,64,128]{2,1,0:T(8,128)(2,1)S(1)}, bf16[3,64,128]{2,1,0:T(8,128)(2,1)S(1)}, u32[]{:S(2)}, u32[]{:S(2)}) collective-permute-start(bf16[3,64,128]{2,1,0:T(8,128)(2,1)S(1)} %collective-permute-done.1), channel_id=1, source_target_pairs={{0,16},{16,32},{32,48},{48,0},{1,17},{17,33},{33,49},{49,1},{2,18}... | collective-permute-start | bytes 147464 | tf_op jit(solution)/shard_map/ppermute | solution.py:23
  20.1 6.6 %collective-permute-start.3 = (bf16[3,64,128]{2,1,0:T(8,128)(2,1)S(1)}, bf16[3,64,128]{2,1,0:T(8,128)(2,1)S(1)}, u32[]{:S(2)}, u32[]{:S(2)}) collective-permute-start(bf16[3,64,128]{2,1,0:T(8,128)(2,1)S(1)} %pad_maximum_fusion), channel_id=1, source_target_pairs={{0,48},{16,0},{32,16},{48,32},{1,49},{17,1},{33,17},{49,33},{2,50}... | collective-permute-start | bytes 147464 | tf_op jit(solution)/shard_map/ppermute | solution.py:26
  26.8 7.9 %collective-permute-start.4 = (bf16[3,256,128]{2,1,0:T(8,128)(2,1)S(1)}, bf16[3,256,128]{2,1,0:T(8,128)(2,1)S(1)}, u32[]{:S(2)}, u32[]{:S(2)}) collective-permute-start(bf16[3,256,128]{2,1,0:T(8,128)(2,1)S(1)} %bitcast.102), channel_id=1, source_target_pairs={{0,64},{64,128},{128,192},{192,256},{256,320},{320,384},{384,448},... | collective-permute-start | bytes 589832 | tf_op jit(solution)/shard_map/ppermute | solution.py:23
  34.6 8.8 %collective-permute-start.5 = (bf16[3,256,128]{2,1,0:T(8,128)(2,1)S(1)}, bf16[3,256,128]{2,1,0:T(8,128)(2,1)S(1)}, u32[]{:S(2)}, u32[]{:S(2)}) collective-permute-start(bf16[3,256,128]{2,1,0:T(8,128)(2,1)S(1)} %collective-permute-done.4), channel_id=1, source_target_pairs={{0,64},{64,128},{128,192},{192,256},{256,320},{320,384},{384,448},... | collective-permute-start | bytes 589832 | tf_op jit(solution)/shard_map/ppermute | solution.py:23
  40.2 8.8 %collective-permute-start.8 = (bf16[3,256,128]{2,1,0:T(8,128)(2,1)S(1)}, bf16[3,256,128]{2,1,0:T(8,128)(2,1)S(1)}, u32[]{:S(2)}, u32[]{:S(2)}) collective-permute-start(bf16[3,256,128]{2,1,0:T(8,128)(2,1)S(1)} %bitcast.103), channel_id=1, source_target_pairs={{0,448},{64,0},{128,64},{192,128},{256,192},{320,256},{384,320},{4... | collective-permute-start | bytes 589832 | tf_op jit(solution)/shard_map/ppermute | solution.py:26
  43.4 8.8 %collective-permute-start.6 = (bf16[3,256,128]{2,1,0:T(8,128)(2,1)S(1)}, bf16[3,256,128]{2,1,0:T(8,128)(2,1)S(1)}, u32[]{:S(2)}, u32[]{:S(2)}) collective-permute-start(bf16[3,256,128]{2,1,0:T(8,128)(2,1)S(1)} %collective-permute-done.5), channel_id=1, source_target_pairs={{0,64},{64,128},{128,192},{192,256},{256,320},{320,384},{384,448},... | collective-permute-start | bytes 589832 | tf_op jit(solution)/shard_map/ppermute | solution.py:23
  49.0 8.8 %collective-permute-start.9 = (bf16[3,256,128]{2,1,0:T(8,128)(2,1)S(1)}, bf16[3,256,128]{2,1,0:T(8,128)(2,1)S(1)}, u32[]{:S(2)}, u32[]{:S(2)}) collective-permute-start(bf16[3,256,128]{2,1,0:T(8,128)(2,1)S(1)} %collective-permute-done.8), channel_id=1, source_target_pairs={{0,448},{64,0},{128,64},{192,128},{256,192},{320,256},{384,320},{4... | collective-permute-start | bytes 589832 | tf_op jit(solution)/shard_map/ppermute | solution.py:26
  52.2 8.8 %collective-permute-start.7 = (bf16[3,256,128]{2,1,0:T(8,128)(2,1)S(1)}, bf16[3,256,128]{2,1,0:T(8,128)(2,1)S(1)}, u32[]{:S(2)}, u32[]{:S(2)}) collective-permute-start(bf16[3,256,128]{2,1,0:T(8,128)(2,1)S(1)} %collective-permute-done.6), channel_id=1, source_target_pairs={{0,64},{64,128},{128,192},{192,256},{256,320},{320,384},{384,448},... | collective-permute-start | bytes 589832 | tf_op jit(solution)/shard_map/ppermute | solution.py:23
  57.8 8.8 %collective-permute-start.10 = (bf16[3,256,128]{2,1,0:T(8,128)(2,1)S(1)}, bf16[3,256,128]{2,1,0:T(8,128)(2,1)S(1)}, u32[]{:S(2)}, u32[]{:S(2)}) collective-permute-start(bf16[3,256,128]{2,1,0:T(8,128)(2,1)S(1)} %collective-permute-done.9), channel_id=1, source_target_pairs={{0,448},{64,0},{128,64},{192,128},{256,192},{320,256},{384,320},{4... | collective-permute-start | bytes 589832 | tf_op jit(solution)/shard_map/ppermute | solution.py:26
  66.9 2.3 %copy-start.3 = (s32[1024]{0:T(1024)S(1)}, s32[1024]{0:T(1024)}, u32[]{:S(2)}) copy-start(s32[1024]{0:T(1024)} %param.7) | copy-start | bytes 12292
  67.2 5.4 %collective-permute-start.11 = (bf16[3,2048,128]{2,1,0:T(8,128)(2,1)S(1)}, bf16[3,2048,128]{2,1,0:T(8,128)(2,1)S(1)}, u32[]{:S(2)}, u32[]{:S(2)}) collective-permute-start(bf16[3,2048,128]{2,1,0:T(8,128)(2,1)S(1)} %bitcast.106), channel_id=1, source_target_pairs={{0,8},{8,0},{1,9},{9,1},{2,10},{10,2},{3,11},{11,3},{4,12},{12,4},... | collective-permute-start | bytes 4718600 | tf_op jit(solution)/shard_map/ppermute | solution.py:46
  95.7 1.2 copy-start
  99.4 18.4 %copy-start.1 = (bf16[3,1024,256]{1,2,0:T(8,128)(2,1)S(1)}, bf16[3,1024,256]{1,2,0:T(8,128)(2,1)}, u32[]{:S(2)}) copy-start(bf16[3,1024,256]{1,2,0:T(8,128)(2,1)} %copy-done) | copy-start | bytes 4718596
  101.6 18.7 %copy-start.2 = (f32[1024,2,128]{2,0,1:T(8,128)S(1)}, f32[1024,2,128]{2,0,1:T(8,128)}, u32[]{:S(2)}) copy-start(f32[1024,2,128]{2,0,1:T(8,128)} %copy.52) | copy-start | bytes 3145732
  102.4 22.8 %collective-permute-start.12 = (f32[264,128]{1,0:T(8,128)S(1)}, f32[264,128]{1,0:T(8,128)}, u32[]{:S(2)}, u32[]{:S(2)}) collective-permute-start(f32[264,128]{1,0:T(8,128)S(1)} %concatenate.34), channel_id=1, source_target_pairs={{0,8},{8,16},{16,24},{24,32},{32,40},{40,48},{48,56},{56,64},{64,7... | collective-permute-start | bytes 405512 | tf_op jit(solution)/shard_map/ppermute | solution.py:15
  104.3 23.4 %collective-permute-start.13 = (f32[264,128]{1,0:T(8,128)S(1)}, f32[264,128]{1,0:T(8,128)}, u32[]{:S(2)}, u32[]{:S(2)}) collective-permute-start(f32[264,128]{1,0:T(8,128)S(1)} %concatenate.34), channel_id=1, source_target_pairs={{0,16},{8,24},{16,32},{24,40},{32,48},{40,56},{48,64},{56,72},{64,... | collective-permute-start | bytes 405512 | tf_op jit(solution)/shard_map/ppermute | solution.py:15
  107.7 22.5 %collective-permute-start.14 = (f32[264,128]{1,0:T(8,128)S(1)}, f32[264,128]{1,0:T(8,128)}, u32[]{:S(2)}, u32[]{:S(2)}) collective-permute-start(f32[264,128]{1,0:T(8,128)S(1)} %concatenate.34), channel_id=1, source_target_pairs={{0,24},{8,32},{16,40},{24,48},{32,56},{40,64},{48,72},{56,80},{64,... | collective-permute-start | bytes 405512 | tf_op jit(solution)/shard_map/ppermute | solution.py:15
  111.7 21.1 %collective-permute-start.15 = (f32[264,128]{1,0:T(8,128)S(1)}, f32[264,128]{1,0:T(8,128)}, u32[]{:S(2)}, u32[]{:S(2)}) collective-permute-start(f32[264,128]{1,0:T(8,128)S(1)} %concatenate.34), channel_id=1, source_target_pairs={{0,32},{8,40},{16,48},{24,56},{32,64},{40,72},{48,80},{56,88},{64,... | collective-permute-start | bytes 405512 | tf_op jit(solution)/shard_map/ppermute | solution.py:15
  125.2 33.8 %copy-start.4 = (f32[256]{0:T(256)S(1)}, f32[256]{0:T(256)}, u32[]{:S(2)}) copy-start(f32[256]{0:T(256)} %param.6) | copy-start | bytes 3076
  137.0 10.6 %collective-permute-start.16 = (f32[264,128]{1,0:T(8,128)S(1)}, f32[264,128]{1,0:T(8,128)S(1)}, u32[]{:S(2)}, u32[]{:S(2)}) collective-permute-start(f32[264,128]{1,0:T(8,128)S(1)} %concatenate.35), channel_id=1, source_target_pairs={{0,32},{8,40},{16,48},{24,56},{32,64},{40,72},{48,80},{56,88},{64,... | collective-permute-start | bytes 405512 | tf_op jit(solution)/shard_map/ppermute | solution.py:15
  140.4 9.0 %collective-permute-start.17 = (f32[264,128]{1,0:T(8,128)S(1)}, f32[264,128]{1,0:T(8,128)S(1)}, u32[]{:S(2)}, u32[]{:S(2)}) collective-permute-start(f32[264,128]{1,0:T(8,128)S(1)} %concatenate.35), channel_id=1, source_target_pairs={{0,64},{8,72},{16,80},{24,88},{32,96},{40,104},{48,112},{56,120},{... | collective-permute-start | bytes 405512 | tf_op jit(solution)/shard_map/ppermute | solution.py:15
  142.9 13.5 %collective-permute-start.18 = (f32[264,128]{1,0:T(8,128)S(1)}, f32[264,128]{1,0:T(8,128)S(1)}, u32[]{:S(2)}, u32[]{:S(2)}) collective-permute-start(f32[264,128]{1,0:T(8,128)S(1)} %concatenate.35), channel_id=1, source_target_pairs={{0,96},{8,104},{16,112},{24,120},{32,128},{40,136},{48,144},{56,15... | collective-permute-start | bytes 405512 | tf_op jit(solution)/shard_map/ppermute | solution.py:15
Sparse Core Ops, SparseCore 0:
  20.2 69.8 all-gather.1

commit v6 on v5

--- a/solution.py
+++ b/solution.py
@@ -83,7 +83,7 @@
 
 
 def per_device(tokens, w_qkv, out_gain, seg_ids):
-    whole = lax.all_gather(tokens, "head", axis=1, tiled=True)
+    whole = ring_gather(tokens, "head", lax.axis_size("head"), 1)
     w_rows = gather_weights(w_qkv)
     projected = jnp.einsum(
         "tr,grc->gtc", whole, w_rows, preferred_element_type=jnp.float32

time: 168 us -> 196 us (1.17)
  the two profiles are of different devices: /device:TPU:24 before, /device:TPU:16 now
where the time goes in v6:
time: 196 us; the launch traced here: 194 us
  starting transfers between devices  91.9 us (47%)
  waiting for transfers between devices  42 us (21%)
  local copies, waits for them, and re-layouts  26.3 us (13%)
  matrix products  14.3 us (7%)
  between operations  9.87 us (5%)
  other arithmetic  9.73 us (5%)
    ppermute x10, starting transfers between devices, ring_gather(): lax.ppermute(ahead, axis, [(j, (j + 1) % count) for j in range(count)])  34.7 us
    ppermute x7, starting transfers between devices, ring_gather(): lax.ppermute(behind, axis, [(j, (j - 1) % count) for j in range(count)])  28.5 us
    ppermute x7, starting transfers between devices, shifted(): lax.ppermute(value, axis, [(source, source + steps) for source in range(c...  24.9 us
    ppermute x7, waiting for transfers between devices, ring_gather(): lax.ppermute(behind, axis, [(j, (j - 1) % count) for j in range(count)])  18.3 us
    ppermute x10, waiting for transfers between devices, ring_gather(): lax.ppermute(ahead, axis, [(j, (j + 1) % count) for j in range(count)])  18.2 us
    reshape x1, local copies, waits for them, and re-layouts, ring_gather(): return moved.reshape(shape)  7.38 us
    dot_general x1, matrix products, per_device(): jnp.einsum('tr,grc->gtc', whole, w_rows, preferred_element_type=jnp.float32)  6.62 us
    slice x6, local copies, waits for them, and re-layouts, state_scan(): g[state_rows, 0] == prev_tail  5.5 us
  transfers between devices with their start and end apart: 26, of which 11 were waited for; matrix products, arithmetic and copies ran while one was open for 15% of the time, Pallas kernels for 0%

profile of v6, /device:TPU:16, one launch (start us, length us, event | category | flops | bytes accessed | tf_op | source)
XLA Modules:
  0.0 194.1 jit_solution(11268565210936179442)
XLA Ops:
  4.1 3.4 %collective-permute-start.1 = (bf16[3,64,128]{2,1,0:T(8,128)(2,1)S(1)}, bf16[3,64,128]{2,1,0:T(8,128)(2,1)S(1)}, u32[]{:S(2)}, u32[]{:S(2)}) collective-permute-start(bf16[3,64,128]{2,1,0:T(8,128)(2,1)S(1)} %pad_maximum_fusion), channel_id=1, source_target_pairs={{0,16},{16,32},{32,48},{48,0},{1,17},{17,33},{33,49},{49,1},{2,18}... | collective-permute-start | bytes 147464 | tf_op jit(solution)/shard_map/ppermute | solution.py:23
  7.5 4.3 %collective-permute-start.12 = (bf16[1024,256]{1,0:T(8,128)(2,1)}, bf16[1024,256]{1,0:T(8,128)(2,1)S(1)}, u32[]{:S(2)}, u32[]{:S(2)}) collective-permute-start(bf16[1024,256]{1,0:T(8,128)(2,1)} %param.4), channel_id=1, source_target_pairs={{0,1},{1,2},{2,3},{3,4},{4,5},{5,6},{6,7},{7,0},{8,9},{9,10},{10,1... | collective-permute-start | bytes 1572872 | tf_op jit(solution)/shard_map/ppermute | solution.py:23
  11.8 8.6 %collective-permute-start.16 = (bf16[1024,256]{1,0:T(8,128)(2,1)}, bf16[1024,256]{1,0:T(8,128)(2,1)S(1)}, u32[]{:S(2)}, u32[]{:S(2)}) collective-permute-start(bf16[1024,256]{1,0:T(8,128)(2,1)} %param.4), channel_id=1, source_target_pairs={{0,7},{1,0},{2,1},{3,2},{4,3},{5,4},{6,5},{7,6},{8,15},{9,8},{10,9... | collective-permute-start | bytes 1572872 | tf_op jit(solution)/shard_map/ppermute | solution.py:26
  20.4 3.4 %collective-permute-start.2 = (bf16[3,64,128]{2,1,0:T(8,128)(2,1)S(1)}, bf16[3,64,128]{2,1,0:T(8,128)(2,1)S(1)}, u32[]{:S(2)}, u32[]{:S(2)}) collective-permute-start(bf16[3,64,128]{2,1,0:T(8,128)(2,1)S(1)} %collective-permute-done.1), channel_id=1, source_target_pairs={{0,16},{16,32},{32,48},{48,0},{1,17},{17,33},{33,49},{49,1},{2,18}... | collective-permute-start | bytes 147464 | tf_op jit(solution)/shard_map/ppermute | solution.py:23
  24.5 3.6 %collective-permute-start.3 = (bf16[3,64,128]{2,1,0:T(8,128)(2,1)S(1)}, bf16[3,64,128]{2,1,0:T(8,128)(2,1)S(1)}, u32[]{:S(2)}, u32[]{:S(2)}) collective-permute-start(bf16[3,64,128]{2,1,0:T(8,128)(2,1)S(1)} %pad_maximum_fusion), channel_id=1, source_target_pairs={{0,48},{16,0},{32,16},{48,32},{1,49},{17,1},{33,17},{49,33},{2,50}... | collective-permute-start | bytes 147464 | tf_op jit(solution)/shard_map/ppermute | solution.py:26
  28.2 2.3 %collective-permute-done.3 = bf16[3,64,128]{2,1,0:T(8,128)(2,1)S(1)} collective-permute-done((bf16[3,64,128]{2,1,0:T(8,128)(2,1)S(1)}, bf16[3,64,128]{2,1,0:T(8,128)(2,1)S(1)}, u32[]{:S(2)}, u32[]{:S(2)}) %collective-permute-start.3) | collective-permute-done | bytes 49184 | tf_op jit(solution)/shard_map/ppermute | solution.py:26
  30.6 3.5 %collective-permute-start.4 = (bf16[3,256,128]{2,1,0:T(8,128)(2,1)S(1)}, bf16[3,256,128]{2,1,0:T(8,128)(2,1)S(1)}, u32[]{:S(2)}, u32[]{:S(2)}) collective-permute-start(bf16[3,256,128]{2,1,0:T(8,128)(2,1)S(1)} %bitcast.122), channel_id=1, source_target_pairs={{0,64},{64,128},{128,192},{192,256},{256,320},{320,384},{384,448},... | collective-permute-start | bytes 589832 | tf_op jit(solution)/shard_map/ppermute | solution.py:23
  34.1 4.1 %collective-permute-done.4 = bf16[3,256,128]{2,1,0:T(8,128)(2,1)S(1)} collective-permute-done((bf16[3,256,128]{2,1,0:T(8,128)(2,1)S(1)}, bf16[3,256,128]{2,1,0:T(8,128)(2,1)S(1)}, u32[]{:S(2)}, u32[]{:S(2)}) %collective-permute-start.4) | collective-permute-done | bytes 196640 | tf_op jit(solution)/shard_map/ppermute | solution.py:23
  38.2 3.8 %collective-permute-start.5 = (bf16[3,256,128]{2,1,0:T(8,128)(2,1)S(1)}, bf16[3,256,128]{2,1,0:T(8,128)(2,1)S(1)}, u32[]{:S(2)}, u32[]{:S(2)}) collective-permute-start(bf16[3,256,128]{2,1,0:T(8,128)(2,1)S(1)} %collective-permute-done.4), channel_id=1, source_target_pairs={{0,64},{64,128},{128,192},{192,256},{256,320},{320,384},{384,448},... | collective-permute-start | bytes 589832 | tf_op jit(solution)/shard_map/ppermute | solution.py:23
  43.9 2.0 %collective-permute-start.8 = (bf16[3,256,128]{2,1,0:T(8,128)(2,1)S(1)}, bf16[3,256,128]{2,1,0:T(8,128)(2,1)S(1)}, u32[]{:S(2)}, u32[]{:S(2)}) collective-permute-start(bf16[3,256,128]{2,1,0:T(8,128)(2,1)S(1)} %bitcast.123), channel_id=1, source_target_pairs={{0,448},{64,0},{128,64},{192,128},{256,192},{320,256},{384,320},{4... | collective-permute-start | bytes 589832 | tf_op jit(solution)/shard_map/ppermute | solution.py:26
  45.9 5.5 %collective-permute-start.6 = (bf16[3,256,128]{2,1,0:T(8,128)(2,1)S(1)}, bf16[3,256,128]{2,1,0:T(8,128)(2,1)S(1)}, u32[]{:S(2)}, u32[]{:S(2)}) collective-permute-start(bf16[3,256,128]{2,1,0:T(8,128)(2,1)S(1)} %collective-permute-done.5), channel_id=1, source_target_pairs={{0,64},{64,128},{128,192},{192,256},{256,320},{320,384},{384,448},... | collective-permute-start | bytes 589832 | tf_op jit(solution)/shard_map/ppermute | solution.py:23
  55.0 5.1 %collective-permute-start.7 = (bf16[3,256,128]{2,1,0:T(8,128)(2,1)S(1)}, bf16[3,256,128]{2,1,0:T(8,128)(2,1)S(1)}, u32[]{:S(2)}, u32[]{:S(2)}) collective-permute-start(bf16[3,256,128]{2,1,0:T(8,128)(2,1)S(1)} %collective-permute-done.6), channel_id=1, source_target_pairs={{0,64},{64,128},{128,192},{192,256},{256,320},{320,384},{384,448},... | collective-permute-start | bytes 589832 | tf_op jit(solution)/shard_map/ppermute | solution.py:23
  63.4 5.1 %collective-permute-start.17 = (bf16[1024,256]{1,0:T(8,128)(2,1)S(1)}, bf16[1024,256]{1,0:T(8,128)(2,1)S(1)}, u32[]{:S(2)}, u32[]{:S(2)}) collective-permute-start(bf16[1024,256]{1,0:T(8,128)(2,1)S(1)} %collective-permute-done.16), channel_id=1, source_target_pairs={{0,7},{1,0},{2,1},{3,2},{4,3},{5,4},{6,5},{7,6},{8,15},{9,8},{10,9... | collective-permute-start | bytes 1572872 | tf_op jit(solution)/shard_map/ppermute | solution.py:26
  70.8 6.6 %collective-permute-done.10 = bf16[3,256,128]{2,1,0:T(8,128)(2,1)S(1)} collective-permute-done((bf16[3,256,128]{2,1,0:T(8,128)(2,1)S(1)}, bf16[3,256,128]{2,1,0:T(8,128)(2,1)S(1)}, u32[]{:S(2)}, u32[]{:S(2)}) %collective-permute-start.10) | collective-permute-done | bytes 196640 | tf_op jit(solution)/shard_map/ppermute | solution.py:26
  77.5 1.9 collective-permute-start.14
  79.5 11.5 %collective-permute-done.14 = bf16[1024,256]{1,0:T(8,128)(2,1)S(1)} collective-permute-done((bf16[1024,256]{1,0:T(8,128)(2,1)S(1)}, bf16[1024,256]{1,0:T(8,128)(2,1)S(1)}, u32[]{:S(2)}, u32[]{:S(2)}) %collective-permute-start.14) | collective-permute-done | bytes 524320 | tf_op jit(solution)/shard_map/ppermute | solution.py:23
  93.3 1.9 collective-permute-start.11
  95.2 5.3 %collective-permute-start.18 = (bf16[1024,256]{1,0:T(8,128)(2,1)S(1)}, bf16[1024,256]{1,0:T(8,128)(2,1)S(1)}, u32[]{:S(2)}, u32[]{:S(2)}) collective-permute-start(bf16[1024,256]{1,0:T(8,128)(2,1)S(1)} %collective-permute-done.17), channel_id=1, source_target_pairs={{0,7},{1,0},{2,1},{3,2},{4,3},{5,4},{6,5},{7,6},{8,15},{9,8},{10,9... | collective-permute-start | bytes 1572872 | tf_op jit(solution)/shard_map/ppermute | solution.py:26
  100.6 2.7 %collective-permute-done.15 = bf16[1024,256]{1,0:T(8,128)(2,1)S(1)} collective-permute-done((bf16[1024,256]{1,0:T(8,128)(2,1)S(1)}, bf16[1024,256]{1,0:T(8,128)(2,1)S(1)}, u32[]{:S(2)}, u32[]{:S(2)}) %collective-permute-start.15) | collective-permute-done | bytes 524320 | tf_op jit(solution)/shard_map/ppermute | solution.py:23
  103.6 8.6 %collective-permute-done.18 = bf16[1024,256]{1,0:T(8,128)(2,1)S(1)} collective-permute-done((bf16[1024,256]{1,0:T(8,128)(2,1)S(1)}, bf16[1024,256]{1,0:T(8,128)(2,1)S(1)}, u32[]{:S(2)}, u32[]{:S(2)}) %collective-permute-start.18) | collective-permute-done | bytes 524320 | tf_op jit(solution)/shard_map/ppermute | solution.py:26
  112.9 4.4 %copy.51 = bf16[1024,8,256]{2,1,0:T(8,128)(2,1)} copy(bf16[1024,8,256]{2,0,1:T(8,128)(2,1)S(1)} %dynamic-slice_bitcast_fusion) | data formatting | bytes 8388608 | tf_op jit(solution)/shard_map/transpose | solution.py:31
  117.3 7.4 %reshape.144 = bf16[1024,2048,1]{1,0,2:T(8,128)(2,1)} reshape(bf16[1024,8,256]{2,1,0:T(8,128)(2,1)} %copy.51) | data formatting | bytes 8388608 | tf_op jit(solution)/shard_map/reshape | solution.py:34
  124.7 6.6 %fusion.10 = bf16[3,1024,256]{1,2,0:T(8,128)(2,1)S(1)} fusion(bf16[1024,2048,1]{1,0,2:T(8,128)(2,1)} %reshape.144, bf16[3,2048,128]{2,1,0:T(8,128)(2,1)} %collective-permute-done.11, bf16[3,2048,128]{2,1,0:T(8,128)(2,1)S(1)} %bitcast.127, pred[]{:T(512)S(6)} %eq.79), kind=kOutput, calls=%fused_computation.24 | convolution fusion | flops 3236167680 | bytes 8912897 | tf_op jit(solution)/shard_map/tr,grc->gtc/dot_general | solution.py:88
  135.8 2.2 %fusion.31 = f32[2,128,128]{2,1,0:T(8,128)S(1)} fusion(bf16[1024,2,128]{0,2,1:T(8,128)(2,1)} %bitcast.128, pred[1024]{0:T(1024)(128)(4,1)S(1)} %broadcast_compare_fusion.1, f32[1024,2,128]{2,0,1:T(8,128)} %copy.55), kind=kOutput, calls=%fused_computation.66 | convolution fusion | flops 68681728 | bytes 1704960 | tf_op jit(solution)/shard_map/thd,the->hde/dot_general | solution.py:99
  138.7 1.9 collective-permute-start.19
  140.6 3.6 %collective-permute-start.22 = (f32[264,128]{1,0:T(8,128)S(1)}, f32[264,128]{1,0:T(8,128)}, u32[]{:S(2)}, u32[]{:S(2)}) collective-permute-start(f32[264,128]{1,0:T(8,128)S(1)} %concatenate.40), channel_id=1, source_target_pairs={{0,32},{8,40},{16,48},{24,56},{32,64},{40,72},{48,80},{56,88},{64,... | collective-permute-start | bytes 405512 | tf_op jit(solution)/shard_map/ppermute | solution.py:15
  144.2 6.7 %collective-permute-start.21 = (f32[264,128]{1,0:T(8,128)S(1)}, f32[264,128]{1,0:T(8,128)}, u32[]{:S(2)}, u32[]{:S(2)}) collective-permute-start(f32[264,128]{1,0:T(8,128)S(1)} %concatenate.40), channel_id=1, source_target_pairs={{0,24},{8,32},{16,40},{24,48},{32,56},{40,64},{48,72},{56,80},{64,... | collective-permute-start | bytes 405512 | tf_op jit(solution)/shard_map/ppermute | solution.py:15
  150.9 2.5 %collective-permute-start.20 = (f32[264,128]{1,0:T(8,128)S(1)}, f32[264,128]{1,0:T(8,128)}, u32[]{:S(2)}, u32[]{:S(2)}) collective-permute-start(f32[264,128]{1,0:T(8,128)S(1)} %concatenate.40), channel_id=1, source_target_pairs={{0,16},{8,24},{16,32},{24,40},{32,48},{40,56},{48,64},{56,72},{64,... | collective-permute-start | bytes 405512 | tf_op jit(solution)/shard_map/ppermute | solution.py:15
  154.8 2.9 %fusion.12 = f32[512,2,128]{0,2,1:T(8,128)S(1)} fusion(bf16[1024,2,128]{0,2,1:T(8,128)(2,1)} %bitcast.129, bf16[512,2,128]{0,2,1:T(8,128)(2,1)} %bitcast.133, pred[512,1024]{1,0:T(8,128)(4,1)} %fusion.7, f32[1024,2,128]{2,0,1:T(8,128)S(1)} %copy-done.2), kind=kOutput, calls=%fused_computation.26 | convolution fusion | flops 540278784 | bytes 2883584 | tf_op jit(solution)/shard_map/hbs,she->bhe/dot_general | solution.py:119
  171.6 5.3 %collective-permute-start.25 = (f32[264,128]{1,0:T(8,128)S(1)}, f32[264,128]{1,0:T(8,128)S(1)}, u32[]{:S(2)}, u32[]{:S(2)}) collective-permute-start(f32[264,128]{1,0:T(8,128)S(1)} %concatenate.41), channel_id=1, source_target_pairs={{0,96},{8,104},{16,112},{24,120},{32,128},{40,136},{48,144},{56,15... | collective-permute-start | bytes 405512 | tf_op jit(solution)/shard_map/ppermute | solution.py:15
  178.9 2.9 %collective-permute-start.23 = (f32[264,128]{1,0:T(8,128)S(1)}, f32[264,128]{1,0:T(8,128)S(1)}, u32[]{:S(2)}, u32[]{:S(2)}) collective-permute-start(f32[264,128]{1,0:T(8,128)S(1)} %concatenate.41), channel_id=1, source_target_pairs={{0,32},{8,40},{16,48},{24,56},{32,64},{40,72},{48,80},{56,88},{64,... | collective-permute-start | bytes 405512 | tf_op jit(solution)/shard_map/ppermute | solution.py:15
  187.2 3.1 %collective-permute-done.23 = f32[264,128]{1,0:T(8,128)S(1)} collective-permute-done((f32[264,128]{1,0:T(8,128)S(1)}, f32[264,128]{1,0:T(8,128)S(1)}, u32[]{:S(2)}, u32[]{:S(2)}) %collective-permute-start.23) | collective-permute-done | bytes 135200 | tf_op jit(solution)/shard_map/ppermute | solution.py:15
  (112 shorter events, 41.4 us)
Async XLA Ops:
  0.0 3.3 %collective-permute-start = (bf16[3,32,256]{2,1,0:T(8,128)(2,1)}, bf16[3,32,256]{2,1,0:T(8,128)(2,1)S(1)}, u32[]{:S(2)}, u32[]{:S(2)}) collective-permute-start(bf16[3,32,256]{2,1,0:T(8,128)(2,1)} %param.5), channel_id=1, source_target_pairs={{0,8},{8,0},{1,9},{9,1},{2,10},{10,2},{3,11},{11,3},{4,12},{12,4},... | collective-permute-start | bytes 147464 | tf_op jit(solution)/shard_map/ppermute | solution.py:40
  4.1 16.3 %collective-permute-start.1 = (bf16[3,64,128]{2,1,0:T(8,128)(2,1)S(1)}, bf16[3,64,128]{2,1,0:T(8,128)(2,1)S(1)}, u32[]{:S(2)}, u32[]{:S(2)}) collective-permute-start(bf16[3,64,128]{2,1,0:T(8,128)(2,1)S(1)} %pad_maximum_fusion), channel_id=1, source_target_pairs={{0,16},{16,32},{32,48},{48,0},{1,17},{17,33},{33,49},{49,1},{2,18}... | collective-permute-start | bytes 147464 | tf_op jit(solution)/shard_map/ppermute | solution.py:23
  7.5 54.0 %collective-permute-start.12 = (bf16[1024,256]{1,0:T(8,128)(2,1)}, bf16[1024,256]{1,0:T(8,128)(2,1)S(1)}, u32[]{:S(2)}, u32[]{:S(2)}) collective-permute-start(bf16[1024,256]{1,0:T(8,128)(2,1)} %param.4), channel_id=1, source_target_pairs={{0,1},{1,2},{2,3},{3,4},{4,5},{5,6},{6,7},{7,0},{8,9},{9,10},{10,1... | collective-permute-start | bytes 1572872 | tf_op jit(solution)/shard_map/ppermute | solution.py:23
  11.8 51.6 %collective-permute-start.16 = (bf16[1024,256]{1,0:T(8,128)(2,1)}, bf16[1024,256]{1,0:T(8,128)(2,1)S(1)}, u32[]{:S(2)}, u32[]{:S(2)}) collective-permute-start(bf16[1024,256]{1,0:T(8,128)(2,1)} %param.4), channel_id=1, source_target_pairs={{0,7},{1,0},{2,1},{3,2},{4,3},{5,4},{6,5},{7,6},{8,15},{9,8},{10,9... | collective-permute-start | bytes 1572872 | tf_op jit(solution)/shard_map/ppermute | solution.py:26
  20.4 7.8 %collective-permute-start.2 = (bf16[3,64,128]{2,1,0:T(8,128)(2,1)S(1)}, bf16[3,64,128]{2,1,0:T(8,128)(2,1)S(1)}, u32[]{:S(2)}, u32[]{:S(2)}) collective-permute-start(bf16[3,64,128]{2,1,0:T(8,128)(2,1)S(1)} %collective-permute-done.1), channel_id=1, source_target_pairs={{0,16},{16,32},{32,48},{48,0},{1,17},{17,33},{33,49},{49,1},{2,18}... | collective-permute-start | bytes 147464 | tf_op jit(solution)/shard_map/ppermute | solution.py:23
  24.5 6.0 %collective-permute-start.3 = (bf16[3,64,128]{2,1,0:T(8,128)(2,1)S(1)}, bf16[3,64,128]{2,1,0:T(8,128)(2,1)S(1)}, u32[]{:S(2)}, u32[]{:S(2)}) collective-permute-start(bf16[3,64,128]{2,1,0:T(8,128)(2,1)S(1)} %pad_maximum_fusion), channel_id=1, source_target_pairs={{0,48},{16,0},{32,16},{48,32},{1,49},{17,1},{33,17},{49,33},{2,50}... | collective-permute-start | bytes 147464 | tf_op jit(solution)/shard_map/ppermute | solution.py:26
  30.6 7.6 %collective-permute-start.4 = (bf16[3,256,128]{2,1,0:T(8,128)(2,1)S(1)}, bf16[3,256,128]{2,1,0:T(8,128)(2,1)S(1)}, u32[]{:S(2)}, u32[]{:S(2)}) collective-permute-start(bf16[3,256,128]{2,1,0:T(8,128)(2,1)S(1)} %bitcast.122), channel_id=1, source_target_pairs={{0,64},{64,128},{128,192},{192,256},{256,320},{320,384},{384,448},... | collective-permute-start | bytes 589832 | tf_op jit(solution)/shard_map/ppermute | solution.py:23
  38.2 7.7 %collective-permute-start.5 = (bf16[3,256,128]{2,1,0:T(8,128)(2,1)S(1)}, bf16[3,256,128]{2,1,0:T(8,128)(2,1)S(1)}, u32[]{:S(2)}, u32[]{:S(2)}) collective-permute-start(bf16[3,256,128]{2,1,0:T(8,128)(2,1)S(1)} %collective-permute-done.4), channel_id=1, source_target_pairs={{0,64},{64,128},{128,192},{192,256},{256,320},{320,384},{384,448},... | collective-permute-start | bytes 589832 | tf_op jit(solution)/shard_map/ppermute | solution.py:23
  43.9 9.2 %collective-permute-start.8 = (bf16[3,256,128]{2,1,0:T(8,128)(2,1)S(1)}, bf16[3,256,128]{2,1,0:T(8,128)(2,1)S(1)}, u32[]{:S(2)}, u32[]{:S(2)}) collective-permute-start(bf16[3,256,128]{2,1,0:T(8,128)(2,1)S(1)} %bitcast.123), channel_id=1, source_target_pairs={{0,448},{64,0},{128,64},{192,128},{256,192},{320,256},{384,320},{4... | collective-permute-start | bytes 589832 | tf_op jit(solution)/shard_map/ppermute | solution.py:26
  45.9 9.1 %collective-permute-start.6 = (bf16[3,256,128]{2,1,0:T(8,128)(2,1)S(1)}, bf16[3,256,128]{2,1,0:T(8,128)(2,1)S(1)}, u32[]{:S(2)}, u32[]{:S(2)}) collective-permute-start(bf16[3,256,128]{2,1,0:T(8,128)(2,1)S(1)} %collective-permute-done.5), channel_id=1, source_target_pairs={{0,64},{64,128},{128,192},{192,256},{256,320},{320,384},{384,448},... | collective-permute-start | bytes 589832 | tf_op jit(solution)/shard_map/ppermute | solution.py:23
  53.1 15.5 %collective-permute-start.9 = (bf16[3,256,128]{2,1,0:T(8,128)(2,1)S(1)}, bf16[3,256,128]{2,1,0:T(8,128)(2,1)S(1)}, u32[]{:S(2)}, u32[]{:S(2)}) collective-permute-start(bf16[3,256,128]{2,1,0:T(8,128)(2,1)S(1)} %collective-permute-done.8), channel_id=1, source_target_pairs={{0,448},{64,0},{128,64},{192,128},{256,192},{320,256},{384,320},{4... | collective-permute-start | bytes 589832 | tf_op jit(solution)/shard_map/ppermute | solution.py:26
  55.0 15.5 %collective-permute-start.7 = (bf16[3,256,128]{2,1,0:T(8,128)(2,1)S(1)}, bf16[3,256,128]{2,1,0:T(8,128)(2,1)S(1)}, u32[]{:S(2)}, u32[]{:S(2)}) collective-permute-start(bf16[3,256,128]{2,1,0:T(8,128)(2,1)S(1)} %collective-permute-done.6), channel_id=1, source_target_pairs={{0,64},{64,128},{128,192},{192,256},{256,320},{320,384},{384,448},... | collective-permute-start | bytes 589832 | tf_op jit(solution)/shard_map/ppermute | solution.py:23
  61.5 16.0 %collective-permute-start.13 = (bf16[1024,256]{1,0:T(8,128)(2,1)S(1)}, bf16[1024,256]{1,0:T(8,128)(2,1)S(1)}, u32[]{:S(2)}, u32[]{:S(2)}) collective-permute-start(bf16[1024,256]{1,0:T(8,128)(2,1)S(1)} %collective-permute-done.12), channel_id=1, source_target_pairs={{0,1},{1,2},{2,3},{3,4},{4,5},{5,6},{6,7},{7,0},{8,9},{9,10},{10,1... | collective-permute-start | bytes 1572872 | tf_op jit(solution)/shard_map/ppermute | solution.py:23
  63.4 31.8 %collective-permute-start.17 = (bf16[1024,256]{1,0:T(8,128)(2,1)S(1)}, bf16[1024,256]{1,0:T(8,128)(2,1)S(1)}, u32[]{:S(2)}, u32[]{:S(2)}) collective-permute-start(bf16[1024,256]{1,0:T(8,128)(2,1)S(1)} %collective-permute-done.16), channel_id=1, source_target_pairs={{0,7},{1,0},{2,1},{3,2},{4,3},{5,4},{6,5},{7,6},{8,15},{9,8},{10,9... | collective-permute-start | bytes 1572872 | tf_op jit(solution)/shard_map/ppermute | solution.py:26
  68.6 8.8 %collective-permute-start.10 = (bf16[3,256,128]{2,1,0:T(8,128)(2,1)S(1)}, bf16[3,256,128]{2,1,0:T(8,128)(2,1)S(1)}, u32[]{:S(2)}, u32[]{:S(2)}) collective-permute-start(bf16[3,256,128]{2,1,0:T(8,128)(2,1)S(1)} %collective-permute-done.9), channel_id=1, source_target_pairs={{0,448},{64,0},{128,64},{192,128},{256,192},{320,256},{384,320},{4... | collective-permute-start | bytes 589832 | tf_op jit(solution)/shard_map/ppermute | solution.py:26
  77.5 13.5 %collective-permute-start.14 = (bf16[1024,256]{1,0:T(8,128)(2,1)S(1)}, bf16[1024,256]{1,0:T(8,128)(2,1)S(1)}, u32[]{:S(2)}, u32[]{:S(2)}) collective-permute-start(bf16[1024,256]{1,0:T(8,128)(2,1)S(1)} %collective-permute-done.13), channel_id=1, source_target_pairs={{0,1},{1,2},{2,3},{3,4},{4,5},{5,6},{6,7},{7,0},{8,9},{9,10},{10,1... | collective-permute-start | bytes 1572872 | tf_op jit(solution)/shard_map/ppermute | solution.py:23
  91.0 12.3 %collective-permute-start.15 = (bf16[1024,256]{1,0:T(8,128)(2,1)S(1)}, bf16[1024,256]{1,0:T(8,128)(2,1)S(1)}, u32[]{:S(2)}, u32[]{:S(2)}) collective-permute-start(bf16[1024,256]{1,0:T(8,128)(2,1)S(1)} %collective-permute-done.14), channel_id=1, source_target_pairs={{0,1},{1,2},{2,3},{3,4},{4,5},{5,6},{6,7},{7,0},{8,9},{9,10},{10,1... | collective-permute-start | bytes 1572872 | tf_op jit(solution)/shard_map/ppermute | solution.py:23
  93.1 10.3 %copy-start = (bf16[1024,256]{1,0:T(8,128)(2,1)S(1)}, bf16[1024,256]{1,0:T(8,128)(2,1)}, u32[]{:S(2)}) copy-start(bf16[1024,256]{1,0:T(8,128)(2,1)} %param.4) | copy-start | bytes 1572868
  93.3 31.4 %collective-permute-start.11 = (bf16[3,2048,128]{2,1,0:T(8,128)(2,1)S(1)}, bf16[3,2048,128]{2,1,0:T(8,128)(2,1)}, u32[]{:S(2)}, u32[]{:S(2)}) collective-permute-start(bf16[3,2048,128]{2,1,0:T(8,128)(2,1)S(1)} %bitcast.126), channel_id=1, source_target_pairs={{0,8},{8,0},{1,9},{9,1},{2,10},{10,2},{3,11},{11,3},{4,12},{12,4},... | collective-permute-start | bytes 4718600 | tf_op jit(solution)/shard_map/ppermute | solution.py:46
  95.2 17.0 %collective-permute-start.18 = (bf16[1024,256]{1,0:T(8,128)(2,1)S(1)}, bf16[1024,256]{1,0:T(8,128)(2,1)S(1)}, u32[]{:S(2)}, u32[]{:S(2)}) collective-permute-start(bf16[1024,256]{1,0:T(8,128)(2,1)S(1)} %collective-permute-done.17), channel_id=1, source_target_pairs={{0,7},{1,0},{2,1},{3,2},{4,3},{5,4},{6,5},{7,6},{8,15},{9,8},{10,9... | collective-permute-start | bytes 1572872 | tf_op jit(solution)/shard_map/ppermute | solution.py:26
  135.8 17.6 %copy-start.1 = (bf16[1024,256]{0,1:T(8,128)(2,1)S(1)}, bf16[1024,256]{0,1:T(8,128)(2,1)}, u32[]{:S(2)}) copy-start(bf16[1024,256]{0,1:T(8,128)(2,1)} %fusion.16) | copy-start | bytes 1572868
  135.8 19.0 %copy-start.2 = (f32[1024,2,128]{2,0,1:T(8,128)S(1)}, f32[1024,2,128]{2,0,1:T(8,128)}, u32[]{:S(2)}) copy-start(f32[1024,2,128]{2,0,1:T(8,128)} %copy.55) | copy-start | bytes 3145732
  138.7 21.0 %collective-permute-start.19 = (f32[264,128]{1,0:T(8,128)S(1)}, f32[264,128]{1,0:T(8,128)}, u32[]{:S(2)}, u32[]{:S(2)}) collective-permute-start(f32[264,128]{1,0:T(8,128)S(1)} %concatenate.40), channel_id=1, source_target_pairs={{0,8},{8,16},{16,24},{24,32},{32,40},{40,48},{48,56},{56,64},{64,7... | collective-permute-start | bytes 405512 | tf_op jit(solution)/shard_map/ppermute | solution.py:15
  140.6 21.6 %collective-permute-start.22 = (f32[264,128]{1,0:T(8,128)S(1)}, f32[264,128]{1,0:T(8,128)}, u32[]{:S(2)}, u32[]{:S(2)}) collective-permute-start(f32[264,128]{1,0:T(8,128)S(1)} %concatenate.40), channel_id=1, source_target_pairs={{0,32},{8,40},{16,48},{24,56},{32,64},{40,72},{48,80},{56,88},{64,... | collective-permute-start | bytes 405512 | tf_op jit(solution)/shard_map/ppermute | solution.py:15
  144.2 20.5 %collective-permute-start.21 = (f32[264,128]{1,0:T(8,128)S(1)}, f32[264,128]{1,0:T(8,128)}, u32[]{:S(2)}, u32[]{:S(2)}) collective-permute-start(f32[264,128]{1,0:T(8,128)S(1)} %concatenate.40), channel_id=1, source_target_pairs={{0,24},{8,32},{16,40},{24,48},{32,56},{40,64},{48,72},{56,80},{64,... | collective-permute-start | bytes 405512 | tf_op jit(solution)/shard_map/ppermute | solution.py:15
  150.9 16.4 %collective-permute-start.20 = (f32[264,128]{1,0:T(8,128)S(1)}, f32[264,128]{1,0:T(8,128)}, u32[]{:S(2)}, u32[]{:S(2)}) collective-permute-start(f32[264,128]{1,0:T(8,128)S(1)} %concatenate.40), channel_id=1, source_target_pairs={{0,16},{8,24},{16,32},{24,40},{32,48},{40,56},{48,64},{56,72},{64,... | collective-permute-start | bytes 405512 | tf_op jit(solution)/shard_map/ppermute | solution.py:15
  157.8 24.1 %copy-start.3 = (s32[1024]{0:T(1024)S(1)}, s32[1024]{0:T(1024)}, u32[]{:S(2)}) copy-start(s32[1024]{0:T(1024)} %param.7) | copy-start | bytes 12292
  159.7 33.2 %copy-start.4 = (f32[256]{0:T(256)S(1)}, f32[256]{0:T(256)}, u32[]{:S(2)}) copy-start(f32[256]{0:T(256)} %param.6) | copy-start | bytes 3076
  171.6 11.6 %collective-permute-start.25 = (f32[264,128]{1,0:T(8,128)S(1)}, f32[264,128]{1,0:T(8,128)S(1)}, u32[]{:S(2)}, u32[]{:S(2)}) collective-permute-start(f32[264,128]{1,0:T(8,128)S(1)} %concatenate.41), channel_id=1, source_target_pairs={{0,96},{8,104},{16,112},{24,120},{32,128},{40,136},{48,144},{56,15... | collective-permute-start | bytes 405512 | tf_op jit(solution)/shard_map/ppermute | solution.py:15
  176.9 8.3 %collective-permute-start.24 = (f32[264,128]{1,0:T(8,128)S(1)}, f32[264,128]{1,0:T(8,128)S(1)}, u32[]{:S(2)}, u32[]{:S(2)}) collective-permute-start(f32[264,128]{1,0:T(8,128)S(1)} %concatenate.41), channel_id=1, source_target_pairs={{0,64},{8,72},{16,80},{24,88},{32,96},{40,104},{48,112},{56,120},{... | collective-permute-start | bytes 405512 | tf_op jit(solution)/shard_map/ppermute | solution.py:15
  178.9 11.4 %collective-permute-start.23 = (f32[264,128]{1,0:T(8,128)S(1)}, f32[264,128]{1,0:T(8,128)S(1)}, u32[]{:S(2)}, u32[]{:S(2)}) collective-permute-start(f32[264,128]{1,0:T(8,128)S(1)} %concatenate.41), channel_id=1, source_target_pairs={{0,32},{8,40},{16,48},{24,56},{32,64},{40,72},{48,80},{56,88},{64,... | collective-permute-start | bytes 405512 | tf_op jit(solution)/shard_map/ppermute | solution.py:15

commit v7 on v5

--- a/solution.py
+++ b/solution.py
@@ -62,43 +62,40 @@
     count = lax.axis_size(CTX)
     window = min(count - 1, 1 + (SPAN - 1) // row_count)
     packed = jnp.concatenate([flat, jnp.full((8, HEAD_DIM), tail_id, jnp.float32)], axis=0)
+    is_state = (lax.broadcasted_iota(jnp.int32, packed.shape, 0) < state_rows)
     radix = 4
-    span = 1
-    running = None
+    got = [shifted(packed, CTX, k, count) for k in range(1, radix + 1)]
+    prev_tail = got[0][state_rows, 0]
+    running = jnp.where(is_state, 0.0, prev_tail)
+    for piece in got:
+        running = running + jnp.where(is_state & (piece[state_rows, 0] == prev_tail), piece, 0.0)
+    span = radix
     while span < window:
-        got = [shifted(packed if running is None else running, CTX, span * k, count)
-               for k in range(1, radix + (running is None))]
-        if running is None:
-            prev_tail = got[0][state_rows, 0]
-            total = sum(jnp.where(g[state_rows, 0] == prev_tail, g[:state_rows], 0.0) for g in got)
-            running = jnp.concatenate([total, jnp.full((8, HEAD_DIM), prev_tail, jnp.float32)], axis=0)
-            span = radix
-        else:
-            total = running[:state_rows] + sum(
-                jnp.where(g[state_rows, 0] == prev_tail, g[:state_rows], 0.0) for g in got
-            )
-            running = jnp.concatenate([total, running[state_rows:]], axis=0)
-            span *= radix
+        got = [shifted(running, CTX, span * k, count) for k in range(1, radix)]
+        for piece in got:
+            running = running + jnp.where(is_state & (piece[state_rows, 0] == prev_tail), piece, 0.0)
+        span *= radix
     return running[:state_rows].reshape(head_count, HEAD_DIM, HEAD_DIM), prev_tail
 
 
 def per_device(tokens, w_qkv, out_gain, seg_ids):
     whole = lax.all_gather(tokens, "head", axis=1, tiled=True)
     w_rows = gather_weights(w_qkv)
-    projected = jnp.einsum(
-        "tr,grc->gtc", whole, w_rows, preferred_element_type=jnp.float32
+    key_value = jnp.einsum(
+        "tr,grc->gtc", whole, w_rows[1:], preferred_element_type=jnp.float32
     ).astype(jnp.bfloat16)
     row_count = seg_ids.shape[0]
-    head_count = projected.shape[2] // HEAD_DIM
-    queries = feature_map(projected[0]).reshape(row_count, head_count, HEAD_DIM)
-    key_map = feature_map(projected[1]).reshape(row_count, head_count, HEAD_DIM)
-    values = projected[2].reshape(row_count, head_count, HEAD_DIM)
+    head_count = key_value.shape[2] // HEAD_DIM
+    key_map = feature_map(key_value[0]).reshape(row_count, head_count, HEAD_DIM)
+    values = key_value[1].reshape(row_count, head_count, HEAD_DIM)
     seg_float = seg_ids.astype(jnp.float32)
     tail_id = seg_float[-1]
     key_tail = jnp.where((seg_float == tail_id)[:, None, None], key_map, jnp.zeros_like(key_map))
     kv_state = jnp.einsum("thd,the->hde", key_tail, values, preferred_element_type=jnp.float32)
 
     state_in, tail_in = state_scan(kv_state, tail_id, row_count)
+    query_proj = jnp.einsum("tr,rc->tc", whole, w_rows[0], preferred_element_type=jnp.float32)
+    queries = feature_map(query_proj.astype(jnp.bfloat16)).reshape(row_count, head_count, HEAD_DIM)
 
     block_rows = min(512, row_count)
     pieces = []

time: 168 us -> 165 us (0.982)
  waiting for transfers between devices: 41.7 us -> 37.8 us
    all_gather x1, waiting for transfers between devices: 17.4 us -> 13 us  [per_device(): whole = lax.all_gather(tokens, 'head', axis=1, tiled=True)]
    select_n x0 -> x2, other arithmetic: none -> 3.43 us  [the longest x1 2.78 us: gather_weights(): jnp.where(core == 0, jnp.concatenate([rows, other], axis=2), jnp.concaten...]
    dot_general x1 -> x2, matrix products: 5.67 us -> 8.02 us  [the longest x1 5.18 us: per_device(): jnp.einsum('tr,grc->gtc', whole, w_rows[1:], preferred_element_type=jnp.f...]
  transfers between devices with their start and end apart: 20 -> 20, of which waited for: 11 -> 12; matrix products, arithmetic and copies ran while one was open for 10% -> 14% of each run, Pallas kernels for 0% -> 0%
where the time goes in v7:
time: 165 us; the launch traced here: 164 us
  starting transfers between devices  66.8 us (40%)
  waiting for transfers between devices  37.8 us (23%)
  between operations  23.3 us (14%)
  matrix products  13.4 us (8%)
  local copies, waits for them, and re-layouts  13.3 us (8%)
  other arithmetic  9.16 us (6%)
    ppermute x6, starting transfers between devices, ring_gather(): lax.ppermute(ahead, axis, [(j, (j + 1) % count) for j in range(count)])  27 us
    ppermute x7, starting transfers between devices, shifted(): lax.ppermute(value, axis, [(source, source + steps) for source in range(c...  25.3 us
    all_gather x1, waiting for transfers between devices, per_device(): whole = lax.all_gather(tokens, 'head', axis=1, tiled=True)  13 us
    ppermute x6, waiting for transfers between devices, ring_gather(): lax.ppermute(ahead, axis, [(j, (j + 1) % count) for j in range(count)])  10.7 us
    ppermute x4, starting transfers between devices, ring_gather(): lax.ppermute(behind, axis, [(j, (j - 1) % count) for j in range(count)])  10.6 us
    ppermute x4, waiting for transfers between devices, ring_gather(): lax.ppermute(behind, axis, [(j, (j - 1) % count) for j in range(count)])  7.04 us
    slice x6, local copies, waits for them, and re-layouts, state_scan(): piece[state_rows, 0] == prev_tail  5.48 us
    dot_general x1, matrix products, per_device(): jnp.einsum('tr,grc->gtc', whole, w_rows[1:], preferred_element_type=jnp.f...  5.18 us
  transfers between devices with their start and end apart: 20, of which 12 were waited for; matrix products, arithmetic and copies ran while one was open for 14% of the time, Pallas kernels for 0%

profile of v7, /device:TPU:24, one launch (start us, length us, event | category | flops | bytes accessed | tf_op | source)
XLA Modules:
  0.0 163.7 jit_solution(16110081900939121639)
XLA Ops:
  6.5 1.9 %collective-permute-start = (bf16[3,32,256]{2,1,0:T(8,128)(2,1)}, bf16[3,32,256]{2,1,0:T(8,128)(2,1)S(1)}, u32[]{:S(2)}, u32[]{:S(2)}) collective-permute-start(bf16[3,32,256]{2,1,0:T(8,128)(2,1)} %param.5), channel_id=1, source_target_pairs={{0,8},{8,0},{1,9},{9,1},{2,10},{10,2},{3,11},{11,3},{4,12},{12,4},... | collective-permute-start | bytes 147464 | tf_op jit(solution)/shard_map/ppermute | solution.py:40
  8.5 1.4 collective-permute-done
  10.6 3.4 %collective-permute-start.1 = (bf16[3,64,128]{2,1,0:T(8,128)(2,1)S(1)}, bf16[3,64,128]{2,1,0:T(8,128)(2,1)S(1)}, u32[]{:S(2)}, u32[]{:S(2)}) collective-permute-start(bf16[3,64,128]{2,1,0:T(8,128)(2,1)S(1)} %pad_maximum_fusion), channel_id=1, source_target_pairs={{0,16},{16,32},{32,48},{48,0},{1,17},{17,33},{33,49},{49,1},{2,18}... | collective-permute-start | bytes 147464 | tf_op jit(solution)/shard_map/ppermute | solution.py:23
  14.0 3.8 %collective-permute-done.1 = bf16[3,64,128]{2,1,0:T(8,128)(2,1)S(1)} collective-permute-done((bf16[3,64,128]{2,1,0:T(8,128)(2,1)S(1)}, bf16[3,64,128]{2,1,0:T(8,128)(2,1)S(1)}, u32[]{:S(2)}, u32[]{:S(2)}) %collective-permute-start.1) | collective-permute-done | bytes 49184 | tf_op jit(solution)/shard_map/ppermute | solution.py:23
  17.8 2.2 %collective-permute-start.2 = (bf16[3,64,128]{2,1,0:T(8,128)(2,1)S(1)}, bf16[3,64,128]{2,1,0:T(8,128)(2,1)S(1)}, u32[]{:S(2)}, u32[]{:S(2)}) collective-permute-start(bf16[3,64,128]{2,1,0:T(8,128)(2,1)S(1)} %collective-permute-done.1), channel_id=1, source_target_pairs={{0,16},{16,32},{32,48},{48,0},{1,17},{17,33},{33,49},{49,1},{2,18}... | collective-permute-start | bytes 147464 | tf_op jit(solution)/shard_map/ppermute | solution.py:23
  20.1 4.9 %collective-permute-start.3 = (bf16[3,64,128]{2,1,0:T(8,128)(2,1)S(1)}, bf16[3,64,128]{2,1,0:T(8,128)(2,1)S(1)}, u32[]{:S(2)}, u32[]{:S(2)}) collective-permute-start(bf16[3,64,128]{2,1,0:T(8,128)(2,1)S(1)} %pad_maximum_fusion), channel_id=1, source_target_pairs={{0,48},{16,0},{32,16},{48,32},{1,49},{17,1},{33,17},{49,33},{2,50}... | collective-permute-start | bytes 147464 | tf_op jit(solution)/shard_map/ppermute | solution.py:26
  25.0 1.6 collective-permute-done.3
  26.8 4.7 %collective-permute-start.4 = (bf16[3,256,128]{2,1,0:T(8,128)(2,1)S(1)}, bf16[3,256,128]{2,1,0:T(8,128)(2,1)S(1)}, u32[]{:S(2)}, u32[]{:S(2)}) collective-permute-start(bf16[3,256,128]{2,1,0:T(8,128)(2,1)S(1)} %bitcast.119), channel_id=1, source_target_pairs={{0,64},{64,128},{128,192},{192,256},{256,320},{320,384},{384,448},... | collective-permute-start | bytes 589832 | tf_op jit(solution)/shard_map/ppermute | solution.py:23
  31.5 3.2 %collective-permute-done.4 = bf16[3,256,128]{2,1,0:T(8,128)(2,1)S(1)} collective-permute-done((bf16[3,256,128]{2,1,0:T(8,128)(2,1)S(1)}, bf16[3,256,128]{2,1,0:T(8,128)(2,1)S(1)}, u32[]{:S(2)}, u32[]{:S(2)}) %collective-permute-start.4) | collective-permute-done | bytes 196640 | tf_op jit(solution)/shard_map/ppermute | solution.py:23
  34.6 5.6 %collective-permute-start.5 = (bf16[3,256,128]{2,1,0:T(8,128)(2,1)S(1)}, bf16[3,256,128]{2,1,0:T(8,128)(2,1)S(1)}, u32[]{:S(2)}, u32[]{:S(2)}) collective-permute-start(bf16[3,256,128]{2,1,0:T(8,128)(2,1)S(1)} %collective-permute-done.4), channel_id=1, source_target_pairs={{0,64},{64,128},{128,192},{192,256},{256,320},{320,384},{384,448},... | collective-permute-start | bytes 589832 | tf_op jit(solution)/shard_map/ppermute | solution.py:23
  40.2 1.9 %collective-permute-start.8 = (bf16[3,256,128]{2,1,0:T(8,128)(2,1)S(1)}, bf16[3,256,128]{2,1,0:T(8,128)(2,1)S(1)}, u32[]{:S(2)}, u32[]{:S(2)}) collective-permute-start(bf16[3,256,128]{2,1,0:T(8,128)(2,1)S(1)} %bitcast.120), channel_id=1, source_target_pairs={{0,448},{64,0},{128,64},{192,128},{256,192},{320,256},{384,320},{4... | collective-permute-start | bytes 589832 | tf_op jit(solution)/shard_map/ppermute | solution.py:26
  43.4 5.6 %collective-permute-start.6 = (bf16[3,256,128]{2,1,0:T(8,128)(2,1)S(1)}, bf16[3,256,128]{2,1,0:T(8,128)(2,1)S(1)}, u32[]{:S(2)}, u32[]{:S(2)}) collective-permute-start(bf16[3,256,128]{2,1,0:T(8,128)(2,1)S(1)} %collective-permute-done.5), channel_id=1, source_target_pairs={{0,64},{64,128},{128,192},{192,256},{256,320},{320,384},{384,448},... | collective-permute-start | bytes 589832 | tf_op jit(solution)/shard_map/ppermute | solution.py:23
  49.0 1.9 %collective-permute-start.9 = (bf16[3,256,128]{2,1,0:T(8,128)(2,1)S(1)}, bf16[3,256,128]{2,1,0:T(8,128)(2,1)S(1)}, u32[]{:S(2)}, u32[]{:S(2)}) collective-permute-start(bf16[3,256,128]{2,1,0:T(8,128)(2,1)S(1)} %collective-permute-done.8), channel_id=1, source_target_pairs={{0,448},{64,0},{128,64},{192,128},{256,192},{320,256},{384,320},{4... | collective-permute-start | bytes 589832 | tf_op jit(solution)/shard_map/ppermute | solution.py:26
  52.2 5.6 %collective-permute-start.7 = (bf16[3,256,128]{2,1,0:T(8,128)(2,1)S(1)}, bf16[3,256,128]{2,1,0:T(8,128)(2,1)S(1)}, u32[]{:S(2)}, u32[]{:S(2)}) collective-permute-start(bf16[3,256,128]{2,1,0:T(8,128)(2,1)S(1)} %collective-permute-done.6), channel_id=1, source_target_pairs={{0,64},{64,128},{128,192},{192,256},{256,320},{320,384},{384,448},... | collective-permute-start | bytes 589832 | tf_op jit(solution)/shard_map/ppermute | solution.py:23
  57.8 1.9 %collective-permute-start.10 = (bf16[3,256,128]{2,1,0:T(8,128)(2,1)S(1)}, bf16[3,256,128]{2,1,0:T(8,128)(2,1)S(1)}, u32[]{:S(2)}, u32[]{:S(2)}) collective-permute-start(bf16[3,256,128]{2,1,0:T(8,128)(2,1)S(1)} %collective-permute-done.9), channel_id=1, source_target_pairs={{0,448},{64,0},{128,64},{192,128},{256,192},{320,256},{384,320},{4... | collective-permute-start | bytes 589832 | tf_op jit(solution)/shard_map/ppermute | solution.py:26
  61.2 5.4 %collective-permute-done.10 = bf16[3,256,128]{2,1,0:T(8,128)(2,1)S(1)} collective-permute-done((bf16[3,256,128]{2,1,0:T(8,128)(2,1)S(1)}, bf16[3,256,128]{2,1,0:T(8,128)(2,1)S(1)}, u32[]{:S(2)}, u32[]{:S(2)}) %collective-permute-start.10) | collective-permute-done | bytes 196640 | tf_op jit(solution)/shard_map/ppermute | solution.py:26
  69.0 1.9 %collective-permute-start.11 = (bf16[3,2048,128]{1,2,0:T(8,128)(2,1)S(1)}, bf16[3,2048,128]{1,2,0:T(8,128)(2,1)S(1)}, u32[]{:S(2)}, u32[]{:S(2)}) collective-permute-start(bf16[3,2048,128]{1,2,0:T(8,128)(2,1)S(1)} %reshape.130), channel_id=1, source_target_pairs={{0,8},{8,0},{1,9},{9,1},{2,10},{10,2},{3,11},{11,3},{4,12},{12,4},... | collective-permute-start | bytes 4718600 | tf_op jit(solution)/shard_map/ppermute | solution.py:46
  74.3 2.8 %maximum_select_fusion = bf16[3,2048,256]{1,2,0:T(8,128)(2,1)} fusion(bf16[3,2048,128]{1,2,0:T(8,128)(2,1)S(1)} %collective-permute-done.11, bf16[3,2048,128]{1,2,0:T(8,128)(2,1)S(1)} %reshape.130, pred[]{:T(512)S(6)} %eq.77), kind=kLoop, calls=%fused_computation.7 | loop fusion | flops 14155776 | bytes 6291457 | tf_op jit(solution)/shard_map/jit(_where)/select_n | solution.py:47
  77.1 13.0 %all-gather.2.cloned.1.call-done = bf16[1024,2048]{1,0:T(8,128)(2,1)} async-done(((bf16[1024,256]{1,0:T(8,128)(2,1)}), bf16[1024,2048]{1,0:T(8,128)(2,1)}) %all-gather.2.cloned.1.call-update) | async-done | bytes 4194320 | tf_op jit(solution)/shard_map/all_gather | solution.py:82
  90.1 5.2 %fusion.7 = bf16[2,1024,256]{1,2,0:T(8,128)(2,1)S(1)} fusion(bf16[3,2048,256]{1,2,0:T(8,128)(2,1)} %maximum_select_fusion, bf16[1024,2048]{1,0:T(8,128)(2,1)} %all-gather.2.cloned.1.call-done), kind=kOutput, calls=%fused_computation.16 | convolution fusion | flops 2148007936 | bytes 8388608 | tf_op jit(solution)/shard_map/tr,grc->gtc/dot_general | solution.py:84
  97.0 1.9 %collective-permute-start.12 = (f32[264,128]{1,0:T(8,128)S(1)}, f32[264,128]{1,0:T(8,128)}, u32[]{:S(2)}, u32[]{:S(2)}) collective-permute-start(f32[264,128]{1,0:T(8,128)S(1)} %concatenate.31), channel_id=1, source_target_pairs={{0,8},{8,16},{16,24},{24,32},{32,40},{40,48},{48,56},{56,64},{64,7... | collective-permute-start | bytes 405512 | tf_op jit(solution)/shard_map/ppermute | solution.py:15
  98.9 3.4 %collective-permute-start.13 = (f32[264,128]{1,0:T(8,128)S(1)}, f32[264,128]{1,0:T(8,128)}, u32[]{:S(2)}, u32[]{:S(2)}) collective-permute-start(f32[264,128]{1,0:T(8,128)S(1)} %concatenate.31), channel_id=1, source_target_pairs={{0,16},{8,24},{16,32},{24,40},{32,48},{40,56},{48,64},{56,72},{64,... | collective-permute-start | bytes 405512 | tf_op jit(solution)/shard_map/ppermute | solution.py:15
  102.3 4.0 %collective-permute-start.14 = (f32[264,128]{1,0:T(8,128)S(1)}, f32[264,128]{1,0:T(8,128)}, u32[]{:S(2)}, u32[]{:S(2)}) collective-permute-start(f32[264,128]{1,0:T(8,128)S(1)} %concatenate.31), channel_id=1, source_target_pairs={{0,24},{8,32},{16,40},{24,48},{32,56},{40,64},{48,72},{56,80},{64,... | collective-permute-start | bytes 405512 | tf_op jit(solution)/shard_map/ppermute | solution.py:15
  106.3 6.1 %collective-permute-start.15 = (f32[264,128]{1,0:T(8,128)S(1)}, f32[264,128]{1,0:T(8,128)}, u32[]{:S(2)}, u32[]{:S(2)}) collective-permute-start(f32[264,128]{1,0:T(8,128)S(1)} %concatenate.31), channel_id=1, source_target_pairs={{0,32},{8,40},{16,48},{24,56},{32,64},{40,72},{48,80},{56,88},{64,... | collective-permute-start | bytes 405512 | tf_op jit(solution)/shard_map/ppermute | solution.py:15
  113.4 2.8 %fusion.17 = bf16[1024,256]{0,1:T(8,128)(2,1)S(1)} fusion(bf16[1024,2048]{1,0:T(8,128)(2,1)S(1)} %copy-done.2, bf16[3,2048,256]{1,2,0:T(8,128)(2,1)} %maximum_select_fusion), kind=kOutput, calls=%fused_computation.25 | convolution fusion | flops 1075576832 | bytes 5767168 | tf_op jit(solution)/shard_map/tr,rc->tc/dot_general | solution.py:97
  117.0 2.5 %fusion.13 = f32[512,2,128]{0,2,1:T(8,128)S(1)} fusion(bf16[1024,2,128]{0,2,1:T(8,128)(2,1)S(1)} %bitcast.126, bf16[512,2,128]{0,2,1:T(8,128)(2,1)} %bitcast.130, pred[512,1024]{1,0:T(8,128)(4,1)S(1)} %fusion.2, f32[1024,2,128]{0,2,1:T(8,128)S(1)} %bitcast.124), kind=kOutput, calls=%fused_computation.21 | convolution fusion | flops 540278784 | bytes 2883584 | tf_op jit(solution)/shard_map/hbs,she->bhe/dot_general | solution.py:116
  119.6 1.9 %fusion.14 = f32[512,2,128]{0,2,1:T(8,128)S(1)} fusion(bf16[512,2,128]{0,2,1:T(8,128)(2,1)} %bitcast.128, bf16[512,2,128]{0,2,1:T(8,128)(2,1)} %bitcast.129, bf16[512,2,128]{0,2,1:T(8,128)(2,1)S(1)} %bitcast.127, pred[512,512]{1,0:T(8,128)(4,1)} %fusion.22), kind=kOutput, calls=%fused_computation.22 | convolution fusion | flops 269484032 | bytes 1572864 | tf_op jit(solution)/shard_map/hbs,she->bhe/dot_general | solution.py:116
  132.4 1.3 select_add_fusion
  133.8 3.4 %collective-permute-start.16 = (f32[264,128]{1,0:T(8,128)S(1)}, f32[264,128]{1,0:T(8,128)S(1)}, u32[]{:S(2)}, u32[]{:S(2)}) collective-permute-start(f32[264,128]{1,0:T(8,128)S(1)} %select_add_fusion), channel_id=1, source_target_pairs={{0,32},{8,40},{16,48},{24,56},{32,64},{40,72},{48,80},{56,88},{64,... | collective-permute-start | bytes 405512 | tf_op jit(solution)/shard_map/ppermute | solution.py:15
  137.2 2.4 %collective-permute-start.17 = (f32[264,128]{1,0:T(8,128)S(1)}, f32[264,128]{1,0:T(8,128)S(1)}, u32[]{:S(2)}, u32[]{:S(2)}) collective-permute-start(f32[264,128]{1,0:T(8,128)S(1)} %select_add_fusion), channel_id=1, source_target_pairs={{0,64},{8,72},{16,80},{24,88},{32,96},{40,104},{48,112},{56,120},{... | collective-permute-start | bytes 405512 | tf_op jit(solution)/shard_map/ppermute | solution.py:15
  139.6 4.0 %collective-permute-start.18 = (f32[264,128]{1,0:T(8,128)S(1)}, f32[264,128]{1,0:T(8,128)S(1)}, u32[]{:S(2)}, u32[]{:S(2)}) collective-permute-start(f32[264,128]{1,0:T(8,128)S(1)} %select_add_fusion), channel_id=1, source_target_pairs={{0,96},{8,104},{16,112},{24,120},{32,128},{40,136},{48,144},{56,15... | collective-permute-start | bytes 405512 | tf_op jit(solution)/shard_map/ppermute | solution.py:15
  148.2 5.0 %collective-permute-done.18 = f32[264,128]{1,0:T(8,128)S(1)} collective-permute-done((f32[264,128]{1,0:T(8,128)S(1)}, f32[264,128]{1,0:T(8,128)S(1)}, u32[]{:S(2)}, u32[]{:S(2)}) %collective-permute-start.18) | collective-permute-done | bytes 135200 | tf_op jit(solution)/shard_map/ppermute | solution.py:15
  (85 shorter events, 23.8 us)
Async XLA Ops:
  6.5 83.5 %all-gather.2.cloned.1.call-start = ((), (), s32[]{:S(2)}) async-start(), calls=%async_computation | async-start | bytes 4718592 | tf_op jit(solution)/shard_map/all_gather | solution.py:82
  6.5 3.3 %collective-permute-start = (bf16[3,32,256]{2,1,0:T(8,128)(2,1)}, bf16[3,32,256]{2,1,0:T(8,128)(2,1)S(1)}, u32[]{:S(2)}, u32[]{:S(2)}) collective-permute-start(bf16[3,32,256]{2,1,0:T(8,128)(2,1)} %param.5), channel_id=1, source_target_pairs={{0,8},{8,0},{1,9},{9,1},{2,10},{10,2},{3,11},{11,3},{4,12},{12,4},... | collective-permute-start | bytes 147464 | tf_op jit(solution)/shard_map/ppermute | solution.py:40
  10.6 7.2 %collective-permute-start.1 = (bf16[3,64,128]{2,1,0:T(8,128)(2,1)S(1)}, bf16[3,64,128]{2,1,0:T(8,128)(2,1)S(1)}, u32[]{:S(2)}, u32[]{:S(2)}) collective-permute-start(bf16[3,64,128]{2,1,0:T(8,128)(2,1)S(1)} %pad_maximum_fusion), channel_id=1, source_target_pairs={{0,16},{16,32},{32,48},{48,0},{1,17},{17,33},{33,49},{49,1},{2,18}... | collective-permute-start | bytes 147464 | tf_op jit(solution)/shard_map/ppermute | solution.py:23
  17.8 7.2 %collective-permute-start.2 = (bf16[3,64,128]{2,1,0:T(8,128)(2,1)S(1)}, bf16[3,64,128]{2,1,0:T(8,128)(2,1)S(1)}, u32[]{:S(2)}, u32[]{:S(2)}) collective-permute-start(bf16[3,64,128]{2,1,0:T(8,128)(2,1)S(1)} %collective-permute-done.1), channel_id=1, source_target_pairs={{0,16},{16,32},{32,48},{48,0},{1,17},{17,33},{33,49},{49,1},{2,18}... | collective-permute-start | bytes 147464 | tf_op jit(solution)/shard_map/ppermute | solution.py:23
  20.1 6.6 %collective-permute-start.3 = (bf16[3,64,128]{2,1,0:T(8,128)(2,1)S(1)}, bf16[3,64,128]{2,1,0:T(8,128)(2,1)S(1)}, u32[]{:S(2)}, u32[]{:S(2)}) collective-permute-start(bf16[3,64,128]{2,1,0:T(8,128)(2,1)S(1)} %pad_maximum_fusion), channel_id=1, source_target_pairs={{0,48},{16,0},{32,16},{48,32},{1,49},{17,1},{33,17},{49,33},{2,50}... | collective-permute-start | bytes 147464 | tf_op jit(solution)/shard_map/ppermute | solution.py:26
  26.8 7.9 %collective-permute-start.4 = (bf16[3,256,128]{2,1,0:T(8,128)(2,1)S(1)}, bf16[3,256,128]{2,1,0:T(8,128)(2,1)S(1)}, u32[]{:S(2)}, u32[]{:S(2)}) collective-permute-start(bf16[3,256,128]{2,1,0:T(8,128)(2,1)S(1)} %bitcast.119), channel_id=1, source_target_pairs={{0,64},{64,128},{128,192},{192,256},{256,320},{320,384},{384,448},... | collective-permute-start | bytes 589832 | tf_op jit(solution)/shard_map/ppermute | solution.py:23
  34.6 8.8 %collective-permute-start.5 = (bf16[3,256,128]{2,1,0:T(8,128)(2,1)S(1)}, bf16[3,256,128]{2,1,0:T(8,128)(2,1)S(1)}, u32[]{:S(2)}, u32[]{:S(2)}) collective-permute-start(bf16[3,256,128]{2,1,0:T(8,128)(2,1)S(1)} %collective-permute-done.4), channel_id=1, source_target_pairs={{0,64},{64,128},{128,192},{192,256},{256,320},{320,384},{384,448},... | collective-permute-start | bytes 589832 | tf_op jit(solution)/shard_map/ppermute | solution.py:23
  40.2 8.8 %collective-permute-start.8 = (bf16[3,256,128]{2,1,0:T(8,128)(2,1)S(1)}, bf16[3,256,128]{2,1,0:T(8,128)(2,1)S(1)}, u32[]{:S(2)}, u32[]{:S(2)}) collective-permute-start(bf16[3,256,128]{2,1,0:T(8,128)(2,1)S(1)} %bitcast.120), channel_id=1, source_target_pairs={{0,448},{64,0},{128,64},{192,128},{256,192},{320,256},{384,320},{4... | collective-permute-start | bytes 589832 | tf_op jit(solution)/shard_map/ppermute | solution.py:26
  43.4 8.8 %collective-permute-start.6 = (bf16[3,256,128]{2,1,0:T(8,128)(2,1)S(1)}, bf16[3,256,128]{2,1,0:T(8,128)(2,1)S(1)}, u32[]{:S(2)}, u32[]{:S(2)}) collective-permute-start(bf16[3,256,128]{2,1,0:T(8,128)(2,1)S(1)} %collective-permute-done.5), channel_id=1, source_target_pairs={{0,64},{64,128},{128,192},{192,256},{256,320},{320,384},{384,448},... | collective-permute-start | bytes 589832 | tf_op jit(solution)/shard_map/ppermute | solution.py:23
  49.0 8.8 %collective-permute-start.9 = (bf16[3,256,128]{2,1,0:T(8,128)(2,1)S(1)}, bf16[3,256,128]{2,1,0:T(8,128)(2,1)S(1)}, u32[]{:S(2)}, u32[]{:S(2)}) collective-permute-start(bf16[3,256,128]{2,1,0:T(8,128)(2,1)S(1)} %collective-permute-done.8), channel_id=1, source_target_pairs={{0,448},{64,0},{128,64},{192,128},{256,192},{320,256},{384,320},{4... | collective-permute-start | bytes 589832 | tf_op jit(solution)/shard_map/ppermute | solution.py:26
  52.2 8.8 %collective-permute-start.7 = (bf16[3,256,128]{2,1,0:T(8,128)(2,1)S(1)}, bf16[3,256,128]{2,1,0:T(8,128)(2,1)S(1)}, u32[]{:S(2)}, u32[]{:S(2)}) collective-permute-start(bf16[3,256,128]{2,1,0:T(8,128)(2,1)S(1)} %collective-permute-done.6), channel_id=1, source_target_pairs={{0,64},{64,128},{128,192},{192,256},{256,320},{320,384},{384,448},... | collective-permute-start | bytes 589832 | tf_op jit(solution)/shard_map/ppermute | solution.py:23
  57.8 8.8 %collective-permute-start.10 = (bf16[3,256,128]{2,1,0:T(8,128)(2,1)S(1)}, bf16[3,256,128]{2,1,0:T(8,128)(2,1)S(1)}, u32[]{:S(2)}, u32[]{:S(2)}) collective-permute-start(bf16[3,256,128]{2,1,0:T(8,128)(2,1)S(1)} %collective-permute-done.9), channel_id=1, source_target_pairs={{0,448},{64,0},{128,64},{192,128},{256,192},{320,256},{384,320},{4... | collective-permute-start | bytes 589832 | tf_op jit(solution)/shard_map/ppermute | solution.py:26
  67.1 3.9 %copy-start = (s32[1024]{0:T(1024)S(1)}, s32[1024]{0:T(1024)}, u32[]{:S(2)}) copy-start(s32[1024]{0:T(1024)} %param.7) | copy-start | bytes 12292
  69.0 5.3 %collective-permute-start.11 = (bf16[3,2048,128]{1,2,0:T(8,128)(2,1)S(1)}, bf16[3,2048,128]{1,2,0:T(8,128)(2,1)S(1)}, u32[]{:S(2)}, u32[]{:S(2)}) collective-permute-start(bf16[3,2048,128]{1,2,0:T(8,128)(2,1)S(1)} %reshape.130), channel_id=1, source_target_pairs={{0,8},{8,0},{1,9},{9,1},{2,10},{10,2},{3,11},{11,3},{4,12},{12,4},... | collective-permute-start | bytes 4718600 | tf_op jit(solution)/shard_map/ppermute | solution.py:46
  95.4 17.9 %copy-start.2 = (bf16[1024,2048]{1,0:T(8,128)(2,1)S(1)}, bf16[1024,2048]{1,0:T(8,128)(2,1)}, u32[]{:S(2)}) copy-start(bf16[1024,2048]{1,0:T(8,128)(2,1)} %all-gather.2.cloned.1.call-done) | copy-start | bytes 12582916
  97.0 24.4 %collective-permute-start.12 = (f32[264,128]{1,0:T(8,128)S(1)}, f32[264,128]{1,0:T(8,128)}, u32[]{:S(2)}, u32[]{:S(2)}) collective-permute-start(f32[264,128]{1,0:T(8,128)S(1)} %concatenate.31), channel_id=1, source_target_pairs={{0,8},{8,16},{16,24},{24,32},{32,40},{40,48},{48,56},{56,64},{64,7... | collective-permute-start | bytes 405512 | tf_op jit(solution)/shard_map/ppermute | solution.py:15
  98.9 23.7 %collective-permute-start.13 = (f32[264,128]{1,0:T(8,128)S(1)}, f32[264,128]{1,0:T(8,128)}, u32[]{:S(2)}, u32[]{:S(2)}) collective-permute-start(f32[264,128]{1,0:T(8,128)S(1)} %concatenate.31), channel_id=1, source_target_pairs={{0,16},{8,24},{16,32},{24,40},{32,48},{40,56},{48,64},{56,72},{64,... | collective-permute-start | bytes 405512 | tf_op jit(solution)/shard_map/ppermute | solution.py:15
  102.3 22.9 %collective-permute-start.14 = (f32[264,128]{1,0:T(8,128)S(1)}, f32[264,128]{1,0:T(8,128)}, u32[]{:S(2)}, u32[]{:S(2)}) collective-permute-start(f32[264,128]{1,0:T(8,128)S(1)} %concatenate.31), channel_id=1, source_target_pairs={{0,24},{8,32},{16,40},{24,48},{32,56},{40,64},{48,72},{56,80},{64,... | collective-permute-start | bytes 405512 | tf_op jit(solution)/shard_map/ppermute | solution.py:15
  106.3 23.5 %collective-permute-start.15 = (f32[264,128]{1,0:T(8,128)S(1)}, f32[264,128]{1,0:T(8,128)}, u32[]{:S(2)}, u32[]{:S(2)}) collective-permute-start(f32[264,128]{1,0:T(8,128)S(1)} %concatenate.31), channel_id=1, source_target_pairs={{0,32},{8,40},{16,48},{24,56},{32,64},{40,72},{48,80},{56,88},{64,... | collective-permute-start | bytes 405512 | tf_op jit(solution)/shard_map/ppermute | solution.py:15
  119.5 36.1 %copy-start.1 = (f32[256]{0:T(256)S(1)}, f32[256]{0:T(256)}, u32[]{:S(2)}) copy-start(f32[256]{0:T(256)} %param.6) | copy-start | bytes 3076
  133.8 10.6 %collective-permute-start.16 = (f32[264,128]{1,0:T(8,128)S(1)}, f32[264,128]{1,0:T(8,128)S(1)}, u32[]{:S(2)}, u32[]{:S(2)}) collective-permute-start(f32[264,128]{1,0:T(8,128)S(1)} %select_add_fusion), channel_id=1, source_target_pairs={{0,32},{8,40},{16,48},{24,56},{32,64},{40,72},{48,80},{56,88},{64,... | collective-permute-start | bytes 405512 | tf_op jit(solution)/shard_map/ppermute | solution.py:15
  137.2 9.1 %collective-permute-start.17 = (f32[264,128]{1,0:T(8,128)S(1)}, f32[264,128]{1,0:T(8,128)S(1)}, u32[]{:S(2)}, u32[]{:S(2)}) collective-permute-start(f32[264,128]{1,0:T(8,128)S(1)} %select_add_fusion), channel_id=1, source_target_pairs={{0,64},{8,72},{16,80},{24,88},{32,96},{40,104},{48,112},{56,120},{... | collective-permute-start | bytes 405512 | tf_op jit(solution)/shard_map/ppermute | solution.py:15
  139.6 13.5 %collective-permute-start.18 = (f32[264,128]{1,0:T(8,128)S(1)}, f32[264,128]{1,0:T(8,128)S(1)}, u32[]{:S(2)}, u32[]{:S(2)}) collective-permute-start(f32[264,128]{1,0:T(8,128)S(1)} %select_add_fusion), channel_id=1, source_target_pairs={{0,96},{8,104},{16,112},{24,120},{32,128},{40,136},{48,144},{56,15... | collective-permute-start | bytes 405512 | tf_op jit(solution)/shard_map/ppermute | solution.py:15
Sparse Core Ops, SparseCore 0:
  20.2 69.8 all-gather.1

commit v8 on v7

--- a/solution.py
+++ b/solution.py
@@ -55,36 +55,45 @@
     return (jax.nn.elu(values.astype(jnp.float32)) + 1.0).astype(jnp.bfloat16)
 
 
-def state_scan(kv_state, tail_id, row_count):
-    head_count = kv_state.shape[0]
-    state_rows = head_count * HEAD_DIM
-    flat = kv_state.reshape(state_rows, HEAD_DIM)
+def state_scan(kv_state, tails, row_count):
     count = lax.axis_size(CTX)
     window = min(count - 1, 1 + (SPAN - 1) // row_count)
-    packed = jnp.concatenate([flat, jnp.full((8, HEAD_DIM), tail_id, jnp.float32)], axis=0)
-    is_state = (lax.broadcasted_iota(jnp.int32, packed.shape, 0) < state_rows)
+    me = lax.axis_index(CTX)
+
+    def tail_of(block):
+        return jnp.where(block >= 0, tails[jnp.clip(block, 0, count - 1)], -1.0)
+
+    prev_tail = tail_of(me - 1)
+
+    def counts(block):
+        return (block >= 0) & (tail_of(block) == prev_tail)
+
     radix = 4
-    got = [shifted(packed, CTX, k, count) for k in range(1, radix + 1)]
-    prev_tail = got[0][state_rows, 0]
-    running = jnp.where(is_state, 0.0, prev_tail)
-    for piece in got:
-        running = running + jnp.where(is_state & (piece[state_rows, 0] == prev_tail), piece, 0.0)
+    got = [shifted(kv_state, CTX, k, count) for k in range(1, radix + 1)]
+    running = sum(jnp.where(counts(me - k), piece, 0.0) for k, piece in zip(range(1, radix + 1), got))
     span = radix
     while span < window:
         got = [shifted(running, CTX, span * k, count) for k in range(1, radix)]
-        for piece in got:
-            running = running + jnp.where(is_state & (piece[state_rows, 0] == prev_tail), piece, 0.0)
+        running = running + sum(
+            jnp.where(counts(me - span * k - 1), piece, 0.0) for k, piece in zip(range(1, radix), got)
+        )
         span *= radix
-    return running[:state_rows].reshape(head_count, HEAD_DIM, HEAD_DIM), prev_tail
+    return running, prev_tail
 
 
 def per_device(tokens, w_qkv, out_gain, seg_ids):
     whole = lax.all_gather(tokens, "head", axis=1, tiled=True)
-    w_rows = gather_weights(w_qkv)
+    row_count = seg_ids.shape[0]
+    groups = lax.axis_size(CTX)
+    own_rows = w_qkv.shape[1]
+    tail_row = jnp.full((w_qkv.shape[0], 1, w_qkv.shape[2]), seg_ids[-1], w_qkv.dtype)
+    carried = gather_weights(jnp.concatenate([w_qkv, tail_row], axis=1))
+    carried = carried.reshape(w_qkv.shape[0], groups, own_rows + 1, w_qkv.shape[2])
+    w_rows = carried[:, :, :own_rows].reshape(w_qkv.shape[0], groups * own_rows, w_qkv.shape[2])
+    tails = carried[0, :, own_rows, 0].astype(jnp.float32)
     key_value = jnp.einsum(
         "tr,grc->gtc", whole, w_rows[1:], preferred_element_type=jnp.float32
     ).astype(jnp.bfloat16)
-    row_count = seg_ids.shape[0]
     head_count = key_value.shape[2] // HEAD_DIM
     key_map = feature_map(key_value[0]).reshape(row_count, head_count, HEAD_DIM)
     values = key_value[1].reshape(row_count, head_count, HEAD_DIM)
@@ -93,9 +102,10 @@
     key_tail = jnp.where((seg_float == tail_id)[:, None, None], key_map, jnp.zeros_like(key_map))
     kv_state = jnp.einsum("thd,the->hde", key_tail, values, preferred_element_type=jnp.float32)
 
-    state_in, tail_in = state_scan(kv_state, tail_id, row_count)
+    state_in, tail_in = state_scan(kv_state, tails, row_count)
     query_proj = jnp.einsum("tr,rc->tc", whole, w_rows[0], preferred_element_type=jnp.float32)
-    queries = feature_map(query_proj.astype(jnp.bfloat16)).reshape(row_count, head_count, HEAD_DIM)
+    query_proj = lax.reduce_precision(query_proj, exponent_bits=8, mantissa_bits=7)
+    queries = feature_map(query_proj).reshape(row_count, head_count, HEAD_DIM)
 
     block_rows = min(512, row_count)
     pieces = []

time: 165 us -> 150 us (0.909)
  the two profiles are of different devices: /device:TPU:24 before, /device:TPU:32 now
where the time goes in v8:
time: 150 us; the launch traced here: 149 us
  starting transfers between devices  62 us (41%)
  waiting for transfers between devices  31.4 us (21%)
  between operations  18.3 us (12%)
  local copies, waits for them, and re-layouts  15.6 us (10%)
  matrix products  13.2 us (9%)
  other arithmetic  8.73 us (6%)
    ppermute x7, starting transfers between devices, shifted(): lax.ppermute(value, axis, [(source, source + steps) for source in range(c...  24.1 us
    ppermute x4, starting transfers between devices, ring_gather(): lax.ppermute(behind, axis, [(j, (j - 1) % count) for j in range(count)])  20.3 us
    ppermute x6, waiting for transfers between devices, ring_gather(): lax.ppermute(ahead, axis, [(j, (j + 1) % count) for j in range(count)])  15.4 us
    ppermute x6, starting transfers between devices, ring_gather(): lax.ppermute(ahead, axis, [(j, (j + 1) % count) for j in range(count)])  13.9 us
    ppermute x7, waiting for transfers between devices, shifted(): lax.ppermute(value, axis, [(source, source + steps) for source in range(c...  7.55 us
    concatenate x2, local copies, waits for them, and re-layouts, gather_weights(): jnp.concatenate([rows, other], axis=2)  6.18 us
    dot_general x2, matrix products, per_device(): jnp.einsum('hbs,she->bhe', weights, values[:key_end], preferred_element_t...  5.31 us
    dot_general x1, matrix products, per_device(): jnp.einsum('tr,grc->gtc', whole, w_rows[1:], preferred_element_type=jnp.f...  4.56 us
  transfers between devices with their start and end apart: 20, of which 13 were waited for; matrix products, arithmetic and copies ran while one was open for 17% of the time, Pallas kernels for 0%

profile of v8, /device:TPU:32, one launch (start us, length us, event | category | flops | bytes accessed | tf_op | source)
XLA Modules:
  0.0 149.3 jit_solution(2068258097206424921)
XLA Ops:
  9.3 1.9 %collective-permute-start = (bf16[3,33,256]{2,1,0:T(8,128)(2,1)S(1)}, bf16[3,33,256]{2,1,0:T(8,128)(2,1)S(1)}, u32[]{:S(2)}, u32[]{:S(2)}) collective-permute-start(bf16[3,33,256]{2,1,0:T(8,128)(2,1)S(1)} %concatenate.31), channel_id=1, source_target_pairs={{0,8},{8,0},{1,9},{9,1},{2,10},{10,2},{3,11},{11,3},{4,12},{12,4},... | collective-permute-start | bytes 152072 | tf_op jit(solution)/shard_map/ppermute | solution.py:40
  13.9 3.4 %collective-permute-start.1 = (bf16[3,66,128]{2,1,0:T(8,128)(2,1)S(1)}, bf16[3,66,128]{2,1,0:T(8,128)(2,1)S(1)}, u32[]{:S(2)}, u32[]{:S(2)}) collective-permute-start(bf16[3,66,128]{2,1,0:T(8,128)(2,1)S(1)} %pad_maximum_fusion), channel_id=1, source_target_pairs={{0,16},{16,32},{32,48},{48,0},{1,17},{17,33},{33,49},{49,1},{2,18}... | collective-permute-start | bytes 152072 | tf_op jit(solution)/shard_map/ppermute | solution.py:23
  17.3 3.9 %collective-permute-done.1 = bf16[3,66,128]{2,1,0:T(8,128)(2,1)S(1)} collective-permute-done((bf16[3,66,128]{2,1,0:T(8,128)(2,1)S(1)}, bf16[3,66,128]{2,1,0:T(8,128)(2,1)S(1)}, u32[]{:S(2)}, u32[]{:S(2)}) %collective-permute-start.1) | collective-permute-done | bytes 50720 | tf_op jit(solution)/shard_map/ppermute | solution.py:23
  21.2 2.2 %collective-permute-start.2 = (bf16[3,66,128]{2,1,0:T(8,128)(2,1)S(1)}, bf16[3,66,128]{2,1,0:T(8,128)(2,1)S(1)}, u32[]{:S(2)}, u32[]{:S(2)}) collective-permute-start(bf16[3,66,128]{2,1,0:T(8,128)(2,1)S(1)} %collective-permute-done.1), channel_id=1, source_target_pairs={{0,16},{16,32},{32,48},{48,0},{1,17},{17,33},{33,49},{49,1},{2,18}... | collective-permute-start | bytes 152072 | tf_op jit(solution)/shard_map/ppermute | solution.py:23
  23.4 4.9 %collective-permute-start.3 = (bf16[3,66,128]{2,1,0:T(8,128)(2,1)S(1)}, bf16[3,66,128]{2,1,0:T(8,128)(2,1)S(1)}, u32[]{:S(2)}, u32[]{:S(2)}) collective-permute-start(bf16[3,66,128]{2,1,0:T(8,128)(2,1)S(1)} %pad_maximum_fusion), channel_id=1, source_target_pairs={{0,48},{16,0},{32,16},{48,32},{1,49},{17,1},{33,17},{49,33},{2,50}... | collective-permute-start | bytes 152072 | tf_op jit(solution)/shard_map/ppermute | solution.py:26
  30.3 2.6 %collective-permute-start.4 = (bf16[3,264,128]{2,1,0:T(8,128)(2,1)S(1)}, bf16[3,264,128]{2,1,0:T(8,128)(2,1)S(1)}, u32[]{:S(2)}, u32[]{:S(2)}) collective-permute-start(bf16[3,264,128]{2,1,0:T(8,128)(2,1)S(1)} %reshape.151), channel_id=1, source_target_pairs={{0,64},{64,128},{128,192},{192,256},{256,320},{320,384},{384,448},... | collective-permute-start | bytes 608264 | tf_op jit(solution)/shard_map/ppermute | solution.py:23
  32.9 6.2 %collective-permute-done.4 = bf16[3,264,128]{2,1,0:T(8,128)(2,1)S(1)} collective-permute-done((bf16[3,264,128]{2,1,0:T(8,128)(2,1)S(1)}, bf16[3,264,128]{2,1,0:T(8,128)(2,1)S(1)}, u32[]{:S(2)}, u32[]{:S(2)}) %collective-permute-start.4) | collective-permute-done | bytes 202784 | tf_op jit(solution)/shard_map/ppermute | solution.py:23
  39.1 1.9 %collective-permute-start.5 = (bf16[3,264,128]{2,1,0:T(8,128)(2,1)S(1)}, bf16[3,264,128]{2,1,0:T(8,128)(2,1)S(1)}, u32[]{:S(2)}, u32[]{:S(2)}) collective-permute-start(bf16[3,264,128]{2,1,0:T(8,128)(2,1)S(1)} %collective-permute-done.4), channel_id=1, source_target_pairs={{0,64},{64,128},{128,192},{192,256},{256,320},{320,384},{384,448},... | collective-permute-start | bytes 608264 | tf_op jit(solution)/shard_map/ppermute | solution.py:23
  41.1 5.1 %collective-permute-start.8 = (bf16[3,264,128]{2,1,0:T(8,128)(2,1)S(1)}, bf16[3,264,128]{2,1,0:T(8,128)(2,1)S(1)}, u32[]{:S(2)}, u32[]{:S(2)}) collective-permute-start(bf16[3,264,128]{2,1,0:T(8,128)(2,1)S(1)} %reshape.151), channel_id=1, source_target_pairs={{0,448},{64,0},{128,64},{192,128},{256,192},{320,256},{384,320},{4... | collective-permute-start | bytes 608264 | tf_op jit(solution)/shard_map/ppermute | solution.py:26
  46.2 1.8 %collective-permute-done.5 = bf16[3,264,128]{2,1,0:T(8,128)(2,1)S(1)} collective-permute-done((bf16[3,264,128]{2,1,0:T(8,128)(2,1)S(1)}, bf16[3,264,128]{2,1,0:T(8,128)(2,1)S(1)}, u32[]{:S(2)}, u32[]{:S(2)}) %collective-permute-start.5) | collective-permute-done | bytes 202784 | tf_op jit(solution)/shard_map/ppermute | solution.py:23
  48.0 1.9 %collective-permute-start.6 = (bf16[3,264,128]{2,1,0:T(8,128)(2,1)S(1)}, bf16[3,264,128]{2,1,0:T(8,128)(2,1)S(1)}, u32[]{:S(2)}, u32[]{:S(2)}) collective-permute-start(bf16[3,264,128]{2,1,0:T(8,128)(2,1)S(1)} %collective-permute-done.5), channel_id=1, source_target_pairs={{0,64},{64,128},{128,192},{192,256},{256,320},{320,384},{384,448},... | collective-permute-start | bytes 608264 | tf_op jit(solution)/shard_map/ppermute | solution.py:23
  49.9 5.1 %collective-permute-start.9 = (bf16[3,264,128]{2,1,0:T(8,128)(2,1)S(1)}, bf16[3,264,128]{2,1,0:T(8,128)(2,1)S(1)}, u32[]{:S(2)}, u32[]{:S(2)}) collective-permute-start(bf16[3,264,128]{2,1,0:T(8,128)(2,1)S(1)} %collective-permute-done.8), channel_id=1, source_target_pairs={{0,448},{64,0},{128,64},{192,128},{256,192},{320,256},{384,320},{4... | collective-permute-start | bytes 608264 | tf_op jit(solution)/shard_map/ppermute | solution.py:26
  55.0 1.8 %collective-permute-done.6 = bf16[3,264,128]{2,1,0:T(8,128)(2,1)S(1)} collective-permute-done((bf16[3,264,128]{2,1,0:T(8,128)(2,1)S(1)}, bf16[3,264,128]{2,1,0:T(8,128)(2,1)S(1)}, u32[]{:S(2)}, u32[]{:S(2)}) %collective-permute-start.6) | collective-permute-done | bytes 202784 | tf_op jit(solution)/shard_map/ppermute | solution.py:23
  56.8 1.9 %collective-permute-start.7 = (bf16[3,264,128]{2,1,0:T(8,128)(2,1)S(1)}, bf16[3,264,128]{2,1,0:T(8,128)(2,1)S(1)}, u32[]{:S(2)}, u32[]{:S(2)}) collective-permute-start(bf16[3,264,128]{2,1,0:T(8,128)(2,1)S(1)} %collective-permute-done.6), channel_id=1, source_target_pairs={{0,64},{64,128},{128,192},{192,256},{256,320},{320,384},{384,448},... | collective-permute-start | bytes 608264 | tf_op jit(solution)/shard_map/ppermute | solution.py:23
  58.8 5.1 %collective-permute-start.10 = (bf16[3,264,128]{2,1,0:T(8,128)(2,1)S(1)}, bf16[3,264,128]{2,1,0:T(8,128)(2,1)S(1)}, u32[]{:S(2)}, u32[]{:S(2)}) collective-permute-start(bf16[3,264,128]{2,1,0:T(8,128)(2,1)S(1)} %collective-permute-done.9), channel_id=1, source_target_pairs={{0,448},{64,0},{128,64},{192,128},{256,192},{320,256},{384,320},{4... | collective-permute-start | bytes 608264 | tf_op jit(solution)/shard_map/ppermute | solution.py:26
  69.0 1.9 %collective-permute-start.11 = (bf16[3,2112,128]{2,1,0:T(8,128)(2,1)}, bf16[3,2112,128]{2,1,0:T(8,128)(2,1)}, u32[]{:S(2)}, u32[]{:S(2)}) collective-permute-start(bf16[3,2112,128]{2,1,0:T(8,128)(2,1)} %bitcast.14), channel_id=1, source_target_pairs={{0,8},{8,0},{1,9},{9,1},{2,10},{10,2},{3,11},{11,3},{4,12},{12,4},... | collective-permute-start | bytes 4866056 | tf_op jit(solution)/shard_map/ppermute | solution.py:46
  73.0 2.5 %concatenate.35 = bf16[3,64,33,128]{3,2,1,0:T(8,128)(2,1)S(1)} reshape(bf16[3,8,264,128]{3,2,1,0:T(8,128)(2,1)} %copy.23) | data formatting | bytes 3244032 | tf_op jit(solution)/shard_map/concatenate | solution.py:49
  75.5 3.7 %concatenate.36 = bf16[3,64,33,128]{3,2,1,0:T(8,128)(2,1)} reshape(bf16[3,2112,128]{2,1,0:T(8,128)(2,1)} %collective-permute-done.11) | data formatting | bytes 3244032 | tf_op jit(solution)/shard_map/concatenate | solution.py:49
  79.2 2.8 %maximum_select_fusion = bf16[3,64,33,256]{3,2,1,0:T(8,128)(2,1)S(1)} fusion(bf16[3,64,33,128]{3,2,1,0:T(8,128)(2,1)} %concatenate.36, bf16[3,64,33,128]{3,2,1,0:T(8,128)(2,1)S(1)} %concatenate.35, pred[]{:T(512)S(6)} %eq.77), kind=kLoop, calls=%fused_computation.3 | loop fusion | flops 14598144 | bytes 6488065 | tf_op jit(solution)/shard_map/jit(_where)/select_n | solution.py:47
  89.1 4.3 %all-gather.2.cloned.1.call-done = bf16[1024,2048]{1,0:T(8,128)(2,1)} async-done(((bf16[1024,256]{1,0:T(8,128)(2,1)}), bf16[1024,2048]{1,0:T(8,128)(2,1)}) %all-gather.2.cloned.1.call-update) | async-done | bytes 4194320 | tf_op jit(solution)/shard_map/all_gather | solution.py:85
  93.3 4.6 %fusion.7 = bf16[2,1024,256]{1,2,0:T(8,128)(2,1)S(1)} fusion(bf16[2,2048,256]{2,1,0:T(8,128)(2,1)S(1)} %bitcast.97, bf16[1024,2048]{1,0:T(8,128)(2,1)} %all-gather.2.cloned.1.call-done), kind=kOutput, calls=%fused_computation.16 | convolution fusion | flops 2148007936 | bytes 7340032 | tf_op jit(solution)/shard_map/tr,grc->gtc/dot_general | solution.py:94
  99.4 5.0 %collective-permute-start.15 = (f32[2,128,128]{2,1,0:T(8,128)}, f32[2,128,128]{2,1,0:T(8,128)S(1)}, u32[]{:S(2)}, u32[]{:S(2)}) collective-permute-start(f32[2,128,128]{2,1,0:T(8,128)} %fusion.28), channel_id=1, source_target_pairs={{0,32},{8,40},{16,48},{24,56},{32,64},{40,72},{48,80},{56,88},{64,... | collective-permute-start | bytes 393224 | tf_op jit(solution)/shard_map/ppermute | solution.py:15
  104.4 1.9 %collective-permute-start.14 = (f32[2,128,128]{2,1,0:T(8,128)}, f32[2,128,128]{2,1,0:T(8,128)}, u32[]{:S(2)}, u32[]{:S(2)}) collective-permute-start(f32[2,128,128]{2,1,0:T(8,128)} %fusion.28), channel_id=1, source_target_pairs={{0,24},{8,32},{16,40},{24,48},{32,56},{40,64},{48,72},{56,80},{64,... | collective-permute-start | bytes 393224 | tf_op jit(solution)/shard_map/ppermute | solution.py:15
  106.4 2.4 %collective-permute-start.13 = (f32[2,128,128]{2,1,0:T(8,128)}, f32[2,128,128]{2,1,0:T(8,128)}, u32[]{:S(2)}, u32[]{:S(2)}) collective-permute-start(f32[2,128,128]{2,1,0:T(8,128)} %fusion.28), channel_id=1, source_target_pairs={{0,16},{8,24},{16,32},{24,40},{32,48},{40,56},{48,64},{56,72},{64,... | collective-permute-start | bytes 393224 | tf_op jit(solution)/shard_map/ppermute | solution.py:15
  108.8 3.2 %collective-permute-start.12 = (f32[2,128,128]{2,1,0:T(8,128)}, f32[2,128,128]{2,1,0:T(8,128)}, u32[]{:S(2)}, u32[]{:S(2)}) collective-permute-start(f32[2,128,128]{2,1,0:T(8,128)} %fusion.28), channel_id=1, source_target_pairs={{0,8},{8,16},{16,24},{24,32},{32,40},{40,48},{48,56},{56,64},{64,7... | collective-permute-start | bytes 393224 | tf_op jit(solution)/shard_map/ppermute | solution.py:15
  115.3 3.5 %fusion.14 = f32[512,2,128]{0,2,1:T(8,128)} fusion(bf16[1024,2,128]{0,2,1:T(8,128)(2,1)S(1)} %bitcast.104, bf16[512,2,128]{0,2,1:T(8,128)(2,1)} %bitcast.108, pred[512,1024]{1,0:T(8,128)(4,1)} %fusion.2, f32[1024,2,128]{0,2,1:T(8,128)S(1)} %bitcast.101), kind=kOutput, calls=%fused_computation.23 | convolution fusion | flops 540278784 | bytes 2883584 | tf_op jit(solution)/shard_map/hbs,she->bhe/dot_general | solution.py:126
  120.3 4.5 %collective-permute-start.18 = (f32[2,128,128]{2,1,0:T(8,128)S(1)}, f32[2,128,128]{2,1,0:T(8,128)S(1)}, u32[]{:S(2)}, u32[]{:S(2)}) collective-permute-start(f32[2,128,128]{2,1,0:T(8,128)S(1)} %select_add_fusion), channel_id=1, source_target_pairs={{0,96},{8,104},{16,112},{24,120},{32,128},{40,136},{48,144},{56,15... | collective-permute-start | bytes 393224 | tf_op jit(solution)/shard_map/ppermute | solution.py:15
  124.8 5.0 %collective-permute-start.17 = (f32[2,128,128]{2,1,0:T(8,128)S(1)}, f32[2,128,128]{2,1,0:T(8,128)S(1)}, u32[]{:S(2)}, u32[]{:S(2)}) collective-permute-start(f32[2,128,128]{2,1,0:T(8,128)S(1)} %select_add_fusion), channel_id=1, source_target_pairs={{0,64},{8,72},{16,80},{24,88},{32,96},{40,104},{48,112},{56,120},{... | collective-permute-start | bytes 393224 | tf_op jit(solution)/shard_map/ppermute | solution.py:15
  129.8 1.9 %collective-permute-start.16 = (f32[2,128,128]{2,1,0:T(8,128)S(1)}, f32[2,128,128]{2,1,0:T(8,128)S(1)}, u32[]{:S(2)}, u32[]{:S(2)}) collective-permute-start(f32[2,128,128]{2,1,0:T(8,128)S(1)} %select_add_fusion), channel_id=1, source_target_pairs={{0,32},{8,40},{16,48},{24,56},{32,64},{40,72},{48,80},{56,88},{64,... | collective-permute-start | bytes 393224 | tf_op jit(solution)/shard_map/ppermute | solution.py:15
  131.8 1.8 %fusion.15 = f32[512,2,128]{0,2,1:T(8,128)S(1)} fusion(bf16[512,2,128]{0,2,1:T(8,128)(2,1)} %bitcast.106, bf16[512,2,128]{0,2,1:T(8,128)(2,1)} %bitcast.107, bf16[512,2,128]{0,2,1:T(8,128)(2,1)S(1)} %bitcast.105, pred[512,512]{1,0:T(8,128)(4,1)S(1)} %fusion.23), kind=kOutput, calls=%fused_computation.24 | convolution fusion | flops 269484032 | bytes 1572864 | tf_op jit(solution)/shard_map/hbs,she->bhe/dot_general | solution.py:126
  133.6 2.0 %collective-permute-done.18 = f32[2,128,128]{2,1,0:T(8,128)S(1)} collective-permute-done((f32[2,128,128]{2,1,0:T(8,128)S(1)}, f32[2,128,128]{2,1,0:T(8,128)S(1)}, u32[]{:S(2)}, u32[]{:S(2)}) %collective-permute-start.18) | collective-permute-done | bytes 131104 | tf_op jit(solution)/shard_map/ppermute | solution.py:15
  135.6 5.3 %collective-permute-done.16 = f32[2,128,128]{2,1,0:T(8,128)S(1)} collective-permute-done((f32[2,128,128]{2,1,0:T(8,128)S(1)}, f32[2,128,128]{2,1,0:T(8,128)S(1)}, u32[]{:S(2)}, u32[]{:S(2)}) %collective-permute-start.16) | collective-permute-done | bytes 131104 | tf_op jit(solution)/shard_map/ppermute | solution.py:15
  (81 shorter events, 24.8 us)
Async XLA Ops:
  6.5 86.8 %all-gather.2.cloned.1.call-start = ((), (), s32[]{:S(2)}) async-start(), calls=%async_computation | async-start | bytes 4718592 | tf_op jit(solution)/shard_map/all_gather | solution.py:85
  9.3 3.1 %collective-permute-start = (bf16[3,33,256]{2,1,0:T(8,128)(2,1)S(1)}, bf16[3,33,256]{2,1,0:T(8,128)(2,1)S(1)}, u32[]{:S(2)}, u32[]{:S(2)}) collective-permute-start(bf16[3,33,256]{2,1,0:T(8,128)(2,1)S(1)} %concatenate.31), channel_id=1, source_target_pairs={{0,8},{8,0},{1,9},{9,1},{2,10},{10,2},{3,11},{11,3},{4,12},{12,4},... | collective-permute-start | bytes 152072 | tf_op jit(solution)/shard_map/ppermute | solution.py:40
  13.9 7.3 %collective-permute-start.1 = (bf16[3,66,128]{2,1,0:T(8,128)(2,1)S(1)}, bf16[3,66,128]{2,1,0:T(8,128)(2,1)S(1)}, u32[]{:S(2)}, u32[]{:S(2)}) collective-permute-start(bf16[3,66,128]{2,1,0:T(8,128)(2,1)S(1)} %pad_maximum_fusion), channel_id=1, source_target_pairs={{0,16},{16,32},{32,48},{48,0},{1,17},{17,33},{33,49},{49,1},{2,18}... | collective-permute-start | bytes 152072 | tf_op jit(solution)/shard_map/ppermute | solution.py:23
  21.2 7.2 %collective-permute-start.2 = (bf16[3,66,128]{2,1,0:T(8,128)(2,1)S(1)}, bf16[3,66,128]{2,1,0:T(8,128)(2,1)S(1)}, u32[]{:S(2)}, u32[]{:S(2)}) collective-permute-start(bf16[3,66,128]{2,1,0:T(8,128)(2,1)S(1)} %collective-permute-done.1), channel_id=1, source_target_pairs={{0,16},{16,32},{32,48},{48,0},{1,17},{17,33},{33,49},{49,1},{2,18}... | collective-permute-start | bytes 152072 | tf_op jit(solution)/shard_map/ppermute | solution.py:23
  23.4 6.7 %collective-permute-start.3 = (bf16[3,66,128]{2,1,0:T(8,128)(2,1)S(1)}, bf16[3,66,128]{2,1,0:T(8,128)(2,1)S(1)}, u32[]{:S(2)}, u32[]{:S(2)}) collective-permute-start(bf16[3,66,128]{2,1,0:T(8,128)(2,1)S(1)} %pad_maximum_fusion), channel_id=1, source_target_pairs={{0,48},{16,0},{32,16},{48,32},{1,49},{17,1},{33,17},{49,33},{2,50}... | collective-permute-start | bytes 152072 | tf_op jit(solution)/shard_map/ppermute | solution.py:26
  30.3 8.8 %collective-permute-start.4 = (bf16[3,264,128]{2,1,0:T(8,128)(2,1)S(1)}, bf16[3,264,128]{2,1,0:T(8,128)(2,1)S(1)}, u32[]{:S(2)}, u32[]{:S(2)}) collective-permute-start(bf16[3,264,128]{2,1,0:T(8,128)(2,1)S(1)} %reshape.151), channel_id=1, source_target_pairs={{0,64},{64,128},{128,192},{192,256},{256,320},{320,384},{384,448},... | collective-permute-start | bytes 608264 | tf_op jit(solution)/shard_map/ppermute | solution.py:23
  39.1 8.8 %collective-permute-start.5 = (bf16[3,264,128]{2,1,0:T(8,128)(2,1)S(1)}, bf16[3,264,128]{2,1,0:T(8,128)(2,1)S(1)}, u32[]{:S(2)}, u32[]{:S(2)}) collective-permute-start(bf16[3,264,128]{2,1,0:T(8,128)(2,1)S(1)} %collective-permute-done.4), channel_id=1, source_target_pairs={{0,64},{64,128},{128,192},{192,256},{256,320},{320,384},{384,448},... | collective-permute-start | bytes 608264 | tf_op jit(solution)/shard_map/ppermute | solution.py:23
  41.1 8.8 %collective-permute-start.8 = (bf16[3,264,128]{2,1,0:T(8,128)(2,1)S(1)}, bf16[3,264,128]{2,1,0:T(8,128)(2,1)S(1)}, u32[]{:S(2)}, u32[]{:S(2)}) collective-permute-start(bf16[3,264,128]{2,1,0:T(8,128)(2,1)S(1)} %reshape.151), channel_id=1, source_target_pairs={{0,448},{64,0},{128,64},{192,128},{256,192},{320,256},{384,320},{4... | collective-permute-start | bytes 608264 | tf_op jit(solution)/shard_map/ppermute | solution.py:26
  48.0 8.8 %collective-permute-start.6 = (bf16[3,264,128]{2,1,0:T(8,128)(2,1)S(1)}, bf16[3,264,128]{2,1,0:T(8,128)(2,1)S(1)}, u32[]{:S(2)}, u32[]{:S(2)}) collective-permute-start(bf16[3,264,128]{2,1,0:T(8,128)(2,1)S(1)} %collective-permute-done.5), channel_id=1, source_target_pairs={{0,64},{64,128},{128,192},{192,256},{256,320},{320,384},{384,448},... | collective-permute-start | bytes 608264 | tf_op jit(solution)/shard_map/ppermute | solution.py:23
  49.9 8.9 %collective-permute-start.9 = (bf16[3,264,128]{2,1,0:T(8,128)(2,1)S(1)}, bf16[3,264,128]{2,1,0:T(8,128)(2,1)S(1)}, u32[]{:S(2)}, u32[]{:S(2)}) collective-permute-start(bf16[3,264,128]{2,1,0:T(8,128)(2,1)S(1)} %collective-permute-done.8), channel_id=1, source_target_pairs={{0,448},{64,0},{128,64},{192,128},{256,192},{320,256},{384,320},{4... | collective-permute-start | bytes 608264 | tf_op jit(solution)/shard_map/ppermute | solution.py:26
  56.8 8.8 %collective-permute-start.7 = (bf16[3,264,128]{2,1,0:T(8,128)(2,1)S(1)}, bf16[3,264,128]{2,1,0:T(8,128)(2,1)S(1)}, u32[]{:S(2)}, u32[]{:S(2)}) collective-permute-start(bf16[3,264,128]{2,1,0:T(8,128)(2,1)S(1)} %collective-permute-done.6), channel_id=1, source_target_pairs={{0,64},{64,128},{128,192},{192,256},{256,320},{320,384},{384,448},... | collective-permute-start | bytes 608264 | tf_op jit(solution)/shard_map/ppermute | solution.py:23
  58.8 8.4 %collective-permute-start.10 = (bf16[3,264,128]{2,1,0:T(8,128)(2,1)S(1)}, bf16[3,264,128]{2,1,0:T(8,128)(2,1)S(1)}, u32[]{:S(2)}, u32[]{:S(2)}) collective-permute-start(bf16[3,264,128]{2,1,0:T(8,128)(2,1)S(1)} %collective-permute-done.9), channel_id=1, source_target_pairs={{0,448},{64,0},{128,64},{192,128},{256,192},{320,256},{384,320},{4... | collective-permute-start | bytes 608264 | tf_op jit(solution)/shard_map/ppermute | solution.py:26
  69.0 6.5 %collective-permute-start.11 = (bf16[3,2112,128]{2,1,0:T(8,128)(2,1)}, bf16[3,2112,128]{2,1,0:T(8,128)(2,1)}, u32[]{:S(2)}, u32[]{:S(2)}) collective-permute-start(bf16[3,2112,128]{2,1,0:T(8,128)(2,1)} %bitcast.14), channel_id=1, source_target_pairs={{0,8},{8,0},{1,9},{9,1},{2,10},{10,2},{3,11},{11,3},{4,12},{12,4},... | collective-permute-start | bytes 4866056 | tf_op jit(solution)/shard_map/ppermute | solution.py:46
  82.1 6.4 %copy-start.2 = (s32[1024]{0:T(1024)S(1)}, s32[1024]{0:T(1024)}, u32[]{:S(2)}) copy-start(s32[1024]{0:T(1024)} %param.7) | copy-start | bytes 12292
  97.9 14.9 %copy-start = (bf16[1,64,32,256]{3,2,1,0:T(8,128)(2,1)S(1)}, bf16[1,64,32,256]{3,2,1,0:T(8,128)(2,1)}, u32[]{:S(2)}) copy-start(bf16[1,64,32,256]{3,2,1,0:T(8,128)(2,1)} %slice.99) | copy-start | bytes 3145732
  97.9 14.9 %copy-start.4 = (bf16[1024,2048]{1,0:T(8,128)(2,1)S(1)}, bf16[1024,2048]{1,0:T(8,128)(2,1)}, u32[]{:S(2)}) copy-start(bf16[1024,2048]{1,0:T(8,128)(2,1)} %all-gather.2.cloned.1.call-done) | copy-start | bytes 12582916
  99.4 19.7 %collective-permute-start.15 = (f32[2,128,128]{2,1,0:T(8,128)}, f32[2,128,128]{2,1,0:T(8,128)S(1)}, u32[]{:S(2)}, u32[]{:S(2)}) collective-permute-start(f32[2,128,128]{2,1,0:T(8,128)} %fusion.28), channel_id=1, source_target_pairs={{0,32},{8,40},{16,48},{24,56},{32,64},{40,72},{48,80},{56,88},{64,... | collective-permute-start | bytes 393224 | tf_op jit(solution)/shard_map/ppermute | solution.py:15
  104.4 14.7 %collective-permute-start.14 = (f32[2,128,128]{2,1,0:T(8,128)}, f32[2,128,128]{2,1,0:T(8,128)}, u32[]{:S(2)}, u32[]{:S(2)}) collective-permute-start(f32[2,128,128]{2,1,0:T(8,128)} %fusion.28), channel_id=1, source_target_pairs={{0,24},{8,32},{16,40},{24,48},{32,56},{40,64},{48,72},{56,80},{64,... | collective-permute-start | bytes 393224 | tf_op jit(solution)/shard_map/ppermute | solution.py:15
  106.4 12.8 %collective-permute-start.13 = (f32[2,128,128]{2,1,0:T(8,128)}, f32[2,128,128]{2,1,0:T(8,128)}, u32[]{:S(2)}, u32[]{:S(2)}) collective-permute-start(f32[2,128,128]{2,1,0:T(8,128)} %fusion.28), channel_id=1, source_target_pairs={{0,16},{8,24},{16,32},{24,40},{32,48},{40,56},{48,64},{56,72},{64,... | collective-permute-start | bytes 393224 | tf_op jit(solution)/shard_map/ppermute | solution.py:15
  108.8 10.5 %collective-permute-start.12 = (f32[2,128,128]{2,1,0:T(8,128)}, f32[2,128,128]{2,1,0:T(8,128)}, u32[]{:S(2)}, u32[]{:S(2)}) collective-permute-start(f32[2,128,128]{2,1,0:T(8,128)} %fusion.28), channel_id=1, source_target_pairs={{0,8},{8,16},{16,24},{24,32},{32,40},{40,48},{48,56},{56,64},{64,7... | collective-permute-start | bytes 393224 | tf_op jit(solution)/shard_map/ppermute | solution.py:15
  118.9 22.1 %copy-start.1 = (f32[512,2,128]{0,2,1:T(8,128)S(1)}, f32[512,2,128]{0,2,1:T(8,128)}, u32[]{:S(2)}) copy-start(f32[512,2,128]{0,2,1:T(8,128)} %fusion.14) | copy-start | bytes 1572868
  119.1 22.2 %copy-start.3 = (f32[256]{0:T(256)S(1)}, f32[256]{0:T(256)}, u32[]{:S(2)}) copy-start(f32[256]{0:T(256)} %param.6) | copy-start | bytes 3076
  120.3 15.3 %collective-permute-start.18 = (f32[2,128,128]{2,1,0:T(8,128)S(1)}, f32[2,128,128]{2,1,0:T(8,128)S(1)}, u32[]{:S(2)}, u32[]{:S(2)}) collective-permute-start(f32[2,128,128]{2,1,0:T(8,128)S(1)} %select_add_fusion), channel_id=1, source_target_pairs={{0,96},{8,104},{16,112},{24,120},{32,128},{40,136},{48,144},{56,15... | collective-permute-start | bytes 393224 | tf_op jit(solution)/shard_map/ppermute | solution.py:15
  124.8 10.8 %collective-permute-start.17 = (f32[2,128,128]{2,1,0:T(8,128)S(1)}, f32[2,128,128]{2,1,0:T(8,128)S(1)}, u32[]{:S(2)}, u32[]{:S(2)}) collective-permute-start(f32[2,128,128]{2,1,0:T(8,128)S(1)} %select_add_fusion), channel_id=1, source_target_pairs={{0,64},{8,72},{16,80},{24,88},{32,96},{40,104},{48,112},{56,120},{... | collective-permute-start | bytes 393224 | tf_op jit(solution)/shard_map/ppermute | solution.py:15
  129.8 11.1 %collective-permute-start.16 = (f32[2,128,128]{2,1,0:T(8,128)S(1)}, f32[2,128,128]{2,1,0:T(8,128)S(1)}, u32[]{:S(2)}, u32[]{:S(2)}) collective-permute-start(f32[2,128,128]{2,1,0:T(8,128)S(1)} %select_add_fusion), channel_id=1, source_target_pairs={{0,32},{8,40},{16,48},{24,56},{32,64},{40,72},{48,80},{56,88},{64,... | collective-permute-start | bytes 393224 | tf_op jit(solution)/shard_map/ppermute | solution.py:15
Sparse Core Ops, SparseCore 0:
  23.5 69.7 all-gather.1

commit v9 on v8

--- a/solution.py
+++ b/solution.py
@@ -82,7 +82,10 @@
 
 
 def per_device(tokens, w_qkv, out_gain, seg_ids):
-    whole = lax.all_gather(tokens, "head", axis=1, tiled=True)
+    half_rows = tokens.shape[0] // 2
+    whole = jnp.concatenate([
+        lax.all_gather(tokens[:half_rows], "head", axis=1, tiled=True),
+        lax.all_gather(tokens[half_rows:], "head", axis=1, tiled=True)], axis=0)
     row_count = seg_ids.shape[0]
     groups = lax.axis_size(CTX)
     own_rows = w_qkv.shape[1]

time: 150 us -> 177 us (1.18)
  the two profiles are of different devices: /device:TPU:32 before, /device:TPU:8 now
where the time goes in v9:
time: 177 us; the launch traced here: 176 us
  starting transfers between devices  65.6 us (37%)
  waiting for transfers between devices  45.8 us (26%)
  local copies, waits for them, and re-layouts  23.8 us (13%)
  between operations  18.7 us (11%)
  matrix products  13.1 us (7%)
  other arithmetic  8.87 us (5%)
    ppermute x7, starting transfers between devices, shifted(): lax.ppermute(value, axis, [(source, source + steps) for source in range(c...  26.7 us
    ppermute x4, starting transfers between devices, ring_gather(): lax.ppermute(behind, axis, [(j, (j - 1) % count) for j in range(count)])  20.3 us
    all_gather x1, waiting for transfers between devices, per_device(): lax.all_gather(tokens[half_rows:], 'head', axis=1, tiled=True)  19.8 us
    ppermute x6, waiting for transfers between devices, ring_gather(): lax.ppermute(ahead, axis, [(j, (j + 1) % count) for j in range(count)])  17.1 us
    ppermute x6, starting transfers between devices, ring_gather(): lax.ppermute(ahead, axis, [(j, (j + 1) % count) for j in range(count)])  14.8 us
    concatenate x2, local copies, waits for them, and re-layouts, gather_weights(): jnp.concatenate([rows, other], axis=2)  6.14 us
    dot_general x2, matrix products, per_device(): jnp.einsum('hbs,she->bhe', weights, values[:key_end], preferred_element_t...  5.29 us
    ppermute x7, waiting for transfers between devices, shifted(): lax.ppermute(value, axis, [(source, source + steps) for source in range(c...  4.7 us
  transfers between devices with their start and end apart: 21, of which 11 were waited for; matrix products, arithmetic and copies ran while one was open for 18% of the time, Pallas kernels for 0%

profile of v9, /device:TPU:8, one launch (start us, length us, event | category | flops | bytes accessed | tf_op | source)
XLA Modules:
  0.0 176.0 jit_solution(11929531912929093189)
XLA Ops:
  6.5 1.9 %fusion.44 = (bf16[512,256]{1,0:T(8,128)(2,1)}, bf16[512,256]{1,0:T(8,128)(2,1)}) fusion(bf16[1024,256]{1,0:T(8,128)(2,1)} %param.4), kind=kLoop, calls=%fused_computation.98 | loop fusion | bytes 1048576 | tf_op jit(solution)/shard_map/slice | solution.py:88
  11.3 1.9 %collective-permute-start = (bf16[3,33,256]{2,1,0:T(8,128)(2,1)S(1)}, bf16[3,33,256]{2,1,0:T(8,128)(2,1)S(1)}, u32[]{:S(2)}, u32[]{:S(2)}) collective-permute-start(bf16[3,33,256]{2,1,0:T(8,128)(2,1)S(1)} %concatenate.34), channel_id=1, source_target_pairs={{0,8},{8,0},{1,9},{9,1},{2,10},{10,2},{3,11},{11,3},{4,12},{12,4},... | collective-permute-start | bytes 152072 | tf_op jit(solution)/shard_map/ppermute | solution.py:40
  15.9 3.4 %collective-permute-start.1 = (bf16[3,66,128]{2,1,0:T(8,128)(2,1)S(1)}, bf16[3,66,128]{2,1,0:T(8,128)(2,1)S(1)}, u32[]{:S(2)}, u32[]{:S(2)}) collective-permute-start(bf16[3,66,128]{2,1,0:T(8,128)(2,1)S(1)} %pad_maximum_fusion), channel_id=1, source_target_pairs={{0,16},{16,32},{32,48},{48,0},{1,17},{17,33},{33,49},{49,1},{2,18}... | collective-permute-start | bytes 152072 | tf_op jit(solution)/shard_map/ppermute | solution.py:23
  19.3 3.9 %collective-permute-done.1 = bf16[3,66,128]{2,1,0:T(8,128)(2,1)S(1)} collective-permute-done((bf16[3,66,128]{2,1,0:T(8,128)(2,1)S(1)}, bf16[3,66,128]{2,1,0:T(8,128)(2,1)S(1)}, u32[]{:S(2)}, u32[]{:S(2)}) %collective-permute-start.1) | collective-permute-done | bytes 50720 | tf_op jit(solution)/shard_map/ppermute | solution.py:23
  23.1 2.2 %collective-permute-start.2 = (bf16[3,66,128]{2,1,0:T(8,128)(2,1)S(1)}, bf16[3,66,128]{2,1,0:T(8,128)(2,1)S(1)}, u32[]{:S(2)}, u32[]{:S(2)}) collective-permute-start(bf16[3,66,128]{2,1,0:T(8,128)(2,1)S(1)} %collective-permute-done.1), channel_id=1, source_target_pairs={{0,16},{16,32},{32,48},{48,0},{1,17},{17,33},{33,49},{49,1},{2,18}... | collective-permute-start | bytes 152072 | tf_op jit(solution)/shard_map/ppermute | solution.py:23
  25.3 4.9 %collective-permute-start.3 = (bf16[3,66,128]{2,1,0:T(8,128)(2,1)S(1)}, bf16[3,66,128]{2,1,0:T(8,128)(2,1)S(1)}, u32[]{:S(2)}, u32[]{:S(2)}) collective-permute-start(bf16[3,66,128]{2,1,0:T(8,128)(2,1)S(1)} %pad_maximum_fusion), channel_id=1, source_target_pairs={{0,48},{16,0},{32,16},{48,32},{1,49},{17,1},{33,17},{49,33},{2,50}... | collective-permute-start | bytes 152072 | tf_op jit(solution)/shard_map/ppermute | solution.py:26
  32.2 3.5 %collective-permute-start.4 = (bf16[3,264,128]{2,1,0:T(8,128)(2,1)S(1)}, bf16[3,264,128]{2,1,0:T(8,128)(2,1)S(1)}, u32[]{:S(2)}, u32[]{:S(2)}) collective-permute-start(bf16[3,264,128]{2,1,0:T(8,128)(2,1)S(1)} %reshape.151), channel_id=1, source_target_pairs={{0,64},{64,128},{128,192},{192,256},{256,320},{320,384},{384,448},... | collective-permute-start | bytes 608264 | tf_op jit(solution)/shard_map/ppermute | solution.py:23
  35.7 7.9 %collective-permute-done.4 = bf16[3,264,128]{2,1,0:T(8,128)(2,1)S(1)} collective-permute-done((bf16[3,264,128]{2,1,0:T(8,128)(2,1)S(1)}, bf16[3,264,128]{2,1,0:T(8,128)(2,1)S(1)}, u32[]{:S(2)}, u32[]{:S(2)}) %collective-permute-start.4) | collective-permute-done | bytes 202784 | tf_op jit(solution)/shard_map/ppermute | solution.py:23
  43.7 1.9 %collective-permute-start.5 = (bf16[3,264,128]{2,1,0:T(8,128)(2,1)S(1)}, bf16[3,264,128]{2,1,0:T(8,128)(2,1)S(1)}, u32[]{:S(2)}, u32[]{:S(2)}) collective-permute-start(bf16[3,264,128]{2,1,0:T(8,128)(2,1)S(1)} %collective-permute-done.4), channel_id=1, source_target_pairs={{0,64},{64,128},{128,192},{192,256},{256,320},{320,384},{384,448},... | collective-permute-start | bytes 608264 | tf_op jit(solution)/shard_map/ppermute | solution.py:23
  45.6 5.1 %collective-permute-start.8 = (bf16[3,264,128]{2,1,0:T(8,128)(2,1)S(1)}, bf16[3,264,128]{2,1,0:T(8,128)(2,1)S(1)}, u32[]{:S(2)}, u32[]{:S(2)}) collective-permute-start(bf16[3,264,128]{2,1,0:T(8,128)(2,1)S(1)} %reshape.151), channel_id=1, source_target_pairs={{0,448},{64,0},{128,64},{192,128},{256,192},{320,256},{384,320},{4... | collective-permute-start | bytes 608264 | tf_op jit(solution)/shard_map/ppermute | solution.py:26
  52.5 1.9 %collective-permute-start.6 = (bf16[3,264,128]{2,1,0:T(8,128)(2,1)S(1)}, bf16[3,264,128]{2,1,0:T(8,128)(2,1)S(1)}, u32[]{:S(2)}, u32[]{:S(2)}) collective-permute-start(bf16[3,264,128]{2,1,0:T(8,128)(2,1)S(1)} %collective-permute-done.5), channel_id=1, source_target_pairs={{0,64},{64,128},{128,192},{192,256},{256,320},{320,384},{384,448},... | collective-permute-start | bytes 608264 | tf_op jit(solution)/shard_map/ppermute | solution.py:23
  54.4 5.1 %collective-permute-start.9 = (bf16[3,264,128]{2,1,0:T(8,128)(2,1)S(1)}, bf16[3,264,128]{2,1,0:T(8,128)(2,1)S(1)}, u32[]{:S(2)}, u32[]{:S(2)}) collective-permute-start(bf16[3,264,128]{2,1,0:T(8,128)(2,1)S(1)} %collective-permute-done.8), channel_id=1, source_target_pairs={{0,448},{64,0},{128,64},{192,128},{256,192},{320,256},{384,320},{4... | collective-permute-start | bytes 608264 | tf_op jit(solution)/shard_map/ppermute | solution.py:26
  61.3 1.9 %collective-permute-start.7 = (bf16[3,264,128]{2,1,0:T(8,128)(2,1)S(1)}, bf16[3,264,128]{2,1,0:T(8,128)(2,1)S(1)}, u32[]{:S(2)}, u32[]{:S(2)}) collective-permute-start(bf16[3,264,128]{2,1,0:T(8,128)(2,1)S(1)} %collective-permute-done.6), channel_id=1, source_target_pairs={{0,64},{64,128},{128,192},{192,256},{256,320},{320,384},{384,448},... | collective-permute-start | bytes 608264 | tf_op jit(solution)/shard_map/ppermute | solution.py:23
  63.4 5.1 %collective-permute-start.10 = (bf16[3,264,128]{2,1,0:T(8,128)(2,1)S(1)}, bf16[3,264,128]{2,1,0:T(8,128)(2,1)S(1)}, u32[]{:S(2)}, u32[]{:S(2)}) collective-permute-start(bf16[3,264,128]{2,1,0:T(8,128)(2,1)S(1)} %collective-permute-done.9), channel_id=1, source_target_pairs={{0,448},{64,0},{128,64},{192,128},{256,192},{320,256},{384,320},{4... | collective-permute-start | bytes 608264 | tf_op jit(solution)/shard_map/ppermute | solution.py:26
  73.5 1.9 %collective-permute-start.11 = (bf16[3,2112,128]{2,1,0:T(8,128)(2,1)}, bf16[3,2112,128]{2,1,0:T(8,128)(2,1)}, u32[]{:S(2)}, u32[]{:S(2)}) collective-permute-start(bf16[3,2112,128]{2,1,0:T(8,128)(2,1)} %bitcast.14), channel_id=1, source_target_pairs={{0,8},{8,0},{1,9},{9,1},{2,10},{10,2},{3,11},{11,3},{4,12},{12,4},... | collective-permute-start | bytes 4866056 | tf_op jit(solution)/shard_map/ppermute | solution.py:46
  77.6 2.5 %concatenate.38 = bf16[3,64,33,128]{3,2,1,0:T(8,128)(2,1)S(1)} reshape(bf16[3,8,264,128]{3,2,1,0:T(8,128)(2,1)} %copy.23) | data formatting | bytes 3244032 | tf_op jit(solution)/shard_map/concatenate | solution.py:49
  80.1 3.7 %concatenate.39 = bf16[3,64,33,128]{3,2,1,0:T(8,128)(2,1)} reshape(bf16[3,2112,128]{2,1,0:T(8,128)(2,1)} %collective-permute-done.11) | data formatting | bytes 3244032 | tf_op jit(solution)/shard_map/concatenate | solution.py:49
  83.8 2.8 %maximum_select_fusion = bf16[3,64,33,256]{3,2,1,0:T(8,128)(2,1)S(1)} fusion(bf16[3,64,33,128]{3,2,1,0:T(8,128)(2,1)} %concatenate.39, bf16[3,64,33,128]{3,2,1,0:T(8,128)(2,1)S(1)} %concatenate.38, pred[]{:T(512)S(6)} %eq.77), kind=kLoop, calls=%fused_computation.3 | loop fusion | flops 14598144 | bytes 6488065 | tf_op jit(solution)/shard_map/jit(_where)/select_n | solution.py:47
  94.0 3.2 %constant_dynamic-update-slice_fusion.11 = bf16[1024,2048]{1,0:T(8,128)(2,1)} fusion(bf16[512,2048]{1,0:T(8,128)(2,1)} %all-gather.3.cloned.1.call-done), kind=kLoop, calls=%fused_computation.78 | loop fusion | bytes 4194304
  97.2 19.8 %all-gather.5.cloned.1.call-done = bf16[512,2048]{1,0:T(8,128)(2,1)} async-done(((bf16[512,256]{1,0:T(8,128)(2,1)}), bf16[512,2048]{1,0:T(8,128)(2,1)}) %all-gather.5.cloned.1.call-update) | async-done | bytes 2097168 | tf_op jit(solution)/shard_map/all_gather | solution.py:88
  117.0 3.2 %constant_dynamic-update-slice_fusion.10 = bf16[1024,2048]{1,0:T(8,128)(2,1)} fusion(bf16[1024,2048]{1,0:T(8,128)(2,1)} %constant_dynamic-update-slice_fusion.11, bf16[512,2048]{1,0:T(8,128)(2,1)} %all-gather.5.cloned.1.call-done), kind=kLoop, calls=%fused_computation.77 | loop fusion | bytes 4194304 | tf_op jit(solution)/shard_map/concatenate | solution.py:86
  120.1 4.6 %fusion.7 = bf16[2,1024,256]{1,2,0:T(8,128)(2,1)S(1)} fusion(bf16[2,2048,256]{2,1,0:T(8,128)(2,1)S(1)} %bitcast.89, bf16[1024,2048]{1,0:T(8,128)(2,1)} %constant_dynamic-update-slice_fusion.10), kind=kOutput, calls=%fused_computation.16 | convolution fusion | flops 2148007936 | bytes 7340032 | tf_op jit(solution)/shard_map/tr,grc->gtc/dot_general | solution.py:97
  126.2 5.0 %collective-permute-start.15 = (f32[2,128,128]{2,1,0:T(8,128)}, f32[2,128,128]{2,1,0:T(8,128)S(1)}, u32[]{:S(2)}, u32[]{:S(2)}) collective-permute-start(f32[2,128,128]{2,1,0:T(8,128)} %fusion.27), channel_id=1, source_target_pairs={{0,32},{8,40},{16,48},{24,56},{32,64},{40,72},{48,80},{56,88},{64,... | collective-permute-start | bytes 393224 | tf_op jit(solution)/shard_map/ppermute | solution.py:15
  131.2 1.9 %collective-permute-start.14 = (f32[2,128,128]{2,1,0:T(8,128)}, f32[2,128,128]{2,1,0:T(8,128)}, u32[]{:S(2)}, u32[]{:S(2)}) collective-permute-start(f32[2,128,128]{2,1,0:T(8,128)} %fusion.27), channel_id=1, source_target_pairs={{0,24},{8,32},{16,40},{24,48},{32,56},{40,64},{48,72},{56,80},{64,... | collective-permute-start | bytes 393224 | tf_op jit(solution)/shard_map/ppermute | solution.py:15
  133.2 2.5 %collective-permute-start.13 = (f32[2,128,128]{2,1,0:T(8,128)}, f32[2,128,128]{2,1,0:T(8,128)}, u32[]{:S(2)}, u32[]{:S(2)}) collective-permute-start(f32[2,128,128]{2,1,0:T(8,128)} %fusion.27), channel_id=1, source_target_pairs={{0,16},{8,24},{16,32},{24,40},{32,48},{40,56},{48,64},{56,72},{64,... | collective-permute-start | bytes 393224 | tf_op jit(solution)/shard_map/ppermute | solution.py:15
  135.6 4.3 %collective-permute-start.12 = (f32[2,128,128]{2,1,0:T(8,128)}, f32[2,128,128]{2,1,0:T(8,128)}, u32[]{:S(2)}, u32[]{:S(2)}) collective-permute-start(f32[2,128,128]{2,1,0:T(8,128)} %fusion.27), channel_id=1, source_target_pairs={{0,8},{8,16},{16,24},{24,32},{32,40},{40,48},{48,56},{56,64},{64,7... | collective-permute-start | bytes 393224 | tf_op jit(solution)/shard_map/ppermute | solution.py:15
  143.2 3.5 %fusion.13 = f32[512,2,128]{0,2,1:T(8,128)} fusion(bf16[1024,2,128]{0,2,1:T(8,128)(2,1)S(1)} %bitcast.96, bf16[512,2,128]{0,2,1:T(8,128)(2,1)} %bitcast.100, pred[512,1024]{1,0:T(8,128)(4,1)} %fusion.2, f32[1024,2,128]{0,2,1:T(8,128)S(1)} %bitcast.93), kind=kOutput, calls=%fused_computation.22 | convolution fusion | flops 540278784 | bytes 2883584 | tf_op jit(solution)/shard_map/hbs,she->bhe/dot_general | solution.py:129
  148.0 5.5 %collective-permute-start.18 = (f32[2,128,128]{2,1,0:T(8,128)S(1)}, f32[2,128,128]{2,1,0:T(8,128)S(1)}, u32[]{:S(2)}, u32[]{:S(2)}) collective-permute-start(f32[2,128,128]{2,1,0:T(8,128)S(1)} %select_add_fusion), channel_id=1, source_target_pairs={{0,96},{8,104},{16,112},{24,120},{32,128},{40,136},{48,144},{56,15... | collective-permute-start | bytes 393224 | tf_op jit(solution)/shard_map/ppermute | solution.py:15
  153.5 4.7 %collective-permute-start.17 = (f32[2,128,128]{2,1,0:T(8,128)S(1)}, f32[2,128,128]{2,1,0:T(8,128)S(1)}, u32[]{:S(2)}, u32[]{:S(2)}) collective-permute-start(f32[2,128,128]{2,1,0:T(8,128)S(1)} %select_add_fusion), channel_id=1, source_target_pairs={{0,64},{8,72},{16,80},{24,88},{32,96},{40,104},{48,112},{56,120},{... | collective-permute-start | bytes 393224 | tf_op jit(solution)/shard_map/ppermute | solution.py:15
  158.1 2.9 %collective-permute-start.16 = (f32[2,128,128]{2,1,0:T(8,128)S(1)}, f32[2,128,128]{2,1,0:T(8,128)S(1)}, u32[]{:S(2)}, u32[]{:S(2)}) collective-permute-start(f32[2,128,128]{2,1,0:T(8,128)S(1)} %select_add_fusion), channel_id=1, source_target_pairs={{0,32},{8,40},{16,48},{24,56},{32,64},{40,72},{48,80},{56,88},{64,... | collective-permute-start | bytes 393224 | tf_op jit(solution)/shard_map/ppermute | solution.py:15
  161.1 1.8 %fusion.14 = f32[512,2,128]{0,2,1:T(8,128)S(1)} fusion(bf16[512,2,128]{0,2,1:T(8,128)(2,1)} %bitcast.98, bf16[512,2,128]{0,2,1:T(8,128)(2,1)} %bitcast.99, bf16[512,2,128]{0,2,1:T(8,128)(2,1)S(1)} %bitcast.97, pred[512,512]{1,0:T(8,128)(4,1)S(1)} %fusion.22), kind=kOutput, calls=%fused_computation.23 | convolution fusion | flops 269484032 | bytes 1572864 | tf_op jit(solution)/shard_map/hbs,she->bhe/dot_general | solution.py:129
  162.9 4.7 %collective-permute-done.16 = f32[2,128,128]{2,1,0:T(8,128)S(1)} collective-permute-done((f32[2,128,128]{2,1,0:T(8,128)S(1)}, f32[2,128,128]{2,1,0:T(8,128)S(1)}, u32[]{:S(2)}, u32[]{:S(2)}) %collective-permute-start.16) | collective-permute-done | bytes 131104 | tf_op jit(solution)/shard_map/ppermute | solution.py:15
  (87 shorter events, 28.3 us)
Async XLA Ops:
  6.5 87.4 %all-gather.3.cloned.1.call-start = ((), (), s32[]{:S(2)}) async-start(), calls=%async_computation | async-start | bytes 2359296 | tf_op jit(solution)/shard_map/all_gather | solution.py:87
  8.4 108.5 %all-gather.5.cloned.1.call-start = ((), (), s32[]{:S(2)}) async-start(), calls=%async_computation.1 | async-start | bytes 2359296 | tf_op jit(solution)/shard_map/all_gather | solution.py:88
  11.3 3.1 %collective-permute-start = (bf16[3,33,256]{2,1,0:T(8,128)(2,1)S(1)}, bf16[3,33,256]{2,1,0:T(8,128)(2,1)S(1)}, u32[]{:S(2)}, u32[]{:S(2)}) collective-permute-start(bf16[3,33,256]{2,1,0:T(8,128)(2,1)S(1)} %concatenate.34), channel_id=1, source_target_pairs={{0,8},{8,0},{1,9},{9,1},{2,10},{10,2},{3,11},{11,3},{4,12},{12,4},... | collective-permute-start | bytes 152072 | tf_op jit(solution)/shard_map/ppermute | solution.py:40
  15.9 7.3 %collective-permute-start.1 = (bf16[3,66,128]{2,1,0:T(8,128)(2,1)S(1)}, bf16[3,66,128]{2,1,0:T(8,128)(2,1)S(1)}, u32[]{:S(2)}, u32[]{:S(2)}) collective-permute-start(bf16[3,66,128]{2,1,0:T(8,128)(2,1)S(1)} %pad_maximum_fusion), channel_id=1, source_target_pairs={{0,16},{16,32},{32,48},{48,0},{1,17},{17,33},{33,49},{49,1},{2,18}... | collective-permute-start | bytes 152072 | tf_op jit(solution)/shard_map/ppermute | solution.py:23
  23.1 7.2 %collective-permute-start.2 = (bf16[3,66,128]{2,1,0:T(8,128)(2,1)S(1)}, bf16[3,66,128]{2,1,0:T(8,128)(2,1)S(1)}, u32[]{:S(2)}, u32[]{:S(2)}) collective-permute-start(bf16[3,66,128]{2,1,0:T(8,128)(2,1)S(1)} %collective-permute-done.1), channel_id=1, source_target_pairs={{0,16},{16,32},{32,48},{48,0},{1,17},{17,33},{33,49},{49,1},{2,18}... | collective-permute-start | bytes 152072 | tf_op jit(solution)/shard_map/ppermute | solution.py:23
  25.3 6.7 %collective-permute-start.3 = (bf16[3,66,128]{2,1,0:T(8,128)(2,1)S(1)}, bf16[3,66,128]{2,1,0:T(8,128)(2,1)S(1)}, u32[]{:S(2)}, u32[]{:S(2)}) collective-permute-start(bf16[3,66,128]{2,1,0:T(8,128)(2,1)S(1)} %pad_maximum_fusion), channel_id=1, source_target_pairs={{0,48},{16,0},{32,16},{48,32},{1,49},{17,1},{33,17},{49,33},{2,50}... | collective-permute-start | bytes 152072 | tf_op jit(solution)/shard_map/ppermute | solution.py:26
  32.2 11.4 %collective-permute-start.4 = (bf16[3,264,128]{2,1,0:T(8,128)(2,1)S(1)}, bf16[3,264,128]{2,1,0:T(8,128)(2,1)S(1)}, u32[]{:S(2)}, u32[]{:S(2)}) collective-permute-start(bf16[3,264,128]{2,1,0:T(8,128)(2,1)S(1)} %reshape.151), channel_id=1, source_target_pairs={{0,64},{64,128},{128,192},{192,256},{256,320},{320,384},{384,448},... | collective-permute-start | bytes 608264 | tf_op jit(solution)/shard_map/ppermute | solution.py:23
  43.7 8.8 %collective-permute-start.5 = (bf16[3,264,128]{2,1,0:T(8,128)(2,1)S(1)}, bf16[3,264,128]{2,1,0:T(8,128)(2,1)S(1)}, u32[]{:S(2)}, u32[]{:S(2)}) collective-permute-start(bf16[3,264,128]{2,1,0:T(8,128)(2,1)S(1)} %collective-permute-done.4), channel_id=1, source_target_pairs={{0,64},{64,128},{128,192},{192,256},{256,320},{320,384},{384,448},... | collective-permute-start | bytes 608264 | tf_op jit(solution)/shard_map/ppermute | solution.py:23
  45.6 8.8 %collective-permute-start.8 = (bf16[3,264,128]{2,1,0:T(8,128)(2,1)S(1)}, bf16[3,264,128]{2,1,0:T(8,128)(2,1)S(1)}, u32[]{:S(2)}, u32[]{:S(2)}) collective-permute-start(bf16[3,264,128]{2,1,0:T(8,128)(2,1)S(1)} %reshape.151), channel_id=1, source_target_pairs={{0,448},{64,0},{128,64},{192,128},{256,192},{320,256},{384,320},{4... | collective-permute-start | bytes 608264 | tf_op jit(solution)/shard_map/ppermute | solution.py:26
  52.5 8.8 %collective-permute-start.6 = (bf16[3,264,128]{2,1,0:T(8,128)(2,1)S(1)}, bf16[3,264,128]{2,1,0:T(8,128)(2,1)S(1)}, u32[]{:S(2)}, u32[]{:S(2)}) collective-permute-start(bf16[3,264,128]{2,1,0:T(8,128)(2,1)S(1)} %collective-permute-done.5), channel_id=1, source_target_pairs={{0,64},{64,128},{128,192},{192,256},{256,320},{320,384},{384,448},... | collective-permute-start | bytes 608264 | tf_op jit(solution)/shard_map/ppermute | solution.py:23
  54.4 8.9 %collective-permute-start.9 = (bf16[3,264,128]{2,1,0:T(8,128)(2,1)S(1)}, bf16[3,264,128]{2,1,0:T(8,128)(2,1)S(1)}, u32[]{:S(2)}, u32[]{:S(2)}) collective-permute-start(bf16[3,264,128]{2,1,0:T(8,128)(2,1)S(1)} %collective-permute-done.8), channel_id=1, source_target_pairs={{0,448},{64,0},{128,64},{192,128},{256,192},{320,256},{384,320},{4... | collective-permute-start | bytes 608264 | tf_op jit(solution)/shard_map/ppermute | solution.py:26
  61.3 8.8 %collective-permute-start.7 = (bf16[3,264,128]{2,1,0:T(8,128)(2,1)S(1)}, bf16[3,264,128]{2,1,0:T(8,128)(2,1)S(1)}, u32[]{:S(2)}, u32[]{:S(2)}) collective-permute-start(bf16[3,264,128]{2,1,0:T(8,128)(2,1)S(1)} %collective-permute-done.6), channel_id=1, source_target_pairs={{0,64},{64,128},{128,192},{192,256},{256,320},{320,384},{384,448},... | collective-permute-start | bytes 608264 | tf_op jit(solution)/shard_map/ppermute | solution.py:23
  63.4 8.4 %collective-permute-start.10 = (bf16[3,264,128]{2,1,0:T(8,128)(2,1)S(1)}, bf16[3,264,128]{2,1,0:T(8,128)(2,1)S(1)}, u32[]{:S(2)}, u32[]{:S(2)}) collective-permute-start(bf16[3,264,128]{2,1,0:T(8,128)(2,1)S(1)} %collective-permute-done.9), channel_id=1, source_target_pairs={{0,448},{64,0},{128,64},{192,128},{256,192},{320,256},{384,320},{4... | collective-permute-start | bytes 608264 | tf_op jit(solution)/shard_map/ppermute | solution.py:26
  73.5 6.5 %collective-permute-start.11 = (bf16[3,2112,128]{2,1,0:T(8,128)(2,1)}, bf16[3,2112,128]{2,1,0:T(8,128)(2,1)}, u32[]{:S(2)}, u32[]{:S(2)}) collective-permute-start(bf16[3,2112,128]{2,1,0:T(8,128)(2,1)} %bitcast.14), channel_id=1, source_target_pairs={{0,8},{8,0},{1,9},{9,1},{2,10},{10,2},{3,11},{11,3},{4,12},{12,4},... | collective-permute-start | bytes 4866056 | tf_op jit(solution)/shard_map/ppermute | solution.py:46
  86.6 6.7 %copy-start.3 = (s32[1024]{0:T(1024)S(1)}, s32[1024]{0:T(1024)}, u32[]{:S(2)}) copy-start(s32[1024]{0:T(1024)} %param.7) | copy-start | bytes 12292
  124.7 16.0 %copy-start = (bf16[1024,2048]{1,0:T(8,128)(2,1)S(1)}, bf16[1024,2048]{1,0:T(8,128)(2,1)}, u32[]{:S(2)}) copy-start(bf16[1024,2048]{1,0:T(8,128)(2,1)} %constant_dynamic-update-slice_fusion.10) | copy-start | bytes 12582916
  124.7 15.9 %copy-start.1 = (bf16[1,64,32,256]{3,2,1,0:T(8,128)(2,1)S(1)}, bf16[1,64,32,256]{3,2,1,0:T(8,128)(2,1)}, u32[]{:S(2)}) copy-start(bf16[1,64,32,256]{3,2,1,0:T(8,128)(2,1)} %slice.107) | copy-start | bytes 3145732
  126.2 20.7 %collective-permute-start.15 = (f32[2,128,128]{2,1,0:T(8,128)}, f32[2,128,128]{2,1,0:T(8,128)S(1)}, u32[]{:S(2)}, u32[]{:S(2)}) collective-permute-start(f32[2,128,128]{2,1,0:T(8,128)} %fusion.27), channel_id=1, source_target_pairs={{0,32},{8,40},{16,48},{24,56},{32,64},{40,72},{48,80},{56,88},{64,... | collective-permute-start | bytes 393224 | tf_op jit(solution)/shard_map/ppermute | solution.py:15
  131.2 15.7 %collective-permute-start.14 = (f32[2,128,128]{2,1,0:T(8,128)}, f32[2,128,128]{2,1,0:T(8,128)}, u32[]{:S(2)}, u32[]{:S(2)}) collective-permute-start(f32[2,128,128]{2,1,0:T(8,128)} %fusion.27), channel_id=1, source_target_pairs={{0,24},{8,32},{16,40},{24,48},{32,56},{40,64},{48,72},{56,80},{64,... | collective-permute-start | bytes 393224 | tf_op jit(solution)/shard_map/ppermute | solution.py:15
  133.2 13.7 %collective-permute-start.13 = (f32[2,128,128]{2,1,0:T(8,128)}, f32[2,128,128]{2,1,0:T(8,128)}, u32[]{:S(2)}, u32[]{:S(2)}) collective-permute-start(f32[2,128,128]{2,1,0:T(8,128)} %fusion.27), channel_id=1, source_target_pairs={{0,16},{8,24},{16,32},{24,40},{32,48},{40,56},{48,64},{56,72},{64,... | collective-permute-start | bytes 393224 | tf_op jit(solution)/shard_map/ppermute | solution.py:15
  135.6 11.3 %collective-permute-start.12 = (f32[2,128,128]{2,1,0:T(8,128)}, f32[2,128,128]{2,1,0:T(8,128)}, u32[]{:S(2)}, u32[]{:S(2)}) collective-permute-start(f32[2,128,128]{2,1,0:T(8,128)} %fusion.27), channel_id=1, source_target_pairs={{0,8},{8,16},{16,24},{24,32},{32,40},{40,48},{48,56},{56,64},{64,7... | collective-permute-start | bytes 393224 | tf_op jit(solution)/shard_map/ppermute | solution.py:15
  146.6 21.0 %copy-start.2 = (f32[512,2,128]{0,2,1:T(8,128)S(1)}, f32[512,2,128]{0,2,1:T(8,128)}, u32[]{:S(2)}) copy-start(f32[512,2,128]{0,2,1:T(8,128)} %fusion.13) | copy-start | bytes 1572868
  146.9 21.1 %copy-start.4 = (f32[256]{0:T(256)S(1)}, f32[256]{0:T(256)}, u32[]{:S(2)}) copy-start(f32[256]{0:T(256)} %param.6) | copy-start | bytes 3076
  148.0 14.9 %collective-permute-start.18 = (f32[2,128,128]{2,1,0:T(8,128)S(1)}, f32[2,128,128]{2,1,0:T(8,128)S(1)}, u32[]{:S(2)}, u32[]{:S(2)}) collective-permute-start(f32[2,128,128]{2,1,0:T(8,128)S(1)} %select_add_fusion), channel_id=1, source_target_pairs={{0,96},{8,104},{16,112},{24,120},{32,128},{40,136},{48,144},{56,15... | collective-permute-start | bytes 393224 | tf_op jit(solution)/shard_map/ppermute | solution.py:15
  153.5 9.4 %collective-permute-start.17 = (f32[2,128,128]{2,1,0:T(8,128)S(1)}, f32[2,128,128]{2,1,0:T(8,128)S(1)}, u32[]{:S(2)}, u32[]{:S(2)}) collective-permute-start(f32[2,128,128]{2,1,0:T(8,128)S(1)} %select_add_fusion), channel_id=1, source_target_pairs={{0,64},{8,72},{16,80},{24,88},{32,96},{40,104},{48,112},{56,120},{... | collective-permute-start | bytes 393224 | tf_op jit(solution)/shard_map/ppermute | solution.py:15
  158.1 9.4 %collective-permute-start.16 = (f32[2,128,128]{2,1,0:T(8,128)S(1)}, f32[2,128,128]{2,1,0:T(8,128)S(1)}, u32[]{:S(2)}, u32[]{:S(2)}) collective-permute-start(f32[2,128,128]{2,1,0:T(8,128)S(1)} %select_add_fusion), channel_id=1, source_target_pairs={{0,32},{8,40},{16,48},{24,56},{32,64},{40,72},{48,80},{56,88},{64,... | collective-permute-start | bytes 393224 | tf_op jit(solution)/shard_map/ppermute | solution.py:15
Sparse Core Ops, SparseCore 0:
  9.4 54.7 all-gather.2
  66.2 50.7 all-gather.4

commit v10 on v8

--- a/solution.py
+++ b/solution.py
@@ -58,27 +58,33 @@
 def state_scan(kv_state, tails, row_count):
     count = lax.axis_size(CTX)
     window = min(count - 1, 1 + (SPAN - 1) // row_count)
+    row_len = lax.axis_size("x") * lax.axis_size("core")
+    assert window <= 2 * row_len
     me = lax.axis_index(CTX)
+    pos = me % row_len
+    first = me - pos
 
     def tail_of(block):
         return jnp.where(block >= 0, tails[jnp.clip(block, 0, count - 1)], -1.0)
 
     prev_tail = tail_of(me - 1)
+    spread = jnp.broadcast_to(kv_state[None], (row_len,) + kv_state.shape)
+    row = lax.all_to_all(spread, ("x", "core"), 0, 0, tiled=True)
+    places = jnp.arange(row_len)
+    row_tails = tail_of(first + places)
+    in_last = row_tails == row_tails[row_len - 1]
 
-    def counts(block):
-        return (block >= 0) & (tail_of(block) == prev_tail)
+    def masked(mask):
+        return jnp.sum(jnp.where(mask[:, None, None, None], row, 0.0), axis=0)
 
-    radix = 4
-    got = [shifted(kv_state, CTX, k, count) for k in range(1, radix + 1)]
-    running = sum(jnp.where(counts(me - k), piece, 0.0) for k, piece in zip(range(1, radix + 1), got))
-    span = radix
-    while span < window:
-        got = [shifted(running, CTX, span * k, count) for k in range(1, radix)]
-        running = running + sum(
-            jnp.where(counts(me - span * k - 1), piece, 0.0) for k, piece in zip(range(1, radix), got)
-        )
-        span *= radix
-    return running, prev_tail
+    y_count = lax.axis_size("y")
+    one_back = shifted(masked(in_last), "y", 1, y_count)
+    two_back = shifted(masked(in_last & (places >= pos)), "y", 2, y_count)
+    state = masked((places < pos) & (row_tails == prev_tail))
+    state = state + jnp.where(tail_of(first - 1) == prev_tail, one_back, 0.0)
+    if window > row_len:
+        state = state + jnp.where(tail_of(first - row_len - 1) == prev_tail, two_back, 0.0)
+    return state, prev_tail
 
 
 def per_device(tokens, w_qkv, out_gain, seg_ids):

time: 150 us -> 156 us (1.040)
  the two profiles are of different devices: /device:TPU:32 before, /device:TPU:24 now
where the time goes in v10:
time: 156 us; the launch traced here: 155 us
  starting transfers between devices  52.9 us (34%)
  waiting for transfers between devices  39.4 us (25%)
  local copies, waits for them, and re-layouts  20.8 us (13%)
  between operations  16 us (10%)
  matrix products  14.6 us (9%)
  other arithmetic  11 us (7%)
    ppermute x6, starting transfers between devices, ring_gather(): lax.ppermute(ahead, axis, [(j, (j + 1) % count) for j in range(count)])  27 us
    ppermute x6, waiting for transfers between devices, ring_gather(): lax.ppermute(ahead, axis, [(j, (j + 1) % count) for j in range(count)])  11 us
    ppermute x4, starting transfers between devices, ring_gather(): lax.ppermute(behind, axis, [(j, (j - 1) % count) for j in range(count)])  10.6 us
    all_gather x1, waiting for transfers between devices, per_device(): whole = lax.all_gather(tokens, 'head', axis=1, tiled=True)  8.52 us
    ppermute x2, starting transfers between devices, shifted(): lax.ppermute(value, axis, [(source, source + steps) for source in range(c...  7.21 us
    ppermute x4, waiting for transfers between devices, ring_gather(): lax.ppermute(behind, axis, [(j, (j - 1) % count) for j in range(count)])  7.06 us
    concatenate x2, local copies, waits for them, and re-layouts, gather_weights(): jnp.concatenate([rows, other], axis=2)  6.16 us
    all_to_all x1, waiting for transfers between devices, state_scan(): row = lax.all_to_all(spread, ('x', 'core'), 0, 0, tiled=True)  6.04 us
  transfers between devices with their start and end apart: 16, of which 13 were waited for; matrix products, arithmetic and copies ran while one was open for 21% of the time, Pallas kernels for 0%

profile of v10, /device:TPU:24, one launch (start us, length us, event | category | flops | bytes accessed | tf_op | source)
XLA Modules:
  0.0 154.7 jit_solution(17341098382175701279)
XLA Ops:
  7.9 1.5 concatenate.31
  9.3 1.9 %collective-permute-start = (bf16[3,33,256]{2,1,0:T(8,128)(2,1)S(1)}, bf16[3,33,256]{2,1,0:T(8,128)(2,1)S(1)}, u32[]{:S(2)}, u32[]{:S(2)}) collective-permute-start(bf16[3,33,256]{2,1,0:T(8,128)(2,1)S(1)} %concatenate.31), channel_id=1, source_target_pairs={{0,8},{8,0},{1,9},{9,1},{2,10},{10,2},{3,11},{11,3},{4,12},{12,4},... | collective-permute-start | bytes 152072 | tf_op jit(solution)/shard_map/ppermute | solution.py:40
  13.9 3.4 %collective-permute-start.1 = (bf16[3,66,128]{2,1,0:T(8,128)(2,1)S(1)}, bf16[3,66,128]{2,1,0:T(8,128)(2,1)S(1)}, u32[]{:S(2)}, u32[]{:S(2)}) collective-permute-start(bf16[3,66,128]{2,1,0:T(8,128)(2,1)S(1)} %pad_maximum_fusion), channel_id=1, source_target_pairs={{0,16},{16,32},{32,48},{48,0},{1,17},{17,33},{33,49},{49,1},{2,18}... | collective-permute-start | bytes 152072 | tf_op jit(solution)/shard_map/ppermute | solution.py:23
  17.3 3.9 %collective-permute-done.1 = bf16[3,66,128]{2,1,0:T(8,128)(2,1)S(1)} collective-permute-done((bf16[3,66,128]{2,1,0:T(8,128)(2,1)S(1)}, bf16[3,66,128]{2,1,0:T(8,128)(2,1)S(1)}, u32[]{:S(2)}, u32[]{:S(2)}) %collective-permute-start.1) | collective-permute-done | bytes 50720 | tf_op jit(solution)/shard_map/ppermute | solution.py:23
  21.2 2.2 %collective-permute-start.2 = (bf16[3,66,128]{2,1,0:T(8,128)(2,1)S(1)}, bf16[3,66,128]{2,1,0:T(8,128)(2,1)S(1)}, u32[]{:S(2)}, u32[]{:S(2)}) collective-permute-start(bf16[3,66,128]{2,1,0:T(8,128)(2,1)S(1)} %collective-permute-done.1), channel_id=1, source_target_pairs={{0,16},{16,32},{32,48},{48,0},{1,17},{17,33},{33,49},{49,1},{2,18}... | collective-permute-start | bytes 152072 | tf_op jit(solution)/shard_map/ppermute | solution.py:23
  23.4 4.9 %collective-permute-start.3 = (bf16[3,66,128]{2,1,0:T(8,128)(2,1)S(1)}, bf16[3,66,128]{2,1,0:T(8,128)(2,1)S(1)}, u32[]{:S(2)}, u32[]{:S(2)}) collective-permute-start(bf16[3,66,128]{2,1,0:T(8,128)(2,1)S(1)} %pad_maximum_fusion), channel_id=1, source_target_pairs={{0,48},{16,0},{32,16},{48,32},{1,49},{17,1},{33,17},{49,33},{2,50}... | collective-permute-start | bytes 152072 | tf_op jit(solution)/shard_map/ppermute | solution.py:26
  28.5 1.6 %collective-permute-done.3 = bf16[3,66,128]{2,1,0:T(8,128)(2,1)S(1)} collective-permute-done((bf16[3,66,128]{2,1,0:T(8,128)(2,1)S(1)}, bf16[3,66,128]{2,1,0:T(8,128)(2,1)S(1)}, u32[]{:S(2)}, u32[]{:S(2)}) %collective-permute-start.3) | collective-permute-done | bytes 50720 | tf_op jit(solution)/shard_map/ppermute | solution.py:26
  30.3 4.7 %collective-permute-start.4 = (bf16[3,264,128]{2,1,0:T(8,128)(2,1)S(1)}, bf16[3,264,128]{2,1,0:T(8,128)(2,1)S(1)}, u32[]{:S(2)}, u32[]{:S(2)}) collective-permute-start(bf16[3,264,128]{2,1,0:T(8,128)(2,1)S(1)} %reshape.188), channel_id=1, source_target_pairs={{0,64},{64,128},{128,192},{192,256},{256,320},{320,384},{384,448},... | collective-permute-start | bytes 608264 | tf_op jit(solution)/shard_map/ppermute | solution.py:23
  35.0 3.2 %collective-permute-done.4 = bf16[3,264,128]{2,1,0:T(8,128)(2,1)S(1)} collective-permute-done((bf16[3,264,128]{2,1,0:T(8,128)(2,1)S(1)}, bf16[3,264,128]{2,1,0:T(8,128)(2,1)S(1)}, u32[]{:S(2)}, u32[]{:S(2)}) %collective-permute-start.4) | collective-permute-done | bytes 202784 | tf_op jit(solution)/shard_map/ppermute | solution.py:23
  38.2 5.6 %collective-permute-start.5 = (bf16[3,264,128]{2,1,0:T(8,128)(2,1)S(1)}, bf16[3,264,128]{2,1,0:T(8,128)(2,1)S(1)}, u32[]{:S(2)}, u32[]{:S(2)}) collective-permute-start(bf16[3,264,128]{2,1,0:T(8,128)(2,1)S(1)} %collective-permute-done.4), channel_id=1, source_target_pairs={{0,64},{64,128},{128,192},{192,256},{256,320},{320,384},{384,448},... | collective-permute-start | bytes 608264 | tf_op jit(solution)/shard_map/ppermute | solution.py:23
  43.8 1.9 %collective-permute-start.8 = (bf16[3,264,128]{2,1,0:T(8,128)(2,1)S(1)}, bf16[3,264,128]{2,1,0:T(8,128)(2,1)S(1)}, u32[]{:S(2)}, u32[]{:S(2)}) collective-permute-start(bf16[3,264,128]{2,1,0:T(8,128)(2,1)S(1)} %reshape.188), channel_id=1, source_target_pairs={{0,448},{64,0},{128,64},{192,128},{256,192},{320,256},{384,320},{4... | collective-permute-start | bytes 608264 | tf_op jit(solution)/shard_map/ppermute | solution.py:26
  47.0 5.6 %collective-permute-start.6 = (bf16[3,264,128]{2,1,0:T(8,128)(2,1)S(1)}, bf16[3,264,128]{2,1,0:T(8,128)(2,1)S(1)}, u32[]{:S(2)}, u32[]{:S(2)}) collective-permute-start(bf16[3,264,128]{2,1,0:T(8,128)(2,1)S(1)} %collective-permute-done.5), channel_id=1, source_target_pairs={{0,64},{64,128},{128,192},{192,256},{256,320},{320,384},{384,448},... | collective-permute-start | bytes 608264 | tf_op jit(solution)/shard_map/ppermute | solution.py:23
  52.7 1.9 %collective-permute-start.9 = (bf16[3,264,128]{2,1,0:T(8,128)(2,1)S(1)}, bf16[3,264,128]{2,1,0:T(8,128)(2,1)S(1)}, u32[]{:S(2)}, u32[]{:S(2)}) collective-permute-start(bf16[3,264,128]{2,1,0:T(8,128)(2,1)S(1)} %collective-permute-done.8), channel_id=1, source_target_pairs={{0,448},{64,0},{128,64},{192,128},{256,192},{320,256},{384,320},{4... | collective-permute-start | bytes 608264 | tf_op jit(solution)/shard_map/ppermute | solution.py:26
  55.9 5.6 %collective-permute-start.7 = (bf16[3,264,128]{2,1,0:T(8,128)(2,1)S(1)}, bf16[3,264,128]{2,1,0:T(8,128)(2,1)S(1)}, u32[]{:S(2)}, u32[]{:S(2)}) collective-permute-start(bf16[3,264,128]{2,1,0:T(8,128)(2,1)S(1)} %collective-permute-done.6), channel_id=1, source_target_pairs={{0,64},{64,128},{128,192},{192,256},{256,320},{320,384},{384,448},... | collective-permute-start | bytes 608264 | tf_op jit(solution)/shard_map/ppermute | solution.py:23
  61.6 1.9 %collective-permute-start.10 = (bf16[3,264,128]{2,1,0:T(8,128)(2,1)S(1)}, bf16[3,264,128]{2,1,0:T(8,128)(2,1)S(1)}, u32[]{:S(2)}, u32[]{:S(2)}) collective-permute-start(bf16[3,264,128]{2,1,0:T(8,128)(2,1)S(1)} %collective-permute-done.9), channel_id=1, source_target_pairs={{0,448},{64,0},{128,64},{192,128},{256,192},{320,256},{384,320},{4... | collective-permute-start | bytes 608264 | tf_op jit(solution)/shard_map/ppermute | solution.py:26
  64.9 5.5 %collective-permute-done.10 = bf16[3,264,128]{2,1,0:T(8,128)(2,1)S(1)} collective-permute-done((bf16[3,264,128]{2,1,0:T(8,128)(2,1)S(1)}, bf16[3,264,128]{2,1,0:T(8,128)(2,1)S(1)}, u32[]{:S(2)}, u32[]{:S(2)}) %collective-permute-start.10) | collective-permute-done | bytes 202784 | tf_op jit(solution)/shard_map/ppermute | solution.py:26
  72.2 1.9 %collective-permute-start.11 = (bf16[3,2112,128]{2,1,0:T(8,128)(2,1)}, bf16[3,2112,128]{2,1,0:T(8,128)(2,1)}, u32[]{:S(2)}, u32[]{:S(2)}) collective-permute-start(bf16[3,2112,128]{2,1,0:T(8,128)(2,1)} %bitcast.14), channel_id=1, source_target_pairs={{0,8},{8,0},{1,9},{9,1},{2,10},{10,2},{3,11},{11,3},{4,12},{12,4},... | collective-permute-start | bytes 4866056 | tf_op jit(solution)/shard_map/ppermute | solution.py:46
  77.0 2.5 %concatenate.35 = bf16[3,64,33,128]{3,2,1,0:T(8,128)(2,1)S(1)} reshape(bf16[3,8,264,128]{3,2,1,0:T(8,128)(2,1)} %copy.31) | data formatting | bytes 3244032 | tf_op jit(solution)/shard_map/concatenate | solution.py:49
  79.5 3.7 %concatenate.36 = bf16[3,64,33,128]{3,2,1,0:T(8,128)(2,1)} reshape(bf16[3,2112,128]{2,1,0:T(8,128)(2,1)} %collective-permute-done.11) | data formatting | bytes 3244032 | tf_op jit(solution)/shard_map/concatenate | solution.py:49
  83.2 2.8 %maximum_select_fusion = bf16[3,64,33,256]{3,2,1,0:T(8,128)(2,1)S(1)} fusion(bf16[3,64,33,128]{3,2,1,0:T(8,128)(2,1)} %concatenate.36, bf16[3,64,33,128]{3,2,1,0:T(8,128)(2,1)S(1)} %concatenate.35, pred[]{:T(512)S(6)} %eq.87), kind=kLoop, calls=%fused_computation.4 | loop fusion | flops 14598144 | bytes 6488065 | tf_op jit(solution)/shard_map/jit(_where)/select_n | solution.py:47
  95.0 8.5 %all-gather.2.cloned.1.call-done = bf16[1024,2048]{1,0:T(8,128)(2,1)} async-done(((bf16[1024,256]{1,0:T(8,128)(2,1)}), bf16[1024,2048]{1,0:T(8,128)(2,1)}) %all-gather.2.cloned.1.call-update) | async-done | bytes 4194320 | tf_op jit(solution)/shard_map/all_gather | solution.py:91
  103.5 4.6 %fusion.7 = bf16[2,1024,256]{1,2,0:T(8,128)(2,1)S(1)} fusion(bf16[2,2048,256]{2,1,0:T(8,128)(2,1)S(1)} %bitcast.97, bf16[1024,2048]{1,0:T(8,128)(2,1)} %all-gather.2.cloned.1.call-done), kind=kOutput, calls=%fused_computation.17 | convolution fusion | flops 2148007936 | bytes 7340032 | tf_op jit(solution)/shard_map/tr,grc->gtc/dot_general | solution.py:100
  111.1 4.2 %all-to-all-start = ((f32[8,2,128,128]{3,2,1,0:T(8,128)}), f32[8,2,128,128]{3,2,1,0:T(8,128)S(1)}, u32[]{:S(2)}, u32[]{:S(2)}) async-start(f32[8,2,128,128]{3,2,1,0:T(8,128)} %broadcast_in_dim.115), calls=%async_computation | async-start | bytes 2097152 | tf_op jit(solution)/shard_map/all_to_all | solution.py:72
  115.3 4.2 %fusion.18 = bf16[1024,256]{0,1:T(8,128)(2,1)S(1)} fusion(bf16[2048,256]{1,0:T(8,128)(2,1)} %bitcast.101, bf16[1024,2048]{1,0:T(8,128)(2,1)} %all-gather.2.cloned.1.call-done), kind=kOutput, calls=%fused_computation.28 | convolution fusion | flops 1075314688 | bytes 5767168 | tf_op jit(solution)/shard_map/tr,rc->tc/dot_general | solution.py:112
  119.5 1.7 %slice.104 = bf16[1,512,256]{1,2,0:T(8,128)(2,1)} slice(bf16[2,1024,256]{1,2,0:T(8,128)(2,1)} %copy-done.1), slice={[1:2], [0:512], [0:256]} | slice | bytes 524288 | tf_op jit(solution)/shard_map/slice | solution.py:132
  122.2 3.0 %fusion.14 = f32[512,2,128]{0,2,1:T(8,128)S(1)} fusion(bf16[1024,2,128]{0,2,1:T(8,128)(2,1)S(1)} %bitcast.103, bf16[512,2,128]{0,2,1:T(8,128)(2,1)} %bitcast.107, pred[512,1024]{1,0:T(8,128)(4,1)} %fusion.2, f32[1024,2,128]{0,2,1:T(8,128)} %bitcast.100), kind=kOutput, calls=%fused_computation.24 | convolution fusion | flops 540278784 | bytes 2883584 | tf_op jit(solution)/shard_map/hbs,she->bhe/dot_general | solution.py:132
  125.2 6.0 %all-to-all-done = f32[8,2,128,128]{3,2,1,0:T(8,128)S(1)} async-done(((f32[8,2,128,128]{3,2,1,0:T(8,128)}), f32[8,2,128,128]{3,2,1,0:T(8,128)S(1)}, u32[]{:S(2)}, u32[]{:S(2)}) %all-to-all-start) | async-done | bytes 1048608 | tf_op jit(solution)/shard_map/all_to_all | solution.py:72
  131.6 4.6 %collective-permute-start.13 = (f32[2,128,128]{2,1,0:T(8,128)S(1)}, f32[2,128,128]{2,1,0:T(8,128)S(1)}, u32[]{:S(2)}, u32[]{:S(2)}) collective-permute-start(f32[2,128,128]{2,1,0:T(8,128)S(1)} %get-tuple-element.6), channel_id=1, source_target_pairs={{0,128},{64,192},{128,256},{192,320},{256,384},{320,448},{1,129},{... | collective-permute-start | bytes 393224 | tf_op jit(solution)/shard_map/ppermute | solution.py:15
  136.3 2.6 %collective-permute-start.12 = (f32[2,128,128]{2,1,0:T(8,128)S(1)}, f32[2,128,128]{2,1,0:T(8,128)S(1)}, u32[]{:S(2)}, u32[]{:S(2)}) collective-permute-start(f32[2,128,128]{2,1,0:T(8,128)S(1)} %get-tuple-element.5), channel_id=1, source_target_pairs={{0,64},{64,128},{128,192},{192,256},{256,320},{320,384},{384,448},... | collective-permute-start | bytes 393224 | tf_op jit(solution)/shard_map/ppermute | solution.py:15
  138.8 1.9 %fusion.15 = f32[512,2,128]{0,2,1:T(8,128)S(1)} fusion(bf16[512,2,128]{0,2,1:T(8,128)(2,1)} %bitcast.105, bf16[512,2,128]{0,2,1:T(8,128)(2,1)} %bitcast.106, bf16[512,2,128]{0,2,1:T(8,128)(2,1)S(1)} %bitcast.104, pred[512,512]{1,0:T(8,128)(4,1)} %fusion.23), kind=kOutput, calls=%fused_computation.25 | convolution fusion | flops 269484032 | bytes 1572864 | tf_op jit(solution)/shard_map/hbs,she->bhe/dot_general | solution.py:132
  140.7 1.7 %collective-permute-done.13 = f32[2,128,128]{2,1,0:T(8,128)S(1)} collective-permute-done((f32[2,128,128]{2,1,0:T(8,128)S(1)}, f32[2,128,128]{2,1,0:T(8,128)S(1)}, u32[]{:S(2)}, u32[]{:S(2)}) %collective-permute-start.13) | collective-permute-done | bytes 131104 | tf_op jit(solution)/shard_map/ppermute | solution.py:15
  142.5 3.8 %collective-permute-done.12 = f32[2,128,128]{2,1,0:T(8,128)S(1)} collective-permute-done((f32[2,128,128]{2,1,0:T(8,128)S(1)}, f32[2,128,128]{2,1,0:T(8,128)S(1)}, u32[]{:S(2)}, u32[]{:S(2)}) %collective-permute-start.12) | collective-permute-done | bytes 131104 | tf_op jit(solution)/shard_map/ppermute | solution.py:15
  (81 shorter events, 25.8 us)
Async XLA Ops:
  6.5 97.0 %all-gather.2.cloned.1.call-start = ((), (), s32[]{:S(2)}) async-start(), calls=%async_computation.1 | async-start | bytes 4718592 | tf_op jit(solution)/shard_map/all_gather | solution.py:91
  9.3 3.1 %collective-permute-start = (bf16[3,33,256]{2,1,0:T(8,128)(2,1)S(1)}, bf16[3,33,256]{2,1,0:T(8,128)(2,1)S(1)}, u32[]{:S(2)}, u32[]{:S(2)}) collective-permute-start(bf16[3,33,256]{2,1,0:T(8,128)(2,1)S(1)} %concatenate.31), channel_id=1, source_target_pairs={{0,8},{8,0},{1,9},{9,1},{2,10},{10,2},{3,11},{11,3},{4,12},{12,4},... | collective-permute-start | bytes 152072 | tf_op jit(solution)/shard_map/ppermute | solution.py:40
  13.9 7.3 %collective-permute-start.1 = (bf16[3,66,128]{2,1,0:T(8,128)(2,1)S(1)}, bf16[3,66,128]{2,1,0:T(8,128)(2,1)S(1)}, u32[]{:S(2)}, u32[]{:S(2)}) collective-permute-start(bf16[3,66,128]{2,1,0:T(8,128)(2,1)S(1)} %pad_maximum_fusion), channel_id=1, source_target_pairs={{0,16},{16,32},{32,48},{48,0},{1,17},{17,33},{33,49},{49,1},{2,18}... | collective-permute-start | bytes 152072 | tf_op jit(solution)/shard_map/ppermute | solution.py:23
  21.2 7.2 %collective-permute-start.2 = (bf16[3,66,128]{2,1,0:T(8,128)(2,1)S(1)}, bf16[3,66,128]{2,1,0:T(8,128)(2,1)S(1)}, u32[]{:S(2)}, u32[]{:S(2)}) collective-permute-start(bf16[3,66,128]{2,1,0:T(8,128)(2,1)S(1)} %collective-permute-done.1), channel_id=1, source_target_pairs={{0,16},{16,32},{32,48},{48,0},{1,17},{17,33},{33,49},{49,1},{2,18}... | collective-permute-start | bytes 152072 | tf_op jit(solution)/shard_map/ppermute | solution.py:23
  23.4 6.7 %collective-permute-start.3 = (bf16[3,66,128]{2,1,0:T(8,128)(2,1)S(1)}, bf16[3,66,128]{2,1,0:T(8,128)(2,1)S(1)}, u32[]{:S(2)}, u32[]{:S(2)}) collective-permute-start(bf16[3,66,128]{2,1,0:T(8,128)(2,1)S(1)} %pad_maximum_fusion), channel_id=1, source_target_pairs={{0,48},{16,0},{32,16},{48,32},{1,49},{17,1},{33,17},{49,33},{2,50}... | collective-permute-start | bytes 152072 | tf_op jit(solution)/shard_map/ppermute | solution.py:26
  30.3 7.9 %collective-permute-start.4 = (bf16[3,264,128]{2,1,0:T(8,128)(2,1)S(1)}, bf16[3,264,128]{2,1,0:T(8,128)(2,1)S(1)}, u32[]{:S(2)}, u32[]{:S(2)}) collective-permute-start(bf16[3,264,128]{2,1,0:T(8,128)(2,1)S(1)} %reshape.188), channel_id=1, source_target_pairs={{0,64},{64,128},{128,192},{192,256},{256,320},{320,384},{384,448},... | collective-permute-start | bytes 608264 | tf_op jit(solution)/shard_map/ppermute | solution.py:23
  38.2 8.8 %collective-permute-start.5 = (bf16[3,264,128]{2,1,0:T(8,128)(2,1)S(1)}, bf16[3,264,128]{2,1,0:T(8,128)(2,1)S(1)}, u32[]{:S(2)}, u32[]{:S(2)}) collective-permute-start(bf16[3,264,128]{2,1,0:T(8,128)(2,1)S(1)} %collective-permute-done.4), channel_id=1, source_target_pairs={{0,64},{64,128},{128,192},{192,256},{256,320},{320,384},{384,448},... | collective-permute-start | bytes 608264 | tf_op jit(solution)/shard_map/ppermute | solution.py:23
  43.8 8.8 %collective-permute-start.8 = (bf16[3,264,128]{2,1,0:T(8,128)(2,1)S(1)}, bf16[3,264,128]{2,1,0:T(8,128)(2,1)S(1)}, u32[]{:S(2)}, u32[]{:S(2)}) collective-permute-start(bf16[3,264,128]{2,1,0:T(8,128)(2,1)S(1)} %reshape.188), channel_id=1, source_target_pairs={{0,448},{64,0},{128,64},{192,128},{256,192},{320,256},{384,320},{4... | collective-permute-start | bytes 608264 | tf_op jit(solution)/shard_map/ppermute | solution.py:26
  47.0 8.8 %collective-permute-start.6 = (bf16[3,264,128]{2,1,0:T(8,128)(2,1)S(1)}, bf16[3,264,128]{2,1,0:T(8,128)(2,1)S(1)}, u32[]{:S(2)}, u32[]{:S(2)}) collective-permute-start(bf16[3,264,128]{2,1,0:T(8,128)(2,1)S(1)} %collective-permute-done.5), channel_id=1, source_target_pairs={{0,64},{64,128},{128,192},{192,256},{256,320},{320,384},{384,448},... | collective-permute-start | bytes 608264 | tf_op jit(solution)/shard_map/ppermute | solution.py:23
  52.7 8.9 %collective-permute-start.9 = (bf16[3,264,128]{2,1,0:T(8,128)(2,1)S(1)}, bf16[3,264,128]{2,1,0:T(8,128)(2,1)S(1)}, u32[]{:S(2)}, u32[]{:S(2)}) collective-permute-start(bf16[3,264,128]{2,1,0:T(8,128)(2,1)S(1)} %collective-permute-done.8), channel_id=1, source_target_pairs={{0,448},{64,0},{128,64},{192,128},{256,192},{320,256},{384,320},{4... | collective-permute-start | bytes 608264 | tf_op jit(solution)/shard_map/ppermute | solution.py:26
  55.9 8.8 %collective-permute-start.7 = (bf16[3,264,128]{2,1,0:T(8,128)(2,1)S(1)}, bf16[3,264,128]{2,1,0:T(8,128)(2,1)S(1)}, u32[]{:S(2)}, u32[]{:S(2)}) collective-permute-start(bf16[3,264,128]{2,1,0:T(8,128)(2,1)S(1)} %collective-permute-done.6), channel_id=1, source_target_pairs={{0,64},{64,128},{128,192},{192,256},{256,320},{320,384},{384,448},... | collective-permute-start | bytes 608264 | tf_op jit(solution)/shard_map/ppermute | solution.py:23
  61.6 8.8 %collective-permute-start.10 = (bf16[3,264,128]{2,1,0:T(8,128)(2,1)S(1)}, bf16[3,264,128]{2,1,0:T(8,128)(2,1)S(1)}, u32[]{:S(2)}, u32[]{:S(2)}) collective-permute-start(bf16[3,264,128]{2,1,0:T(8,128)(2,1)S(1)} %collective-permute-done.9), channel_id=1, source_target_pairs={{0,448},{64,0},{128,64},{192,128},{256,192},{320,256},{384,320},{4... | collective-permute-start | bytes 608264 | tf_op jit(solution)/shard_map/ppermute | solution.py:26
  72.2 7.3 %collective-permute-start.11 = (bf16[3,2112,128]{2,1,0:T(8,128)(2,1)}, bf16[3,2112,128]{2,1,0:T(8,128)(2,1)}, u32[]{:S(2)}, u32[]{:S(2)}) collective-permute-start(bf16[3,2112,128]{2,1,0:T(8,128)(2,1)} %bitcast.14), channel_id=1, source_target_pairs={{0,8},{8,0},{1,9},{9,1},{2,10},{10,2},{3,11},{11,3},{4,12},{12,4},... | collective-permute-start | bytes 4866056 | tf_op jit(solution)/shard_map/ppermute | solution.py:46
  86.0 2.2 %copy-start = (bf16[3,64,33,256]{3,2,1,0:T(8,128)(2,1)}, bf16[3,64,33,256]{3,2,1,0:T(8,128)(2,1)S(1)}, u32[]{:S(2)}) copy-start(bf16[3,64,33,256]{3,2,1,0:T(8,128)(2,1)S(1)} %maximum_select_fusion) | copy-start | bytes 9732100
  86.0 8.4 %copy-start.3 = (s32[1024]{0:T(1024)S(1)}, s32[1024]{0:T(1024)}, u32[]{:S(2)}) copy-start(s32[1024]{0:T(1024)} %param.7) | copy-start | bytes 12292
  108.1 1.9 %copy-start.1 = (bf16[2,1024,256]{1,2,0:T(8,128)(2,1)}, bf16[2,1024,256]{1,2,0:T(8,128)(2,1)S(1)}, u32[]{:S(2)}) copy-start(bf16[2,1024,256]{1,2,0:T(8,128)(2,1)S(1)} %fusion.7) | copy-start | bytes 3145732
  108.3 1.2 copy-start.2
  111.1 20.1 %all-to-all-start = ((f32[8,2,128,128]{3,2,1,0:T(8,128)}), f32[8,2,128,128]{3,2,1,0:T(8,128)S(1)}, u32[]{:S(2)}, u32[]{:S(2)}) async-start(f32[8,2,128,128]{3,2,1,0:T(8,128)} %broadcast_in_dim.115), calls=%async_computation | async-start | bytes 2097152 | tf_op jit(solution)/shard_map/all_to_all | solution.py:72
  131.6 15.1 %copy-start.4 = (f32[256]{0:T(256)S(1)}, f32[256]{0:T(256)}, u32[]{:S(2)}) copy-start(f32[256]{0:T(256)} %param.6) | copy-start | bytes 3076
  131.6 10.8 %collective-permute-start.13 = (f32[2,128,128]{2,1,0:T(8,128)S(1)}, f32[2,128,128]{2,1,0:T(8,128)S(1)}, u32[]{:S(2)}, u32[]{:S(2)}) collective-permute-start(f32[2,128,128]{2,1,0:T(8,128)S(1)} %get-tuple-element.6), channel_id=1, source_target_pairs={{0,128},{64,192},{128,256},{192,320},{256,384},{320,448},{1,129},{... | collective-permute-start | bytes 393224 | tf_op jit(solution)/shard_map/ppermute | solution.py:15
  136.3 10.0 %collective-permute-start.12 = (f32[2,128,128]{2,1,0:T(8,128)S(1)}, f32[2,128,128]{2,1,0:T(8,128)S(1)}, u32[]{:S(2)}, u32[]{:S(2)}) collective-permute-start(f32[2,128,128]{2,1,0:T(8,128)S(1)} %get-tuple-element.5), channel_id=1, source_target_pairs={{0,64},{64,128},{128,192},{192,256},{256,320},{320,384},{384,448},... | collective-permute-start | bytes 393224 | tf_op jit(solution)/shard_map/ppermute | solution.py:15
Sparse Core Ops, SparseCore 0:
  35.1 68.3 all-gather.1

commit v11 on v10

--- a/solution.py
+++ b/solution.py
@@ -108,6 +108,7 @@
     key_tail = jnp.where((seg_float == tail_id)[:, None, None], key_map, jnp.zeros_like(key_map))
     kv_state = jnp.einsum("thd,the->hde", key_tail, values, preferred_element_type=jnp.float32)
 
+    tails, kv_state = lax.optimization_barrier((tails, kv_state))
     state_in, tail_in = state_scan(kv_state, tails, row_count)
     query_proj = jnp.einsum("tr,rc->tc", whole, w_rows[0], preferred_element_type=jnp.float32)
     query_proj = lax.reduce_precision(query_proj, exponent_bits=8, mantissa_bits=7)

time: 156 us -> 147 us (0.942)
  the two profiles are of different devices: /device:TPU:24 before, /device:TPU:26 now
where the time goes in v11:
time: 147 us; the launch traced here: 146 us
  starting transfers between devices  52.2 us (36%)
  waiting for transfers between devices  33.2 us (23%)
  local copies, waits for them, and re-layouts  20 us (14%)
  between operations  15.8 us (11%)
  matrix products  14.6 us (10%)
  other arithmetic  10 us (7%)
    ppermute x6, starting transfers between devices, ring_gather(): lax.ppermute(ahead, axis, [(j, (j + 1) % count) for j in range(count)])  28.2 us
    ppermute x6, waiting for transfers between devices, ring_gather(): lax.ppermute(ahead, axis, [(j, (j + 1) % count) for j in range(count)])  9.81 us
    ppermute x4, waiting for transfers between devices, ring_gather(): lax.ppermute(behind, axis, [(j, (j - 1) % count) for j in range(count)])  8.89 us
    ppermute x4, starting transfers between devices, ring_gather(): lax.ppermute(behind, axis, [(j, (j - 1) % count) for j in range(count)])  8.2 us
    ppermute x2, waiting for transfers between devices, shifted(): lax.ppermute(value, axis, [(source, source + steps) for source in range(c...  8.06 us
    ppermute x2, starting transfers between devices, shifted(): lax.ppermute(value, axis, [(source, source + steps) for source in range(c...  7.08 us
    concatenate x2, local copies, waits for them, and re-layouts, gather_weights(): jnp.concatenate([rows, other], axis=2)  6.16 us
    all_gather x1, waiting for transfers between devices, per_device(): whole = lax.all_gather(tokens, 'head', axis=1, tiled=True)  5.21 us
  transfers between devices with their start and end apart: 16, of which 12 were waited for; matrix products, arithmetic and copies ran while one was open for 21% of the time, Pallas kernels for 0%

profile of v11, /device:TPU:26, one launch (start us, length us, event | category | flops | bytes accessed | tf_op | source)
XLA Modules:
  0.0 145.9 jit_solution(1234789222695364054)
XLA Ops:
  7.9 1.5 concatenate.31
  9.3 1.9 %collective-permute-start = (bf16[3,33,256]{2,1,0:T(8,128)(2,1)S(1)}, bf16[3,33,256]{2,1,0:T(8,128)(2,1)S(1)}, u32[]{:S(2)}, u32[]{:S(2)}) collective-permute-start(bf16[3,33,256]{2,1,0:T(8,128)(2,1)S(1)} %concatenate.31), channel_id=1, source_target_pairs={{0,8},{8,0},{1,9},{9,1},{2,10},{10,2},{3,11},{11,3},{4,12},{12,4},... | collective-permute-start | bytes 152072 | tf_op jit(solution)/shard_map/ppermute | solution.py:40
  12.5 1.4 slice_select_fusion.1
  13.9 3.4 %collective-permute-start.1 = (bf16[3,66,128]{2,1,0:T(8,128)(2,1)S(1)}, bf16[3,66,128]{2,1,0:T(8,128)(2,1)S(1)}, u32[]{:S(2)}, u32[]{:S(2)}) collective-permute-start(bf16[3,66,128]{2,1,0:T(8,128)(2,1)S(1)} %pad_maximum_fusion), channel_id=1, source_target_pairs={{0,16},{16,32},{32,48},{48,0},{1,17},{17,33},{33,49},{49,1},{2,18}... | collective-permute-start | bytes 152072 | tf_op jit(solution)/shard_map/ppermute | solution.py:23
  17.3 2.6 %collective-permute-done.1 = bf16[3,66,128]{2,1,0:T(8,128)(2,1)S(1)} collective-permute-done((bf16[3,66,128]{2,1,0:T(8,128)(2,1)S(1)}, bf16[3,66,128]{2,1,0:T(8,128)(2,1)S(1)}, u32[]{:S(2)}, u32[]{:S(2)}) %collective-permute-start.1) | collective-permute-done | bytes 50720 | tf_op jit(solution)/shard_map/ppermute | solution.py:23
  20.0 3.4 %collective-permute-start.2 = (bf16[3,66,128]{2,1,0:T(8,128)(2,1)S(1)}, bf16[3,66,128]{2,1,0:T(8,128)(2,1)S(1)}, u32[]{:S(2)}, u32[]{:S(2)}) collective-permute-start(bf16[3,66,128]{2,1,0:T(8,128)(2,1)S(1)} %collective-permute-done.1), channel_id=1, source_target_pairs={{0,16},{16,32},{32,48},{48,0},{1,17},{17,33},{33,49},{49,1},{2,18}... | collective-permute-start | bytes 152072 | tf_op jit(solution)/shard_map/ppermute | solution.py:23
  23.4 2.4 %collective-permute-start.3 = (bf16[3,66,128]{2,1,0:T(8,128)(2,1)S(1)}, bf16[3,66,128]{2,1,0:T(8,128)(2,1)S(1)}, u32[]{:S(2)}, u32[]{:S(2)}) collective-permute-start(bf16[3,66,128]{2,1,0:T(8,128)(2,1)S(1)} %pad_maximum_fusion), channel_id=1, source_target_pairs={{0,48},{16,0},{32,16},{48,32},{1,49},{17,1},{33,17},{49,33},{2,50}... | collective-permute-start | bytes 152072 | tf_op jit(solution)/shard_map/ppermute | solution.py:26
  26.1 3.4 %collective-permute-done.3 = bf16[3,66,128]{2,1,0:T(8,128)(2,1)S(1)} collective-permute-done((bf16[3,66,128]{2,1,0:T(8,128)(2,1)S(1)}, bf16[3,66,128]{2,1,0:T(8,128)(2,1)S(1)}, u32[]{:S(2)}, u32[]{:S(2)}) %collective-permute-start.3) | collective-permute-done | bytes 50720 | tf_op jit(solution)/shard_map/ppermute | solution.py:26
  29.7 4.7 %collective-permute-start.4 = (bf16[3,264,128]{2,1,0:T(8,128)(2,1)S(1)}, bf16[3,264,128]{2,1,0:T(8,128)(2,1)S(1)}, u32[]{:S(2)}, u32[]{:S(2)}) collective-permute-start(bf16[3,264,128]{2,1,0:T(8,128)(2,1)S(1)} %reshape.183), channel_id=1, source_target_pairs={{0,64},{64,128},{128,192},{192,256},{256,320},{320,384},{384,448},... | collective-permute-start | bytes 608264 | tf_op jit(solution)/shard_map/ppermute | solution.py:23
  34.4 3.2 %collective-permute-done.4 = bf16[3,264,128]{2,1,0:T(8,128)(2,1)S(1)} collective-permute-done((bf16[3,264,128]{2,1,0:T(8,128)(2,1)S(1)}, bf16[3,264,128]{2,1,0:T(8,128)(2,1)S(1)}, u32[]{:S(2)}, u32[]{:S(2)}) %collective-permute-start.4) | collective-permute-done | bytes 202784 | tf_op jit(solution)/shard_map/ppermute | solution.py:23
  37.6 5.6 %collective-permute-start.5 = (bf16[3,264,128]{2,1,0:T(8,128)(2,1)S(1)}, bf16[3,264,128]{2,1,0:T(8,128)(2,1)S(1)}, u32[]{:S(2)}, u32[]{:S(2)}) collective-permute-start(bf16[3,264,128]{2,1,0:T(8,128)(2,1)S(1)} %collective-permute-done.4), channel_id=1, source_target_pairs={{0,64},{64,128},{128,192},{192,256},{256,320},{320,384},{384,448},... | collective-permute-start | bytes 608264 | tf_op jit(solution)/shard_map/ppermute | solution.py:23
  43.2 1.9 %collective-permute-start.8 = (bf16[3,264,128]{2,1,0:T(8,128)(2,1)S(1)}, bf16[3,264,128]{2,1,0:T(8,128)(2,1)S(1)}, u32[]{:S(2)}, u32[]{:S(2)}) collective-permute-start(bf16[3,264,128]{2,1,0:T(8,128)(2,1)S(1)} %reshape.183), channel_id=1, source_target_pairs={{0,448},{64,0},{128,64},{192,128},{256,192},{320,256},{384,320},{4... | collective-permute-start | bytes 608264 | tf_op jit(solution)/shard_map/ppermute | solution.py:26
  46.5 5.6 %collective-permute-start.6 = (bf16[3,264,128]{2,1,0:T(8,128)(2,1)S(1)}, bf16[3,264,128]{2,1,0:T(8,128)(2,1)S(1)}, u32[]{:S(2)}, u32[]{:S(2)}) collective-permute-start(bf16[3,264,128]{2,1,0:T(8,128)(2,1)S(1)} %collective-permute-done.5), channel_id=1, source_target_pairs={{0,64},{64,128},{128,192},{192,256},{256,320},{320,384},{384,448},... | collective-permute-start | bytes 608264 | tf_op jit(solution)/shard_map/ppermute | solution.py:23
  52.1 1.9 %collective-permute-start.9 = (bf16[3,264,128]{2,1,0:T(8,128)(2,1)S(1)}, bf16[3,264,128]{2,1,0:T(8,128)(2,1)S(1)}, u32[]{:S(2)}, u32[]{:S(2)}) collective-permute-start(bf16[3,264,128]{2,1,0:T(8,128)(2,1)S(1)} %collective-permute-done.8), channel_id=1, source_target_pairs={{0,448},{64,0},{128,64},{192,128},{256,192},{320,256},{384,320},{4... | collective-permute-start | bytes 608264 | tf_op jit(solution)/shard_map/ppermute | solution.py:26
  55.3 5.6 %collective-permute-start.7 = (bf16[3,264,128]{2,1,0:T(8,128)(2,1)S(1)}, bf16[3,264,128]{2,1,0:T(8,128)(2,1)S(1)}, u32[]{:S(2)}, u32[]{:S(2)}) collective-permute-start(bf16[3,264,128]{2,1,0:T(8,128)(2,1)S(1)} %collective-permute-done.6), channel_id=1, source_target_pairs={{0,64},{64,128},{128,192},{192,256},{256,320},{320,384},{384,448},... | collective-permute-start | bytes 608264 | tf_op jit(solution)/shard_map/ppermute | solution.py:23
  61.0 1.9 %collective-permute-start.10 = (bf16[3,264,128]{2,1,0:T(8,128)(2,1)S(1)}, bf16[3,264,128]{2,1,0:T(8,128)(2,1)S(1)}, u32[]{:S(2)}, u32[]{:S(2)}) collective-permute-start(bf16[3,264,128]{2,1,0:T(8,128)(2,1)S(1)} %collective-permute-done.9), channel_id=1, source_target_pairs={{0,448},{64,0},{128,64},{192,128},{256,192},{320,256},{384,320},{4... | collective-permute-start | bytes 608264 | tf_op jit(solution)/shard_map/ppermute | solution.py:26
  64.4 5.5 %collective-permute-done.10 = bf16[3,264,128]{2,1,0:T(8,128)(2,1)S(1)} collective-permute-done((bf16[3,264,128]{2,1,0:T(8,128)(2,1)S(1)}, bf16[3,264,128]{2,1,0:T(8,128)(2,1)S(1)}, u32[]{:S(2)}, u32[]{:S(2)}) %collective-permute-start.10) | collective-permute-done | bytes 202784 | tf_op jit(solution)/shard_map/ppermute | solution.py:26
  71.6 1.9 %collective-permute-start.11 = (bf16[3,2112,128]{2,1,0:T(8,128)(2,1)}, bf16[3,2112,128]{2,1,0:T(8,128)(2,1)}, u32[]{:S(2)}, u32[]{:S(2)}) collective-permute-start(bf16[3,2112,128]{2,1,0:T(8,128)(2,1)} %bitcast.14), channel_id=1, source_target_pairs={{0,8},{8,0},{1,9},{9,1},{2,10},{10,2},{3,11},{11,3},{4,12},{12,4},... | collective-permute-start | bytes 4866056 | tf_op jit(solution)/shard_map/ppermute | solution.py:46
  77.1 2.5 %concatenate.35 = bf16[3,64,33,128]{3,2,1,0:T(8,128)(2,1)S(1)} reshape(bf16[3,8,264,128]{3,2,1,0:T(8,128)(2,1)} %copy.31) | data formatting | bytes 3244032 | tf_op jit(solution)/shard_map/concatenate | solution.py:49
  79.6 3.7 %concatenate.36 = bf16[3,64,33,128]{3,2,1,0:T(8,128)(2,1)} reshape(bf16[3,2112,128]{2,1,0:T(8,128)(2,1)} %collective-permute-done.11) | data formatting | bytes 3244032 | tf_op jit(solution)/shard_map/concatenate | solution.py:49
  83.3 2.9 %maximum_select_fusion = bf16[3,64,33,256]{3,2,1,0:T(8,128)(2,1)S(1)} fusion(bf16[3,64,33,128]{3,2,1,0:T(8,128)(2,1)} %concatenate.36, bf16[3,64,33,128]{3,2,1,0:T(8,128)(2,1)S(1)} %concatenate.35, pred[]{:T(512)S(6)} %eq.87), kind=kLoop, calls=%fused_computation.4 | loop fusion | flops 14598144 | bytes 6488065 | tf_op jit(solution)/shard_map/jit(_where)/select_n | solution.py:47
  88.2 5.2 %all-gather.2.cloned.1.call-done = bf16[1024,2048]{1,0:T(8,128)(2,1)} async-done(((bf16[1024,256]{1,0:T(8,128)(2,1)}), bf16[1024,2048]{1,0:T(8,128)(2,1)}) %all-gather.2.cloned.1.call-update) | async-done | bytes 4194320 | tf_op jit(solution)/shard_map/all_gather | solution.py:91
  93.4 4.6 %fusion.7 = bf16[2,1024,256]{1,2,0:T(8,128)(2,1)S(1)} fusion(bf16[2,2048,256]{2,1,0:T(8,128)(2,1)S(1)} %bitcast.97, bf16[1024,2048]{1,0:T(8,128)(2,1)} %all-gather.2.cloned.1.call-done), kind=kOutput, calls=%fused_computation.17 | convolution fusion | flops 2148007936 | bytes 7340032 | tf_op jit(solution)/shard_map/tr,grc->gtc/dot_general | solution.py:100
  101.0 4.8 %all-to-all-start = ((f32[8,2,128,128]{3,2,1,0:T(8,128)}), f32[8,2,128,128]{3,2,1,0:T(8,128)S(1)}, u32[]{:S(2)}, u32[]{:S(2)}) async-start(f32[8,2,128,128]{3,2,1,0:T(8,128)} %broadcast_in_dim.115), calls=%async_computation | async-start | bytes 2097152 | tf_op jit(solution)/shard_map/all_to_all | solution.py:72
  108.2 4.2 %fusion.18 = bf16[1024,256]{0,1:T(8,128)(2,1)S(1)} fusion(bf16[2048,256]{1,0:T(8,128)(2,1)} %bitcast.101, bf16[1024,2048]{1,0:T(8,128)(2,1)} %all-gather.2.cloned.1.call-done), kind=kOutput, calls=%fused_computation.28 | convolution fusion | flops 1075314688 | bytes 5767168 | tf_op jit(solution)/shard_map/tr,rc->tc/dot_general | solution.py:113
  113.8 1.7 %slice.104 = bf16[1,512,256]{1,2,0:T(8,128)(2,1)} slice(bf16[2,1024,256]{1,2,0:T(8,128)(2,1)} %copy-done), slice={[1:2], [0:512], [0:256]} | slice | bytes 524288 | tf_op jit(solution)/shard_map/slice | solution.py:133
  117.0 1.9 %fusion.15 = f32[512,2,128]{0,2,1:T(8,128)S(1)} fusion(bf16[512,2,128]{0,2,1:T(8,128)(2,1)} %bitcast.105, bf16[512,2,128]{0,2,1:T(8,128)(2,1)} %bitcast.107, bf16[512,2,128]{0,2,1:T(8,128)(2,1)S(1)} %bitcast.104, pred[512,512]{1,0:T(8,128)(4,1)} %fusion.23), kind=kOutput, calls=%fused_computation.25 | convolution fusion | flops 269484032 | bytes 1572864 | tf_op jit(solution)/shard_map/hbs,she->bhe/dot_general | solution.py:133
  118.9 3.0 %fusion.14 = f32[512,2,128]{0,2,1:T(8,128)S(1)} fusion(bf16[1024,2,128]{0,2,1:T(8,128)(2,1)S(1)} %bitcast.103, bf16[512,2,128]{0,2,1:T(8,128)(2,1)} %bitcast.106, pred[512,1024]{1,0:T(8,128)(4,1)} %fusion.2, f32[1024,2,128]{0,2,1:T(8,128)} %bitcast.100), kind=kOutput, calls=%fused_computation.24 | convolution fusion | flops 540278784 | bytes 2883584 | tf_op jit(solution)/shard_map/hbs,she->bhe/dot_general | solution.py:133
  122.3 4.6 %collective-permute-start.13 = (f32[2,128,128]{2,1,0:T(8,128)S(1)}, f32[2,128,128]{2,1,0:T(8,128)S(1)}, u32[]{:S(2)}, u32[]{:S(2)}) collective-permute-start(f32[2,128,128]{2,1,0:T(8,128)S(1)} %get-tuple-element.10), channel_id=1, source_target_pairs={{0,128},{64,192},{128,256},{192,320},{256,384},{320,448},{1,129},{... | collective-permute-start | bytes 393224 | tf_op jit(solution)/shard_map/ppermute | solution.py:15
  126.9 2.5 %collective-permute-start.12 = (f32[2,128,128]{2,1,0:T(8,128)S(1)}, f32[2,128,128]{2,1,0:T(8,128)S(1)}, u32[]{:S(2)}, u32[]{:S(2)}) collective-permute-start(f32[2,128,128]{2,1,0:T(8,128)S(1)} %get-tuple-element.9), channel_id=1, source_target_pairs={{0,64},{64,128},{128,192},{192,256},{256,320},{320,384},{384,448},... | collective-permute-start | bytes 393224 | tf_op jit(solution)/shard_map/ppermute | solution.py:15
  129.4 4.1 %collective-permute-done.13 = f32[2,128,128]{2,1,0:T(8,128)S(1)} collective-permute-done((f32[2,128,128]{2,1,0:T(8,128)S(1)}, f32[2,128,128]{2,1,0:T(8,128)S(1)}, u32[]{:S(2)}, u32[]{:S(2)}) %collective-permute-start.13) | collective-permute-done | bytes 131104 | tf_op jit(solution)/shard_map/ppermute | solution.py:15
  133.5 3.9 %collective-permute-done.12 = f32[2,128,128]{2,1,0:T(8,128)S(1)} collective-permute-done((f32[2,128,128]{2,1,0:T(8,128)S(1)}, f32[2,128,128]{2,1,0:T(8,128)S(1)}, u32[]{:S(2)}, u32[]{:S(2)}) %collective-permute-start.12) | collective-permute-done | bytes 131104 | tf_op jit(solution)/shard_map/ppermute | solution.py:15
  (79 shorter events, 22.6 us)
Async XLA Ops:
  6.5 86.9 %all-gather.2.cloned.1.call-start = ((), (), s32[]{:S(2)}) async-start(), calls=%async_computation.1 | async-start | bytes 4718592 | tf_op jit(solution)/shard_map/all_gather | solution.py:91
  9.3 3.1 %collective-permute-start = (bf16[3,33,256]{2,1,0:T(8,128)(2,1)S(1)}, bf16[3,33,256]{2,1,0:T(8,128)(2,1)S(1)}, u32[]{:S(2)}, u32[]{:S(2)}) collective-permute-start(bf16[3,33,256]{2,1,0:T(8,128)(2,1)S(1)} %concatenate.31), channel_id=1, source_target_pairs={{0,8},{8,0},{1,9},{9,1},{2,10},{10,2},{3,11},{11,3},{4,12},{12,4},... | collective-permute-start | bytes 152072 | tf_op jit(solution)/shard_map/ppermute | solution.py:40
  13.9 6.0 %collective-permute-start.1 = (bf16[3,66,128]{2,1,0:T(8,128)(2,1)S(1)}, bf16[3,66,128]{2,1,0:T(8,128)(2,1)S(1)}, u32[]{:S(2)}, u32[]{:S(2)}) collective-permute-start(bf16[3,66,128]{2,1,0:T(8,128)(2,1)S(1)} %pad_maximum_fusion), channel_id=1, source_target_pairs={{0,16},{16,32},{32,48},{48,0},{1,17},{17,33},{33,49},{49,1},{2,18}... | collective-permute-start | bytes 152072 | tf_op jit(solution)/shard_map/ppermute | solution.py:23
  20.0 6.0 %collective-permute-start.2 = (bf16[3,66,128]{2,1,0:T(8,128)(2,1)S(1)}, bf16[3,66,128]{2,1,0:T(8,128)(2,1)S(1)}, u32[]{:S(2)}, u32[]{:S(2)}) collective-permute-start(bf16[3,66,128]{2,1,0:T(8,128)(2,1)S(1)} %collective-permute-done.1), channel_id=1, source_target_pairs={{0,16},{16,32},{32,48},{48,0},{1,17},{17,33},{33,49},{49,1},{2,18}... | collective-permute-start | bytes 152072 | tf_op jit(solution)/shard_map/ppermute | solution.py:23
  23.4 6.0 %collective-permute-start.3 = (bf16[3,66,128]{2,1,0:T(8,128)(2,1)S(1)}, bf16[3,66,128]{2,1,0:T(8,128)(2,1)S(1)}, u32[]{:S(2)}, u32[]{:S(2)}) collective-permute-start(bf16[3,66,128]{2,1,0:T(8,128)(2,1)S(1)} %pad_maximum_fusion), channel_id=1, source_target_pairs={{0,48},{16,0},{32,16},{48,32},{1,49},{17,1},{33,17},{49,33},{2,50}... | collective-permute-start | bytes 152072 | tf_op jit(solution)/shard_map/ppermute | solution.py:26
  29.7 7.9 %collective-permute-start.4 = (bf16[3,264,128]{2,1,0:T(8,128)(2,1)S(1)}, bf16[3,264,128]{2,1,0:T(8,128)(2,1)S(1)}, u32[]{:S(2)}, u32[]{:S(2)}) collective-permute-start(bf16[3,264,128]{2,1,0:T(8,128)(2,1)S(1)} %reshape.183), channel_id=1, source_target_pairs={{0,64},{64,128},{128,192},{192,256},{256,320},{320,384},{384,448},... | collective-permute-start | bytes 608264 | tf_op jit(solution)/shard_map/ppermute | solution.py:23
  37.6 8.8 %collective-permute-start.5 = (bf16[3,264,128]{2,1,0:T(8,128)(2,1)S(1)}, bf16[3,264,128]{2,1,0:T(8,128)(2,1)S(1)}, u32[]{:S(2)}, u32[]{:S(2)}) collective-permute-start(bf16[3,264,128]{2,1,0:T(8,128)(2,1)S(1)} %collective-permute-done.4), channel_id=1, source_target_pairs={{0,64},{64,128},{128,192},{192,256},{256,320},{320,384},{384,448},... | collective-permute-start | bytes 608264 | tf_op jit(solution)/shard_map/ppermute | solution.py:23
  43.2 8.8 %collective-permute-start.8 = (bf16[3,264,128]{2,1,0:T(8,128)(2,1)S(1)}, bf16[3,264,128]{2,1,0:T(8,128)(2,1)S(1)}, u32[]{:S(2)}, u32[]{:S(2)}) collective-permute-start(bf16[3,264,128]{2,1,0:T(8,128)(2,1)S(1)} %reshape.183), channel_id=1, source_target_pairs={{0,448},{64,0},{128,64},{192,128},{256,192},{320,256},{384,320},{4... | collective-permute-start | bytes 608264 | tf_op jit(solution)/shard_map/ppermute | solution.py:26
  46.5 8.8 %collective-permute-start.6 = (bf16[3,264,128]{2,1,0:T(8,128)(2,1)S(1)}, bf16[3,264,128]{2,1,0:T(8,128)(2,1)S(1)}, u32[]{:S(2)}, u32[]{:S(2)}) collective-permute-start(bf16[3,264,128]{2,1,0:T(8,128)(2,1)S(1)} %collective-permute-done.5), channel_id=1, source_target_pairs={{0,64},{64,128},{128,192},{192,256},{256,320},{320,384},{384,448},... | collective-permute-start | bytes 608264 | tf_op jit(solution)/shard_map/ppermute | solution.py:23
  52.1 8.9 %collective-permute-start.9 = (bf16[3,264,128]{2,1,0:T(8,128)(2,1)S(1)}, bf16[3,264,128]{2,1,0:T(8,128)(2,1)S(1)}, u32[]{:S(2)}, u32[]{:S(2)}) collective-permute-start(bf16[3,264,128]{2,1,0:T(8,128)(2,1)S(1)} %collective-permute-done.8), channel_id=1, source_target_pairs={{0,448},{64,0},{128,64},{192,128},{256,192},{320,256},{384,320},{4... | collective-permute-start | bytes 608264 | tf_op jit(solution)/shard_map/ppermute | solution.py:26
  55.3 8.8 %collective-permute-start.7 = (bf16[3,264,128]{2,1,0:T(8,128)(2,1)S(1)}, bf16[3,264,128]{2,1,0:T(8,128)(2,1)S(1)}, u32[]{:S(2)}, u32[]{:S(2)}) collective-permute-start(bf16[3,264,128]{2,1,0:T(8,128)(2,1)S(1)} %collective-permute-done.6), channel_id=1, source_target_pairs={{0,64},{64,128},{128,192},{192,256},{256,320},{320,384},{384,448},... | collective-permute-start | bytes 608264 | tf_op jit(solution)/shard_map/ppermute | solution.py:23
  61.0 8.8 %collective-permute-start.10 = (bf16[3,264,128]{2,1,0:T(8,128)(2,1)S(1)}, bf16[3,264,128]{2,1,0:T(8,128)(2,1)S(1)}, u32[]{:S(2)}, u32[]{:S(2)}) collective-permute-start(bf16[3,264,128]{2,1,0:T(8,128)(2,1)S(1)} %collective-permute-done.9), channel_id=1, source_target_pairs={{0,448},{64,0},{128,64},{192,128},{256,192},{320,256},{384,320},{4... | collective-permute-start | bytes 608264 | tf_op jit(solution)/shard_map/ppermute | solution.py:26
  70.2 4.0 %copy-start.2 = (s32[1024]{0:T(1024)S(1)}, s32[1024]{0:T(1024)}, u32[]{:S(2)}) copy-start(s32[1024]{0:T(1024)} %param.7) | copy-start | bytes 12292
  71.6 8.0 %collective-permute-start.11 = (bf16[3,2112,128]{2,1,0:T(8,128)(2,1)}, bf16[3,2112,128]{2,1,0:T(8,128)(2,1)}, u32[]{:S(2)}, u32[]{:S(2)}) collective-permute-start(bf16[3,2112,128]{2,1,0:T(8,128)(2,1)} %bitcast.14), channel_id=1, source_target_pairs={{0,8},{8,0},{1,9},{9,1},{2,10},{10,2},{3,11},{11,3},{4,12},{12,4},... | collective-permute-start | bytes 4866056 | tf_op jit(solution)/shard_map/ppermute | solution.py:46
  98.0 2.0 %copy-start = (bf16[2,1024,256]{1,2,0:T(8,128)(2,1)}, bf16[2,1024,256]{1,2,0:T(8,128)(2,1)S(1)}, u32[]{:S(2)}) copy-start(bf16[2,1024,256]{1,2,0:T(8,128)(2,1)S(1)} %fusion.7) | copy-start | bytes 3145732
  98.2 1.2 copy-start.1
  101.0 20.9 %all-to-all-start = ((f32[8,2,128,128]{3,2,1,0:T(8,128)}), f32[8,2,128,128]{3,2,1,0:T(8,128)S(1)}, u32[]{:S(2)}, u32[]{:S(2)}) async-start(f32[8,2,128,128]{3,2,1,0:T(8,128)} %broadcast_in_dim.115), calls=%async_computation | async-start | bytes 2097152 | tf_op jit(solution)/shard_map/all_to_all | solution.py:72
  121.9 15.9 %copy-start.3 = (f32[256]{0:T(256)S(1)}, f32[256]{0:T(256)}, u32[]{:S(2)}) copy-start(f32[256]{0:T(256)} %param.6) | copy-start | bytes 3076
  122.3 11.2 %collective-permute-start.13 = (f32[2,128,128]{2,1,0:T(8,128)S(1)}, f32[2,128,128]{2,1,0:T(8,128)S(1)}, u32[]{:S(2)}, u32[]{:S(2)}) collective-permute-start(f32[2,128,128]{2,1,0:T(8,128)S(1)} %get-tuple-element.10), channel_id=1, source_target_pairs={{0,128},{64,192},{128,256},{192,320},{256,384},{320,448},{1,129},{... | collective-permute-start | bytes 393224 | tf_op jit(solution)/shard_map/ppermute | solution.py:15
  126.9 10.5 %collective-permute-start.12 = (f32[2,128,128]{2,1,0:T(8,128)S(1)}, f32[2,128,128]{2,1,0:T(8,128)S(1)}, u32[]{:S(2)}, u32[]{:S(2)}) collective-permute-start(f32[2,128,128]{2,1,0:T(8,128)S(1)} %get-tuple-element.9), channel_id=1, source_target_pairs={{0,64},{64,128},{128,192},{192,256},{256,320},{320,384},{384,448},... | collective-permute-start | bytes 393224 | tf_op jit(solution)/shard_map/ppermute | solution.py:15
Sparse Core Ops, SparseCore 0:
  23.5 69.8 all-gather.1

commit v12 on v11

--- a/solution.py
+++ b/solution.py
@@ -68,8 +68,8 @@
         return jnp.where(block >= 0, tails[jnp.clip(block, 0, count - 1)], -1.0)
 
     prev_tail = tail_of(me - 1)
-    spread = jnp.broadcast_to(kv_state[None], (row_len,) + kv_state.shape)
-    row = lax.all_to_all(spread, ("x", "core"), 0, 0, tiled=True)
+    spread = jnp.broadcast_to(kv_state.astype(jnp.bfloat16)[None], (row_len,) + kv_state.shape)
+    row = lax.all_to_all(spread, ("x", "core"), 0, 0, tiled=True).astype(jnp.float32)
     places = jnp.arange(row_len)
     row_tails = tail_of(first + places)
     in_last = row_tails == row_tails[row_len - 1]
@@ -78,8 +78,10 @@
         return jnp.sum(jnp.where(mask[:, None, None, None], row, 0.0), axis=0)
 
     y_count = lax.axis_size("y")
-    one_back = shifted(masked(in_last), "y", 1, y_count)
-    two_back = shifted(masked(in_last & (places >= pos)), "y", 2, y_count)
+    one_back = shifted(masked(in_last).astype(jnp.bfloat16), "y", 1, y_count).astype(jnp.float32)
+    two_back = shifted(
+        masked(in_last & (places >= pos)).astype(jnp.bfloat16), "y", 2, y_count
+    ).astype(jnp.float32)
     state = masked((places < pos) & (row_tails == prev_tail))
     state = state + jnp.where(tail_of(first - 1) == prev_tail, one_back, 0.0)
     if window > row_len:

time: 147 us -> 140 us (0.952)
  the two profiles are of different devices: /device:TPU:26 before, /device:TPU:18 now
where the time goes in v12:
time: 140 us; the launch traced here: 139 us
  starting transfers between devices  48.8 us (35%)
  waiting for transfers between devices  31.9 us (23%)
  local copies, waits for them, and re-layouts  17.8 us (13%)
  between operations  15.9 us (11%)
  matrix products  14.4 us (10%)
  other arithmetic  10.2 us (7%)
    ppermute x6, starting transfers between devices, ring_gather(): lax.ppermute(ahead, axis, [(j, (j + 1) % count) for j in range(count)])  23.7 us
    ppermute x6, waiting for transfers between devices, ring_gather(): lax.ppermute(ahead, axis, [(j, (j + 1) % count) for j in range(count)])  11.9 us
    ppermute x4, waiting for transfers between devices, ring_gather(): lax.ppermute(behind, axis, [(j, (j - 1) % count) for j in range(count)])  9.46 us
    ppermute x4, starting transfers between devices, ring_gather(): lax.ppermute(behind, axis, [(j, (j - 1) % count) for j in range(count)])  8.48 us
    ppermute x2, starting transfers between devices, shifted(): lax.ppermute(value, axis, [(source, source + steps) for source in range(c...  8.03 us
    all_gather x1, waiting for transfers between devices, per_device(): whole = lax.all_gather(tokens, 'head', axis=1, tiled=True)  6.91 us
    concatenate x2, local copies, waits for them, and re-layouts, gather_weights(): jnp.concatenate([rows, other], axis=2)  6.17 us
    all_to_all x1, starting transfers between devices, state_scan(): lax.all_to_all(spread, ('x', 'core'), 0, 0, tiled=True).astype(jnp.float32)  4.81 us
  transfers between devices with their start and end apart: 16, of which 13 were waited for; matrix products, arithmetic and copies ran while one was open for 21% of the time, Pallas kernels for 0%

profile of v12, /device:TPU:18, one launch (start us, length us, event | category | flops | bytes accessed | tf_op | source)
XLA Modules:
  0.0 139.0 jit_solution(3170597371363449845)
XLA Ops:
  7.9 1.5 %concatenate.31 = bf16[3,33,256]{2,1,0:T(8,128)(2,1)S(1)} pad(bf16[3,32,256]{2,1,0:T(8,128)(2,1)} %param.5, bf16[]{:T(256)} %bitcast), padding=0_0x0_1x0_0 | pad | bytes 99842 | tf_op jit(solution)/shard_map/concatenate | solution.py:98
  9.3 1.9 %collective-permute-start = (bf16[3,33,256]{2,1,0:T(8,128)(2,1)S(1)}, bf16[3,33,256]{2,1,0:T(8,128)(2,1)S(1)}, u32[]{:S(2)}, u32[]{:S(2)}) collective-permute-start(bf16[3,33,256]{2,1,0:T(8,128)(2,1)S(1)} %concatenate.31), channel_id=1, source_target_pairs={{0,8},{8,0},{1,9},{9,1},{2,10},{10,2},{3,11},{11,3},{4,12},{12,4},... | collective-permute-start | bytes 152072 | tf_op jit(solution)/shard_map/ppermute | solution.py:40
  13.9 3.4 %collective-permute-start.1 = (bf16[3,66,128]{2,1,0:T(8,128)(2,1)S(1)}, bf16[3,66,128]{2,1,0:T(8,128)(2,1)S(1)}, u32[]{:S(2)}, u32[]{:S(2)}) collective-permute-start(bf16[3,66,128]{2,1,0:T(8,128)(2,1)S(1)} %pad_maximum_fusion), channel_id=1, source_target_pairs={{0,16},{16,32},{32,48},{48,0},{1,17},{17,33},{33,49},{49,1},{2,18}... | collective-permute-start | bytes 152072 | tf_op jit(solution)/shard_map/ppermute | solution.py:23
  17.3 2.6 %collective-permute-done.1 = bf16[3,66,128]{2,1,0:T(8,128)(2,1)S(1)} collective-permute-done((bf16[3,66,128]{2,1,0:T(8,128)(2,1)S(1)}, bf16[3,66,128]{2,1,0:T(8,128)(2,1)S(1)}, u32[]{:S(2)}, u32[]{:S(2)}) %collective-permute-start.1) | collective-permute-done | bytes 50720 | tf_op jit(solution)/shard_map/ppermute | solution.py:23
  20.0 3.4 %collective-permute-start.2 = (bf16[3,66,128]{2,1,0:T(8,128)(2,1)S(1)}, bf16[3,66,128]{2,1,0:T(8,128)(2,1)S(1)}, u32[]{:S(2)}, u32[]{:S(2)}) collective-permute-start(bf16[3,66,128]{2,1,0:T(8,128)(2,1)S(1)} %collective-permute-done.1), channel_id=1, source_target_pairs={{0,16},{16,32},{32,48},{48,0},{1,17},{17,33},{33,49},{49,1},{2,18}... | collective-permute-start | bytes 152072 | tf_op jit(solution)/shard_map/ppermute | solution.py:23
  23.4 2.4 %collective-permute-start.3 = (bf16[3,66,128]{2,1,0:T(8,128)(2,1)S(1)}, bf16[3,66,128]{2,1,0:T(8,128)(2,1)S(1)}, u32[]{:S(2)}, u32[]{:S(2)}) collective-permute-start(bf16[3,66,128]{2,1,0:T(8,128)(2,1)S(1)} %pad_maximum_fusion), channel_id=1, source_target_pairs={{0,48},{16,0},{32,16},{48,32},{1,49},{17,1},{33,17},{49,33},{2,50}... | collective-permute-start | bytes 152072 | tf_op jit(solution)/shard_map/ppermute | solution.py:26
  26.1 3.4 %collective-permute-done.3 = bf16[3,66,128]{2,1,0:T(8,128)(2,1)S(1)} collective-permute-done((bf16[3,66,128]{2,1,0:T(8,128)(2,1)S(1)}, bf16[3,66,128]{2,1,0:T(8,128)(2,1)S(1)}, u32[]{:S(2)}, u32[]{:S(2)}) %collective-permute-start.3) | collective-permute-done | bytes 50720 | tf_op jit(solution)/shard_map/ppermute | solution.py:26
  29.7 3.5 %collective-permute-start.4 = (bf16[3,264,128]{2,1,0:T(8,128)(2,1)S(1)}, bf16[3,264,128]{2,1,0:T(8,128)(2,1)S(1)}, u32[]{:S(2)}, u32[]{:S(2)}) collective-permute-start(bf16[3,264,128]{2,1,0:T(8,128)(2,1)S(1)} %reshape.183), channel_id=1, source_target_pairs={{0,64},{64,128},{128,192},{192,256},{256,320},{320,384},{384,448},... | collective-permute-start | bytes 608264 | tf_op jit(solution)/shard_map/ppermute | solution.py:23
  33.2 4.1 %collective-permute-done.4 = bf16[3,264,128]{2,1,0:T(8,128)(2,1)S(1)} collective-permute-done((bf16[3,264,128]{2,1,0:T(8,128)(2,1)S(1)}, bf16[3,264,128]{2,1,0:T(8,128)(2,1)S(1)}, u32[]{:S(2)}, u32[]{:S(2)}) %collective-permute-start.4) | collective-permute-done | bytes 202784 | tf_op jit(solution)/shard_map/ppermute | solution.py:23
  37.3 3.8 %collective-permute-start.5 = (bf16[3,264,128]{2,1,0:T(8,128)(2,1)S(1)}, bf16[3,264,128]{2,1,0:T(8,128)(2,1)S(1)}, u32[]{:S(2)}, u32[]{:S(2)}) collective-permute-start(bf16[3,264,128]{2,1,0:T(8,128)(2,1)S(1)} %collective-permute-done.4), channel_id=1, source_target_pairs={{0,64},{64,128},{128,192},{192,256},{256,320},{320,384},{384,448},... | collective-permute-start | bytes 608264 | tf_op jit(solution)/shard_map/ppermute | solution.py:23
  41.1 2.2 %collective-permute-start.8 = (bf16[3,264,128]{2,1,0:T(8,128)(2,1)S(1)}, bf16[3,264,128]{2,1,0:T(8,128)(2,1)S(1)}, u32[]{:S(2)}, u32[]{:S(2)}) collective-permute-start(bf16[3,264,128]{2,1,0:T(8,128)(2,1)S(1)} %reshape.183), channel_id=1, source_target_pairs={{0,448},{64,0},{128,64},{192,128},{256,192},{320,256},{384,320},{4... | collective-permute-start | bytes 608264 | tf_op jit(solution)/shard_map/ppermute | solution.py:26
  43.3 1.8 %collective-permute-done.5 = bf16[3,264,128]{2,1,0:T(8,128)(2,1)S(1)} collective-permute-done((bf16[3,264,128]{2,1,0:T(8,128)(2,1)S(1)}, bf16[3,264,128]{2,1,0:T(8,128)(2,1)S(1)}, u32[]{:S(2)}, u32[]{:S(2)}) %collective-permute-start.5) | collective-permute-done | bytes 202784 | tf_op jit(solution)/shard_map/ppermute | solution.py:23
  45.1 4.8 %collective-permute-start.6 = (bf16[3,264,128]{2,1,0:T(8,128)(2,1)S(1)}, bf16[3,264,128]{2,1,0:T(8,128)(2,1)S(1)}, u32[]{:S(2)}, u32[]{:S(2)}) collective-permute-start(bf16[3,264,128]{2,1,0:T(8,128)(2,1)S(1)} %collective-permute-done.5), channel_id=1, source_target_pairs={{0,64},{64,128},{128,192},{192,256},{256,320},{320,384},{384,448},... | collective-permute-start | bytes 608264 | tf_op jit(solution)/shard_map/ppermute | solution.py:23
  50.4 1.9 %collective-permute-start.9 = (bf16[3,264,128]{2,1,0:T(8,128)(2,1)S(1)}, bf16[3,264,128]{2,1,0:T(8,128)(2,1)S(1)}, u32[]{:S(2)}, u32[]{:S(2)}) collective-permute-start(bf16[3,264,128]{2,1,0:T(8,128)(2,1)S(1)} %collective-permute-done.8), channel_id=1, source_target_pairs={{0,448},{64,0},{128,64},{192,128},{256,192},{320,256},{384,320},{4... | collective-permute-start | bytes 608264 | tf_op jit(solution)/shard_map/ppermute | solution.py:26
  52.3 1.6 %collective-permute-done.6 = bf16[3,264,128]{2,1,0:T(8,128)(2,1)S(1)} collective-permute-done((bf16[3,264,128]{2,1,0:T(8,128)(2,1)S(1)}, bf16[3,264,128]{2,1,0:T(8,128)(2,1)S(1)}, u32[]{:S(2)}, u32[]{:S(2)}) %collective-permute-start.6) | collective-permute-done | bytes 202784 | tf_op jit(solution)/shard_map/ppermute | solution.py:23
  53.9 4.8 %collective-permute-start.7 = (bf16[3,264,128]{2,1,0:T(8,128)(2,1)S(1)}, bf16[3,264,128]{2,1,0:T(8,128)(2,1)S(1)}, u32[]{:S(2)}, u32[]{:S(2)}) collective-permute-start(bf16[3,264,128]{2,1,0:T(8,128)(2,1)S(1)} %collective-permute-done.6), channel_id=1, source_target_pairs={{0,64},{64,128},{128,192},{192,256},{256,320},{320,384},{384,448},... | collective-permute-start | bytes 608264 | tf_op jit(solution)/shard_map/ppermute | solution.py:23
  59.3 1.9 %collective-permute-start.10 = (bf16[3,264,128]{2,1,0:T(8,128)(2,1)S(1)}, bf16[3,264,128]{2,1,0:T(8,128)(2,1)S(1)}, u32[]{:S(2)}, u32[]{:S(2)}) collective-permute-start(bf16[3,264,128]{2,1,0:T(8,128)(2,1)S(1)} %collective-permute-done.9), channel_id=1, source_target_pairs={{0,448},{64,0},{128,64},{192,128},{256,192},{320,256},{384,320},{4... | collective-permute-start | bytes 608264 | tf_op jit(solution)/shard_map/ppermute | solution.py:26
  61.2 1.6 %collective-permute-done.7 = bf16[3,264,128]{2,1,0:T(8,128)(2,1)S(1)} collective-permute-done((bf16[3,264,128]{2,1,0:T(8,128)(2,1)S(1)}, bf16[3,264,128]{2,1,0:T(8,128)(2,1)S(1)}, u32[]{:S(2)}, u32[]{:S(2)}) %collective-permute-start.7) | collective-permute-done | bytes 202784 | tf_op jit(solution)/shard_map/ppermute | solution.py:23
  63.0 5.2 %collective-permute-done.10 = bf16[3,264,128]{2,1,0:T(8,128)(2,1)S(1)} collective-permute-done((bf16[3,264,128]{2,1,0:T(8,128)(2,1)S(1)}, bf16[3,264,128]{2,1,0:T(8,128)(2,1)S(1)}, u32[]{:S(2)}, u32[]{:S(2)}) %collective-permute-start.10) | collective-permute-done | bytes 202784 | tf_op jit(solution)/shard_map/ppermute | solution.py:26
  70.0 1.9 %collective-permute-start.11 = (bf16[3,2112,128]{2,1,0:T(8,128)(2,1)}, bf16[3,2112,128]{2,1,0:T(8,128)(2,1)}, u32[]{:S(2)}, u32[]{:S(2)}) collective-permute-start(bf16[3,2112,128]{2,1,0:T(8,128)(2,1)} %bitcast.14), channel_id=1, source_target_pairs={{0,8},{8,0},{1,9},{9,1},{2,10},{10,2},{3,11},{11,3},{4,12},{12,4},... | collective-permute-start | bytes 4866056 | tf_op jit(solution)/shard_map/ppermute | solution.py:46
  75.5 2.5 %concatenate.35 = bf16[3,64,33,128]{3,2,1,0:T(8,128)(2,1)S(1)} reshape(bf16[3,8,264,128]{3,2,1,0:T(8,128)(2,1)} %copy.31) | data formatting | bytes 3244032 | tf_op jit(solution)/shard_map/concatenate | solution.py:49
  78.0 3.7 %concatenate.36 = bf16[3,64,33,128]{3,2,1,0:T(8,128)(2,1)} reshape(bf16[3,2112,128]{2,1,0:T(8,128)(2,1)} %collective-permute-done.11) | data formatting | bytes 3244032 | tf_op jit(solution)/shard_map/concatenate | solution.py:49
  81.7 2.9 %maximum_select_fusion = bf16[3,64,33,256]{3,2,1,0:T(8,128)(2,1)S(1)} fusion(bf16[3,64,33,128]{3,2,1,0:T(8,128)(2,1)} %concatenate.36, bf16[3,64,33,128]{3,2,1,0:T(8,128)(2,1)S(1)} %concatenate.35, pred[]{:T(512)S(6)} %eq.87), kind=kLoop, calls=%fused_computation.4 | loop fusion | flops 14598144 | bytes 6488065 | tf_op jit(solution)/shard_map/jit(_where)/select_n | solution.py:47
  86.6 6.9 %all-gather.2.cloned.1.call-done = bf16[1024,2048]{1,0:T(8,128)(2,1)} async-done(((bf16[1024,256]{1,0:T(8,128)(2,1)}), bf16[1024,2048]{1,0:T(8,128)(2,1)}) %all-gather.2.cloned.1.call-update) | async-done | bytes 4194320 | tf_op jit(solution)/shard_map/all_gather | solution.py:93
  93.5 4.6 %fusion.7 = bf16[2,1024,256]{1,2,0:T(8,128)(2,1)S(1)} fusion(bf16[2,2048,256]{2,1,0:T(8,128)(2,1)S(1)} %bitcast.97, bf16[1024,2048]{1,0:T(8,128)(2,1)} %all-gather.2.cloned.1.call-done), kind=kOutput, calls=%fused_computation.20 | convolution fusion | flops 2148007936 | bytes 7340032 | tf_op jit(solution)/shard_map/tr,grc->gtc/dot_general | solution.py:102
  100.6 4.8 %all-to-all-start = ((bf16[8,2,128,128]{3,2,1,0:T(8,128)(2,1)}), bf16[8,2,128,128]{3,2,1,0:T(8,128)(2,1)S(1)}, u32[]{:S(2)}, u32[]{:S(2)}) async-start(bf16[8,2,128,128]{3,2,1,0:T(8,128)(2,1)} %broadcast_in_dim.115), calls=%async_computation | async-start | bytes 1048576 | tf_op jit(solution)/shard_map/all_to_all | solution.py:72
  107.9 4.2 %fusion.21 = bf16[1024,256]{0,1:T(8,128)(2,1)S(1)} fusion(bf16[2048,256]{1,0:T(8,128)(2,1)} %bitcast.101, bf16[1024,2048]{1,0:T(8,128)(2,1)} %all-gather.2.cloned.1.call-done), kind=kOutput, calls=%fused_computation.34 | convolution fusion | flops 1075314688 | bytes 5767168 | tf_op jit(solution)/shard_map/tr,rc->tc/dot_general | solution.py:115
  113.2 1.9 %fusion.15 = f32[512,2,128]{0,2,1:T(8,128)S(1)} fusion(bf16[512,2,128]{0,2,1:T(8,128)(2,1)} %bitcast.105, bf16[512,2,128]{0,2,1:T(8,128)(2,1)} %bitcast.107, bf16[512,2,128]{0,2,1:T(8,128)(2,1)S(1)} %bitcast.104, pred[512,512]{1,0:T(8,128)(4,1)} %fusion.26), kind=kOutput, calls=%fused_computation.28 | convolution fusion | flops 269484032 | bytes 1572864 | tf_op jit(solution)/shard_map/hbs,she->bhe/dot_general | solution.py:135
  115.6 2.8 %fusion.14 = f32[512,2,128]{0,2,1:T(8,128)S(1)} fusion(bf16[1024,2,128]{0,2,1:T(8,128)(2,1)} %bitcast.103, bf16[512,2,128]{0,2,1:T(8,128)(2,1)} %bitcast.106, pred[512,1024]{1,0:T(8,128)(4,1)} %fusion.2, f32[1024,2,128]{0,2,1:T(8,128)S(1)} %bitcast.100), kind=kOutput, calls=%fused_computation.27 | convolution fusion | flops 540278784 | bytes 2883584 | tf_op jit(solution)/shard_map/hbs,she->bhe/dot_general | solution.py:135
  118.9 5.6 %collective-permute-start.13 = (bf16[2,128,128]{2,1,0:T(8,128)(2,1)S(1)}, bf16[2,128,128]{2,1,0:T(8,128)(2,1)S(1)}, u32[]{:S(2)}, u32[]{:S(2)}) collective-permute-start(bf16[2,128,128]{2,1,0:T(8,128)(2,1)S(1)} %get-tuple-element.10), channel_id=1, source_target_pairs={{0,128},{64,192},{128,256},{192,320},{256,384},{320,448},{1,129},{... | collective-permute-start | bytes 196616 | tf_op jit(solution)/shard_map/ppermute | solution.py:15
  124.5 2.4 %collective-permute-start.12 = (bf16[2,128,128]{2,1,0:T(8,128)(2,1)S(1)}, bf16[2,128,128]{2,1,0:T(8,128)(2,1)S(1)}, u32[]{:S(2)}, u32[]{:S(2)}) collective-permute-start(bf16[2,128,128]{2,1,0:T(8,128)(2,1)S(1)} %get-tuple-element.9), channel_id=1, source_target_pairs={{0,64},{64,128},{128,192},{192,256},{256,320},{320,384},{384,448},... | collective-permute-start | bytes 196616 | tf_op jit(solution)/shard_map/ppermute | solution.py:15
  128.2 2.5 %collective-permute-done.12 = bf16[2,128,128]{2,1,0:T(8,128)(2,1)S(1)} collective-permute-done((bf16[2,128,128]{2,1,0:T(8,128)(2,1)S(1)}, bf16[2,128,128]{2,1,0:T(8,128)(2,1)S(1)}, u32[]{:S(2)}, u32[]{:S(2)}) %collective-permute-start.12) | collective-permute-done | bytes 65568 | tf_op jit(solution)/shard_map/ppermute | solution.py:15
  (77 shorter events, 20.6 us)
Async XLA Ops:
  6.5 86.9 %all-gather.2.cloned.1.call-start = ((), (), s32[]{:S(2)}) async-start(), calls=%async_computation.1 | async-start | bytes 4718592 | tf_op jit(solution)/shard_map/all_gather | solution.py:93
  9.3 3.1 %collective-permute-start = (bf16[3,33,256]{2,1,0:T(8,128)(2,1)S(1)}, bf16[3,33,256]{2,1,0:T(8,128)(2,1)S(1)}, u32[]{:S(2)}, u32[]{:S(2)}) collective-permute-start(bf16[3,33,256]{2,1,0:T(8,128)(2,1)S(1)} %concatenate.31), channel_id=1, source_target_pairs={{0,8},{8,0},{1,9},{9,1},{2,10},{10,2},{3,11},{11,3},{4,12},{12,4},... | collective-permute-start | bytes 152072 | tf_op jit(solution)/shard_map/ppermute | solution.py:40
  13.9 6.0 %collective-permute-start.1 = (bf16[3,66,128]{2,1,0:T(8,128)(2,1)S(1)}, bf16[3,66,128]{2,1,0:T(8,128)(2,1)S(1)}, u32[]{:S(2)}, u32[]{:S(2)}) collective-permute-start(bf16[3,66,128]{2,1,0:T(8,128)(2,1)S(1)} %pad_maximum_fusion), channel_id=1, source_target_pairs={{0,16},{16,32},{32,48},{48,0},{1,17},{17,33},{33,49},{49,1},{2,18}... | collective-permute-start | bytes 152072 | tf_op jit(solution)/shard_map/ppermute | solution.py:23
  20.0 6.0 %collective-permute-start.2 = (bf16[3,66,128]{2,1,0:T(8,128)(2,1)S(1)}, bf16[3,66,128]{2,1,0:T(8,128)(2,1)S(1)}, u32[]{:S(2)}, u32[]{:S(2)}) collective-permute-start(bf16[3,66,128]{2,1,0:T(8,128)(2,1)S(1)} %collective-permute-done.1), channel_id=1, source_target_pairs={{0,16},{16,32},{32,48},{48,0},{1,17},{17,33},{33,49},{49,1},{2,18}... | collective-permute-start | bytes 152072 | tf_op jit(solution)/shard_map/ppermute | solution.py:23
  23.4 6.0 %collective-permute-start.3 = (bf16[3,66,128]{2,1,0:T(8,128)(2,1)S(1)}, bf16[3,66,128]{2,1,0:T(8,128)(2,1)S(1)}, u32[]{:S(2)}, u32[]{:S(2)}) collective-permute-start(bf16[3,66,128]{2,1,0:T(8,128)(2,1)S(1)} %pad_maximum_fusion), channel_id=1, source_target_pairs={{0,48},{16,0},{32,16},{48,32},{1,49},{17,1},{33,17},{49,33},{2,50}... | collective-permute-start | bytes 152072 | tf_op jit(solution)/shard_map/ppermute | solution.py:26
  29.7 7.6 %collective-permute-start.4 = (bf16[3,264,128]{2,1,0:T(8,128)(2,1)S(1)}, bf16[3,264,128]{2,1,0:T(8,128)(2,1)S(1)}, u32[]{:S(2)}, u32[]{:S(2)}) collective-permute-start(bf16[3,264,128]{2,1,0:T(8,128)(2,1)S(1)} %reshape.183), channel_id=1, source_target_pairs={{0,64},{64,128},{128,192},{192,256},{256,320},{320,384},{384,448},... | collective-permute-start | bytes 608264 | tf_op jit(solution)/shard_map/ppermute | solution.py:23
  37.3 7.8 %collective-permute-start.5 = (bf16[3,264,128]{2,1,0:T(8,128)(2,1)S(1)}, bf16[3,264,128]{2,1,0:T(8,128)(2,1)S(1)}, u32[]{:S(2)}, u32[]{:S(2)}) collective-permute-start(bf16[3,264,128]{2,1,0:T(8,128)(2,1)S(1)} %collective-permute-done.4), channel_id=1, source_target_pairs={{0,64},{64,128},{128,192},{192,256},{256,320},{320,384},{384,448},... | collective-permute-start | bytes 608264 | tf_op jit(solution)/shard_map/ppermute | solution.py:23
  41.1 9.3 %collective-permute-start.8 = (bf16[3,264,128]{2,1,0:T(8,128)(2,1)S(1)}, bf16[3,264,128]{2,1,0:T(8,128)(2,1)S(1)}, u32[]{:S(2)}, u32[]{:S(2)}) collective-permute-start(bf16[3,264,128]{2,1,0:T(8,128)(2,1)S(1)} %reshape.183), channel_id=1, source_target_pairs={{0,448},{64,0},{128,64},{192,128},{256,192},{320,256},{384,320},{4... | collective-permute-start | bytes 608264 | tf_op jit(solution)/shard_map/ppermute | solution.py:26
  45.1 8.8 %collective-permute-start.6 = (bf16[3,264,128]{2,1,0:T(8,128)(2,1)S(1)}, bf16[3,264,128]{2,1,0:T(8,128)(2,1)S(1)}, u32[]{:S(2)}, u32[]{:S(2)}) collective-permute-start(bf16[3,264,128]{2,1,0:T(8,128)(2,1)S(1)} %collective-permute-done.5), channel_id=1, source_target_pairs={{0,64},{64,128},{128,192},{192,256},{256,320},{320,384},{384,448},... | collective-permute-start | bytes 608264 | tf_op jit(solution)/shard_map/ppermute | solution.py:23
  50.4 8.8 %collective-permute-start.9 = (bf16[3,264,128]{2,1,0:T(8,128)(2,1)S(1)}, bf16[3,264,128]{2,1,0:T(8,128)(2,1)S(1)}, u32[]{:S(2)}, u32[]{:S(2)}) collective-permute-start(bf16[3,264,128]{2,1,0:T(8,128)(2,1)S(1)} %collective-permute-done.8), channel_id=1, source_target_pairs={{0,448},{64,0},{128,64},{192,128},{256,192},{320,256},{384,320},{4... | collective-permute-start | bytes 608264 | tf_op jit(solution)/shard_map/ppermute | solution.py:26
  53.9 8.8 %collective-permute-start.7 = (bf16[3,264,128]{2,1,0:T(8,128)(2,1)S(1)}, bf16[3,264,128]{2,1,0:T(8,128)(2,1)S(1)}, u32[]{:S(2)}, u32[]{:S(2)}) collective-permute-start(bf16[3,264,128]{2,1,0:T(8,128)(2,1)S(1)} %collective-permute-done.6), channel_id=1, source_target_pairs={{0,64},{64,128},{128,192},{192,256},{256,320},{320,384},{384,448},... | collective-permute-start | bytes 608264 | tf_op jit(solution)/shard_map/ppermute | solution.py:23
  59.3 8.9 %collective-permute-start.10 = (bf16[3,264,128]{2,1,0:T(8,128)(2,1)S(1)}, bf16[3,264,128]{2,1,0:T(8,128)(2,1)S(1)}, u32[]{:S(2)}, u32[]{:S(2)}) collective-permute-start(bf16[3,264,128]{2,1,0:T(8,128)(2,1)S(1)} %collective-permute-done.9), channel_id=1, source_target_pairs={{0,448},{64,0},{128,64},{192,128},{256,192},{320,256},{384,320},{4... | collective-permute-start | bytes 608264 | tf_op jit(solution)/shard_map/ppermute | solution.py:26
  68.5 4.0 %copy-start.1 = (s32[1024]{0:T(1024)S(1)}, s32[1024]{0:T(1024)}, u32[]{:S(2)}) copy-start(s32[1024]{0:T(1024)} %param.7) | copy-start | bytes 12292
  70.0 8.0 %collective-permute-start.11 = (bf16[3,2112,128]{2,1,0:T(8,128)(2,1)}, bf16[3,2112,128]{2,1,0:T(8,128)(2,1)}, u32[]{:S(2)}, u32[]{:S(2)}) collective-permute-start(bf16[3,2112,128]{2,1,0:T(8,128)(2,1)} %bitcast.14), channel_id=1, source_target_pairs={{0,8},{8,0},{1,9},{9,1},{2,10},{10,2},{3,11},{11,3},{4,12},{12,4},... | collective-permute-start | bytes 4866056 | tf_op jit(solution)/shard_map/ppermute | solution.py:46
  98.3 2.3 %copy-start = (bf16[1,1024,256]{1,2,0:T(8,128)(2,1)}, bf16[1,1024,256]{1,2,0:T(8,128)(2,1)S(1)}, u32[]{:S(2)}) copy-start(bf16[1,1024,256]{1,2,0:T(8,128)(2,1)S(1)} %get-tuple-element.17) | copy-start | bytes 1572868
  100.6 17.9 %all-to-all-start = ((bf16[8,2,128,128]{3,2,1,0:T(8,128)(2,1)}), bf16[8,2,128,128]{3,2,1,0:T(8,128)(2,1)S(1)}, u32[]{:S(2)}, u32[]{:S(2)}) async-start(bf16[8,2,128,128]{3,2,1,0:T(8,128)(2,1)} %broadcast_in_dim.115), calls=%async_computation | async-start | bytes 1048576 | tf_op jit(solution)/shard_map/all_to_all | solution.py:72
  118.5 12.5 %copy-start.2 = (f32[256]{0:T(256)S(1)}, f32[256]{0:T(256)}, u32[]{:S(2)}) copy-start(f32[256]{0:T(256)} %param.6) | copy-start | bytes 3076
  118.9 9.3 %collective-permute-start.13 = (bf16[2,128,128]{2,1,0:T(8,128)(2,1)S(1)}, bf16[2,128,128]{2,1,0:T(8,128)(2,1)S(1)}, u32[]{:S(2)}, u32[]{:S(2)}) collective-permute-start(bf16[2,128,128]{2,1,0:T(8,128)(2,1)S(1)} %get-tuple-element.10), channel_id=1, source_target_pairs={{0,128},{64,192},{128,256},{192,320},{256,384},{320,448},{1,129},{... | collective-permute-start | bytes 196616 | tf_op jit(solution)/shard_map/ppermute | solution.py:15
  124.5 6.2 %collective-permute-start.12 = (bf16[2,128,128]{2,1,0:T(8,128)(2,1)S(1)}, bf16[2,128,128]{2,1,0:T(8,128)(2,1)S(1)}, u32[]{:S(2)}, u32[]{:S(2)}) collective-permute-start(bf16[2,128,128]{2,1,0:T(8,128)(2,1)S(1)} %get-tuple-element.9), channel_id=1, source_target_pairs={{0,64},{64,128},{128,192},{192,256},{256,320},{320,384},{384,448},... | collective-permute-start | bytes 196616 | tf_op jit(solution)/shard_map/ppermute | solution.py:15
Sparse Core Ops, SparseCore 0:
  23.5 69.9 all-gather.1

commit v13 on v12

--- a/solution.py
+++ b/solution.py
@@ -55,7 +55,7 @@
     return (jax.nn.elu(values.astype(jnp.float32)) + 1.0).astype(jnp.bfloat16)
 
 
-def state_scan(kv_state, tails, row_count):
+def state_scan(kv_state, tails, row_count, held):
     count = lax.axis_size(CTX)
     window = min(count - 1, 1 + (SPAN - 1) // row_count)
     row_len = lax.axis_size("x") * lax.axis_size("core")
@@ -70,6 +70,7 @@
     prev_tail = tail_of(me - 1)
     spread = jnp.broadcast_to(kv_state.astype(jnp.bfloat16)[None], (row_len,) + kv_state.shape)
     row = lax.all_to_all(spread, ("x", "core"), 0, 0, tiled=True).astype(jnp.float32)
+    row, held = lax.optimization_barrier((row, held))
     places = jnp.arange(row_len)
     row_tails = tail_of(first + places)
     in_last = row_tails == row_tails[row_len - 1]
@@ -86,7 +87,7 @@
     state = state + jnp.where(tail_of(first - 1) == prev_tail, one_back, 0.0)
     if window > row_len:
         state = state + jnp.where(tail_of(first - row_len - 1) == prev_tail, two_back, 0.0)
-    return state, prev_tail
+    return state, prev_tail, held
 
 
 def per_device(tokens, w_qkv, out_gain, seg_ids):
@@ -111,17 +112,19 @@
     kv_state = jnp.einsum("thd,the->hde", key_tail, values, preferred_element_type=jnp.float32)
 
     tails, kv_state = lax.optimization_barrier((tails, kv_state))
-    state_in, tail_in = state_scan(kv_state, tails, row_count)
     query_proj = jnp.einsum("tr,rc->tc", whole, w_rows[0], preferred_element_type=jnp.float32)
     query_proj = lax.reduce_precision(query_proj, exponent_bits=8, mantissa_bits=7)
     queries = feature_map(query_proj).reshape(row_count, head_count, HEAD_DIM)
+    split = min(512, row_count)
+    state_in, tail_in, late_queries = state_scan(kv_state, tails, row_count, queries[split:])
+    queries_used = jnp.concatenate([queries[:split], late_queries], axis=0)
 
     block_rows = min(512, row_count)
     pieces = []
     for blk_no in range(row_count // block_rows):
         first_row = blk_no * block_rows
         key_end = first_row + block_rows
-        query_blk = queries[first_row:key_end]
+        query_blk = queries_used[first_row:key_end]
         query_pos = first_row + jnp.arange(block_rows, dtype=jnp.int32)
         query_seg = seg_float[first_row:key_end]
         scores = jnp.einsum(

time: 140 us -> 141 us (level)
  the two profiles are of different devices: /device:TPU:18 before, /device:TPU:10 now
where the time goes in v13:
time: 141 us; the launch traced here: 140 us
  starting transfers between devices  51.4 us (36%)
  waiting for transfers between devices  28 us (20%)
  local copies, waits for them, and re-layouts  18.1 us (13%)
  between operations  15.9 us (11%)
  matrix products  15.6 us (11%)
  other arithmetic  11.1 us (8%)
    ppermute x4, starting transfers between devices, ring_gather(): lax.ppermute(behind, axis, [(j, (j - 1) % count) for j in range(count)])  17.8 us
    ppermute x6, starting transfers between devices, ring_gather(): lax.ppermute(ahead, axis, [(j, (j + 1) % count) for j in range(count)])  16 us
    ppermute x6, waiting for transfers between devices, ring_gather(): lax.ppermute(ahead, axis, [(j, (j + 1) % count) for j in range(count)])  13.8 us
    ppermute x2, starting transfers between devices, shifted(): lax.ppermute(value, axis, [(source, source + steps) for source in range(c...  8.99 us
    all_gather x1, waiting for transfers between devices, per_device(): whole = lax.all_gather(tokens, 'head', axis=1, tiled=True)  8.14 us
    concatenate x2, local copies, waits for them, and re-layouts, gather_weights(): jnp.concatenate([rows, other], axis=2)  6.17 us
    all_to_all x1, starting transfers between devices, state_scan(): lax.all_to_all(spread, ('x', 'core'), 0, 0, tiled=True).astype(jnp.float32)  4.78 us
    ppermute x4, waiting for transfers between devices, ring_gather(): lax.ppermute(behind, axis, [(j, (j - 1) % count) for j in range(count)])  4.74 us
  transfers between devices with their start and end apart: 16, of which 10 were waited for; matrix products, arithmetic and copies ran while one was open for 21% of the time, Pallas kernels for 0%

profile of v13, /device:TPU:10, one launch (start us, length us, event | category | flops | bytes accessed | tf_op | source)
XLA Modules:
  0.0 140.0 jit_solution(16922029357634217693)
XLA Ops:
  7.9 1.5 %concatenate.31 = bf16[3,33,256]{2,1,0:T(8,128)(2,1)S(1)} pad(bf16[3,32,256]{2,1,0:T(8,128)(2,1)} %param.5, bf16[]{:T(256)} %bitcast), padding=0_0x0_1x0_0 | pad | bytes 99842 | tf_op jit(solution)/shard_map/concatenate | solution.py:99
  9.3 1.9 %collective-permute-start = (bf16[3,33,256]{2,1,0:T(8,128)(2,1)S(1)}, bf16[3,33,256]{2,1,0:T(8,128)(2,1)S(1)}, u32[]{:S(2)}, u32[]{:S(2)}) collective-permute-start(bf16[3,33,256]{2,1,0:T(8,128)(2,1)S(1)} %concatenate.31), channel_id=1, source_target_pairs={{0,8},{8,0},{1,9},{9,1},{2,10},{10,2},{3,11},{11,3},{4,12},{12,4},... | collective-permute-start | bytes 152072 | tf_op jit(solution)/shard_map/ppermute | solution.py:40
  12.5 1.4 %slice_select_fusion.1 = (bf16[3,33,128]{2,1,0:T(8,128)(2,1)S(1)}, bf16[3,33,128]{2,1,0:T(8,128)(2,1)S(1)}) fusion(bf16[3,33,256]{2,1,0:T(8,128)(2,1)S(1)} %collective-permute-done, pred[]{:T(512)S(6)} %eq.87, bf16[3,32,256]{2,1,0:T(8,128)(2,1)} %param.5, bf16[]{:T(256)} %bitcast), kind=kLoop, calls=%fused_computation.83 | loop fusion | flops 25344 | bytes 150531 | tf_op jit(solution)/shard_map/jit(_where)/select_n | solution.py:41
  13.9 3.4 %collective-permute-start.1 = (bf16[3,66,128]{2,1,0:T(8,128)(2,1)S(1)}, bf16[3,66,128]{2,1,0:T(8,128)(2,1)S(1)}, u32[]{:S(2)}, u32[]{:S(2)}) collective-permute-start(bf16[3,66,128]{2,1,0:T(8,128)(2,1)S(1)} %pad_maximum_fusion), channel_id=1, source_target_pairs={{0,16},{16,32},{32,48},{48,0},{1,17},{17,33},{33,49},{49,1},{2,18}... | collective-permute-start | bytes 152072 | tf_op jit(solution)/shard_map/ppermute | solution.py:23
  17.3 2.6 %collective-permute-done.1 = bf16[3,66,128]{2,1,0:T(8,128)(2,1)S(1)} collective-permute-done((bf16[3,66,128]{2,1,0:T(8,128)(2,1)S(1)}, bf16[3,66,128]{2,1,0:T(8,128)(2,1)S(1)}, u32[]{:S(2)}, u32[]{:S(2)}) %collective-permute-start.1) | collective-permute-done | bytes 50720 | tf_op jit(solution)/shard_map/ppermute | solution.py:23
  20.0 3.4 %collective-permute-start.2 = (bf16[3,66,128]{2,1,0:T(8,128)(2,1)S(1)}, bf16[3,66,128]{2,1,0:T(8,128)(2,1)S(1)}, u32[]{:S(2)}, u32[]{:S(2)}) collective-permute-start(bf16[3,66,128]{2,1,0:T(8,128)(2,1)S(1)} %collective-permute-done.1), channel_id=1, source_target_pairs={{0,16},{16,32},{32,48},{48,0},{1,17},{17,33},{33,49},{49,1},{2,18}... | collective-permute-start | bytes 152072 | tf_op jit(solution)/shard_map/ppermute | solution.py:23
  23.4 2.4 %collective-permute-start.3 = (bf16[3,66,128]{2,1,0:T(8,128)(2,1)S(1)}, bf16[3,66,128]{2,1,0:T(8,128)(2,1)S(1)}, u32[]{:S(2)}, u32[]{:S(2)}) collective-permute-start(bf16[3,66,128]{2,1,0:T(8,128)(2,1)S(1)} %pad_maximum_fusion), channel_id=1, source_target_pairs={{0,48},{16,0},{32,16},{48,32},{1,49},{17,1},{33,17},{49,33},{2,50}... | collective-permute-start | bytes 152072 | tf_op jit(solution)/shard_map/ppermute | solution.py:26
  26.1 3.4 %collective-permute-done.3 = bf16[3,66,128]{2,1,0:T(8,128)(2,1)S(1)} collective-permute-done((bf16[3,66,128]{2,1,0:T(8,128)(2,1)S(1)}, bf16[3,66,128]{2,1,0:T(8,128)(2,1)S(1)}, u32[]{:S(2)}, u32[]{:S(2)}) %collective-permute-start.3) | collective-permute-done | bytes 50720 | tf_op jit(solution)/shard_map/ppermute | solution.py:26
  29.7 3.5 %collective-permute-start.4 = (bf16[3,264,128]{2,1,0:T(8,128)(2,1)S(1)}, bf16[3,264,128]{2,1,0:T(8,128)(2,1)S(1)}, u32[]{:S(2)}, u32[]{:S(2)}) collective-permute-start(bf16[3,264,128]{2,1,0:T(8,128)(2,1)S(1)} %reshape.183), channel_id=1, source_target_pairs={{0,64},{64,128},{128,192},{192,256},{256,320},{320,384},{384,448},... | collective-permute-start | bytes 608264 | tf_op jit(solution)/shard_map/ppermute | solution.py:23
  33.2 5.9 %collective-permute-done.4 = bf16[3,264,128]{2,1,0:T(8,128)(2,1)S(1)} collective-permute-done((bf16[3,264,128]{2,1,0:T(8,128)(2,1)S(1)}, bf16[3,264,128]{2,1,0:T(8,128)(2,1)S(1)}, u32[]{:S(2)}, u32[]{:S(2)}) %collective-permute-start.4) | collective-permute-done | bytes 202784 | tf_op jit(solution)/shard_map/ppermute | solution.py:23
  39.1 1.9 %collective-permute-start.5 = (bf16[3,264,128]{2,1,0:T(8,128)(2,1)S(1)}, bf16[3,264,128]{2,1,0:T(8,128)(2,1)S(1)}, u32[]{:S(2)}, u32[]{:S(2)}) collective-permute-start(bf16[3,264,128]{2,1,0:T(8,128)(2,1)S(1)} %collective-permute-done.4), channel_id=1, source_target_pairs={{0,64},{64,128},{128,192},{192,256},{256,320},{320,384},{384,448},... | collective-permute-start | bytes 608264 | tf_op jit(solution)/shard_map/ppermute | solution.py:23
  41.0 5.1 %collective-permute-start.8 = (bf16[3,264,128]{2,1,0:T(8,128)(2,1)S(1)}, bf16[3,264,128]{2,1,0:T(8,128)(2,1)S(1)}, u32[]{:S(2)}, u32[]{:S(2)}) collective-permute-start(bf16[3,264,128]{2,1,0:T(8,128)(2,1)S(1)} %reshape.183), channel_id=1, source_target_pairs={{0,448},{64,0},{128,64},{192,128},{256,192},{320,256},{384,320},{4... | collective-permute-start | bytes 608264 | tf_op jit(solution)/shard_map/ppermute | solution.py:26
  46.1 1.8 %collective-permute-done.5 = bf16[3,264,128]{2,1,0:T(8,128)(2,1)S(1)} collective-permute-done((bf16[3,264,128]{2,1,0:T(8,128)(2,1)S(1)}, bf16[3,264,128]{2,1,0:T(8,128)(2,1)S(1)}, u32[]{:S(2)}, u32[]{:S(2)}) %collective-permute-start.5) | collective-permute-done | bytes 202784 | tf_op jit(solution)/shard_map/ppermute | solution.py:23
  47.9 1.9 %collective-permute-start.6 = (bf16[3,264,128]{2,1,0:T(8,128)(2,1)S(1)}, bf16[3,264,128]{2,1,0:T(8,128)(2,1)S(1)}, u32[]{:S(2)}, u32[]{:S(2)}) collective-permute-start(bf16[3,264,128]{2,1,0:T(8,128)(2,1)S(1)} %collective-permute-done.5), channel_id=1, source_target_pairs={{0,64},{64,128},{128,192},{192,256},{256,320},{320,384},{384,448},... | collective-permute-start | bytes 608264 | tf_op jit(solution)/shard_map/ppermute | solution.py:23
  49.8 5.1 %collective-permute-start.9 = (bf16[3,264,128]{2,1,0:T(8,128)(2,1)S(1)}, bf16[3,264,128]{2,1,0:T(8,128)(2,1)S(1)}, u32[]{:S(2)}, u32[]{:S(2)}) collective-permute-start(bf16[3,264,128]{2,1,0:T(8,128)(2,1)S(1)} %collective-permute-done.8), channel_id=1, source_target_pairs={{0,448},{64,0},{128,64},{192,128},{256,192},{320,256},{384,320},{4... | collective-permute-start | bytes 608264 | tf_op jit(solution)/shard_map/ppermute | solution.py:26
  55.0 1.8 %collective-permute-done.6 = bf16[3,264,128]{2,1,0:T(8,128)(2,1)S(1)} collective-permute-done((bf16[3,264,128]{2,1,0:T(8,128)(2,1)S(1)}, bf16[3,264,128]{2,1,0:T(8,128)(2,1)S(1)}, u32[]{:S(2)}, u32[]{:S(2)}) %collective-permute-start.6) | collective-permute-done | bytes 202784 | tf_op jit(solution)/shard_map/ppermute | solution.py:23
  56.7 1.9 %collective-permute-start.7 = (bf16[3,264,128]{2,1,0:T(8,128)(2,1)S(1)}, bf16[3,264,128]{2,1,0:T(8,128)(2,1)S(1)}, u32[]{:S(2)}, u32[]{:S(2)}) collective-permute-start(bf16[3,264,128]{2,1,0:T(8,128)(2,1)S(1)} %collective-permute-done.6), channel_id=1, source_target_pairs={{0,64},{64,128},{128,192},{192,256},{256,320},{320,384},{384,448},... | collective-permute-start | bytes 608264 | tf_op jit(solution)/shard_map/ppermute | solution.py:23
  58.7 5.1 %collective-permute-start.10 = (bf16[3,264,128]{2,1,0:T(8,128)(2,1)S(1)}, bf16[3,264,128]{2,1,0:T(8,128)(2,1)S(1)}, u32[]{:S(2)}, u32[]{:S(2)}) collective-permute-start(bf16[3,264,128]{2,1,0:T(8,128)(2,1)S(1)} %collective-permute-done.9), channel_id=1, source_target_pairs={{0,448},{64,0},{128,64},{192,128},{256,192},{320,256},{384,320},{4... | collective-permute-start | bytes 608264 | tf_op jit(solution)/shard_map/ppermute | solution.py:26
  63.9 1.7 %collective-permute-done.7 = bf16[3,264,128]{2,1,0:T(8,128)(2,1)S(1)} collective-permute-done((bf16[3,264,128]{2,1,0:T(8,128)(2,1)S(1)}, bf16[3,264,128]{2,1,0:T(8,128)(2,1)S(1)}, u32[]{:S(2)}, u32[]{:S(2)}) %collective-permute-start.7) | collective-permute-done | bytes 202784 | tf_op jit(solution)/shard_map/ppermute | solution.py:23
  68.9 1.9 %collective-permute-start.11 = (bf16[3,2112,128]{2,1,0:T(8,128)(2,1)}, bf16[3,2112,128]{2,1,0:T(8,128)(2,1)}, u32[]{:S(2)}, u32[]{:S(2)}) collective-permute-start(bf16[3,2112,128]{2,1,0:T(8,128)(2,1)} %bitcast.14), channel_id=1, source_target_pairs={{0,8},{8,0},{1,9},{9,1},{2,10},{10,2},{3,11},{11,3},{4,12},{12,4},... | collective-permute-start | bytes 4866056 | tf_op jit(solution)/shard_map/ppermute | solution.py:46
  74.5 2.5 %concatenate.35 = bf16[3,64,33,128]{3,2,1,0:T(8,128)(2,1)S(1)} reshape(bf16[3,8,264,128]{3,2,1,0:T(8,128)(2,1)} %copy.34) | data formatting | bytes 3244032 | tf_op jit(solution)/shard_map/concatenate | solution.py:49
  77.0 3.7 %concatenate.36 = bf16[3,64,33,128]{3,2,1,0:T(8,128)(2,1)} reshape(bf16[3,2112,128]{2,1,0:T(8,128)(2,1)} %collective-permute-done.11) | data formatting | bytes 3244032 | tf_op jit(solution)/shard_map/concatenate | solution.py:49
  80.6 2.8 %maximum_select_fusion = bf16[3,64,33,256]{3,2,1,0:T(8,128)(2,1)S(1)} fusion(bf16[3,64,33,128]{3,2,1,0:T(8,128)(2,1)} %concatenate.36, bf16[3,64,33,128]{3,2,1,0:T(8,128)(2,1)S(1)} %concatenate.35, pred[]{:T(512)S(6)} %eq.87), kind=kLoop, calls=%fused_computation.4 | loop fusion | flops 14598144 | bytes 6488065 | tf_op jit(solution)/shard_map/jit(_where)/select_n | solution.py:47
  85.5 8.1 %all-gather.2.cloned.1.call-done = bf16[1024,2048]{1,0:T(8,128)(2,1)} async-done(((bf16[1024,256]{1,0:T(8,128)(2,1)}), bf16[1024,2048]{1,0:T(8,128)(2,1)}) %all-gather.2.cloned.1.call-update) | async-done | bytes 4194320 | tf_op jit(solution)/shard_map/all_gather | solution.py:94
  93.6 4.6 %fusion.7 = bf16[2,1024,256]{1,2,0:T(8,128)(2,1)S(1)} fusion(bf16[2,2048,256]{2,1,0:T(8,128)(2,1)S(1)} %bitcast.98, bf16[1024,2048]{1,0:T(8,128)(2,1)} %all-gather.2.cloned.1.call-done), kind=kOutput, calls=%fused_computation.17 | convolution fusion | flops 2148007936 | bytes 7340032 | tf_op jit(solution)/shard_map/tr,grc->gtc/dot_general | solution.py:103
  100.3 1.8 %fusion.28 = bf16[2,128,128]{2,1,0:T(8,128)(2,1)S(1)} fusion(bf16[1024,2,128]{0,2,1:T(8,128)(2,1)} %bitcast.101, pred[1024]{0:T(1024)(128)(4,1)S(1)} %broadcast_compare_fusion.1, f32[1024,2,128]{2,0,1:T(8,128)S(1)} %copy.39), kind=kOutput, calls=%fused_computation.45 | convolution fusion | flops 68681728 | bytes 1639424 | tf_op jit(solution)/shard_map/thd,the->hde/dot_general | solution.py:112
  103.0 4.8 %all-to-all-start = ((bf16[8,2,128,128]{3,2,1,0:T(8,128)(2,1)}), bf16[8,2,128,128]{3,2,1,0:T(8,128)(2,1)S(1)}, u32[]{:S(2)}, u32[]{:S(2)}) async-start(bf16[8,2,128,128]{3,2,1,0:T(8,128)(2,1)} %broadcast_in_dim.111), calls=%async_computation | async-start | bytes 1048576 | tf_op jit(solution)/shard_map/all_to_all | solution.py:72
  107.8 4.2 %fusion.18 = bf16[1024,256]{0,1:T(8,128)(2,1)S(1)} fusion(bf16[2048,256]{1,0:T(8,128)(2,1)} %bitcast.100, bf16[1024,2048]{1,0:T(8,128)(2,1)} %all-gather.2.cloned.1.call-done), kind=kOutput, calls=%fused_computation.28 | convolution fusion | flops 1075314688 | bytes 5767168 | tf_op jit(solution)/shard_map/tr,rc->tc/dot_general | solution.py:115
  117.5 1.9 %fusion.15 = f32[512,2,128]{0,2,1:T(8,128)S(1)} fusion(bf16[512,2,128]{0,2,1:T(8,128)(2,1)} %bitcast.104, bf16[512,2,128]{0,2,1:T(8,128)(2,1)} %bitcast.106, bf16[512,2,128]{0,2,1:T(8,128)(2,1)S(1)} %bitcast.103, pred[512,512]{1,0:T(8,128)(4,1)} %fusion.23), kind=kOutput, calls=%fused_computation.25 | convolution fusion | flops 269484032 | bytes 1572864 | tf_op jit(solution)/shard_map/hbs,she->bhe/dot_general | solution.py:138
  119.8 4.3 %collective-permute-start.13 = (bf16[2,128,128]{2,1,0:T(8,128)(2,1)S(1)}, bf16[2,128,128]{2,1,0:T(8,128)(2,1)S(1)}, u32[]{:S(2)}, u32[]{:S(2)}) collective-permute-start(bf16[2,128,128]{2,1,0:T(8,128)(2,1)S(1)} %get-tuple-element.14), channel_id=1, source_target_pairs={{0,128},{64,192},{128,256},{192,320},{256,384},{320,448},{1,129},{... | collective-permute-start | bytes 196616 | tf_op jit(solution)/shard_map/ppermute | solution.py:15
  124.1 4.7 %collective-permute-start.12 = (bf16[2,128,128]{2,1,0:T(8,128)(2,1)S(1)}, bf16[2,128,128]{2,1,0:T(8,128)(2,1)S(1)}, u32[]{:S(2)}, u32[]{:S(2)}) collective-permute-start(bf16[2,128,128]{2,1,0:T(8,128)(2,1)S(1)} %get-tuple-element.13), channel_id=1, source_target_pairs={{0,64},{64,128},{128,192},{192,256},{256,320},{320,384},{384,448},... | collective-permute-start | bytes 196616 | tf_op jit(solution)/shard_map/ppermute | solution.py:15
  128.8 2.8 %fusion.14 = f32[512,2,128]{0,2,1:T(8,128)S(1)} fusion(bf16[1024,2,128]{0,2,1:T(8,128)(2,1)S(1)} %bitcast.102, bf16[512,2,128]{0,2,1:T(8,128)(2,1)} %bitcast.105, pred[512,1024]{1,0:T(8,128)(4,1)} %fusion.2, f32[1024,2,128]{2,0,1:T(8,128)S(1)} %copy.39), kind=kOutput, calls=%fused_computation.24 | convolution fusion | flops 540278784 | bytes 2883584 | tf_op jit(solution)/shard_map/hbs,she->bhe/dot_general | solution.py:138
  (79 shorter events, 20.3 us)
Async XLA Ops:
  6.5 87.1 %all-gather.2.cloned.1.call-start = ((), (), s32[]{:S(2)}) async-start(), calls=%async_computation.1 | async-start | bytes 4718592 | tf_op jit(solution)/shard_map/all_gather | solution.py:94
  9.3 3.1 %collective-permute-start = (bf16[3,33,256]{2,1,0:T(8,128)(2,1)S(1)}, bf16[3,33,256]{2,1,0:T(8,128)(2,1)S(1)}, u32[]{:S(2)}, u32[]{:S(2)}) collective-permute-start(bf16[3,33,256]{2,1,0:T(8,128)(2,1)S(1)} %concatenate.31), channel_id=1, source_target_pairs={{0,8},{8,0},{1,9},{9,1},{2,10},{10,2},{3,11},{11,3},{4,12},{12,4},... | collective-permute-start | bytes 152072 | tf_op jit(solution)/shard_map/ppermute | solution.py:40
  13.9 6.0 %collective-permute-start.1 = (bf16[3,66,128]{2,1,0:T(8,128)(2,1)S(1)}, bf16[3,66,128]{2,1,0:T(8,128)(2,1)S(1)}, u32[]{:S(2)}, u32[]{:S(2)}) collective-permute-start(bf16[3,66,128]{2,1,0:T(8,128)(2,1)S(1)} %pad_maximum_fusion), channel_id=1, source_target_pairs={{0,16},{16,32},{32,48},{48,0},{1,17},{17,33},{33,49},{49,1},{2,18}... | collective-permute-start | bytes 152072 | tf_op jit(solution)/shard_map/ppermute | solution.py:23
  20.0 6.0 %collective-permute-start.2 = (bf16[3,66,128]{2,1,0:T(8,128)(2,1)S(1)}, bf16[3,66,128]{2,1,0:T(8,128)(2,1)S(1)}, u32[]{:S(2)}, u32[]{:S(2)}) collective-permute-start(bf16[3,66,128]{2,1,0:T(8,128)(2,1)S(1)} %collective-permute-done.1), channel_id=1, source_target_pairs={{0,16},{16,32},{32,48},{48,0},{1,17},{17,33},{33,49},{49,1},{2,18}... | collective-permute-start | bytes 152072 | tf_op jit(solution)/shard_map/ppermute | solution.py:23
  23.4 6.0 %collective-permute-start.3 = (bf16[3,66,128]{2,1,0:T(8,128)(2,1)S(1)}, bf16[3,66,128]{2,1,0:T(8,128)(2,1)S(1)}, u32[]{:S(2)}, u32[]{:S(2)}) collective-permute-start(bf16[3,66,128]{2,1,0:T(8,128)(2,1)S(1)} %pad_maximum_fusion), channel_id=1, source_target_pairs={{0,48},{16,0},{32,16},{48,32},{1,49},{17,1},{33,17},{49,33},{2,50}... | collective-permute-start | bytes 152072 | tf_op jit(solution)/shard_map/ppermute | solution.py:26
  29.7 9.4 %collective-permute-start.4 = (bf16[3,264,128]{2,1,0:T(8,128)(2,1)S(1)}, bf16[3,264,128]{2,1,0:T(8,128)(2,1)S(1)}, u32[]{:S(2)}, u32[]{:S(2)}) collective-permute-start(bf16[3,264,128]{2,1,0:T(8,128)(2,1)S(1)} %reshape.183), channel_id=1, source_target_pairs={{0,64},{64,128},{128,192},{192,256},{256,320},{320,384},{384,448},... | collective-permute-start | bytes 608264 | tf_op jit(solution)/shard_map/ppermute | solution.py:23
  39.1 8.8 %collective-permute-start.5 = (bf16[3,264,128]{2,1,0:T(8,128)(2,1)S(1)}, bf16[3,264,128]{2,1,0:T(8,128)(2,1)S(1)}, u32[]{:S(2)}, u32[]{:S(2)}) collective-permute-start(bf16[3,264,128]{2,1,0:T(8,128)(2,1)S(1)} %collective-permute-done.4), channel_id=1, source_target_pairs={{0,64},{64,128},{128,192},{192,256},{256,320},{320,384},{384,448},... | collective-permute-start | bytes 608264 | tf_op jit(solution)/shard_map/ppermute | solution.py:23
  41.0 8.8 %collective-permute-start.8 = (bf16[3,264,128]{2,1,0:T(8,128)(2,1)S(1)}, bf16[3,264,128]{2,1,0:T(8,128)(2,1)S(1)}, u32[]{:S(2)}, u32[]{:S(2)}) collective-permute-start(bf16[3,264,128]{2,1,0:T(8,128)(2,1)S(1)} %reshape.183), channel_id=1, source_target_pairs={{0,448},{64,0},{128,64},{192,128},{256,192},{320,256},{384,320},{4... | collective-permute-start | bytes 608264 | tf_op jit(solution)/shard_map/ppermute | solution.py:26
  47.9 8.8 %collective-permute-start.6 = (bf16[3,264,128]{2,1,0:T(8,128)(2,1)S(1)}, bf16[3,264,128]{2,1,0:T(8,128)(2,1)S(1)}, u32[]{:S(2)}, u32[]{:S(2)}) collective-permute-start(bf16[3,264,128]{2,1,0:T(8,128)(2,1)S(1)} %collective-permute-done.5), channel_id=1, source_target_pairs={{0,64},{64,128},{128,192},{192,256},{256,320},{320,384},{384,448},... | collective-permute-start | bytes 608264 | tf_op jit(solution)/shard_map/ppermute | solution.py:23
  49.8 8.9 %collective-permute-start.9 = (bf16[3,264,128]{2,1,0:T(8,128)(2,1)S(1)}, bf16[3,264,128]{2,1,0:T(8,128)(2,1)S(1)}, u32[]{:S(2)}, u32[]{:S(2)}) collective-permute-start(bf16[3,264,128]{2,1,0:T(8,128)(2,1)S(1)} %collective-permute-done.8), channel_id=1, source_target_pairs={{0,448},{64,0},{128,64},{192,128},{256,192},{320,256},{384,320},{4... | collective-permute-start | bytes 608264 | tf_op jit(solution)/shard_map/ppermute | solution.py:26
  56.7 8.8 %collective-permute-start.7 = (bf16[3,264,128]{2,1,0:T(8,128)(2,1)S(1)}, bf16[3,264,128]{2,1,0:T(8,128)(2,1)S(1)}, u32[]{:S(2)}, u32[]{:S(2)}) collective-permute-start(bf16[3,264,128]{2,1,0:T(8,128)(2,1)S(1)} %collective-permute-done.6), channel_id=1, source_target_pairs={{0,64},{64,128},{128,192},{192,256},{256,320},{320,384},{384,448},... | collective-permute-start | bytes 608264 | tf_op jit(solution)/shard_map/ppermute | solution.py:23
  58.7 8.4 %collective-permute-start.10 = (bf16[3,264,128]{2,1,0:T(8,128)(2,1)S(1)}, bf16[3,264,128]{2,1,0:T(8,128)(2,1)S(1)}, u32[]{:S(2)}, u32[]{:S(2)}) collective-permute-start(bf16[3,264,128]{2,1,0:T(8,128)(2,1)S(1)} %collective-permute-done.9), channel_id=1, source_target_pairs={{0,448},{64,0},{128,64},{192,128},{256,192},{320,256},{384,320},{4... | collective-permute-start | bytes 608264 | tf_op jit(solution)/shard_map/ppermute | solution.py:26
  67.4 4.0 %copy-start.1 = (s32[1024]{0:T(1024)S(1)}, s32[1024]{0:T(1024)}, u32[]{:S(2)}) copy-start(s32[1024]{0:T(1024)} %param.7) | copy-start | bytes 12292
  68.9 8.0 %collective-permute-start.11 = (bf16[3,2112,128]{2,1,0:T(8,128)(2,1)}, bf16[3,2112,128]{2,1,0:T(8,128)(2,1)}, u32[]{:S(2)}, u32[]{:S(2)}) collective-permute-start(bf16[3,2112,128]{2,1,0:T(8,128)(2,1)} %bitcast.14), channel_id=1, source_target_pairs={{0,8},{8,0},{1,9},{9,1},{2,10},{10,2},{3,11},{11,3},{4,12},{12,4},... | collective-permute-start | bytes 4866056 | tf_op jit(solution)/shard_map/ppermute | solution.py:46
  103.0 16.3 %all-to-all-start = ((bf16[8,2,128,128]{3,2,1,0:T(8,128)(2,1)}), bf16[8,2,128,128]{3,2,1,0:T(8,128)(2,1)S(1)}, u32[]{:S(2)}, u32[]{:S(2)}) async-start(bf16[8,2,128,128]{3,2,1,0:T(8,128)(2,1)} %broadcast_in_dim.111), calls=%async_computation | async-start | bytes 1048576 | tf_op jit(solution)/shard_map/all_to_all | solution.py:72
  116.8 12.0 %copy-start = (bf16[1,1024,256]{1,2,0:T(8,128)(2,1)S(1)}, bf16[1,1024,256]{1,2,0:T(8,128)(2,1)}, u32[]{:S(2)}) copy-start(bf16[1,1024,256]{1,2,0:T(8,128)(2,1)} %get-tuple-element.21) | copy-start | bytes 1572868
  119.8 11.8 %collective-permute-start.13 = (bf16[2,128,128]{2,1,0:T(8,128)(2,1)S(1)}, bf16[2,128,128]{2,1,0:T(8,128)(2,1)S(1)}, u32[]{:S(2)}, u32[]{:S(2)}) collective-permute-start(bf16[2,128,128]{2,1,0:T(8,128)(2,1)S(1)} %get-tuple-element.14), channel_id=1, source_target_pairs={{0,128},{64,192},{128,256},{192,320},{256,384},{320,448},{1,129},{... | collective-permute-start | bytes 196616 | tf_op jit(solution)/shard_map/ppermute | solution.py:15
  124.1 7.9 %copy-start.2 = (f32[256]{0:T(256)S(1)}, f32[256]{0:T(256)}, u32[]{:S(2)}) copy-start(f32[256]{0:T(256)} %param.6) | copy-start | bytes 3076
  124.1 7.5 %collective-permute-start.12 = (bf16[2,128,128]{2,1,0:T(8,128)(2,1)S(1)}, bf16[2,128,128]{2,1,0:T(8,128)(2,1)S(1)}, u32[]{:S(2)}, u32[]{:S(2)}) collective-permute-start(bf16[2,128,128]{2,1,0:T(8,128)(2,1)S(1)} %get-tuple-element.13), channel_id=1, source_target_pairs={{0,64},{64,128},{128,192},{192,256},{256,320},{320,384},{384,448},... | collective-permute-start | bytes 196616 | tf_op jit(solution)/shard_map/ppermute | solution.py:15
Sparse Core Ops, SparseCore 0:
  23.5 70.0 all-gather.1

commit v14 on v12

--- a/solution.py
+++ b/solution.py
@@ -78,14 +78,20 @@
         return jnp.sum(jnp.where(mask[:, None, None, None], row, 0.0), axis=0)
 
     y_count = lax.axis_size("y")
-    one_back = shifted(masked(in_last).astype(jnp.bfloat16), "y", 1, y_count).astype(jnp.float32)
-    two_back = shifted(
-        masked(in_last & (places >= pos)).astype(jnp.bfloat16), "y", 2, y_count
-    ).astype(jnp.float32)
+    assert y_count > 2
+    y = lax.axis_index("y")
+    send = jnp.zeros((y_count,) + kv_state.shape, jnp.bfloat16)
+    send = send.at[(y + 1) % y_count].set(masked(in_last).astype(jnp.bfloat16))
+    send = send.at[(y + 2) % y_count].set(masked(in_last & (places >= pos)).astype(jnp.bfloat16))
+    got = lax.all_to_all(send, "y", 0, 0, tiled=True)
+    one_back = got[(y + y_count - 1) % y_count].astype(jnp.float32)
+    two_back = got[(y + y_count - 2) % y_count].astype(jnp.float32)
     state = masked((places < pos) & (row_tails == prev_tail))
-    state = state + jnp.where(tail_of(first - 1) == prev_tail, one_back, 0.0)
+    state = state + jnp.where((y >= 1) & (tail_of(first - 1) == prev_tail), one_back, 0.0)
     if window > row_len:
-        state = state + jnp.where(tail_of(first - row_len - 1) == prev_tail, two_back, 0.0)
+        state = state + jnp.where(
+            (y >= 2) & (tail_of(first - row_len - 1) == prev_tail), two_back, 0.0
+        )
     return state, prev_tail
 
 

time: 140 us -> 156 us (1.11)
  the two profiles are of different devices: /device:TPU:18 before, /device:TPU:1 now
where the time goes in v14:
time: 156 us; the launch traced here: 155 us
  starting transfers between devices  60.2 us (39%)
  waiting for transfers between devices  29.1 us (19%)
  local copies, waits for them, and re-layouts  18.7 us (12%)
  matrix products  16.1 us (10%)
  between operations  16 us (10%)
  other arithmetic  14.5 us (9%)
    ppermute x4, starting transfers between devices, ring_gather(): lax.ppermute(behind, axis, [(j, (j - 1) % count) for j in range(count)])  18.3 us
    ppermute x6, waiting for transfers between devices, ring_gather(): lax.ppermute(ahead, axis, [(j, (j + 1) % count) for j in range(count)])  14.6 us
    ppermute x6, starting transfers between devices, ring_gather(): lax.ppermute(ahead, axis, [(j, (j + 1) % count) for j in range(count)])  11.5 us
    all_to_all x1, waiting for transfers between devices, state_scan(): got = lax.all_to_all(send, 'y', 0, 0, tiled=True)  10.3 us
    ppermute x1, starting transfers between devices, gather_weights(): partner = lax.ppermute(w_local, 'core', [(0, 1), (1, 0)])  8.77 us
    ppermute x1, starting transfers between devices, gather_weights(): other = lax.ppermute(rows, 'core', [(0, 1), (1, 0)])  8.31 us
    all_to_all x1, starting transfers between devices, state_scan(): lax.all_to_all(spread, ('x', 'core'), 0, 0, tiled=True).astype(jnp.float32)  8.17 us
    concatenate x2, local copies, waits for them, and re-layouts, gather_weights(): jnp.concatenate([rows, other], axis=2)  6.17 us
  transfers between devices with their start and end apart: 15, of which 10 were waited for; matrix products, arithmetic and copies ran while one was open for 20% of the time, Pallas kernels for 0%

profile of v14, /device:TPU:1, one launch (start us, length us, event | category | flops | bytes accessed | tf_op | source)
XLA Modules:
  0.0 154.5 jit_solution(6717357514331403695)
XLA Ops:
  7.9 1.5 concatenate.39
  9.3 8.8 %collective-permute-start = (bf16[3,33,256]{2,1,0:T(8,128)(2,1)S(1)}, bf16[3,33,256]{2,1,0:T(8,128)(2,1)S(1)}, u32[]{:S(2)}, u32[]{:S(2)}) collective-permute-start(bf16[3,33,256]{2,1,0:T(8,128)(2,1)S(1)} %concatenate.39), channel_id=1, source_target_pairs={{0,8},{8,0},{1,9},{9,1},{2,10},{10,2},{3,11},{11,3},{4,12},{12,4},... | collective-permute-start | bytes 152072 | tf_op jit(solution)/shard_map/ppermute | solution.py:40
  19.0 1.4 slice_select_fusion.1
  20.4 1.9 %collective-permute-start.1 = (bf16[3,66,128]{2,1,0:T(8,128)(2,1)S(1)}, bf16[3,66,128]{2,1,0:T(8,128)(2,1)S(1)}, u32[]{:S(2)}, u32[]{:S(2)}) collective-permute-start(bf16[3,66,128]{2,1,0:T(8,128)(2,1)S(1)} %pad_maximum_fusion), channel_id=1, source_target_pairs={{0,16},{16,32},{32,48},{48,0},{1,17},{17,33},{33,49},{49,1},{2,18}... | collective-permute-start | bytes 152072 | tf_op jit(solution)/shard_map/ppermute | solution.py:23
  22.4 4.2 %collective-permute-done.1 = bf16[3,66,128]{2,1,0:T(8,128)(2,1)S(1)} collective-permute-done((bf16[3,66,128]{2,1,0:T(8,128)(2,1)S(1)}, bf16[3,66,128]{2,1,0:T(8,128)(2,1)S(1)}, u32[]{:S(2)}, u32[]{:S(2)}) %collective-permute-start.1) | collective-permute-done | bytes 50720 | tf_op jit(solution)/shard_map/ppermute | solution.py:23
  26.6 1.9 %collective-permute-start.2 = (bf16[3,66,128]{2,1,0:T(8,128)(2,1)S(1)}, bf16[3,66,128]{2,1,0:T(8,128)(2,1)S(1)}, u32[]{:S(2)}, u32[]{:S(2)}) collective-permute-start(bf16[3,66,128]{2,1,0:T(8,128)(2,1)S(1)} %collective-permute-done.1), channel_id=1, source_target_pairs={{0,16},{16,32},{32,48},{48,0},{1,17},{17,33},{33,49},{49,1},{2,18}... | collective-permute-start | bytes 152072 | tf_op jit(solution)/shard_map/ppermute | solution.py:23
  28.5 4.6 %collective-permute-start.3 = (bf16[3,66,128]{2,1,0:T(8,128)(2,1)S(1)}, bf16[3,66,128]{2,1,0:T(8,128)(2,1)S(1)}, u32[]{:S(2)}, u32[]{:S(2)}) collective-permute-start(bf16[3,66,128]{2,1,0:T(8,128)(2,1)S(1)} %pad_maximum_fusion), channel_id=1, source_target_pairs={{0,48},{16,0},{32,16},{48,32},{1,49},{17,1},{33,17},{49,33},{2,50}... | collective-permute-start | bytes 152072 | tf_op jit(solution)/shard_map/ppermute | solution.py:26
  34.6 1.9 %collective-permute-start.4 = (bf16[3,264,128]{2,1,0:T(8,128)(2,1)S(1)}, bf16[3,264,128]{2,1,0:T(8,128)(2,1)S(1)}, u32[]{:S(2)}, u32[]{:S(2)}) collective-permute-start(bf16[3,264,128]{2,1,0:T(8,128)(2,1)S(1)} %reshape.282), channel_id=1, source_target_pairs={{0,64},{64,128},{128,192},{192,256},{256,320},{320,384},{384,448},... | collective-permute-start | bytes 608264 | tf_op jit(solution)/shard_map/ppermute | solution.py:23
  36.5 5.8 %collective-permute-done.4 = bf16[3,264,128]{2,1,0:T(8,128)(2,1)S(1)} collective-permute-done((bf16[3,264,128]{2,1,0:T(8,128)(2,1)S(1)}, bf16[3,264,128]{2,1,0:T(8,128)(2,1)S(1)}, u32[]{:S(2)}, u32[]{:S(2)}) %collective-permute-start.4) | collective-permute-done | bytes 202784 | tf_op jit(solution)/shard_map/ppermute | solution.py:23
  42.2 1.9 %collective-permute-start.5 = (bf16[3,264,128]{2,1,0:T(8,128)(2,1)S(1)}, bf16[3,264,128]{2,1,0:T(8,128)(2,1)S(1)}, u32[]{:S(2)}, u32[]{:S(2)}) collective-permute-start(bf16[3,264,128]{2,1,0:T(8,128)(2,1)S(1)} %collective-permute-done.4), channel_id=1, source_target_pairs={{0,64},{64,128},{128,192},{192,256},{256,320},{320,384},{384,448},... | collective-permute-start | bytes 608264 | tf_op jit(solution)/shard_map/ppermute | solution.py:23
  44.2 4.6 %collective-permute-start.8 = (bf16[3,264,128]{2,1,0:T(8,128)(2,1)S(1)}, bf16[3,264,128]{2,1,0:T(8,128)(2,1)S(1)}, u32[]{:S(2)}, u32[]{:S(2)}) collective-permute-start(bf16[3,264,128]{2,1,0:T(8,128)(2,1)S(1)} %reshape.282), channel_id=1, source_target_pairs={{0,448},{64,0},{128,64},{192,128},{256,192},{320,256},{384,320},{4... | collective-permute-start | bytes 608264 | tf_op jit(solution)/shard_map/ppermute | solution.py:26
  48.7 1.6 %collective-permute-done.5 = bf16[3,264,128]{2,1,0:T(8,128)(2,1)S(1)} collective-permute-done((bf16[3,264,128]{2,1,0:T(8,128)(2,1)S(1)}, bf16[3,264,128]{2,1,0:T(8,128)(2,1)S(1)}, u32[]{:S(2)}, u32[]{:S(2)}) %collective-permute-start.5) | collective-permute-done | bytes 202784 | tf_op jit(solution)/shard_map/ppermute | solution.py:23
  50.3 1.9 %collective-permute-start.6 = (bf16[3,264,128]{2,1,0:T(8,128)(2,1)S(1)}, bf16[3,264,128]{2,1,0:T(8,128)(2,1)S(1)}, u32[]{:S(2)}, u32[]{:S(2)}) collective-permute-start(bf16[3,264,128]{2,1,0:T(8,128)(2,1)S(1)} %collective-permute-done.5), channel_id=1, source_target_pairs={{0,64},{64,128},{128,192},{192,256},{256,320},{320,384},{384,448},... | collective-permute-start | bytes 608264 | tf_op jit(solution)/shard_map/ppermute | solution.py:23
  52.2 4.6 %collective-permute-start.9 = (bf16[3,264,128]{2,1,0:T(8,128)(2,1)S(1)}, bf16[3,264,128]{2,1,0:T(8,128)(2,1)S(1)}, u32[]{:S(2)}, u32[]{:S(2)}) collective-permute-start(bf16[3,264,128]{2,1,0:T(8,128)(2,1)S(1)} %collective-permute-done.8), channel_id=1, source_target_pairs={{0,448},{64,0},{128,64},{192,128},{256,192},{320,256},{384,320},{4... | collective-permute-start | bytes 608264 | tf_op jit(solution)/shard_map/ppermute | solution.py:26
  56.8 1.6 %collective-permute-done.6 = bf16[3,264,128]{2,1,0:T(8,128)(2,1)S(1)} collective-permute-done((bf16[3,264,128]{2,1,0:T(8,128)(2,1)S(1)}, bf16[3,264,128]{2,1,0:T(8,128)(2,1)S(1)}, u32[]{:S(2)}, u32[]{:S(2)}) %collective-permute-start.6) | collective-permute-done | bytes 202784 | tf_op jit(solution)/shard_map/ppermute | solution.py:23
  58.4 1.9 %collective-permute-start.7 = (bf16[3,264,128]{2,1,0:T(8,128)(2,1)S(1)}, bf16[3,264,128]{2,1,0:T(8,128)(2,1)S(1)}, u32[]{:S(2)}, u32[]{:S(2)}) collective-permute-start(bf16[3,264,128]{2,1,0:T(8,128)(2,1)S(1)} %collective-permute-done.6), channel_id=1, source_target_pairs={{0,64},{64,128},{128,192},{192,256},{256,320},{320,384},{384,448},... | collective-permute-start | bytes 608264 | tf_op jit(solution)/shard_map/ppermute | solution.py:23
  60.4 4.6 %collective-permute-start.10 = (bf16[3,264,128]{2,1,0:T(8,128)(2,1)S(1)}, bf16[3,264,128]{2,1,0:T(8,128)(2,1)S(1)}, u32[]{:S(2)}, u32[]{:S(2)}) collective-permute-start(bf16[3,264,128]{2,1,0:T(8,128)(2,1)S(1)} %collective-permute-done.9), channel_id=1, source_target_pairs={{0,448},{64,0},{128,64},{192,128},{256,192},{320,256},{384,320},{4... | collective-permute-start | bytes 608264 | tf_op jit(solution)/shard_map/ppermute | solution.py:26
  65.0 1.5 collective-permute-done.7
  69.5 8.3 %collective-permute-start.11 = (bf16[3,2112,128]{2,1,0:T(8,128)(2,1)}, bf16[3,2112,128]{2,1,0:T(8,128)(2,1)}, u32[]{:S(2)}, u32[]{:S(2)}) collective-permute-start(bf16[3,2112,128]{2,1,0:T(8,128)(2,1)} %bitcast.14), channel_id=1, source_target_pairs={{0,8},{8,0},{1,9},{9,1},{2,10},{10,2},{3,11},{11,3},{4,12},{12,4},... | collective-permute-start | bytes 4866056 | tf_op jit(solution)/shard_map/ppermute | solution.py:46
  80.2 1.4 fusion.2
  81.5 2.5 %concatenate.43 = bf16[3,64,33,128]{3,2,1,0:T(8,128)(2,1)S(1)} reshape(bf16[3,8,264,128]{3,2,1,0:T(8,128)(2,1)} %copy.31) | data formatting | bytes 3244032 | tf_op jit(solution)/shard_map/concatenate | solution.py:49
  84.0 3.7 %concatenate.44 = bf16[3,64,33,128]{3,2,1,0:T(8,128)(2,1)} reshape(bf16[3,2112,128]{2,1,0:T(8,128)(2,1)} %collective-permute-done.11) | data formatting | bytes 3244032 | tf_op jit(solution)/shard_map/concatenate | solution.py:49
  87.7 2.9 %maximum_select_fusion = bf16[3,64,33,256]{3,2,1,0:T(8,128)(2,1)S(1)} fusion(bf16[3,64,33,128]{3,2,1,0:T(8,128)(2,1)} %concatenate.44, bf16[3,64,33,128]{3,2,1,0:T(8,128)(2,1)S(1)} %concatenate.43, pred[]{:T(512)S(6)} %eq.91), kind=kLoop, calls=%fused_computation.4 | loop fusion | flops 14598144 | bytes 6488065 | tf_op jit(solution)/shard_map/jit(_where)/select_n | solution.py:47
  92.6 4.6 %fusion.7 = bf16[2,1024,256]{1,2,0:T(8,128)(2,1)S(1)} fusion(bf16[2,2048,256]{2,1,0:T(8,128)(2,1)S(1)} %bitcast.118, bf16[1024,2048]{1,0:T(8,128)(2,1)} %all-gather.2.cloned.1.call-done), kind=kOutput, calls=%fused_computation.20 | convolution fusion | flops 2148007936 | bytes 7340032 | tf_op jit(solution)/shard_map/tr,grc->gtc/dot_general | solution.py:108
  98.2 2.0 %fusion.31 = bf16[2,128,128]{2,1,0:T(8,128)(2,1)S(1)} fusion(bf16[1024,2,128]{0,2,1:T(8,128)(2,1)} %bitcast.25, pred[1024]{0:T(1024)(128)(4,1)S(1)} %broadcast_compare_fusion.1, f32[1024,2,128]{0,2,1:T(8,128)S(1)} %bitcast.121), kind=kOutput, calls=%fused_computation.48 | convolution fusion | flops 68681728 | bytes 1639424 | tf_op jit(solution)/shard_map/thd,the->hde/dot_general | solution.py:117
  101.1 8.2 %all-to-all-start = ((bf16[8,2,128,128]{3,2,1,0:T(8,128)(2,1)}), bf16[8,2,128,128]{3,2,1,0:T(8,128)(2,1)S(1)}, u32[]{:S(2)}, u32[]{:S(2)}) async-start(bf16[8,2,128,128]{3,2,1,0:T(8,128)(2,1)} %broadcast_in_dim.120), calls=%async_computation | async-start | bytes 1048576 | tf_op jit(solution)/shard_map/all_to_all | solution.py:72
  111.8 4.2 %fusion.21 = bf16[1024,256]{0,1:T(8,128)(2,1)S(1)} fusion(bf16[2048,256]{1,0:T(8,128)(2,1)} %bitcast.123, bf16[1024,2048]{1,0:T(8,128)(2,1)} %all-gather.2.cloned.1.call-done), kind=kOutput, calls=%fused_computation.34 | convolution fusion | flops 1075314688 | bytes 5767168 | tf_op jit(solution)/shard_map/tr,rc->tc/dot_general | solution.py:121
  121.3 2.2 %fusion.38 = bf16[8,2,128,128]{3,2,1,0:T(8,128)(2,1)} fusion(bf16[8,2,128,128]{3,2,1,0:T(8,128)(2,1)} %bitcast_dynamic-update-slice_fusion.14, s32[]{:T(128)} %select_n.220, bf16[2,128,128]{2,1,0:T(8,128)(2,1)S(1)} %get-tuple-element.33, pred[]{:T(512)} %get-tuple-element.36), kind=kLoop, calls=%fused_computation.72 | loop fusion | flops 32768 | bytes 197632 | tf_op jit(solution)/shard_map/scatter | solution.py:85
  123.4 5.1 %all-to-all-start.1 = ((bf16[8,2,128,128]{3,2,1,0:T(8,128)(2,1)}), bf16[8,2,128,128]{3,2,1,0:T(8,128)(2,1)S(1)}, u32[]{:S(2)}, u32[]{:S(2)}) async-start(bf16[8,2,128,128]{3,2,1,0:T(8,128)(2,1)} %fusion.38), calls=%async_computation.1 | async-start | bytes 1048576 | tf_op jit(solution)/shard_map/all_to_all | solution.py:86
  130.8 1.8 %fusion.15 = f32[512,2,128]{0,2,1:T(8,128)S(1)} fusion(bf16[512,2,128]{0,2,1:T(8,128)(2,1)} %bitcast.125, bf16[512,2,128]{0,2,1:T(8,128)(2,1)} %bitcast.127, bf16[512,2,128]{0,2,1:T(8,128)(2,1)S(1)} %bitcast.124, pred[512,512]{1,0:T(8,128)(4,1)S(1)} %fusion.26), kind=kOutput, calls=%fused_computation.28 | convolution fusion | flops 269484032 | bytes 1572864 | tf_op jit(solution)/shard_map/hbs,she->bhe/dot_general | solution.py:141
  132.7 3.2 %fusion.14 = f32[512,2,128]{0,2,1:T(8,128)S(1)} fusion(bf16[1024,2,128]{0,2,1:T(8,128)(2,1)} %bitcast.25, bf16[512,2,128]{0,2,1:T(8,128)(2,1)} %bitcast.126, pred[512,1024]{1,0:T(8,128)(4,1)} %fusion.2, f32[1024,2,128]{0,2,1:T(8,128)} %bitcast.122), kind=kOutput, calls=%fused_computation.27 | convolution fusion | flops 540278784 | bytes 2883584 | tf_op jit(solution)/shard_map/hbs,she->bhe/dot_general | solution.py:141
  135.8 10.3 %all-to-all-done.1 = bf16[8,2,128,128]{3,2,1,0:T(8,128)(2,1)S(1)} async-done(((bf16[8,2,128,128]{3,2,1,0:T(8,128)(2,1)}), bf16[8,2,128,128]{3,2,1,0:T(8,128)(2,1)S(1)}, u32[]{:S(2)}, u32[]{:S(2)}) %all-to-all-start.1) | async-done | bytes 524320 | tf_op jit(solution)/shard_map/all_to_all | solution.py:86
  (81 shorter events, 22.3 us)
Async XLA Ops:
  6.5 86.0 %all-gather.2.cloned.1.call-start = ((), (), s32[]{:S(2)}) async-start(), calls=%async_computation.2 | async-start | bytes 4718592 | tf_op jit(solution)/shard_map/all_gather | solution.py:99
  9.3 9.7 %collective-permute-start = (bf16[3,33,256]{2,1,0:T(8,128)(2,1)S(1)}, bf16[3,33,256]{2,1,0:T(8,128)(2,1)S(1)}, u32[]{:S(2)}, u32[]{:S(2)}) collective-permute-start(bf16[3,33,256]{2,1,0:T(8,128)(2,1)S(1)} %concatenate.39), channel_id=1, source_target_pairs={{0,8},{8,0},{1,9},{9,1},{2,10},{10,2},{3,11},{11,3},{4,12},{12,4},... | collective-permute-start | bytes 152072 | tf_op jit(solution)/shard_map/ppermute | solution.py:40
  20.4 6.1 %collective-permute-start.1 = (bf16[3,66,128]{2,1,0:T(8,128)(2,1)S(1)}, bf16[3,66,128]{2,1,0:T(8,128)(2,1)S(1)}, u32[]{:S(2)}, u32[]{:S(2)}) collective-permute-start(bf16[3,66,128]{2,1,0:T(8,128)(2,1)S(1)} %pad_maximum_fusion), channel_id=1, source_target_pairs={{0,16},{16,32},{32,48},{48,0},{1,17},{17,33},{33,49},{49,1},{2,18}... | collective-permute-start | bytes 152072 | tf_op jit(solution)/shard_map/ppermute | solution.py:23
  26.6 6.6 %collective-permute-start.2 = (bf16[3,66,128]{2,1,0:T(8,128)(2,1)S(1)}, bf16[3,66,128]{2,1,0:T(8,128)(2,1)S(1)}, u32[]{:S(2)}, u32[]{:S(2)}) collective-permute-start(bf16[3,66,128]{2,1,0:T(8,128)(2,1)S(1)} %collective-permute-done.1), channel_id=1, source_target_pairs={{0,16},{16,32},{32,48},{48,0},{1,17},{17,33},{33,49},{49,1},{2,18}... | collective-permute-start | bytes 152072 | tf_op jit(solution)/shard_map/ppermute | solution.py:23
  28.5 5.8 %collective-permute-start.3 = (bf16[3,66,128]{2,1,0:T(8,128)(2,1)S(1)}, bf16[3,66,128]{2,1,0:T(8,128)(2,1)S(1)}, u32[]{:S(2)}, u32[]{:S(2)}) collective-permute-start(bf16[3,66,128]{2,1,0:T(8,128)(2,1)S(1)} %pad_maximum_fusion), channel_id=1, source_target_pairs={{0,48},{16,0},{32,16},{48,32},{1,49},{17,1},{33,17},{49,33},{2,50}... | collective-permute-start | bytes 152072 | tf_op jit(solution)/shard_map/ppermute | solution.py:26
  34.6 7.7 %collective-permute-start.4 = (bf16[3,264,128]{2,1,0:T(8,128)(2,1)S(1)}, bf16[3,264,128]{2,1,0:T(8,128)(2,1)S(1)}, u32[]{:S(2)}, u32[]{:S(2)}) collective-permute-start(bf16[3,264,128]{2,1,0:T(8,128)(2,1)S(1)} %reshape.282), channel_id=1, source_target_pairs={{0,64},{64,128},{128,192},{192,256},{256,320},{320,384},{384,448},... | collective-permute-start | bytes 608264 | tf_op jit(solution)/shard_map/ppermute | solution.py:23
  42.2 8.1 %collective-permute-start.5 = (bf16[3,264,128]{2,1,0:T(8,128)(2,1)S(1)}, bf16[3,264,128]{2,1,0:T(8,128)(2,1)S(1)}, u32[]{:S(2)}, u32[]{:S(2)}) collective-permute-start(bf16[3,264,128]{2,1,0:T(8,128)(2,1)S(1)} %collective-permute-done.4), channel_id=1, source_target_pairs={{0,64},{64,128},{128,192},{192,256},{256,320},{320,384},{384,448},... | collective-permute-start | bytes 608264 | tf_op jit(solution)/shard_map/ppermute | solution.py:23
  44.2 8.1 %collective-permute-start.8 = (bf16[3,264,128]{2,1,0:T(8,128)(2,1)S(1)}, bf16[3,264,128]{2,1,0:T(8,128)(2,1)S(1)}, u32[]{:S(2)}, u32[]{:S(2)}) collective-permute-start(bf16[3,264,128]{2,1,0:T(8,128)(2,1)S(1)} %reshape.282), channel_id=1, source_target_pairs={{0,448},{64,0},{128,64},{192,128},{256,192},{320,256},{384,320},{4... | collective-permute-start | bytes 608264 | tf_op jit(solution)/shard_map/ppermute | solution.py:26
  50.3 8.1 %collective-permute-start.6 = (bf16[3,264,128]{2,1,0:T(8,128)(2,1)S(1)}, bf16[3,264,128]{2,1,0:T(8,128)(2,1)S(1)}, u32[]{:S(2)}, u32[]{:S(2)}) collective-permute-start(bf16[3,264,128]{2,1,0:T(8,128)(2,1)S(1)} %collective-permute-done.5), channel_id=1, source_target_pairs={{0,64},{64,128},{128,192},{192,256},{256,320},{320,384},{384,448},... | collective-permute-start | bytes 608264 | tf_op jit(solution)/shard_map/ppermute | solution.py:23
  52.2 8.2 %collective-permute-start.9 = (bf16[3,264,128]{2,1,0:T(8,128)(2,1)S(1)}, bf16[3,264,128]{2,1,0:T(8,128)(2,1)S(1)}, u32[]{:S(2)}, u32[]{:S(2)}) collective-permute-start(bf16[3,264,128]{2,1,0:T(8,128)(2,1)S(1)} %collective-permute-done.8), channel_id=1, source_target_pairs={{0,448},{64,0},{128,64},{192,128},{256,192},{320,256},{384,320},{4... | collective-permute-start | bytes 608264 | tf_op jit(solution)/shard_map/ppermute | solution.py:26
  58.4 8.1 %collective-permute-start.7 = (bf16[3,264,128]{2,1,0:T(8,128)(2,1)S(1)}, bf16[3,264,128]{2,1,0:T(8,128)(2,1)S(1)}, u32[]{:S(2)}, u32[]{:S(2)}) collective-permute-start(bf16[3,264,128]{2,1,0:T(8,128)(2,1)S(1)} %collective-permute-done.6), channel_id=1, source_target_pairs={{0,64},{64,128},{128,192},{192,256},{256,320},{320,384},{384,448},... | collective-permute-start | bytes 608264 | tf_op jit(solution)/shard_map/ppermute | solution.py:23
  60.4 7.2 %collective-permute-start.10 = (bf16[3,264,128]{2,1,0:T(8,128)(2,1)S(1)}, bf16[3,264,128]{2,1,0:T(8,128)(2,1)S(1)}, u32[]{:S(2)}, u32[]{:S(2)}) collective-permute-start(bf16[3,264,128]{2,1,0:T(8,128)(2,1)S(1)} %collective-permute-done.9), channel_id=1, source_target_pairs={{0,448},{64,0},{128,64},{192,128},{256,192},{320,256},{384,320},{4... | collective-permute-start | bytes 608264 | tf_op jit(solution)/shard_map/ppermute | solution.py:26
  68.0 10.5 %copy-start.3 = (s32[4]{0:T(128)S(1)}, s32[4]{0:T(128)}, u32[]{:S(2)}) copy-start(s32[4]{0:T(128)} %constant.168.clone.1) | copy-start | bytes 52
  68.0 11.3 %copy-start.1 = (s32[1024]{0:T(1024)S(1)}, s32[1024]{0:T(1024)}, u32[]{:S(2)}) copy-start(s32[1024]{0:T(1024)} %param.11) | copy-start | bytes 12292
  69.5 14.5 %collective-permute-start.11 = (bf16[3,2112,128]{2,1,0:T(8,128)(2,1)}, bf16[3,2112,128]{2,1,0:T(8,128)(2,1)}, u32[]{:S(2)}, u32[]{:S(2)}) collective-permute-start(bf16[3,2112,128]{2,1,0:T(8,128)(2,1)} %bitcast.14), channel_id=1, source_target_pairs={{0,8},{8,0},{1,9},{9,1},{2,10},{10,2},{3,11},{11,3},{4,12},{12,4},... | collective-permute-start | bytes 4866056 | tf_op jit(solution)/shard_map/ppermute | solution.py:46
  98.2 2.9 %copy-start = (f32[1,1024,256]{1,2,0:T(8,128)}, f32[1,1024,256]{1,2,0:T(8,128)S(1)}, u32[]{:S(2)}) copy-start(f32[1,1024,256]{1,2,0:T(8,128)S(1)} %get-tuple-element.44) | copy-start | bytes 3145732
  101.1 17.7 %all-to-all-start = ((bf16[8,2,128,128]{3,2,1,0:T(8,128)(2,1)}), bf16[8,2,128,128]{3,2,1,0:T(8,128)(2,1)S(1)}, u32[]{:S(2)}, u32[]{:S(2)}) async-start(bf16[8,2,128,128]{3,2,1,0:T(8,128)(2,1)} %broadcast_in_dim.120), calls=%async_computation | async-start | bytes 1048576 | tf_op jit(solution)/shard_map/all_to_all | solution.py:72
  123.4 22.7 %all-to-all-start.1 = ((bf16[8,2,128,128]{3,2,1,0:T(8,128)(2,1)}), bf16[8,2,128,128]{3,2,1,0:T(8,128)(2,1)S(1)}, u32[]{:S(2)}, u32[]{:S(2)}) async-start(bf16[8,2,128,128]{3,2,1,0:T(8,128)(2,1)} %fusion.38), calls=%async_computation.1 | async-start | bytes 1048576 | tf_op jit(solution)/shard_map/all_to_all | solution.py:86
  132.7 13.9 %copy-start.2 = (f32[256]{0:T(256)S(1)}, f32[256]{0:T(256)}, u32[]{:S(2)}) copy-start(f32[256]{0:T(256)} %param.10) | copy-start | bytes 3076
Sparse Core Ops, SparseCore 0:
  28.6 63.6 all-gather.1

commit v15 on v11

--- a/solution.py
+++ b/solution.py
@@ -8,7 +8,8 @@
 SPAN = 16384
 
 
-CTX = ("y", "x", "core")
+CTX = ("y_hi", "y_lo", "x", "core")
+Y = ("y_hi", "y_lo")
 
 
 def shifted(value, axis, steps, count):
@@ -42,7 +43,7 @@
     high_rows = jnp.where(core == 0, partner[:, :, :half], w_local[:, :, half:])
     rows = jnp.concatenate([low_rows, high_rows], axis=1)
     rows = ring_gather(rows, "x", lax.axis_size("x"), 1)
-    rows = ring_gather(rows, "y", lax.axis_size("y"), 1)
+    rows = ring_gather(rows, Y, lax.axis_size(Y), 1)
     other = lax.ppermute(rows, "core", [(0, 1), (1, 0)])
     return jnp.where(
         core == 0,
@@ -58,32 +59,32 @@
 def state_scan(kv_state, tails, row_count):
     count = lax.axis_size(CTX)
     window = min(count - 1, 1 + (SPAN - 1) // row_count)
-    row_len = lax.axis_size("x") * lax.axis_size("core")
-    assert window <= 2 * row_len
+    group = ("y_lo", "x", "core")
+    group_len = lax.axis_size(group)
+    assert window <= group_len
     me = lax.axis_index(CTX)
-    pos = me % row_len
+    pos = me % group_len
     first = me - pos
 
     def tail_of(block):
         return jnp.where(block >= 0, tails[jnp.clip(block, 0, count - 1)], -1.0)
 
     prev_tail = tail_of(me - 1)
-    spread = jnp.broadcast_to(kv_state[None], (row_len,) + kv_state.shape)
-    row = lax.all_to_all(spread, ("x", "core"), 0, 0, tiled=True)
-    places = jnp.arange(row_len)
-    row_tails = tail_of(first + places)
-    in_last = row_tails == row_tails[row_len - 1]
+    spread = jnp.broadcast_to(kv_state.astype(jnp.bfloat16)[None], (group_len,) + kv_state.shape)
+    block_states = lax.all_to_all(spread, group, 0, 0, tiled=True).astype(jnp.float32)
+    places = jnp.arange(group_len)
+    group_tails = tail_of(first + places)
+    in_last = group_tails == group_tails[group_len - 1]
 
     def masked(mask):
-        return jnp.sum(jnp.where(mask[:, None, None, None], row, 0.0), axis=0)
+        return jnp.sum(jnp.where(mask[:, None, None, None], block_states, 0.0), axis=0)
 
-    y_count = lax.axis_size("y")
-    one_back = shifted(masked(in_last), "y", 1, y_count)
-    two_back = shifted(masked(in_last & (places >= pos)), "y", 2, y_count)
-    state = masked((places < pos) & (row_tails == prev_tail))
-    state = state + jnp.where(tail_of(first - 1) == prev_tail, one_back, 0.0)
-    if window > row_len:
-        state = state + jnp.where(tail_of(first - row_len - 1) == prev_tail, two_back, 0.0)
+    rest = masked(in_last & (places >= pos)).astype(jnp.bfloat16)
+    one_back = shifted(rest, "y_hi", 1, lax.axis_size("y_hi")).astype(jnp.float32)
+    state = masked((places < pos) & (group_tails == prev_tail))
+    state = state + jnp.where(
+        (first > 0) & (tail_of(first - 1) == prev_tail), one_back, 0.0
+    )
     return state, prev_tail
 
 
@@ -146,7 +147,7 @@
 def solution(mesh):
     shape = dict(zip(mesh.axis_names, mesh.devices.shape))
     head = shape["head"]
-    fine = Mesh(mesh.devices.reshape(-1, 4, 2, head), (*CTX, "head"))
+    fine = Mesh(mesh.devices.reshape(-1, 2, 4, 2, head), (*CTX, "head"))
     placed = (P(CTX, "head"), P(None, CTX, "head"), P("head"), P(CTX))
     return jax.shard_map(
         per_device, mesh=fine, in_specs=placed, out_specs=P(CTX, "head"), check_vma=False

time: 147 us -> 141 us (0.959)
  the two profiles are of different devices: /device:TPU:26 before, /device:TPU:40 now
where the time goes in v15:
time: 141 us; the launch traced here: 140 us
  starting transfers between devices  44.2 us (31%)
  waiting for transfers between devices  37.1 us (26%)
  local copies, waits for them, and re-layouts  18.5 us (13%)
  between operations  15.4 us (11%)
  matrix products  14.6 us (10%)
  other arithmetic  10.3 us (7%)
    ppermute x6, starting transfers between devices, ring_gather(): lax.ppermute(ahead, axis, [(j, (j + 1) % count) for j in range(count)])  16.5 us
    ppermute x4, starting transfers between devices, ring_gather(): lax.ppermute(behind, axis, [(j, (j - 1) % count) for j in range(count)])  15.7 us
    ppermute x6, waiting for transfers between devices, ring_gather(): lax.ppermute(ahead, axis, [(j, (j + 1) % count) for j in range(count)])  14.2 us
    all_gather x1, waiting for transfers between devices, per_device(): whole = lax.all_gather(tokens, 'head', axis=1, tiled=True)  7.37 us
    ppermute x4, waiting for transfers between devices, ring_gather(): lax.ppermute(behind, axis, [(j, (j - 1) % count) for j in range(count)])  6.53 us
    concatenate x2, local copies, waits for them, and re-layouts, gather_weights(): jnp.concatenate([rows, other], axis=2)  6.17 us
    ppermute x1, waiting for transfers between devices, shifted(): lax.ppermute(value, axis, [(source, source + steps) for source in range(c...  6.06 us
    all_to_all x1, starting transfers between devices, state_scan(): lax.all_to_all(spread, group, 0, 0, tiled=True).astype(jnp.float32)  5.68 us
  transfers between devices with their start and end apart: 15, of which 14 were waited for; matrix products, arithmetic and copies ran while one was open for 21% of the time, Pallas kernels for 0%

profile of v15, /device:TPU:40, one launch (start us, length us, event | category | flops | bytes accessed | tf_op | source)
XLA Modules:
  0.0 140.1 jit_solution(6892703260152388201)
XLA Ops:
  7.9 1.5 %concatenate.31 = bf16[3,33,256]{2,1,0:T(8,128)(2,1)S(1)} pad(bf16[3,32,256]{2,1,0:T(8,128)(2,1)} %param.5, bf16[]{:T(256)} %bitcast), padding=0_0x0_1x0_0 | pad | bytes 99842 | tf_op jit(solution)/shard_map/concatenate | solution.py:97
  9.3 1.9 %collective-permute-start = (bf16[3,33,256]{2,1,0:T(8,128)(2,1)S(1)}, bf16[3,33,256]{2,1,0:T(8,128)(2,1)S(1)}, u32[]{:S(2)}, u32[]{:S(2)}) collective-permute-start(bf16[3,33,256]{2,1,0:T(8,128)(2,1)S(1)} %concatenate.31), channel_id=1, source_target_pairs={{0,8},{8,0},{1,9},{9,1},{2,10},{10,2},{3,11},{11,3},{4,12},{12,4},... | collective-permute-start | bytes 152072 | tf_op jit(solution)/shard_map/ppermute | solution.py:41
  13.9 3.4 %collective-permute-start.1 = (bf16[3,66,128]{2,1,0:T(8,128)(2,1)S(1)}, bf16[3,66,128]{2,1,0:T(8,128)(2,1)S(1)}, u32[]{:S(2)}, u32[]{:S(2)}) collective-permute-start(bf16[3,66,128]{2,1,0:T(8,128)(2,1)S(1)} %pad_maximum_fusion), channel_id=1, source_target_pairs={{0,16},{16,32},{32,48},{48,0},{1,17},{17,33},{33,49},{49,1},{2,18}... | collective-permute-start | bytes 152072 | tf_op jit(solution)/shard_map/ppermute | solution.py:24
  17.3 3.9 %collective-permute-done.1 = bf16[3,66,128]{2,1,0:T(8,128)(2,1)S(1)} collective-permute-done((bf16[3,66,128]{2,1,0:T(8,128)(2,1)S(1)}, bf16[3,66,128]{2,1,0:T(8,128)(2,1)S(1)}, u32[]{:S(2)}, u32[]{:S(2)}) %collective-permute-start.1) | collective-permute-done | bytes 50720 | tf_op jit(solution)/shard_map/ppermute | solution.py:24
  21.2 2.2 %collective-permute-start.2 = (bf16[3,66,128]{2,1,0:T(8,128)(2,1)S(1)}, bf16[3,66,128]{2,1,0:T(8,128)(2,1)S(1)}, u32[]{:S(2)}, u32[]{:S(2)}) collective-permute-start(bf16[3,66,128]{2,1,0:T(8,128)(2,1)S(1)} %collective-permute-done.1), channel_id=1, source_target_pairs={{0,16},{16,32},{32,48},{48,0},{1,17},{17,33},{33,49},{49,1},{2,18}... | collective-permute-start | bytes 152072 | tf_op jit(solution)/shard_map/ppermute | solution.py:24
  23.4 4.9 %collective-permute-start.3 = (bf16[3,66,128]{2,1,0:T(8,128)(2,1)S(1)}, bf16[3,66,128]{2,1,0:T(8,128)(2,1)S(1)}, u32[]{:S(2)}, u32[]{:S(2)}) collective-permute-start(bf16[3,66,128]{2,1,0:T(8,128)(2,1)S(1)} %pad_maximum_fusion), channel_id=1, source_target_pairs={{0,48},{16,0},{32,16},{48,32},{1,49},{17,1},{33,17},{49,33},{2,50}... | collective-permute-start | bytes 152072 | tf_op jit(solution)/shard_map/ppermute | solution.py:27
  28.5 1.6 %collective-permute-done.3 = bf16[3,66,128]{2,1,0:T(8,128)(2,1)S(1)} collective-permute-done((bf16[3,66,128]{2,1,0:T(8,128)(2,1)S(1)}, bf16[3,66,128]{2,1,0:T(8,128)(2,1)S(1)}, u32[]{:S(2)}, u32[]{:S(2)}) %collective-permute-start.3) | collective-permute-done | bytes 50720 | tf_op jit(solution)/shard_map/ppermute | solution.py:27
  30.3 2.6 %collective-permute-start.4 = (bf16[3,264,128]{2,1,0:T(8,128)(2,1)S(1)}, bf16[3,264,128]{2,1,0:T(8,128)(2,1)S(1)}, u32[]{:S(2)}, u32[]{:S(2)}) collective-permute-start(bf16[3,264,128]{2,1,0:T(8,128)(2,1)S(1)} %reshape.179), channel_id=1, source_target_pairs={{0,64},{64,128},{128,192},{192,256},{256,320},{320,384},{384,448},... | collective-permute-start | bytes 608264 | tf_op jit(solution)/shard_map/ppermute | solution.py:24
  32.9 5.0 %collective-permute-done.4 = bf16[3,264,128]{2,1,0:T(8,128)(2,1)S(1)} collective-permute-done((bf16[3,264,128]{2,1,0:T(8,128)(2,1)S(1)}, bf16[3,264,128]{2,1,0:T(8,128)(2,1)S(1)}, u32[]{:S(2)}, u32[]{:S(2)}) %collective-permute-start.4) | collective-permute-done | bytes 202784 | tf_op jit(solution)/shard_map/ppermute | solution.py:24
  37.9 2.6 %collective-permute-start.5 = (bf16[3,264,128]{2,1,0:T(8,128)(2,1)S(1)}, bf16[3,264,128]{2,1,0:T(8,128)(2,1)S(1)}, u32[]{:S(2)}, u32[]{:S(2)}) collective-permute-start(bf16[3,264,128]{2,1,0:T(8,128)(2,1)S(1)} %collective-permute-done.4), channel_id=1, source_target_pairs={{0,64},{64,128},{128,192},{192,256},{256,320},{320,384},{384,448},... | collective-permute-start | bytes 608264 | tf_op jit(solution)/shard_map/ppermute | solution.py:24
  40.5 3.8 %collective-permute-start.8 = (bf16[3,264,128]{2,1,0:T(8,128)(2,1)S(1)}, bf16[3,264,128]{2,1,0:T(8,128)(2,1)S(1)}, u32[]{:S(2)}, u32[]{:S(2)}) collective-permute-start(bf16[3,264,128]{2,1,0:T(8,128)(2,1)S(1)} %reshape.179), channel_id=1, source_target_pairs={{0,448},{64,0},{128,64},{192,128},{256,192},{320,256},{384,320},{4... | collective-permute-start | bytes 608264 | tf_op jit(solution)/shard_map/ppermute | solution.py:27
  44.3 1.8 %collective-permute-done.5 = bf16[3,264,128]{2,1,0:T(8,128)(2,1)S(1)} collective-permute-done((bf16[3,264,128]{2,1,0:T(8,128)(2,1)S(1)}, bf16[3,264,128]{2,1,0:T(8,128)(2,1)S(1)}, u32[]{:S(2)}, u32[]{:S(2)}) %collective-permute-start.5) | collective-permute-done | bytes 202784 | tf_op jit(solution)/shard_map/ppermute | solution.py:24
  46.1 2.9 %collective-permute-start.6 = (bf16[3,264,128]{2,1,0:T(8,128)(2,1)S(1)}, bf16[3,264,128]{2,1,0:T(8,128)(2,1)S(1)}, u32[]{:S(2)}, u32[]{:S(2)}) collective-permute-start(bf16[3,264,128]{2,1,0:T(8,128)(2,1)S(1)} %collective-permute-done.5), channel_id=1, source_target_pairs={{0,64},{64,128},{128,192},{192,256},{256,320},{320,384},{384,448},... | collective-permute-start | bytes 608264 | tf_op jit(solution)/shard_map/ppermute | solution.py:24
  49.5 3.7 %collective-permute-start.9 = (bf16[3,264,128]{2,1,0:T(8,128)(2,1)S(1)}, bf16[3,264,128]{2,1,0:T(8,128)(2,1)S(1)}, u32[]{:S(2)}, u32[]{:S(2)}) collective-permute-start(bf16[3,264,128]{2,1,0:T(8,128)(2,1)S(1)} %collective-permute-done.8), channel_id=1, source_target_pairs={{0,448},{64,0},{128,64},{192,128},{256,192},{320,256},{384,320},{4... | collective-permute-start | bytes 608264 | tf_op jit(solution)/shard_map/ppermute | solution.py:27
  53.2 1.8 %collective-permute-done.6 = bf16[3,264,128]{2,1,0:T(8,128)(2,1)S(1)} collective-permute-done((bf16[3,264,128]{2,1,0:T(8,128)(2,1)S(1)}, bf16[3,264,128]{2,1,0:T(8,128)(2,1)S(1)}, u32[]{:S(2)}, u32[]{:S(2)}) %collective-permute-start.6) | collective-permute-done | bytes 202784 | tf_op jit(solution)/shard_map/ppermute | solution.py:24
  54.9 2.9 %collective-permute-start.7 = (bf16[3,264,128]{2,1,0:T(8,128)(2,1)S(1)}, bf16[3,264,128]{2,1,0:T(8,128)(2,1)S(1)}, u32[]{:S(2)}, u32[]{:S(2)}) collective-permute-start(bf16[3,264,128]{2,1,0:T(8,128)(2,1)S(1)} %collective-permute-done.6), channel_id=1, source_target_pairs={{0,64},{64,128},{128,192},{192,256},{256,320},{320,384},{384,448},... | collective-permute-start | bytes 608264 | tf_op jit(solution)/shard_map/ppermute | solution.py:24
  58.8 3.3 %collective-permute-start.10 = (bf16[3,264,128]{2,1,0:T(8,128)(2,1)S(1)}, bf16[3,264,128]{2,1,0:T(8,128)(2,1)S(1)}, u32[]{:S(2)}, u32[]{:S(2)}) collective-permute-start(bf16[3,264,128]{2,1,0:T(8,128)(2,1)S(1)} %collective-permute-done.9), channel_id=1, source_target_pairs={{0,448},{64,0},{128,64},{192,128},{256,192},{320,256},{384,320},{4... | collective-permute-start | bytes 608264 | tf_op jit(solution)/shard_map/ppermute | solution.py:27
  62.1 1.7 %collective-permute-done.7 = bf16[3,264,128]{2,1,0:T(8,128)(2,1)S(1)} collective-permute-done((bf16[3,264,128]{2,1,0:T(8,128)(2,1)S(1)}, bf16[3,264,128]{2,1,0:T(8,128)(2,1)S(1)}, u32[]{:S(2)}, u32[]{:S(2)}) %collective-permute-start.7) | collective-permute-done | bytes 202784 | tf_op jit(solution)/shard_map/ppermute | solution.py:24
  64.0 3.6 %collective-permute-done.10 = bf16[3,264,128]{2,1,0:T(8,128)(2,1)S(1)} collective-permute-done((bf16[3,264,128]{2,1,0:T(8,128)(2,1)S(1)}, bf16[3,264,128]{2,1,0:T(8,128)(2,1)S(1)}, u32[]{:S(2)}, u32[]{:S(2)}) %collective-permute-start.10) | collective-permute-done | bytes 202784 | tf_op jit(solution)/shard_map/ppermute | solution.py:27
  69.4 1.9 %collective-permute-start.11 = (bf16[3,2112,128]{2,1,0:T(8,128)(2,1)}, bf16[3,2112,128]{2,1,0:T(8,128)(2,1)}, u32[]{:S(2)}, u32[]{:S(2)}) collective-permute-start(bf16[3,2112,128]{2,1,0:T(8,128)(2,1)} %bitcast.14), channel_id=1, source_target_pairs={{0,8},{8,0},{1,9},{9,1},{2,10},{10,2},{3,11},{11,3},{4,12},{12,4},... | collective-permute-start | bytes 4866056 | tf_op jit(solution)/shard_map/ppermute | solution.py:47
  74.9 2.5 %concatenate.35 = bf16[3,64,33,128]{3,2,1,0:T(8,128)(2,1)S(1)} reshape(bf16[3,8,264,128]{3,2,1,0:T(8,128)(2,1)} %copy.31) | data formatting | bytes 3244032 | tf_op jit(solution)/shard_map/concatenate | solution.py:50
  77.4 3.7 %concatenate.36 = bf16[3,64,33,128]{3,2,1,0:T(8,128)(2,1)} reshape(bf16[3,2112,128]{2,1,0:T(8,128)(2,1)} %collective-permute-done.11) | data formatting | bytes 3244032 | tf_op jit(solution)/shard_map/concatenate | solution.py:50
  81.1 2.9 %maximum_select_fusion = bf16[3,64,33,256]{3,2,1,0:T(8,128)(2,1)S(1)} fusion(bf16[3,64,33,128]{3,2,1,0:T(8,128)(2,1)} %concatenate.36, bf16[3,64,33,128]{3,2,1,0:T(8,128)(2,1)S(1)} %concatenate.35, pred[]{:T(512)S(6)} %eq.81), kind=kLoop, calls=%fused_computation.4 | loop fusion | flops 14598144 | bytes 6488065 | tf_op jit(solution)/shard_map/jit(_where)/select_n | solution.py:48
  85.9 7.4 %all-gather.2.cloned.1.call-done = bf16[1024,2048]{1,0:T(8,128)(2,1)} async-done(((bf16[1024,256]{1,0:T(8,128)(2,1)}), bf16[1024,2048]{1,0:T(8,128)(2,1)}) %all-gather.2.cloned.1.call-update) | async-done | bytes 4194320 | tf_op jit(solution)/shard_map/all_gather | solution.py:92
  93.3 4.6 %fusion.9 = bf16[2,1024,256]{1,2,0:T(8,128)(2,1)S(1)} fusion(bf16[2,2048,256]{2,1,0:T(8,128)(2,1)S(1)} %bitcast.95, bf16[1024,2048]{1,0:T(8,128)(2,1)} %all-gather.2.cloned.1.call-done), kind=kOutput, calls=%fused_computation.21 | convolution fusion | flops 2148007936 | bytes 7340032 | tf_op jit(solution)/shard_map/tr,grc->gtc/dot_general | solution.py:101
  101.0 5.7 %all-to-all-start = ((bf16[16,2,128,128]{3,2,1,0:T(8,128)(2,1)}), bf16[16,2,128,128]{3,2,1,0:T(8,128)(2,1)S(1)}, u32[]{:S(2)}, u32[]{:S(2)}) async-start(bf16[16,2,128,128]{3,2,1,0:T(8,128)(2,1)} %broadcast_in_dim.107), calls=%async_computation | async-start | bytes 2097152 | tf_op jit(solution)/shard_map/all_to_all | solution.py:74
  110.0 4.2 %fusion.20 = bf16[1024,256]{0,1:T(8,128)(2,1)S(1)} fusion(bf16[2048,256]{1,0:T(8,128)(2,1)} %bitcast.100, bf16[1024,2048]{1,0:T(8,128)(2,1)} %all-gather.2.cloned.1.call-done), kind=kOutput, calls=%fused_computation.32 | convolution fusion | flops 1075314688 | bytes 5767168 | tf_op jit(solution)/shard_map/tr,rc->tc/dot_general | solution.py:114
  115.3 1.9 %fusion.17 = f32[512,2,128]{0,2,1:T(8,128)S(1)} fusion(bf16[512,2,128]{0,2,1:T(8,128)(2,1)} %bitcast.104, bf16[512,2,128]{0,2,1:T(8,128)(2,1)} %bitcast.106, bf16[512,2,128]{0,2,1:T(8,128)(2,1)S(1)} %bitcast.103, pred[512,512]{1,0:T(8,128)(4,1)} %fusion.25), kind=kOutput, calls=%fused_computation.29 | convolution fusion | flops 269484032 | bytes 1572864 | tf_op jit(solution)/shard_map/hbs,she->bhe/dot_general | solution.py:134
  117.2 3.0 %fusion.16 = f32[512,2,128]{0,2,1:T(8,128)S(1)} fusion(bf16[1024,2,128]{0,2,1:T(8,128)(2,1)S(1)} %bitcast.102, bf16[512,2,128]{0,2,1:T(8,128)(2,1)} %bitcast.105, pred[512,1024]{1,0:T(8,128)(4,1)} %fusion.4, f32[1024,2,128]{0,2,1:T(8,128)} %bitcast.99), kind=kOutput, calls=%fused_computation.28 | convolution fusion | flops 540278784 | bytes 2883584 | tf_op jit(solution)/shard_map/hbs,she->bhe/dot_general | solution.py:134
  120.2 1.7 %all-to-all-done = bf16[16,2,128,128]{3,2,1,0:T(8,128)(2,1)S(1)} async-done(((bf16[16,2,128,128]{3,2,1,0:T(8,128)(2,1)}), bf16[16,2,128,128]{3,2,1,0:T(8,128)(2,1)S(1)}, u32[]{:S(2)}, u32[]{:S(2)}) %all-to-all-start) | async-done | bytes 1048608 | tf_op jit(solution)/shard_map/all_to_all | solution.py:74
  122.4 2.5 %collective-permute-start.12 = (bf16[2,128,128]{2,1,0:T(8,128)(2,1)S(1)}, bf16[2,128,128]{2,1,0:T(8,128)(2,1)S(1)}, u32[]{:S(2)}, u32[]{:S(2)}) collective-permute-start(bf16[2,128,128]{2,1,0:T(8,128)(2,1)S(1)} %get-tuple-element.9), channel_id=1, source_target_pairs={{0,128},{128,256},{256,384},{1,129},{129,257},{257,385},{2,130},{1... | collective-permute-start | bytes 196616 | tf_op jit(solution)/shard_map/ppermute | solution.py:16
  125.6 6.1 %collective-permute-done.12 = bf16[2,128,128]{2,1,0:T(8,128)(2,1)S(1)} collective-permute-done((bf16[2,128,128]{2,1,0:T(8,128)(2,1)S(1)}, bf16[2,128,128]{2,1,0:T(8,128)(2,1)S(1)}, u32[]{:S(2)}, u32[]{:S(2)}) %collective-permute-start.12) | collective-permute-done | bytes 65568 | tf_op jit(solution)/shard_map/ppermute | solution.py:16
  (75 shorter events, 22.0 us)
Async XLA Ops:
  6.5 86.8 %all-gather.2.cloned.1.call-start = ((), (), s32[]{:S(2)}) async-start(), calls=%async_computation.1 | async-start | bytes 4718592 | tf_op jit(solution)/shard_map/all_gather | solution.py:92
  9.3 3.1 %collective-permute-start = (bf16[3,33,256]{2,1,0:T(8,128)(2,1)S(1)}, bf16[3,33,256]{2,1,0:T(8,128)(2,1)S(1)}, u32[]{:S(2)}, u32[]{:S(2)}) collective-permute-start(bf16[3,33,256]{2,1,0:T(8,128)(2,1)S(1)} %concatenate.31), channel_id=1, source_target_pairs={{0,8},{8,0},{1,9},{9,1},{2,10},{10,2},{3,11},{11,3},{4,12},{12,4},... | collective-permute-start | bytes 152072 | tf_op jit(solution)/shard_map/ppermute | solution.py:41
  13.9 7.3 %collective-permute-start.1 = (bf16[3,66,128]{2,1,0:T(8,128)(2,1)S(1)}, bf16[3,66,128]{2,1,0:T(8,128)(2,1)S(1)}, u32[]{:S(2)}, u32[]{:S(2)}) collective-permute-start(bf16[3,66,128]{2,1,0:T(8,128)(2,1)S(1)} %pad_maximum_fusion), channel_id=1, source_target_pairs={{0,16},{16,32},{32,48},{48,0},{1,17},{17,33},{33,49},{49,1},{2,18}... | collective-permute-start | bytes 152072 | tf_op jit(solution)/shard_map/ppermute | solution.py:24
  21.2 7.2 %collective-permute-start.2 = (bf16[3,66,128]{2,1,0:T(8,128)(2,1)S(1)}, bf16[3,66,128]{2,1,0:T(8,128)(2,1)S(1)}, u32[]{:S(2)}, u32[]{:S(2)}) collective-permute-start(bf16[3,66,128]{2,1,0:T(8,128)(2,1)S(1)} %collective-permute-done.1), channel_id=1, source_target_pairs={{0,16},{16,32},{32,48},{48,0},{1,17},{17,33},{33,49},{49,1},{2,18}... | collective-permute-start | bytes 152072 | tf_op jit(solution)/shard_map/ppermute | solution.py:24
  23.4 6.7 %collective-permute-start.3 = (bf16[3,66,128]{2,1,0:T(8,128)(2,1)S(1)}, bf16[3,66,128]{2,1,0:T(8,128)(2,1)S(1)}, u32[]{:S(2)}, u32[]{:S(2)}) collective-permute-start(bf16[3,66,128]{2,1,0:T(8,128)(2,1)S(1)} %pad_maximum_fusion), channel_id=1, source_target_pairs={{0,48},{16,0},{32,16},{48,32},{1,49},{17,1},{33,17},{49,33},{2,50}... | collective-permute-start | bytes 152072 | tf_op jit(solution)/shard_map/ppermute | solution.py:27
  30.3 7.6 %collective-permute-start.4 = (bf16[3,264,128]{2,1,0:T(8,128)(2,1)S(1)}, bf16[3,264,128]{2,1,0:T(8,128)(2,1)S(1)}, u32[]{:S(2)}, u32[]{:S(2)}) collective-permute-start(bf16[3,264,128]{2,1,0:T(8,128)(2,1)S(1)} %reshape.179), channel_id=1, source_target_pairs={{0,64},{64,128},{128,192},{192,256},{256,320},{320,384},{384,448},... | collective-permute-start | bytes 608264 | tf_op jit(solution)/shard_map/ppermute | solution.py:24
  37.9 8.2 %collective-permute-start.5 = (bf16[3,264,128]{2,1,0:T(8,128)(2,1)S(1)}, bf16[3,264,128]{2,1,0:T(8,128)(2,1)S(1)}, u32[]{:S(2)}, u32[]{:S(2)}) collective-permute-start(bf16[3,264,128]{2,1,0:T(8,128)(2,1)S(1)} %collective-permute-done.4), channel_id=1, source_target_pairs={{0,64},{64,128},{128,192},{192,256},{256,320},{320,384},{384,448},... | collective-permute-start | bytes 608264 | tf_op jit(solution)/shard_map/ppermute | solution.py:24
  40.5 9.0 %collective-permute-start.8 = (bf16[3,264,128]{2,1,0:T(8,128)(2,1)S(1)}, bf16[3,264,128]{2,1,0:T(8,128)(2,1)S(1)}, u32[]{:S(2)}, u32[]{:S(2)}) collective-permute-start(bf16[3,264,128]{2,1,0:T(8,128)(2,1)S(1)} %reshape.179), channel_id=1, source_target_pairs={{0,448},{64,0},{128,64},{192,128},{256,192},{320,256},{384,320},{4... | collective-permute-start | bytes 608264 | tf_op jit(solution)/shard_map/ppermute | solution.py:27
  46.1 8.8 %collective-permute-start.6 = (bf16[3,264,128]{2,1,0:T(8,128)(2,1)S(1)}, bf16[3,264,128]{2,1,0:T(8,128)(2,1)S(1)}, u32[]{:S(2)}, u32[]{:S(2)}) collective-permute-start(bf16[3,264,128]{2,1,0:T(8,128)(2,1)S(1)} %collective-permute-done.5), channel_id=1, source_target_pairs={{0,64},{64,128},{128,192},{192,256},{256,320},{320,384},{384,448},... | collective-permute-start | bytes 608264 | tf_op jit(solution)/shard_map/ppermute | solution.py:24
  49.5 9.3 %collective-permute-start.9 = (bf16[3,264,128]{2,1,0:T(8,128)(2,1)S(1)}, bf16[3,264,128]{2,1,0:T(8,128)(2,1)S(1)}, u32[]{:S(2)}, u32[]{:S(2)}) collective-permute-start(bf16[3,264,128]{2,1,0:T(8,128)(2,1)S(1)} %collective-permute-done.8), channel_id=1, source_target_pairs={{0,448},{64,0},{128,64},{192,128},{256,192},{320,256},{384,320},{4... | collective-permute-start | bytes 608264 | tf_op jit(solution)/shard_map/ppermute | solution.py:27
  54.9 8.8 %collective-permute-start.7 = (bf16[3,264,128]{2,1,0:T(8,128)(2,1)S(1)}, bf16[3,264,128]{2,1,0:T(8,128)(2,1)S(1)}, u32[]{:S(2)}, u32[]{:S(2)}) collective-permute-start(bf16[3,264,128]{2,1,0:T(8,128)(2,1)S(1)} %collective-permute-done.6), channel_id=1, source_target_pairs={{0,64},{64,128},{128,192},{192,256},{256,320},{320,384},{384,448},... | collective-permute-start | bytes 608264 | tf_op jit(solution)/shard_map/ppermute | solution.py:24
  58.8 8.8 %collective-permute-start.10 = (bf16[3,264,128]{2,1,0:T(8,128)(2,1)S(1)}, bf16[3,264,128]{2,1,0:T(8,128)(2,1)S(1)}, u32[]{:S(2)}, u32[]{:S(2)}) collective-permute-start(bf16[3,264,128]{2,1,0:T(8,128)(2,1)S(1)} %collective-permute-done.9), channel_id=1, source_target_pairs={{0,448},{64,0},{128,64},{192,128},{256,192},{320,256},{384,320},{4... | collective-permute-start | bytes 608264 | tf_op jit(solution)/shard_map/ppermute | solution.py:27
  67.9 4.0 %copy-start.1 = (s32[1024]{0:T(1024)S(1)}, s32[1024]{0:T(1024)}, u32[]{:S(2)}) copy-start(s32[1024]{0:T(1024)} %param.7) | copy-start | bytes 12292
  69.4 8.0 %collective-permute-start.11 = (bf16[3,2112,128]{2,1,0:T(8,128)(2,1)}, bf16[3,2112,128]{2,1,0:T(8,128)(2,1)}, u32[]{:S(2)}, u32[]{:S(2)}) collective-permute-start(bf16[3,2112,128]{2,1,0:T(8,128)(2,1)} %bitcast.14), channel_id=1, source_target_pairs={{0,8},{8,0},{1,9},{9,1},{2,10},{10,2},{3,11},{11,3},{4,12},{12,4},... | collective-permute-start | bytes 4866056 | tf_op jit(solution)/shard_map/ppermute | solution.py:47
  98.1 1.1 copy-start
  101.0 20.9 %all-to-all-start = ((bf16[16,2,128,128]{3,2,1,0:T(8,128)(2,1)}), bf16[16,2,128,128]{3,2,1,0:T(8,128)(2,1)S(1)}, u32[]{:S(2)}, u32[]{:S(2)}) async-start(bf16[16,2,128,128]{3,2,1,0:T(8,128)(2,1)} %broadcast_in_dim.107), calls=%async_computation | async-start | bytes 2097152 | tf_op jit(solution)/shard_map/all_to_all | solution.py:74
  120.2 11.9 %copy-start.2 = (f32[256]{0:T(256)S(1)}, f32[256]{0:T(256)}, u32[]{:S(2)}) copy-start(f32[256]{0:T(256)} %param.6) | copy-start | bytes 3076
  122.4 9.3 %collective-permute-start.12 = (bf16[2,128,128]{2,1,0:T(8,128)(2,1)S(1)}, bf16[2,128,128]{2,1,0:T(8,128)(2,1)S(1)}, u32[]{:S(2)}, u32[]{:S(2)}) collective-permute-start(bf16[2,128,128]{2,1,0:T(8,128)(2,1)S(1)} %get-tuple-element.9), channel_id=1, source_target_pairs={{0,128},{128,256},{256,384},{1,129},{129,257},{257,385},{2,130},{1... | collective-permute-start | bytes 196616 | tf_op jit(solution)/shard_map/ppermute | solution.py:16
Sparse Core Ops, SparseCore 0:
  23.5 69.7 all-gather.1

commit v16 on v12

--- a/solution.py
+++ b/solution.py
@@ -41,7 +41,7 @@
     low_rows = jnp.where(core == 0, w_local[:, :, :half], partner[:, :, half:])
     high_rows = jnp.where(core == 0, partner[:, :, :half], w_local[:, :, half:])
     rows = jnp.concatenate([low_rows, high_rows], axis=1)
-    rows = ring_gather(rows, "x", lax.axis_size("x"), 1)
+    rows = direct_gather(rows, "x", lax.axis_size("x"), 1)
     rows = ring_gather(rows, "y", lax.axis_size("y"), 1)
     other = lax.ppermute(rows, "core", [(0, 1), (1, 0)])
     return jnp.where(
@@ -49,6 +49,20 @@
         jnp.concatenate([rows, other], axis=2),
         jnp.concatenate([other, rows], axis=2),
     )
+
+
+def direct_gather(value, axis, count, dim):
+    low = -(count // 2)
+    by_offset = {0: value}
+    for off in range(low, low + count):
+        if off != 0:
+            by_offset[off] = lax.ppermute(value, axis, [(j, (j - off) % count) for j in range(count)])
+    stacked = jnp.stack([by_offset[off] for off in range(low, low + count)], axis=0)
+    ordered = jnp.roll(stacked, lax.axis_index(axis) + low, axis=0)
+    moved = jnp.moveaxis(ordered, 0, dim)
+    shape = list(value.shape)
+    shape[dim] *= count
+    return moved.reshape(shape)
 
 
 def feature_map(values):

time: 140 us -> 134 us (0.957)
  waiting for transfers between devices: 31.9 us -> 23.2 us
  starting transfers between devices: 48.8 us -> 51.1 us
    ppermute x6 -> x4, starting transfers between devices: 23.7 us -> 13 us  [ring_gather(): lax.ppermute(ahead, axis, [(j, (j + 1) % count) for j in range(count)])]
    ppermute x0 -> x3, starting transfers between devices: none -> 9.88 us  [direct_gather(): lax.ppermute(value, axis, [(j, (j - off) % count) for j in range(count)])]
    ppermute x4 -> x3, waiting for transfers between devices: 9.46 us -> 4.11 us  [ring_gather(): lax.ppermute(behind, axis, [(j, (j - 1) % count) for j in range(count)])]
    ppermute x4 -> x3, starting transfers between devices: 8.48 us -> 11.6 us  [ring_gather(): lax.ppermute(behind, axis, [(j, (j - 1) % count) for j in range(count)])]
    all_gather x1, waiting for transfers between devices: 6.91 us -> 4.14 us  [per_device(): whole = lax.all_gather(tokens, 'head', axis=1, tiled=True)]
    ppermute x6 -> x4, waiting for transfers between devices: 11.9 us -> 9.33 us  [ring_gather(): lax.ppermute(ahead, axis, [(j, (j + 1) % count) for j in range(count)])]
    ppermute x0 -> x3, waiting for transfers between devices: none -> 2.06 us  [direct_gather(): lax.ppermute(value, axis, [(j, (j - off) % count) for j in range(count)])]
  transfers between devices with their start and end apart: 16 -> 16, of which waited for: 13 -> 12; matrix products, arithmetic and copies ran while one was open for 21% -> 22% of each run, Pallas kernels for 0% -> 0%
where the time goes in v16:
time: 134 us; the launch traced here: 133 us
  starting transfers between devices  51.1 us (38%)
  waiting for transfers between devices  23.2 us (17%)
  local copies, waits for them, and re-layouts  17.8 us (13%)
  between operations  15.9 us (12%)
  matrix products  14.4 us (11%)
  other arithmetic  10.1 us (8%)
    ppermute x4, starting transfers between devices, ring_gather(): lax.ppermute(ahead, axis, [(j, (j + 1) % count) for j in range(count)])  13 us
    ppermute x3, starting transfers between devices, ring_gather(): lax.ppermute(behind, axis, [(j, (j - 1) % count) for j in range(count)])  11.6 us
    ppermute x3, starting transfers between devices, direct_gather(): lax.ppermute(value, axis, [(j, (j - off) % count) for j in range(count)])  9.88 us
    ppermute x4, waiting for transfers between devices, ring_gather(): lax.ppermute(ahead, axis, [(j, (j + 1) % count) for j in range(count)])  9.33 us
    ppermute x2, starting transfers between devices, shifted(): lax.ppermute(value, axis, [(source, source + steps) for source in range(c...  8.02 us
    concatenate x2, local copies, waits for them, and re-layouts, gather_weights(): jnp.concatenate([rows, other], axis=2)  6.16 us
    all_to_all x1, starting transfers between devices, state_scan(): lax.all_to_all(spread, ('x', 'core'), 0, 0, tiled=True).astype(jnp.float32)  4.78 us
    dot_general x2, matrix products, per_device(): jnp.einsum('hbs,she->bhe', weights, values[:key_end], preferred_element_t...  4.73 us
  transfers between devices with their start and end apart: 16, of which 12 were waited for; matrix products, arithmetic and copies ran while one was open for 22% of the time, Pallas kernels for 0%

profile of v16, /device:TPU:18, one launch (start us, length us, event | category | flops | bytes accessed | tf_op | source)
XLA Modules:
  0.0 132.6 jit_solution(4561768235735514698)
XLA Ops:
  7.9 1.5 %concatenate.31 = bf16[3,33,256]{2,1,0:T(8,128)(2,1)S(1)} pad(bf16[3,32,256]{2,1,0:T(8,128)(2,1)} %param.5, bf16[]{:T(256)} %bitcast), padding=0_0x0_1x0_0 | pad | bytes 99842 | tf_op jit(solution)/shard_map/concatenate | solution.py:112
  9.3 1.9 %collective-permute-start = (bf16[3,33,256]{2,1,0:T(8,128)(2,1)S(1)}, bf16[3,33,256]{2,1,0:T(8,128)(2,1)S(1)}, u32[]{:S(2)}, u32[]{:S(2)}) collective-permute-start(bf16[3,33,256]{2,1,0:T(8,128)(2,1)S(1)} %concatenate.31), channel_id=1, source_target_pairs={{0,8},{8,0},{1,9},{9,1},{2,10},{10,2},{3,11},{11,3},{4,12},{12,4},... | collective-permute-start | bytes 152072 | tf_op jit(solution)/shard_map/ppermute | solution.py:40
  12.5 1.4 %slice_select_fusion.1 = (bf16[3,33,128]{2,1,0:T(8,128)(2,1)S(1)}, bf16[3,33,128]{2,1,0:T(8,128)(2,1)S(1)}) fusion(bf16[3,33,256]{2,1,0:T(8,128)(2,1)S(1)} %collective-permute-done, pred[]{:T(512)S(6)} %eq.87, bf16[3,32,256]{2,1,0:T(8,128)(2,1)} %param.5, bf16[]{:T(256)} %bitcast), kind=kLoop, calls=%fused_computation.86 | loop fusion | flops 25344 | bytes 150531 | tf_op jit(solution)/shard_map/jit(_where)/select_n | solution.py:41
  13.9 4.0 %collective-permute-start.1 = (bf16[3,66,128]{2,1,0:T(8,128)(2,1)S(1)}, bf16[3,66,128]{2,1,0:T(8,128)(2,1)S(1)}, u32[]{:S(2)}, u32[]{:S(2)}) collective-permute-start(bf16[3,66,128]{2,1,0:T(8,128)(2,1)S(1)} %pad_maximum_fusion), channel_id=1, source_target_pairs={{0,32},{16,48},{32,0},{48,16},{1,33},{17,49},{33,1},{49,17},{2,34}... | collective-permute-start | bytes 152072 | tf_op jit(solution)/shard_map/ppermute | solution.py:59
  18.0 1.9 %collective-permute-start.2 = (bf16[3,66,128]{2,1,0:T(8,128)(2,1)S(1)}, bf16[3,66,128]{2,1,0:T(8,128)(2,1)S(1)}, u32[]{:S(2)}, u32[]{:S(2)}) collective-permute-start(bf16[3,66,128]{2,1,0:T(8,128)(2,1)S(1)} %pad_maximum_fusion), channel_id=1, source_target_pairs={{0,16},{16,32},{32,48},{48,0},{1,17},{17,33},{33,49},{49,1},{2,18}... | collective-permute-start | bytes 152072 | tf_op jit(solution)/shard_map/ppermute | solution.py:59
  19.9 3.9 %collective-permute-start.3 = (bf16[3,66,128]{2,1,0:T(8,128)(2,1)S(1)}, bf16[3,66,128]{2,1,0:T(8,128)(2,1)S(1)}, u32[]{:S(2)}, u32[]{:S(2)}) collective-permute-start(bf16[3,66,128]{2,1,0:T(8,128)(2,1)S(1)} %pad_maximum_fusion), channel_id=1, source_target_pairs={{0,48},{16,0},{32,16},{48,32},{1,49},{17,1},{33,17},{49,33},{2,50}... | collective-permute-start | bytes 152072 | tf_op jit(solution)/shard_map/ppermute | solution.py:59
  24.1 1.9 %collective-permute-done.3 = bf16[3,66,128]{2,1,0:T(8,128)(2,1)S(1)} collective-permute-done((bf16[3,66,128]{2,1,0:T(8,128)(2,1)S(1)}, bf16[3,66,128]{2,1,0:T(8,128)(2,1)S(1)}, u32[]{:S(2)}, u32[]{:S(2)}) %collective-permute-start.3) | collective-permute-done | bytes 50720 | tf_op jit(solution)/shard_map/ppermute | solution.py:59
  26.2 3.5 %collective-permute-start.4 = (bf16[3,264,128]{2,1,0:T(8,128)(2,1)S(1)}, bf16[3,264,128]{2,1,0:T(8,128)(2,1)S(1)}, u32[]{:S(2)}, u32[]{:S(2)}) collective-permute-start(bf16[3,264,128]{2,1,0:T(8,128)(2,1)S(1)} %reshape.183), channel_id=1, source_target_pairs={{0,64},{64,128},{128,192},{192,256},{256,320},{320,384},{384,448},... | collective-permute-start | bytes 608264 | tf_op jit(solution)/shard_map/ppermute | solution.py:23
  29.7 4.1 %collective-permute-done.4 = bf16[3,264,128]{2,1,0:T(8,128)(2,1)S(1)} collective-permute-done((bf16[3,264,128]{2,1,0:T(8,128)(2,1)S(1)}, bf16[3,264,128]{2,1,0:T(8,128)(2,1)S(1)}, u32[]{:S(2)}, u32[]{:S(2)}) %collective-permute-start.4) | collective-permute-done | bytes 202784 | tf_op jit(solution)/shard_map/ppermute | solution.py:23
  33.9 3.8 %collective-permute-start.5 = (bf16[3,264,128]{2,1,0:T(8,128)(2,1)S(1)}, bf16[3,264,128]{2,1,0:T(8,128)(2,1)S(1)}, u32[]{:S(2)}, u32[]{:S(2)}) collective-permute-start(bf16[3,264,128]{2,1,0:T(8,128)(2,1)S(1)} %collective-permute-done.4), channel_id=1, source_target_pairs={{0,64},{64,128},{128,192},{192,256},{256,320},{320,384},{384,448},... | collective-permute-start | bytes 608264 | tf_op jit(solution)/shard_map/ppermute | solution.py:23
  37.6 4.2 %collective-permute-start.8 = (bf16[3,264,128]{2,1,0:T(8,128)(2,1)S(1)}, bf16[3,264,128]{2,1,0:T(8,128)(2,1)S(1)}, u32[]{:S(2)}, u32[]{:S(2)}) collective-permute-start(bf16[3,264,128]{2,1,0:T(8,128)(2,1)S(1)} %reshape.183), channel_id=1, source_target_pairs={{0,448},{64,0},{128,64},{192,128},{256,192},{320,256},{384,320},{4... | collective-permute-start | bytes 608264 | tf_op jit(solution)/shard_map/ppermute | solution.py:26
  41.8 1.8 %collective-permute-done.5 = bf16[3,264,128]{2,1,0:T(8,128)(2,1)S(1)} collective-permute-done((bf16[3,264,128]{2,1,0:T(8,128)(2,1)S(1)}, bf16[3,264,128]{2,1,0:T(8,128)(2,1)S(1)}, u32[]{:S(2)}, u32[]{:S(2)}) %collective-permute-start.5) | collective-permute-done | bytes 202784 | tf_op jit(solution)/shard_map/ppermute | solution.py:23
  43.6 2.9 %collective-permute-start.6 = (bf16[3,264,128]{2,1,0:T(8,128)(2,1)S(1)}, bf16[3,264,128]{2,1,0:T(8,128)(2,1)S(1)}, u32[]{:S(2)}, u32[]{:S(2)}) collective-permute-start(bf16[3,264,128]{2,1,0:T(8,128)(2,1)S(1)} %collective-permute-done.5), channel_id=1, source_target_pairs={{0,64},{64,128},{128,192},{192,256},{256,320},{320,384},{384,448},... | collective-permute-start | bytes 608264 | tf_op jit(solution)/shard_map/ppermute | solution.py:23
  46.9 3.7 %collective-permute-start.9 = (bf16[3,264,128]{2,1,0:T(8,128)(2,1)S(1)}, bf16[3,264,128]{2,1,0:T(8,128)(2,1)S(1)}, u32[]{:S(2)}, u32[]{:S(2)}) collective-permute-start(bf16[3,264,128]{2,1,0:T(8,128)(2,1)S(1)} %collective-permute-done.8), channel_id=1, source_target_pairs={{0,448},{64,0},{128,64},{192,128},{256,192},{320,256},{384,320},{4... | collective-permute-start | bytes 608264 | tf_op jit(solution)/shard_map/ppermute | solution.py:26
  50.6 1.8 %collective-permute-done.6 = bf16[3,264,128]{2,1,0:T(8,128)(2,1)S(1)} collective-permute-done((bf16[3,264,128]{2,1,0:T(8,128)(2,1)S(1)}, bf16[3,264,128]{2,1,0:T(8,128)(2,1)S(1)}, u32[]{:S(2)}, u32[]{:S(2)}) %collective-permute-start.6) | collective-permute-done | bytes 202784 | tf_op jit(solution)/shard_map/ppermute | solution.py:23
  52.4 2.9 %collective-permute-start.7 = (bf16[3,264,128]{2,1,0:T(8,128)(2,1)S(1)}, bf16[3,264,128]{2,1,0:T(8,128)(2,1)S(1)}, u32[]{:S(2)}, u32[]{:S(2)}) collective-permute-start(bf16[3,264,128]{2,1,0:T(8,128)(2,1)S(1)} %collective-permute-done.6), channel_id=1, source_target_pairs={{0,64},{64,128},{128,192},{192,256},{256,320},{320,384},{384,448},... | collective-permute-start | bytes 608264 | tf_op jit(solution)/shard_map/ppermute | solution.py:23
  55.8 3.8 %collective-permute-start.10 = (bf16[3,264,128]{2,1,0:T(8,128)(2,1)S(1)}, bf16[3,264,128]{2,1,0:T(8,128)(2,1)S(1)}, u32[]{:S(2)}, u32[]{:S(2)}) collective-permute-start(bf16[3,264,128]{2,1,0:T(8,128)(2,1)S(1)} %collective-permute-done.9), channel_id=1, source_target_pairs={{0,448},{64,0},{128,64},{192,128},{256,192},{320,256},{384,320},{4... | collective-permute-start | bytes 608264 | tf_op jit(solution)/shard_map/ppermute | solution.py:26
  59.6 1.7 %collective-permute-done.7 = bf16[3,264,128]{2,1,0:T(8,128)(2,1)S(1)} collective-permute-done((bf16[3,264,128]{2,1,0:T(8,128)(2,1)S(1)}, bf16[3,264,128]{2,1,0:T(8,128)(2,1)S(1)}, u32[]{:S(2)}, u32[]{:S(2)}) %collective-permute-start.7) | collective-permute-done | bytes 202784 | tf_op jit(solution)/shard_map/ppermute | solution.py:23
  61.5 3.2 %collective-permute-done.10 = bf16[3,264,128]{2,1,0:T(8,128)(2,1)S(1)} collective-permute-done((bf16[3,264,128]{2,1,0:T(8,128)(2,1)S(1)}, bf16[3,264,128]{2,1,0:T(8,128)(2,1)S(1)}, u32[]{:S(2)}, u32[]{:S(2)}) %collective-permute-start.10) | collective-permute-done | bytes 202784 | tf_op jit(solution)/shard_map/ppermute | solution.py:26
  66.5 1.9 %collective-permute-start.11 = (bf16[3,2112,128]{2,1,0:T(8,128)(2,1)}, bf16[3,2112,128]{2,1,0:T(8,128)(2,1)}, u32[]{:S(2)}, u32[]{:S(2)}) collective-permute-start(bf16[3,2112,128]{2,1,0:T(8,128)(2,1)} %bitcast.14), channel_id=1, source_target_pairs={{0,8},{8,0},{1,9},{9,1},{2,10},{10,2},{3,11},{11,3},{4,12},{12,4},... | collective-permute-start | bytes 4866056 | tf_op jit(solution)/shard_map/ppermute | solution.py:46
  72.1 2.5 %concatenate.35 = bf16[3,64,33,128]{3,2,1,0:T(8,128)(2,1)S(1)} reshape(bf16[3,8,264,128]{3,2,1,0:T(8,128)(2,1)} %copy.31) | data formatting | bytes 3244032 | tf_op jit(solution)/shard_map/concatenate | solution.py:49
  74.5 3.7 %concatenate.36 = bf16[3,64,33,128]{3,2,1,0:T(8,128)(2,1)} reshape(bf16[3,2112,128]{2,1,0:T(8,128)(2,1)} %collective-permute-done.11) | data formatting | bytes 3244032 | tf_op jit(solution)/shard_map/concatenate | solution.py:49
  78.2 2.8 %maximum_select_fusion = bf16[3,64,33,256]{3,2,1,0:T(8,128)(2,1)S(1)} fusion(bf16[3,64,33,128]{3,2,1,0:T(8,128)(2,1)} %concatenate.36, bf16[3,64,33,128]{3,2,1,0:T(8,128)(2,1)S(1)} %concatenate.35, pred[]{:T(512)S(6)} %eq.87), kind=kLoop, calls=%fused_computation.4 | loop fusion | flops 14598144 | bytes 6488065 | tf_op jit(solution)/shard_map/jit(_where)/select_n | solution.py:47
  83.0 4.1 %all-gather.2.cloned.1.call-done = bf16[1024,2048]{1,0:T(8,128)(2,1)} async-done(((bf16[1024,256]{1,0:T(8,128)(2,1)}), bf16[1024,2048]{1,0:T(8,128)(2,1)}) %all-gather.2.cloned.1.call-update) | async-done | bytes 4194320 | tf_op jit(solution)/shard_map/all_gather | solution.py:107
  87.2 4.6 %fusion.7 = bf16[2,1024,256]{1,2,0:T(8,128)(2,1)S(1)} fusion(bf16[2,2048,256]{2,1,0:T(8,128)(2,1)S(1)} %bitcast.97, bf16[1024,2048]{1,0:T(8,128)(2,1)} %all-gather.2.cloned.1.call-done), kind=kOutput, calls=%fused_computation.20 | convolution fusion | flops 2148007936 | bytes 7340032 | tf_op jit(solution)/shard_map/tr,grc->gtc/dot_general | solution.py:116
  94.3 4.8 %all-to-all-start = ((bf16[8,2,128,128]{3,2,1,0:T(8,128)(2,1)}), bf16[8,2,128,128]{3,2,1,0:T(8,128)(2,1)S(1)}, u32[]{:S(2)}, u32[]{:S(2)}) async-start(bf16[8,2,128,128]{3,2,1,0:T(8,128)(2,1)} %broadcast_in_dim.115), calls=%async_computation | async-start | bytes 1048576 | tf_op jit(solution)/shard_map/all_to_all | solution.py:86
  101.6 4.2 %fusion.21 = bf16[1024,256]{0,1:T(8,128)(2,1)S(1)} fusion(bf16[2048,256]{1,0:T(8,128)(2,1)} %bitcast.101, bf16[1024,2048]{1,0:T(8,128)(2,1)} %all-gather.2.cloned.1.call-done), kind=kOutput, calls=%fused_computation.34 | convolution fusion | flops 1075314688 | bytes 5767168 | tf_op jit(solution)/shard_map/tr,rc->tc/dot_general | solution.py:129
  106.9 1.9 %fusion.15 = f32[512,2,128]{0,2,1:T(8,128)S(1)} fusion(bf16[512,2,128]{0,2,1:T(8,128)(2,1)} %bitcast.105, bf16[512,2,128]{0,2,1:T(8,128)(2,1)} %bitcast.107, bf16[512,2,128]{0,2,1:T(8,128)(2,1)S(1)} %bitcast.104, pred[512,512]{1,0:T(8,128)(4,1)} %fusion.26), kind=kOutput, calls=%fused_computation.28 | convolution fusion | flops 269484032 | bytes 1572864 | tf_op jit(solution)/shard_map/hbs,she->bhe/dot_general | solution.py:149
  109.3 2.8 %fusion.14 = f32[512,2,128]{0,2,1:T(8,128)S(1)} fusion(bf16[1024,2,128]{0,2,1:T(8,128)(2,1)} %bitcast.103, bf16[512,2,128]{0,2,1:T(8,128)(2,1)} %bitcast.106, pred[512,1024]{1,0:T(8,128)(4,1)} %fusion.2, f32[1024,2,128]{0,2,1:T(8,128)S(1)} %bitcast.100), kind=kOutput, calls=%fused_computation.27 | convolution fusion | flops 540278784 | bytes 2883584 | tf_op jit(solution)/shard_map/hbs,she->bhe/dot_general | solution.py:149
  112.5 5.5 %collective-permute-start.13 = (bf16[2,128,128]{2,1,0:T(8,128)(2,1)S(1)}, bf16[2,128,128]{2,1,0:T(8,128)(2,1)S(1)}, u32[]{:S(2)}, u32[]{:S(2)}) collective-permute-start(bf16[2,128,128]{2,1,0:T(8,128)(2,1)S(1)} %get-tuple-element.10), channel_id=1, source_target_pairs={{0,128},{64,192},{128,256},{192,320},{256,384},{320,448},{1,129},{... | collective-permute-start | bytes 196616 | tf_op jit(solution)/shard_map/ppermute | solution.py:15
  118.0 2.5 %collective-permute-start.12 = (bf16[2,128,128]{2,1,0:T(8,128)(2,1)S(1)}, bf16[2,128,128]{2,1,0:T(8,128)(2,1)S(1)}, u32[]{:S(2)}, u32[]{:S(2)}) collective-permute-start(bf16[2,128,128]{2,1,0:T(8,128)(2,1)S(1)} %get-tuple-element.9), channel_id=1, source_target_pairs={{0,64},{64,128},{128,192},{192,256},{256,320},{320,384},{384,448},... | collective-permute-start | bytes 196616 | tf_op jit(solution)/shard_map/ppermute | solution.py:15
  121.8 2.4 %collective-permute-done.12 = bf16[2,128,128]{2,1,0:T(8,128)(2,1)S(1)} collective-permute-done((bf16[2,128,128]{2,1,0:T(8,128)(2,1)S(1)}, bf16[2,128,128]{2,1,0:T(8,128)(2,1)S(1)}, u32[]{:S(2)}, u32[]{:S(2)}) %collective-permute-start.12) | collective-permute-done | bytes 65568 | tf_op jit(solution)/shard_map/ppermute | solution.py:15
  (77 shorter events, 19.2 us)
Async XLA Ops:
  6.5 80.7 %all-gather.2.cloned.1.call-start = ((), (), s32[]{:S(2)}) async-start(), calls=%async_computation.1 | async-start | bytes 4718592 | tf_op jit(solution)/shard_map/all_gather | solution.py:107
  9.3 3.1 %collective-permute-start = (bf16[3,33,256]{2,1,0:T(8,128)(2,1)S(1)}, bf16[3,33,256]{2,1,0:T(8,128)(2,1)S(1)}, u32[]{:S(2)}, u32[]{:S(2)}) collective-permute-start(bf16[3,33,256]{2,1,0:T(8,128)(2,1)S(1)} %concatenate.31), channel_id=1, source_target_pairs={{0,8},{8,0},{1,9},{9,1},{2,10},{10,2},{3,11},{11,3},{4,12},{12,4},... | collective-permute-start | bytes 152072 | tf_op jit(solution)/shard_map/ppermute | solution.py:40
  13.9 10.0 %collective-permute-start.1 = (bf16[3,66,128]{2,1,0:T(8,128)(2,1)S(1)}, bf16[3,66,128]{2,1,0:T(8,128)(2,1)S(1)}, u32[]{:S(2)}, u32[]{:S(2)}) collective-permute-start(bf16[3,66,128]{2,1,0:T(8,128)(2,1)S(1)} %pad_maximum_fusion), channel_id=1, source_target_pairs={{0,32},{16,48},{32,0},{48,16},{1,33},{17,49},{33,1},{49,17},{2,34}... | collective-permute-start | bytes 152072 | tf_op jit(solution)/shard_map/ppermute | solution.py:59
  18.0 6.0 %collective-permute-start.2 = (bf16[3,66,128]{2,1,0:T(8,128)(2,1)S(1)}, bf16[3,66,128]{2,1,0:T(8,128)(2,1)S(1)}, u32[]{:S(2)}, u32[]{:S(2)}) collective-permute-start(bf16[3,66,128]{2,1,0:T(8,128)(2,1)S(1)} %pad_maximum_fusion), channel_id=1, source_target_pairs={{0,16},{16,32},{32,48},{48,0},{1,17},{17,33},{33,49},{49,1},{2,18}... | collective-permute-start | bytes 152072 | tf_op jit(solution)/shard_map/ppermute | solution.py:59
  19.9 6.0 %collective-permute-start.3 = (bf16[3,66,128]{2,1,0:T(8,128)(2,1)S(1)}, bf16[3,66,128]{2,1,0:T(8,128)(2,1)S(1)}, u32[]{:S(2)}, u32[]{:S(2)}) collective-permute-start(bf16[3,66,128]{2,1,0:T(8,128)(2,1)S(1)} %pad_maximum_fusion), channel_id=1, source_target_pairs={{0,48},{16,0},{32,16},{48,32},{1,49},{17,1},{33,17},{49,33},{2,50}... | collective-permute-start | bytes 152072 | tf_op jit(solution)/shard_map/ppermute | solution.py:59
  26.2 7.6 %collective-permute-start.4 = (bf16[3,264,128]{2,1,0:T(8,128)(2,1)S(1)}, bf16[3,264,128]{2,1,0:T(8,128)(2,1)S(1)}, u32[]{:S(2)}, u32[]{:S(2)}) collective-permute-start(bf16[3,264,128]{2,1,0:T(8,128)(2,1)S(1)} %reshape.183), channel_id=1, source_target_pairs={{0,64},{64,128},{128,192},{192,256},{256,320},{320,384},{384,448},... | collective-permute-start | bytes 608264 | tf_op jit(solution)/shard_map/ppermute | solution.py:23
  33.9 9.7 %collective-permute-start.5 = (bf16[3,264,128]{2,1,0:T(8,128)(2,1)S(1)}, bf16[3,264,128]{2,1,0:T(8,128)(2,1)S(1)}, u32[]{:S(2)}, u32[]{:S(2)}) collective-permute-start(bf16[3,264,128]{2,1,0:T(8,128)(2,1)S(1)} %collective-permute-done.4), channel_id=1, source_target_pairs={{0,64},{64,128},{128,192},{192,256},{256,320},{320,384},{384,448},... | collective-permute-start | bytes 608264 | tf_op jit(solution)/shard_map/ppermute | solution.py:23
  37.6 9.3 %collective-permute-start.8 = (bf16[3,264,128]{2,1,0:T(8,128)(2,1)S(1)}, bf16[3,264,128]{2,1,0:T(8,128)(2,1)S(1)}, u32[]{:S(2)}, u32[]{:S(2)}) collective-permute-start(bf16[3,264,128]{2,1,0:T(8,128)(2,1)S(1)} %reshape.183), channel_id=1, source_target_pairs={{0,448},{64,0},{128,64},{192,128},{256,192},{320,256},{384,320},{4... | collective-permute-start | bytes 608264 | tf_op jit(solution)/shard_map/ppermute | solution.py:26
  43.6 8.8 %collective-permute-start.6 = (bf16[3,264,128]{2,1,0:T(8,128)(2,1)S(1)}, bf16[3,264,128]{2,1,0:T(8,128)(2,1)S(1)}, u32[]{:S(2)}, u32[]{:S(2)}) collective-permute-start(bf16[3,264,128]{2,1,0:T(8,128)(2,1)S(1)} %collective-permute-done.5), channel_id=1, source_target_pairs={{0,64},{64,128},{128,192},{192,256},{256,320},{320,384},{384,448},... | collective-permute-start | bytes 608264 | tf_op jit(solution)/shard_map/ppermute | solution.py:23
  46.9 8.8 %collective-permute-start.9 = (bf16[3,264,128]{2,1,0:T(8,128)(2,1)S(1)}, bf16[3,264,128]{2,1,0:T(8,128)(2,1)S(1)}, u32[]{:S(2)}, u32[]{:S(2)}) collective-permute-start(bf16[3,264,128]{2,1,0:T(8,128)(2,1)S(1)} %collective-permute-done.8), channel_id=1, source_target_pairs={{0,448},{64,0},{128,64},{192,128},{256,192},{320,256},{384,320},{4... | collective-permute-start | bytes 608264 | tf_op jit(solution)/shard_map/ppermute | solution.py:26
  52.4 8.8 %collective-permute-start.7 = (bf16[3,264,128]{2,1,0:T(8,128)(2,1)S(1)}, bf16[3,264,128]{2,1,0:T(8,128)(2,1)S(1)}, u32[]{:S(2)}, u32[]{:S(2)}) collective-permute-start(bf16[3,264,128]{2,1,0:T(8,128)(2,1)S(1)} %collective-permute-done.6), channel_id=1, source_target_pairs={{0,64},{64,128},{128,192},{192,256},{256,320},{320,384},{384,448},... | collective-permute-start | bytes 608264 | tf_op jit(solution)/shard_map/ppermute | solution.py:23
  55.8 8.9 %collective-permute-start.10 = (bf16[3,264,128]{2,1,0:T(8,128)(2,1)S(1)}, bf16[3,264,128]{2,1,0:T(8,128)(2,1)S(1)}, u32[]{:S(2)}, u32[]{:S(2)}) collective-permute-start(bf16[3,264,128]{2,1,0:T(8,128)(2,1)S(1)} %collective-permute-done.9), channel_id=1, source_target_pairs={{0,448},{64,0},{128,64},{192,128},{256,192},{320,256},{384,320},{4... | collective-permute-start | bytes 608264 | tf_op jit(solution)/shard_map/ppermute | solution.py:26
  65.0 4.0 %copy-start.1 = (s32[1024]{0:T(1024)S(1)}, s32[1024]{0:T(1024)}, u32[]{:S(2)}) copy-start(s32[1024]{0:T(1024)} %param.7) | copy-start | bytes 12292
  66.5 8.0 %collective-permute-start.11 = (bf16[3,2112,128]{2,1,0:T(8,128)(2,1)}, bf16[3,2112,128]{2,1,0:T(8,128)(2,1)}, u32[]{:S(2)}, u32[]{:S(2)}) collective-permute-start(bf16[3,2112,128]{2,1,0:T(8,128)(2,1)} %bitcast.14), channel_id=1, source_target_pairs={{0,8},{8,0},{1,9},{9,1},{2,10},{10,2},{3,11},{11,3},{4,12},{12,4},... | collective-permute-start | bytes 4866056 | tf_op jit(solution)/shard_map/ppermute | solution.py:46
  92.0 2.3 %copy-start = (bf16[1,1024,256]{1,2,0:T(8,128)(2,1)}, bf16[1,1024,256]{1,2,0:T(8,128)(2,1)S(1)}, u32[]{:S(2)}) copy-start(bf16[1,1024,256]{1,2,0:T(8,128)(2,1)S(1)} %get-tuple-element.17) | copy-start | bytes 1572868
  94.3 17.9 %all-to-all-start = ((bf16[8,2,128,128]{3,2,1,0:T(8,128)(2,1)}), bf16[8,2,128,128]{3,2,1,0:T(8,128)(2,1)S(1)}, u32[]{:S(2)}, u32[]{:S(2)}) async-start(bf16[8,2,128,128]{3,2,1,0:T(8,128)(2,1)} %broadcast_in_dim.115), calls=%async_computation | async-start | bytes 1048576 | tf_op jit(solution)/shard_map/all_to_all | solution.py:86
  112.2 12.4 %copy-start.2 = (f32[256]{0:T(256)S(1)}, f32[256]{0:T(256)}, u32[]{:S(2)}) copy-start(f32[256]{0:T(256)} %param.6) | copy-start | bytes 3076
  112.5 9.3 %collective-permute-start.13 = (bf16[2,128,128]{2,1,0:T(8,128)(2,1)S(1)}, bf16[2,128,128]{2,1,0:T(8,128)(2,1)S(1)}, u32[]{:S(2)}, u32[]{:S(2)}) collective-permute-start(bf16[2,128,128]{2,1,0:T(8,128)(2,1)S(1)} %get-tuple-element.10), channel_id=1, source_target_pairs={{0,128},{64,192},{128,256},{192,320},{256,384},{320,448},{1,129},{... | collective-permute-start | bytes 196616 | tf_op jit(solution)/shard_map/ppermute | solution.py:15
  118.0 6.2 %collective-permute-start.12 = (bf16[2,128,128]{2,1,0:T(8,128)(2,1)S(1)}, bf16[2,128,128]{2,1,0:T(8,128)(2,1)S(1)}, u32[]{:S(2)}, u32[]{:S(2)}) collective-permute-start(bf16[2,128,128]{2,1,0:T(8,128)(2,1)S(1)} %get-tuple-element.9), channel_id=1, source_target_pairs={{0,64},{64,128},{128,192},{192,256},{256,320},{320,384},{384,448},... | collective-permute-start | bytes 196616 | tf_op jit(solution)/shard_map/ppermute | solution.py:15
Sparse Core Ops, SparseCore 0:
  18.1 69.0 all-gather.1

commit v17 on v16

--- a/solution.py
+++ b/solution.py
@@ -37,11 +37,18 @@
 def gather_weights(w_local):
     half = w_local.shape[2] // 2
     core = lax.axis_index("core")
-    partner = lax.ppermute(w_local, "core", [(0, 1), (1, 0)])
-    low_rows = jnp.where(core == 0, w_local[:, :, :half], partner[:, :, half:])
-    high_rows = jnp.where(core == 0, partner[:, :, :half], w_local[:, :, half:])
-    rows = jnp.concatenate([low_rows, high_rows], axis=1)
-    rows = direct_gather(rows, "x", lax.axis_size("x"), 1)
+    x_count = lax.axis_size("x")
+    gathered = direct_gather(w_local, "x", x_count, 1)
+    partner = lax.ppermute(gathered, "core", [(0, 1), (1, 0)])
+    own_half = jnp.where(core == 0, gathered[:, :, :half], gathered[:, :, half:])
+    partner_half = jnp.where(core == 0, partner[:, :, :half], partner[:, :, half:])
+    core0_rows = jnp.where(core == 0, own_half, partner_half)
+    core1_rows = jnp.where(core == 0, partner_half, own_half)
+    groups, per = w_local.shape[0], w_local.shape[1]
+    rows = jnp.stack(
+        [core0_rows.reshape(groups, x_count, per, half), core1_rows.reshape(groups, x_count, per, half)],
+        axis=2,
+    ).reshape(groups, x_count * 2 * per, half)
     rows = ring_gather(rows, "y", lax.axis_size("y"), 1)
     other = lax.ppermute(rows, "core", [(0, 1), (1, 0)])
     return jnp.where(

time: 134 us -> 136 us (1.015)
  local copies, waits for them, and re-layouts: 17.8 us -> 20.8 us
  other arithmetic: 10.1 us -> 8.72 us
    unnamed x26 -> x28, local copies, waits for them, and re-layouts: 0.5 us -> 3.38 us
    ppermute x4, waiting for transfers between devices: 9.33 us -> 12 us  [ring_gather(): lax.ppermute(ahead, axis, [(j, (j + 1) % count) for j in range(count)])]
    ppermute x4, starting transfers between devices: 13 us -> 11.6 us  [ring_gather(): lax.ppermute(ahead, axis, [(j, (j + 1) % count) for j in range(count)])]
    ppermute x3, waiting for transfers between devices: 2.06 us -> 0.65 us  [direct_gather(): lax.ppermute(value, axis, [(j, (j - off) % count) for j in range(count)])]
  transfers between devices with their start and end apart: 16 -> 16, of which waited for: 12 -> 12; matrix products, arithmetic and copies ran while one was open for 22% -> 24% of each run, Pallas kernels for 0% -> 0%
where the time goes in v17:
time: 136 us; the launch traced here: 135 us
  starting transfers between devices  50.4 us (37%)
  waiting for transfers between devices  24.2 us (18%)
  local copies, waits for them, and re-layouts  20.8 us (15%)
  between operations  15.9 us (12%)
  matrix products  14.4 us (11%)
  other arithmetic  8.72 us (6%)
    ppermute x3, starting transfers between devices, ring_gather(): lax.ppermute(behind, axis, [(j, (j - 1) % count) for j in range(count)])  12.2 us
    ppermute x4, waiting for transfers between devices, ring_gather(): lax.ppermute(ahead, axis, [(j, (j + 1) % count) for j in range(count)])  12 us
    ppermute x4, starting transfers between devices, ring_gather(): lax.ppermute(ahead, axis, [(j, (j + 1) % count) for j in range(count)])  11.6 us
    ppermute x3, starting transfers between devices, direct_gather(): lax.ppermute(value, axis, [(j, (j - off) % count) for j in range(count)])  9.86 us
    ppermute x2, starting transfers between devices, shifted(): lax.ppermute(value, axis, [(source, source + steps) for source in range(c...  8.1 us
    concatenate x2, local copies, waits for them, and re-layouts, gather_weights(): jnp.concatenate([rows, other], axis=2)  6.17 us
    all_to_all x1, starting transfers between devices, state_scan(): lax.all_to_all(spread, ('x', 'core'), 0, 0, tiled=True).astype(jnp.float32)  4.77 us
    dot_general x2, matrix products, per_device(): jnp.einsum('hbs,she->bhe', weights, values[:key_end], preferred_element_t...  4.73 us
  transfers between devices with their start and end apart: 16, of which 12 were waited for; matrix products, arithmetic and copies ran while one was open for 24% of the time, Pallas kernels for 0%

profile of v17, /device:TPU:18, one launch (start us, length us, event | category | flops | bytes accessed | tf_op | source)
XLA Modules:
  0.0 134.5 jit_solution(11126563330833689150)
XLA Ops:
  7.9 1.5 %concatenate.28 = bf16[3,33,256]{2,1,0:T(8,128)(2,1)S(1)} pad(bf16[3,32,256]{2,1,0:T(8,128)(2,1)} %param.5, bf16[]{:T(256)} %bitcast), padding=0_0x0_1x0_0 | pad | bytes 99842 | tf_op jit(solution)/shard_map/concatenate | solution.py:119
  9.3 4.0 %collective-permute-start = (bf16[3,33,256]{2,1,0:T(8,128)(2,1)S(1)}, bf16[3,33,256]{2,1,0:T(8,128)(2,1)S(1)}, u32[]{:S(2)}, u32[]{:S(2)}) collective-permute-start(bf16[3,33,256]{2,1,0:T(8,128)(2,1)S(1)} %concatenate.28), channel_id=1, source_target_pairs={{0,32},{16,48},{32,0},{48,16},{1,33},{17,49},{33,1},{49,17},{2,34}... | collective-permute-start | bytes 152072 | tf_op jit(solution)/shard_map/ppermute | solution.py:66
  13.4 1.9 %collective-permute-start.1 = (bf16[3,33,256]{2,1,0:T(8,128)(2,1)S(1)}, bf16[3,33,256]{2,1,0:T(8,128)(2,1)S(1)}, u32[]{:S(2)}, u32[]{:S(2)}) collective-permute-start(bf16[3,33,256]{2,1,0:T(8,128)(2,1)S(1)} %concatenate.28), channel_id=1, source_target_pairs={{0,16},{16,32},{32,48},{48,0},{1,17},{17,33},{33,49},{49,1},{2,18}... | collective-permute-start | bytes 152072 | tf_op jit(solution)/shard_map/ppermute | solution.py:66
  15.3 3.9 %collective-permute-start.2 = (bf16[3,33,256]{2,1,0:T(8,128)(2,1)S(1)}, bf16[3,33,256]{2,1,0:T(8,128)(2,1)S(1)}, u32[]{:S(2)}, u32[]{:S(2)}) collective-permute-start(bf16[3,33,256]{2,1,0:T(8,128)(2,1)S(1)} %concatenate.28), channel_id=1, source_target_pairs={{0,48},{16,0},{32,16},{48,32},{1,49},{17,1},{33,17},{49,33},{2,50}... | collective-permute-start | bytes 152072 | tf_op jit(solution)/shard_map/ppermute | solution.py:66
  19.5 1.5 %bitcast_dynamic-update-slice_fusion.16 = bf16[8,3,33,256]{3,2,1,0:T(8,128)(2,1)S(1)} fusion(bf16[8,3,33,256]{3,2,1,0:T(8,128)(2,1)S(1)} %bitcast_dynamic-update-slice_fusion.18, bf16[3,32,256]{2,1,0:T(8,128)(2,1)} %param.5, bf16[]{:T(256)} %bitcast), kind=kLoop, calls=%fused_computation.79 | loop fusion | bytes 110594
  21.4 1.5 %bitcast_dynamic-update-slice_fusion.17 = bf16[8,3,33,256]{3,2,1,0:T(8,128)(2,1)S(1)} fusion(bf16[8,3,33,256]{3,2,1,0:T(8,128)(2,1)S(1)} %bitcast_dynamic-update-slice_fusion.19, bf16[3,32,256]{2,1,0:T(8,128)(2,1)} %param.5, bf16[]{:T(256)} %bitcast), kind=kLoop, calls=%fused_computation.80 | loop fusion | bytes 110594
  23.0 1.9 %collective-permute-start.3 = (bf16[3,132,256]{2,1,0:T(8,128)(2,1)S(1)}, bf16[3,132,256]{2,1,0:T(8,128)(2,1)S(1)}, u32[]{:S(2)}, u32[]{:S(2)}) collective-permute-start(bf16[3,132,256]{2,1,0:T(8,128)(2,1)S(1)} %reshape.186), channel_id=1, source_target_pairs={{0,8},{8,0},{1,9},{9,1},{2,10},{10,2},{3,11},{11,3},{4,12},{12,4},... | collective-permute-start | bytes 608264 | tf_op jit(solution)/shard_map/ppermute | solution.py:42
  26.7 3.5 %collective-permute-start.4 = (bf16[3,264,128]{2,1,0:T(8,128)(2,1)S(1)}, bf16[3,264,128]{2,1,0:T(8,128)(2,1)S(1)}, u32[]{:S(2)}, u32[]{:S(2)}) collective-permute-start(bf16[3,264,128]{2,1,0:T(8,128)(2,1)S(1)} %reshape.187), channel_id=1, source_target_pairs={{0,64},{64,128},{128,192},{192,256},{256,320},{320,384},{384,448},... | collective-permute-start | bytes 608264 | tf_op jit(solution)/shard_map/ppermute | solution.py:23
  30.2 5.5 %collective-permute-done.4 = bf16[3,264,128]{2,1,0:T(8,128)(2,1)S(1)} collective-permute-done((bf16[3,264,128]{2,1,0:T(8,128)(2,1)S(1)}, bf16[3,264,128]{2,1,0:T(8,128)(2,1)S(1)}, u32[]{:S(2)}, u32[]{:S(2)}) %collective-permute-start.4) | collective-permute-done | bytes 202784 | tf_op jit(solution)/shard_map/ppermute | solution.py:23
  35.7 3.8 %collective-permute-start.5 = (bf16[3,264,128]{2,1,0:T(8,128)(2,1)S(1)}, bf16[3,264,128]{2,1,0:T(8,128)(2,1)S(1)}, u32[]{:S(2)}, u32[]{:S(2)}) collective-permute-start(bf16[3,264,128]{2,1,0:T(8,128)(2,1)S(1)} %collective-permute-done.4), channel_id=1, source_target_pairs={{0,64},{64,128},{128,192},{192,256},{256,320},{320,384},{384,448},... | collective-permute-start | bytes 608264 | tf_op jit(solution)/shard_map/ppermute | solution.py:23
  39.5 4.4 %collective-permute-start.8 = (bf16[3,264,128]{2,1,0:T(8,128)(2,1)S(1)}, bf16[3,264,128]{2,1,0:T(8,128)(2,1)S(1)}, u32[]{:S(2)}, u32[]{:S(2)}) collective-permute-start(bf16[3,264,128]{2,1,0:T(8,128)(2,1)S(1)} %reshape.187), channel_id=1, source_target_pairs={{0,448},{64,0},{128,64},{192,128},{256,192},{320,256},{384,320},{4... | collective-permute-start | bytes 608264 | tf_op jit(solution)/shard_map/ppermute | solution.py:26
  43.9 2.9 %collective-permute-done.5 = bf16[3,264,128]{2,1,0:T(8,128)(2,1)S(1)} collective-permute-done((bf16[3,264,128]{2,1,0:T(8,128)(2,1)S(1)}, bf16[3,264,128]{2,1,0:T(8,128)(2,1)S(1)}, u32[]{:S(2)}, u32[]{:S(2)}) %collective-permute-start.5) | collective-permute-done | bytes 202784 | tf_op jit(solution)/shard_map/ppermute | solution.py:23
  46.8 2.0 %collective-permute-start.6 = (bf16[3,264,128]{2,1,0:T(8,128)(2,1)S(1)}, bf16[3,264,128]{2,1,0:T(8,128)(2,1)S(1)}, u32[]{:S(2)}, u32[]{:S(2)}) collective-permute-start(bf16[3,264,128]{2,1,0:T(8,128)(2,1)S(1)} %collective-permute-done.5), channel_id=1, source_target_pairs={{0,64},{64,128},{128,192},{192,256},{256,320},{320,384},{384,448},... | collective-permute-start | bytes 608264 | tf_op jit(solution)/shard_map/ppermute | solution.py:23
  49.3 4.0 %collective-permute-start.9 = (bf16[3,264,128]{2,1,0:T(8,128)(2,1)S(1)}, bf16[3,264,128]{2,1,0:T(8,128)(2,1)S(1)}, u32[]{:S(2)}, u32[]{:S(2)}) collective-permute-start(bf16[3,264,128]{2,1,0:T(8,128)(2,1)S(1)} %collective-permute-done.8), channel_id=1, source_target_pairs={{0,448},{64,0},{128,64},{192,128},{256,192},{320,256},{384,320},{4... | collective-permute-start | bytes 608264 | tf_op jit(solution)/shard_map/ppermute | solution.py:26
  53.3 2.0 %collective-permute-done.6 = bf16[3,264,128]{2,1,0:T(8,128)(2,1)S(1)} collective-permute-done((bf16[3,264,128]{2,1,0:T(8,128)(2,1)S(1)}, bf16[3,264,128]{2,1,0:T(8,128)(2,1)S(1)}, u32[]{:S(2)}, u32[]{:S(2)}) %collective-permute-start.6) | collective-permute-done | bytes 202784 | tf_op jit(solution)/shard_map/ppermute | solution.py:23
  55.3 2.3 %collective-permute-start.7 = (bf16[3,264,128]{2,1,0:T(8,128)(2,1)S(1)}, bf16[3,264,128]{2,1,0:T(8,128)(2,1)S(1)}, u32[]{:S(2)}, u32[]{:S(2)}) collective-permute-start(bf16[3,264,128]{2,1,0:T(8,128)(2,1)S(1)} %collective-permute-done.6), channel_id=1, source_target_pairs={{0,64},{64,128},{128,192},{192,256},{256,320},{320,384},{384,448},... | collective-permute-start | bytes 608264 | tf_op jit(solution)/shard_map/ppermute | solution.py:23
  58.1 3.8 %collective-permute-start.10 = (bf16[3,264,128]{2,1,0:T(8,128)(2,1)S(1)}, bf16[3,264,128]{2,1,0:T(8,128)(2,1)S(1)}, u32[]{:S(2)}, u32[]{:S(2)}) collective-permute-start(bf16[3,264,128]{2,1,0:T(8,128)(2,1)S(1)} %collective-permute-done.9), channel_id=1, source_target_pairs={{0,448},{64,0},{128,64},{192,128},{256,192},{320,256},{384,320},{4... | collective-permute-start | bytes 608264 | tf_op jit(solution)/shard_map/ppermute | solution.py:26
  61.9 1.6 %collective-permute-done.7 = bf16[3,264,128]{2,1,0:T(8,128)(2,1)S(1)} collective-permute-done((bf16[3,264,128]{2,1,0:T(8,128)(2,1)S(1)}, bf16[3,264,128]{2,1,0:T(8,128)(2,1)S(1)}, u32[]{:S(2)}, u32[]{:S(2)}) %collective-permute-start.7) | collective-permute-done | bytes 202784 | tf_op jit(solution)/shard_map/ppermute | solution.py:23
  63.8 3.2 %collective-permute-done.10 = bf16[3,264,128]{2,1,0:T(8,128)(2,1)S(1)} collective-permute-done((bf16[3,264,128]{2,1,0:T(8,128)(2,1)S(1)}, bf16[3,264,128]{2,1,0:T(8,128)(2,1)S(1)}, u32[]{:S(2)}, u32[]{:S(2)}) %collective-permute-start.10) | collective-permute-done | bytes 202784 | tf_op jit(solution)/shard_map/ppermute | solution.py:26
  68.9 1.9 %collective-permute-start.11 = (bf16[3,2112,128]{2,1,0:T(8,128)(2,1)}, bf16[3,2112,128]{2,1,0:T(8,128)(2,1)}, u32[]{:S(2)}, u32[]{:S(2)}) collective-permute-start(bf16[3,2112,128]{2,1,0:T(8,128)(2,1)} %bitcast.14), channel_id=1, source_target_pairs={{0,8},{8,0},{1,9},{9,1},{2,10},{10,2},{3,11},{11,3},{4,12},{12,4},... | collective-permute-start | bytes 4866056 | tf_op jit(solution)/shard_map/ppermute | solution.py:53
  74.4 2.5 %concatenate.31 = bf16[3,64,33,128]{3,2,1,0:T(8,128)(2,1)S(1)} reshape(bf16[3,8,264,128]{3,2,1,0:T(8,128)(2,1)} %copy.34) | data formatting | bytes 3244032 | tf_op jit(solution)/shard_map/concatenate | solution.py:56
  76.9 3.7 %concatenate.32 = bf16[3,64,33,128]{3,2,1,0:T(8,128)(2,1)} reshape(bf16[3,2112,128]{2,1,0:T(8,128)(2,1)} %collective-permute-done.11) | data formatting | bytes 3244032 | tf_op jit(solution)/shard_map/concatenate | solution.py:56
  80.6 2.8 %maximum_select_fusion = bf16[3,64,33,256]{3,2,1,0:T(8,128)(2,1)S(1)} fusion(bf16[3,64,33,128]{3,2,1,0:T(8,128)(2,1)} %concatenate.32, bf16[3,64,33,128]{3,2,1,0:T(8,128)(2,1)S(1)} %concatenate.31, pred[]{:T(512)S(6)} %eq.89), kind=kLoop, calls=%fused_computation.4 | loop fusion | flops 14598144 | bytes 6488065 | tf_op jit(solution)/shard_map/jit(_where)/select_n | solution.py:54
  85.4 3.6 %all-gather.2.cloned.1.call-done = bf16[1024,2048]{1,0:T(8,128)(2,1)} async-done(((bf16[1024,256]{1,0:T(8,128)(2,1)}), bf16[1024,2048]{1,0:T(8,128)(2,1)}) %all-gather.2.cloned.1.call-update) | async-done | bytes 4194320 | tf_op jit(solution)/shard_map/all_gather | solution.py:114
  89.1 4.6 %fusion.7 = bf16[2,1024,256]{1,2,0:T(8,128)(2,1)S(1)} fusion(bf16[2,2048,256]{2,1,0:T(8,128)(2,1)S(1)} %bitcast.97, bf16[1024,2048]{1,0:T(8,128)(2,1)} %all-gather.2.cloned.1.call-done), kind=kOutput, calls=%fused_computation.20 | convolution fusion | flops 2148007936 | bytes 7340032 | tf_op jit(solution)/shard_map/tr,grc->gtc/dot_general | solution.py:123
  96.2 4.8 %all-to-all-start = ((bf16[8,2,128,128]{3,2,1,0:T(8,128)(2,1)}), bf16[8,2,128,128]{3,2,1,0:T(8,128)(2,1)S(1)}, u32[]{:S(2)}, u32[]{:S(2)}) async-start(bf16[8,2,128,128]{3,2,1,0:T(8,128)(2,1)} %broadcast_in_dim.115), calls=%async_computation | async-start | bytes 1048576 | tf_op jit(solution)/shard_map/all_to_all | solution.py:93
  103.5 4.2 %fusion.21 = bf16[1024,256]{0,1:T(8,128)(2,1)S(1)} fusion(bf16[2048,256]{1,0:T(8,128)(2,1)} %bitcast.101, bf16[1024,2048]{1,0:T(8,128)(2,1)} %all-gather.2.cloned.1.call-done), kind=kOutput, calls=%fused_computation.34 | convolution fusion | flops 1075314688 | bytes 5767168 | tf_op jit(solution)/shard_map/tr,rc->tc/dot_general | solution.py:136
  108.7 1.9 %fusion.15 = f32[512,2,128]{0,2,1:T(8,128)S(1)} fusion(bf16[512,2,128]{0,2,1:T(8,128)(2,1)} %bitcast.105, bf16[512,2,128]{0,2,1:T(8,128)(2,1)} %bitcast.107, bf16[512,2,128]{0,2,1:T(8,128)(2,1)S(1)} %bitcast.104, pred[512,512]{1,0:T(8,128)(4,1)} %fusion.26), kind=kOutput, calls=%fused_computation.28 | convolution fusion | flops 269484032 | bytes 1572864 | tf_op jit(solution)/shard_map/hbs,she->bhe/dot_general | solution.py:156
  111.2 2.8 %fusion.14 = f32[512,2,128]{0,2,1:T(8,128)S(1)} fusion(bf16[1024,2,128]{0,2,1:T(8,128)(2,1)} %bitcast.103, bf16[512,2,128]{0,2,1:T(8,128)(2,1)} %bitcast.106, pred[512,1024]{1,0:T(8,128)(4,1)} %fusion.2, f32[1024,2,128]{0,2,1:T(8,128)S(1)} %bitcast.100), kind=kOutput, calls=%fused_computation.27 | convolution fusion | flops 540278784 | bytes 2883584 | tf_op jit(solution)/shard_map/hbs,she->bhe/dot_general | solution.py:156
  114.4 5.6 %collective-permute-start.13 = (bf16[2,128,128]{2,1,0:T(8,128)(2,1)S(1)}, bf16[2,128,128]{2,1,0:T(8,128)(2,1)S(1)}, u32[]{:S(2)}, u32[]{:S(2)}) collective-permute-start(bf16[2,128,128]{2,1,0:T(8,128)(2,1)S(1)} %get-tuple-element.10), channel_id=1, source_target_pairs={{0,128},{64,192},{128,256},{192,320},{256,384},{320,448},{1,129},{... | collective-permute-start | bytes 196616 | tf_op jit(solution)/shard_map/ppermute | solution.py:15
  120.0 2.6 %collective-permute-start.12 = (bf16[2,128,128]{2,1,0:T(8,128)(2,1)S(1)}, bf16[2,128,128]{2,1,0:T(8,128)(2,1)S(1)}, u32[]{:S(2)}, u32[]{:S(2)}) collective-permute-start(bf16[2,128,128]{2,1,0:T(8,128)(2,1)S(1)} %get-tuple-element.9), channel_id=1, source_target_pairs={{0,64},{64,128},{128,192},{192,256},{256,320},{320,384},{384,448},... | collective-permute-start | bytes 196616 | tf_op jit(solution)/shard_map/ppermute | solution.py:15
  123.8 2.3 %collective-permute-done.12 = bf16[2,128,128]{2,1,0:T(8,128)(2,1)S(1)} collective-permute-done((bf16[2,128,128]{2,1,0:T(8,128)(2,1)S(1)}, bf16[2,128,128]{2,1,0:T(8,128)(2,1)S(1)}, u32[]{:S(2)}, u32[]{:S(2)}) %collective-permute-start.12) | collective-permute-done | bytes 65568 | tf_op jit(solution)/shard_map/ppermute | solution.py:15
  (81 shorter events, 20.1 us)
Async XLA Ops:
  6.5 82.5 %all-gather.2.cloned.1.call-start = ((), (), s32[]{:S(2)}) async-start(), calls=%async_computation.1 | async-start | bytes 4718592 | tf_op jit(solution)/shard_map/all_gather | solution.py:114
  9.3 9.9 %collective-permute-start = (bf16[3,33,256]{2,1,0:T(8,128)(2,1)S(1)}, bf16[3,33,256]{2,1,0:T(8,128)(2,1)S(1)}, u32[]{:S(2)}, u32[]{:S(2)}) collective-permute-start(bf16[3,33,256]{2,1,0:T(8,128)(2,1)S(1)} %concatenate.28), channel_id=1, source_target_pairs={{0,32},{16,48},{32,0},{48,16},{1,33},{17,49},{33,1},{49,17},{2,34}... | collective-permute-start | bytes 152072 | tf_op jit(solution)/shard_map/ppermute | solution.py:66
  13.4 6.1 %collective-permute-start.1 = (bf16[3,33,256]{2,1,0:T(8,128)(2,1)S(1)}, bf16[3,33,256]{2,1,0:T(8,128)(2,1)S(1)}, u32[]{:S(2)}, u32[]{:S(2)}) collective-permute-start(bf16[3,33,256]{2,1,0:T(8,128)(2,1)S(1)} %concatenate.28), channel_id=1, source_target_pairs={{0,16},{16,32},{32,48},{48,0},{1,17},{17,33},{33,49},{49,1},{2,18}... | collective-permute-start | bytes 152072 | tf_op jit(solution)/shard_map/ppermute | solution.py:66
  15.3 6.1 %collective-permute-start.2 = (bf16[3,33,256]{2,1,0:T(8,128)(2,1)S(1)}, bf16[3,33,256]{2,1,0:T(8,128)(2,1)S(1)}, u32[]{:S(2)}, u32[]{:S(2)}) collective-permute-start(bf16[3,33,256]{2,1,0:T(8,128)(2,1)S(1)} %concatenate.28), channel_id=1, source_target_pairs={{0,48},{16,0},{32,16},{48,32},{1,49},{17,1},{33,17},{49,33},{2,50}... | collective-permute-start | bytes 152072 | tf_op jit(solution)/shard_map/ppermute | solution.py:66
  23.0 3.4 %collective-permute-start.3 = (bf16[3,132,256]{2,1,0:T(8,128)(2,1)S(1)}, bf16[3,132,256]{2,1,0:T(8,128)(2,1)S(1)}, u32[]{:S(2)}, u32[]{:S(2)}) collective-permute-start(bf16[3,132,256]{2,1,0:T(8,128)(2,1)S(1)} %reshape.186), channel_id=1, source_target_pairs={{0,8},{8,0},{1,9},{9,1},{2,10},{10,2},{3,11},{11,3},{4,12},{12,4},... | collective-permute-start | bytes 608264 | tf_op jit(solution)/shard_map/ppermute | solution.py:42
  26.7 9.0 %collective-permute-start.4 = (bf16[3,264,128]{2,1,0:T(8,128)(2,1)S(1)}, bf16[3,264,128]{2,1,0:T(8,128)(2,1)S(1)}, u32[]{:S(2)}, u32[]{:S(2)}) collective-permute-start(bf16[3,264,128]{2,1,0:T(8,128)(2,1)S(1)} %reshape.187), channel_id=1, source_target_pairs={{0,64},{64,128},{128,192},{192,256},{256,320},{320,384},{384,448},... | collective-permute-start | bytes 608264 | tf_op jit(solution)/shard_map/ppermute | solution.py:23
  35.7 11.1 %collective-permute-start.5 = (bf16[3,264,128]{2,1,0:T(8,128)(2,1)S(1)}, bf16[3,264,128]{2,1,0:T(8,128)(2,1)S(1)}, u32[]{:S(2)}, u32[]{:S(2)}) collective-permute-start(bf16[3,264,128]{2,1,0:T(8,128)(2,1)S(1)} %collective-permute-done.4), channel_id=1, source_target_pairs={{0,64},{64,128},{128,192},{192,256},{256,320},{320,384},{384,448},... | collective-permute-start | bytes 608264 | tf_op jit(solution)/shard_map/ppermute | solution.py:23
  39.5 9.8 %collective-permute-start.8 = (bf16[3,264,128]{2,1,0:T(8,128)(2,1)S(1)}, bf16[3,264,128]{2,1,0:T(8,128)(2,1)S(1)}, u32[]{:S(2)}, u32[]{:S(2)}) collective-permute-start(bf16[3,264,128]{2,1,0:T(8,128)(2,1)S(1)} %reshape.187), channel_id=1, source_target_pairs={{0,448},{64,0},{128,64},{192,128},{256,192},{320,256},{384,320},{4... | collective-permute-start | bytes 608264 | tf_op jit(solution)/shard_map/ppermute | solution.py:26
  46.8 8.5 %collective-permute-start.6 = (bf16[3,264,128]{2,1,0:T(8,128)(2,1)S(1)}, bf16[3,264,128]{2,1,0:T(8,128)(2,1)S(1)}, u32[]{:S(2)}, u32[]{:S(2)}) collective-permute-start(bf16[3,264,128]{2,1,0:T(8,128)(2,1)S(1)} %collective-permute-done.5), channel_id=1, source_target_pairs={{0,64},{64,128},{128,192},{192,256},{256,320},{320,384},{384,448},... | collective-permute-start | bytes 608264 | tf_op jit(solution)/shard_map/ppermute | solution.py:23
  49.3 8.8 %collective-permute-start.9 = (bf16[3,264,128]{2,1,0:T(8,128)(2,1)S(1)}, bf16[3,264,128]{2,1,0:T(8,128)(2,1)S(1)}, u32[]{:S(2)}, u32[]{:S(2)}) collective-permute-start(bf16[3,264,128]{2,1,0:T(8,128)(2,1)S(1)} %collective-permute-done.8), channel_id=1, source_target_pairs={{0,448},{64,0},{128,64},{192,128},{256,192},{320,256},{384,320},{4... | collective-permute-start | bytes 608264 | tf_op jit(solution)/shard_map/ppermute | solution.py:26
  55.3 8.3 %collective-permute-start.7 = (bf16[3,264,128]{2,1,0:T(8,128)(2,1)S(1)}, bf16[3,264,128]{2,1,0:T(8,128)(2,1)S(1)}, u32[]{:S(2)}, u32[]{:S(2)}) collective-permute-start(bf16[3,264,128]{2,1,0:T(8,128)(2,1)S(1)} %collective-permute-done.6), channel_id=1, source_target_pairs={{0,64},{64,128},{128,192},{192,256},{256,320},{320,384},{384,448},... | collective-permute-start | bytes 608264 | tf_op jit(solution)/shard_map/ppermute | solution.py:23
  58.1 8.9 %collective-permute-start.10 = (bf16[3,264,128]{2,1,0:T(8,128)(2,1)S(1)}, bf16[3,264,128]{2,1,0:T(8,128)(2,1)S(1)}, u32[]{:S(2)}, u32[]{:S(2)}) collective-permute-start(bf16[3,264,128]{2,1,0:T(8,128)(2,1)S(1)} %collective-permute-done.9), channel_id=1, source_target_pairs={{0,448},{64,0},{128,64},{192,128},{256,192},{320,256},{384,320},{4... | collective-permute-start | bytes 608264 | tf_op jit(solution)/shard_map/ppermute | solution.py:26
  67.4 4.0 %copy-start.1 = (s32[1024]{0:T(1024)S(1)}, s32[1024]{0:T(1024)}, u32[]{:S(2)}) copy-start(s32[1024]{0:T(1024)} %param.7) | copy-start | bytes 12292
  68.9 8.0 %collective-permute-start.11 = (bf16[3,2112,128]{2,1,0:T(8,128)(2,1)}, bf16[3,2112,128]{2,1,0:T(8,128)(2,1)}, u32[]{:S(2)}, u32[]{:S(2)}) collective-permute-start(bf16[3,2112,128]{2,1,0:T(8,128)(2,1)} %bitcast.14), channel_id=1, source_target_pairs={{0,8},{8,0},{1,9},{9,1},{2,10},{10,2},{3,11},{11,3},{4,12},{12,4},... | collective-permute-start | bytes 4866056 | tf_op jit(solution)/shard_map/ppermute | solution.py:53
  93.9 2.3 %copy-start = (bf16[1,1024,256]{1,2,0:T(8,128)(2,1)}, bf16[1,1024,256]{1,2,0:T(8,128)(2,1)S(1)}, u32[]{:S(2)}) copy-start(bf16[1,1024,256]{1,2,0:T(8,128)(2,1)S(1)} %get-tuple-element.17) | copy-start | bytes 1572868
  96.2 17.9 %all-to-all-start = ((bf16[8,2,128,128]{3,2,1,0:T(8,128)(2,1)}), bf16[8,2,128,128]{3,2,1,0:T(8,128)(2,1)S(1)}, u32[]{:S(2)}, u32[]{:S(2)}) async-start(bf16[8,2,128,128]{3,2,1,0:T(8,128)(2,1)} %broadcast_in_dim.115), calls=%async_computation | async-start | bytes 1048576 | tf_op jit(solution)/shard_map/all_to_all | solution.py:93
  114.0 12.5 %copy-start.2 = (f32[256]{0:T(256)S(1)}, f32[256]{0:T(256)}, u32[]{:S(2)}) copy-start(f32[256]{0:T(256)} %param.6) | copy-start | bytes 3076
  114.4 9.4 %collective-permute-start.13 = (bf16[2,128,128]{2,1,0:T(8,128)(2,1)S(1)}, bf16[2,128,128]{2,1,0:T(8,128)(2,1)S(1)}, u32[]{:S(2)}, u32[]{:S(2)}) collective-permute-start(bf16[2,128,128]{2,1,0:T(8,128)(2,1)S(1)} %get-tuple-element.10), channel_id=1, source_target_pairs={{0,128},{64,192},{128,256},{192,320},{256,384},{320,448},{1,129},{... | collective-permute-start | bytes 196616 | tf_op jit(solution)/shard_map/ppermute | solution.py:15
  120.0 6.2 %collective-permute-start.12 = (bf16[2,128,128]{2,1,0:T(8,128)(2,1)S(1)}, bf16[2,128,128]{2,1,0:T(8,128)(2,1)S(1)}, u32[]{:S(2)}, u32[]{:S(2)}) collective-permute-start(bf16[2,128,128]{2,1,0:T(8,128)(2,1)S(1)} %get-tuple-element.9), channel_id=1, source_target_pairs={{0,64},{64,128},{128,192},{192,256},{256,320},{320,384},{384,448},... | collective-permute-start | bytes 196616 | tf_op jit(solution)/shard_map/ppermute | solution.py:15
Sparse Core Ops, SparseCore 0:
  19.4 69.6 all-gather.1

commit v18 on v16

--- a/solution.py
+++ b/solution.py
@@ -42,7 +42,7 @@
     high_rows = jnp.where(core == 0, partner[:, :, :half], w_local[:, :, half:])
     rows = jnp.concatenate([low_rows, high_rows], axis=1)
     rows = direct_gather(rows, "x", lax.axis_size("x"), 1)
-    rows = ring_gather(rows, "y", lax.axis_size("y"), 1)
+    rows = direct_gather(rows, "y", lax.axis_size("y"), 1)
     other = lax.ppermute(rows, "core", [(0, 1), (1, 0)])
     return jnp.where(
         core == 0,

time: 134 us -> 141 us (1.052)
  the two profiles are of different devices: /device:TPU:18 before, /device:TPU:10 now
where the time goes in v18:
time: 141 us; the launch traced here: 140 us
  starting transfers between devices  56.4 us (40%)
  waiting for transfers between devices  25.8 us (18%)
  local copies, waits for them, and re-layouts  17.7 us (13%)
  between operations  15.9 us (11%)
  matrix products  14.5 us (10%)
  other arithmetic  10.1 us (7%)
    ppermute x10, starting transfers between devices, direct_gather(): lax.ppermute(value, axis, [(j, (j - off) % count) for j in range(count)])  39.6 us
    ppermute x10, waiting for transfers between devices, direct_gather(): lax.ppermute(value, axis, [(j, (j - off) % count) for j in range(count)])  22.3 us
    ppermute x2, starting transfers between devices, shifted(): lax.ppermute(value, axis, [(source, source + steps) for source in range(c...  7.42 us
    concatenate x2, local copies, waits for them, and re-layouts, gather_weights(): jnp.concatenate([rows, other], axis=2)  6.15 us
    all_to_all x1, starting transfers between devices, state_scan(): lax.all_to_all(spread, ('x', 'core'), 0, 0, tiled=True).astype(jnp.float32)  5.57 us
    dot_general x2, matrix products, per_device(): jnp.einsum('hbs,she->bhe', weights, values[:key_end], preferred_element_t...  4.73 us
    dot_general x1, matrix products, per_device(): jnp.einsum('tr,grc->gtc', whole, w_rows[1:], preferred_element_type=jnp.f...  4.59 us
    dot_general x1, matrix products, per_device(): jnp.einsum('tr,rc->tc', whole, w_rows[0], preferred_element_type=jnp.floa...  4.19 us
  transfers between devices with their start and end apart: 16, of which 8 were waited for; matrix products, arithmetic and copies ran while one was open for 21% of the time, Pallas kernels for 0%

profile of v18, /device:TPU:10, one launch (start us, length us, event | category | flops | bytes accessed | tf_op | source)
XLA Modules:
  0.0 140.4 jit_solution(14926042641526318636)
XLA Ops:
  7.9 1.5 %concatenate.31 = bf16[3,33,256]{2,1,0:T(8,128)(2,1)S(1)} pad(bf16[3,32,256]{2,1,0:T(8,128)(2,1)} %param.5, bf16[]{:T(256)} %bitcast), padding=0_0x0_1x0_0 | pad | bytes 99842 | tf_op jit(solution)/shard_map/concatenate | solution.py:112
  9.3 1.9 %collective-permute-start = (bf16[3,33,256]{2,1,0:T(8,128)(2,1)S(1)}, bf16[3,33,256]{2,1,0:T(8,128)(2,1)S(1)}, u32[]{:S(2)}, u32[]{:S(2)}) collective-permute-start(bf16[3,33,256]{2,1,0:T(8,128)(2,1)S(1)} %concatenate.31), channel_id=1, source_target_pairs={{0,8},{8,0},{1,9},{9,1},{2,10},{10,2},{3,11},{11,3},{4,12},{12,4},... | collective-permute-start | bytes 152072 | tf_op jit(solution)/shard_map/ppermute | solution.py:40
  12.5 1.4 %slice_select_fusion.1 = (bf16[3,33,128]{2,1,0:T(8,128)(2,1)S(1)}, bf16[3,33,128]{2,1,0:T(8,128)(2,1)S(1)}) fusion(bf16[3,33,256]{2,1,0:T(8,128)(2,1)S(1)} %collective-permute-done, pred[]{:T(512)S(6)} %eq.87, bf16[3,32,256]{2,1,0:T(8,128)(2,1)} %param.5, bf16[]{:T(256)} %bitcast), kind=kLoop, calls=%fused_computation.86 | loop fusion | flops 25344 | bytes 150531 | tf_op jit(solution)/shard_map/jit(_where)/select_n | solution.py:41
  13.9 4.0 %collective-permute-start.1 = (bf16[3,66,128]{2,1,0:T(8,128)(2,1)S(1)}, bf16[3,66,128]{2,1,0:T(8,128)(2,1)S(1)}, u32[]{:S(2)}, u32[]{:S(2)}) collective-permute-start(bf16[3,66,128]{2,1,0:T(8,128)(2,1)S(1)} %pad_maximum_fusion), channel_id=1, source_target_pairs={{0,32},{16,48},{32,0},{48,16},{1,33},{17,49},{33,1},{49,17},{2,34}... | collective-permute-start | bytes 152072 | tf_op jit(solution)/shard_map/ppermute | solution.py:59
  18.0 1.9 %collective-permute-start.2 = (bf16[3,66,128]{2,1,0:T(8,128)(2,1)S(1)}, bf16[3,66,128]{2,1,0:T(8,128)(2,1)S(1)}, u32[]{:S(2)}, u32[]{:S(2)}) collective-permute-start(bf16[3,66,128]{2,1,0:T(8,128)(2,1)S(1)} %pad_maximum_fusion), channel_id=1, source_target_pairs={{0,16},{16,32},{32,48},{48,0},{1,17},{17,33},{33,49},{49,1},{2,18}... | collective-permute-start | bytes 152072 | tf_op jit(solution)/shard_map/ppermute | solution.py:59
  19.9 3.9 %collective-permute-start.3 = (bf16[3,66,128]{2,1,0:T(8,128)(2,1)S(1)}, bf16[3,66,128]{2,1,0:T(8,128)(2,1)S(1)}, u32[]{:S(2)}, u32[]{:S(2)}) collective-permute-start(bf16[3,66,128]{2,1,0:T(8,128)(2,1)S(1)} %pad_maximum_fusion), channel_id=1, source_target_pairs={{0,48},{16,0},{32,16},{48,32},{1,49},{17,1},{33,17},{49,33},{2,50}... | collective-permute-start | bytes 152072 | tf_op jit(solution)/shard_map/ppermute | solution.py:59
  24.1 1.9 %collective-permute-done.3 = bf16[3,66,128]{2,1,0:T(8,128)(2,1)S(1)} collective-permute-done((bf16[3,66,128]{2,1,0:T(8,128)(2,1)S(1)}, bf16[3,66,128]{2,1,0:T(8,128)(2,1)S(1)}, u32[]{:S(2)}, u32[]{:S(2)}) %collective-permute-start.3) | collective-permute-done | bytes 50720 | tf_op jit(solution)/shard_map/ppermute | solution.py:59
  26.2 6.8 %collective-permute-start.4 = (bf16[3,264,128]{2,1,0:T(8,128)(2,1)S(1)}, bf16[3,264,128]{2,1,0:T(8,128)(2,1)S(1)}, u32[]{:S(2)}, u32[]{:S(2)}) collective-permute-start(bf16[3,264,128]{2,1,0:T(8,128)(2,1)S(1)} %reshape.183), channel_id=1, source_target_pairs={{0,256},{64,320},{128,384},{192,448},{256,0},{320,64},{384,128},{4... | collective-permute-start | bytes 608264 | tf_op jit(solution)/shard_map/ppermute | solution.py:59
  33.1 7.1 %collective-permute-start.5 = (bf16[3,264,128]{2,1,0:T(8,128)(2,1)S(1)}, bf16[3,264,128]{2,1,0:T(8,128)(2,1)S(1)}, u32[]{:S(2)}, u32[]{:S(2)}) collective-permute-start(bf16[3,264,128]{2,1,0:T(8,128)(2,1)S(1)} %reshape.183), channel_id=1, source_target_pairs={{0,192},{64,256},{128,320},{192,384},{256,448},{320,0},{384,64},{4... | collective-permute-start | bytes 608264 | tf_op jit(solution)/shard_map/ppermute | solution.py:59
  40.2 1.9 %collective-permute-start.6 = (bf16[3,264,128]{2,1,0:T(8,128)(2,1)S(1)}, bf16[3,264,128]{2,1,0:T(8,128)(2,1)S(1)}, u32[]{:S(2)}, u32[]{:S(2)}) collective-permute-start(bf16[3,264,128]{2,1,0:T(8,128)(2,1)S(1)} %reshape.183), channel_id=1, source_target_pairs={{0,128},{64,192},{128,256},{192,320},{256,384},{320,448},{384,0},{... | collective-permute-start | bytes 608264 | tf_op jit(solution)/shard_map/ppermute | solution.py:59
  42.2 2.5 %collective-permute-start.7 = (bf16[3,264,128]{2,1,0:T(8,128)(2,1)S(1)}, bf16[3,264,128]{2,1,0:T(8,128)(2,1)S(1)}, u32[]{:S(2)}, u32[]{:S(2)}) collective-permute-start(bf16[3,264,128]{2,1,0:T(8,128)(2,1)S(1)} %reshape.183), channel_id=1, source_target_pairs={{0,64},{64,128},{128,192},{192,256},{256,320},{320,384},{384,448},... | collective-permute-start | bytes 608264 | tf_op jit(solution)/shard_map/ppermute | solution.py:59
  44.7 3.4 %collective-permute-start.8 = (bf16[3,264,128]{2,1,0:T(8,128)(2,1)S(1)}, bf16[3,264,128]{2,1,0:T(8,128)(2,1)S(1)}, u32[]{:S(2)}, u32[]{:S(2)}) collective-permute-start(bf16[3,264,128]{2,1,0:T(8,128)(2,1)S(1)} %reshape.183), channel_id=1, source_target_pairs={{0,448},{64,0},{128,64},{192,128},{256,192},{320,256},{384,320},{4... | collective-permute-start | bytes 608264 | tf_op jit(solution)/shard_map/ppermute | solution.py:59
  48.1 6.0 %collective-permute-start.9 = (bf16[3,264,128]{2,1,0:T(8,128)(2,1)S(1)}, bf16[3,264,128]{2,1,0:T(8,128)(2,1)S(1)}, u32[]{:S(2)}, u32[]{:S(2)}) collective-permute-start(bf16[3,264,128]{2,1,0:T(8,128)(2,1)S(1)} %reshape.183), channel_id=1, source_target_pairs={{0,384},{64,448},{128,0},{192,64},{256,128},{320,192},{384,256},{4... | collective-permute-start | bytes 608264 | tf_op jit(solution)/shard_map/ppermute | solution.py:59
  54.2 4.7 %collective-permute-done.5 = bf16[3,264,128]{2,1,0:T(8,128)(2,1)S(1)} collective-permute-done((bf16[3,264,128]{2,1,0:T(8,128)(2,1)S(1)}, bf16[3,264,128]{2,1,0:T(8,128)(2,1)S(1)}, u32[]{:S(2)}, u32[]{:S(2)}) %collective-permute-start.5) | collective-permute-done | bytes 202784 | tf_op jit(solution)/shard_map/ppermute | solution.py:59
  58.9 1.9 %collective-permute-start.10 = (bf16[3,264,128]{2,1,0:T(8,128)(2,1)S(1)}, bf16[3,264,128]{2,1,0:T(8,128)(2,1)S(1)}, u32[]{:S(2)}, u32[]{:S(2)}) collective-permute-start(bf16[3,264,128]{2,1,0:T(8,128)(2,1)S(1)} %reshape.183), channel_id=1, source_target_pairs={{0,320},{64,384},{128,448},{192,0},{256,64},{320,128},{384,192},{4... | collective-permute-start | bytes 608264 | tf_op jit(solution)/shard_map/ppermute | solution.py:59
  60.9 4.4 %collective-permute-done.6 = bf16[3,264,128]{2,1,0:T(8,128)(2,1)S(1)} collective-permute-done((bf16[3,264,128]{2,1,0:T(8,128)(2,1)S(1)}, bf16[3,264,128]{2,1,0:T(8,128)(2,1)S(1)}, u32[]{:S(2)}, u32[]{:S(2)}) %collective-permute-start.6) | collective-permute-done | bytes 202784 | tf_op jit(solution)/shard_map/ppermute | solution.py:59
  65.3 3.0 %collective-permute-done.7 = bf16[3,264,128]{2,1,0:T(8,128)(2,1)S(1)} collective-permute-done((bf16[3,264,128]{2,1,0:T(8,128)(2,1)S(1)}, bf16[3,264,128]{2,1,0:T(8,128)(2,1)S(1)}, u32[]{:S(2)}, u32[]{:S(2)}) %collective-permute-start.7) | collective-permute-done | bytes 202784 | tf_op jit(solution)/shard_map/ppermute | solution.py:59
  68.4 8.2 %collective-permute-done.10 = bf16[3,264,128]{2,1,0:T(8,128)(2,1)S(1)} collective-permute-done((bf16[3,264,128]{2,1,0:T(8,128)(2,1)S(1)}, bf16[3,264,128]{2,1,0:T(8,128)(2,1)S(1)}, u32[]{:S(2)}, u32[]{:S(2)}) %collective-permute-start.10) | collective-permute-done | bytes 202784 | tf_op jit(solution)/shard_map/ppermute | solution.py:59
  77.0 1.3 copy.31
  78.4 1.9 %collective-permute-start.11 = (bf16[3,2112,128]{2,1,0:T(8,128)(2,1)}, bf16[3,2112,128]{2,1,0:T(8,128)(2,1)}, u32[]{:S(2)}, u32[]{:S(2)}) collective-permute-start(bf16[3,2112,128]{2,1,0:T(8,128)(2,1)} %bitcast.14), channel_id=1, source_target_pairs={{0,8},{8,0},{1,9},{9,1},{2,10},{10,2},{3,11},{11,3},{4,12},{12,4},... | collective-permute-start | bytes 4866056 | tf_op jit(solution)/shard_map/ppermute | solution.py:46
  82.6 1.3 fusion.2
  83.9 2.5 %concatenate.35 = bf16[3,64,33,128]{3,2,1,0:T(8,128)(2,1)S(1)} reshape(bf16[3,8,264,128]{3,2,1,0:T(8,128)(2,1)} %copy.31) | data formatting | bytes 3244032 | tf_op jit(solution)/shard_map/concatenate | solution.py:49
  86.4 3.7 %concatenate.36 = bf16[3,64,33,128]{3,2,1,0:T(8,128)(2,1)} reshape(bf16[3,2112,128]{2,1,0:T(8,128)(2,1)} %collective-permute-done.11) | data formatting | bytes 3244032 | tf_op jit(solution)/shard_map/concatenate | solution.py:49
  90.1 2.8 %maximum_select_fusion = bf16[3,64,33,256]{3,2,1,0:T(8,128)(2,1)S(1)} fusion(bf16[3,64,33,128]{3,2,1,0:T(8,128)(2,1)} %concatenate.36, bf16[3,64,33,128]{3,2,1,0:T(8,128)(2,1)S(1)} %concatenate.35, pred[]{:T(512)S(6)} %eq.87), kind=kLoop, calls=%fused_computation.4 | loop fusion | flops 14598144 | bytes 6488065 | tf_op jit(solution)/shard_map/jit(_where)/select_n | solution.py:47
  94.9 4.6 %fusion.7 = bf16[2,1024,256]{1,2,0:T(8,128)(2,1)S(1)} fusion(bf16[2,2048,256]{2,1,0:T(8,128)(2,1)S(1)} %bitcast.97, bf16[1024,2048]{1,0:T(8,128)(2,1)} %all-gather.2.cloned.1.call-done), kind=kOutput, calls=%fused_computation.20 | convolution fusion | flops 2148007936 | bytes 7340032 | tf_op jit(solution)/shard_map/tr,grc->gtc/dot_general | solution.py:116
  102.0 5.6 %all-to-all-start = ((bf16[8,2,128,128]{3,2,1,0:T(8,128)(2,1)}), bf16[8,2,128,128]{3,2,1,0:T(8,128)(2,1)S(1)}, u32[]{:S(2)}, u32[]{:S(2)}) async-start(bf16[8,2,128,128]{3,2,1,0:T(8,128)(2,1)} %broadcast_in_dim.115), calls=%async_computation | async-start | bytes 1048576 | tf_op jit(solution)/shard_map/all_to_all | solution.py:86
  110.1 4.2 %fusion.21 = bf16[1024,256]{0,1:T(8,128)(2,1)S(1)} fusion(bf16[2048,256]{1,0:T(8,128)(2,1)} %bitcast.101, bf16[1024,2048]{1,0:T(8,128)(2,1)} %all-gather.2.cloned.1.call-done), kind=kOutput, calls=%fused_computation.34 | convolution fusion | flops 1075314688 | bytes 5767168 | tf_op jit(solution)/shard_map/tr,rc->tc/dot_general | solution.py:129
  115.4 1.9 %fusion.15 = f32[512,2,128]{0,2,1:T(8,128)S(1)} fusion(bf16[512,2,128]{0,2,1:T(8,128)(2,1)} %bitcast.105, bf16[512,2,128]{0,2,1:T(8,128)(2,1)} %bitcast.107, bf16[512,2,128]{0,2,1:T(8,128)(2,1)S(1)} %bitcast.104, pred[512,512]{1,0:T(8,128)(4,1)} %fusion.26), kind=kOutput, calls=%fused_computation.28 | convolution fusion | flops 269484032 | bytes 1572864 | tf_op jit(solution)/shard_map/hbs,she->bhe/dot_general | solution.py:149
  117.8 2.8 %fusion.14 = f32[512,2,128]{0,2,1:T(8,128)S(1)} fusion(bf16[1024,2,128]{0,2,1:T(8,128)(2,1)} %bitcast.103, bf16[512,2,128]{0,2,1:T(8,128)(2,1)} %bitcast.106, pred[512,1024]{1,0:T(8,128)(4,1)} %fusion.2, f32[1024,2,128]{0,2,1:T(8,128)S(1)} %bitcast.100), kind=kOutput, calls=%fused_computation.27 | convolution fusion | flops 540278784 | bytes 2883584 | tf_op jit(solution)/shard_map/hbs,she->bhe/dot_general | solution.py:149
  121.0 4.8 %collective-permute-start.13 = (bf16[2,128,128]{2,1,0:T(8,128)(2,1)S(1)}, bf16[2,128,128]{2,1,0:T(8,128)(2,1)S(1)}, u32[]{:S(2)}, u32[]{:S(2)}) collective-permute-start(bf16[2,128,128]{2,1,0:T(8,128)(2,1)S(1)} %get-tuple-element.10), channel_id=1, source_target_pairs={{0,128},{64,192},{128,256},{192,320},{256,384},{320,448},{1,129},{... | collective-permute-start | bytes 196616 | tf_op jit(solution)/shard_map/ppermute | solution.py:15
  125.8 2.7 %collective-permute-start.12 = (bf16[2,128,128]{2,1,0:T(8,128)(2,1)S(1)}, bf16[2,128,128]{2,1,0:T(8,128)(2,1)S(1)}, u32[]{:S(2)}, u32[]{:S(2)}) collective-permute-start(bf16[2,128,128]{2,1,0:T(8,128)(2,1)S(1)} %get-tuple-element.9), channel_id=1, source_target_pairs={{0,64},{64,128},{128,192},{192,256},{256,320},{320,384},{384,448},... | collective-permute-start | bytes 196616 | tf_op jit(solution)/shard_map/ppermute | solution.py:15
  129.8 2.2 %collective-permute-done.12 = bf16[2,128,128]{2,1,0:T(8,128)(2,1)S(1)} collective-permute-done((bf16[2,128,128]{2,1,0:T(8,128)(2,1)S(1)}, bf16[2,128,128]{2,1,0:T(8,128)(2,1)S(1)}, u32[]{:S(2)}, u32[]{:S(2)}) %collective-permute-start.12) | collective-permute-done | bytes 65568 | tf_op jit(solution)/shard_map/ppermute | solution.py:15
  (77 shorter events, 15.7 us)
Async XLA Ops:
  6.5 88.4 %all-gather.2.cloned.1.call-start = ((), (), s32[]{:S(2)}) async-start(), calls=%async_computation.1 | async-start | bytes 4718592 | tf_op jit(solution)/shard_map/all_gather | solution.py:107
  9.3 3.1 %collective-permute-start = (bf16[3,33,256]{2,1,0:T(8,128)(2,1)S(1)}, bf16[3,33,256]{2,1,0:T(8,128)(2,1)S(1)}, u32[]{:S(2)}, u32[]{:S(2)}) collective-permute-start(bf16[3,33,256]{2,1,0:T(8,128)(2,1)S(1)} %concatenate.31), channel_id=1, source_target_pairs={{0,8},{8,0},{1,9},{9,1},{2,10},{10,2},{3,11},{11,3},{4,12},{12,4},... | collective-permute-start | bytes 152072 | tf_op jit(solution)/shard_map/ppermute | solution.py:40
  13.9 10.0 %collective-permute-start.1 = (bf16[3,66,128]{2,1,0:T(8,128)(2,1)S(1)}, bf16[3,66,128]{2,1,0:T(8,128)(2,1)S(1)}, u32[]{:S(2)}, u32[]{:S(2)}) collective-permute-start(bf16[3,66,128]{2,1,0:T(8,128)(2,1)S(1)} %pad_maximum_fusion), channel_id=1, source_target_pairs={{0,32},{16,48},{32,0},{48,16},{1,33},{17,49},{33,1},{49,17},{2,34}... | collective-permute-start | bytes 152072 | tf_op jit(solution)/shard_map/ppermute | solution.py:59
  18.0 6.0 %collective-permute-start.2 = (bf16[3,66,128]{2,1,0:T(8,128)(2,1)S(1)}, bf16[3,66,128]{2,1,0:T(8,128)(2,1)S(1)}, u32[]{:S(2)}, u32[]{:S(2)}) collective-permute-start(bf16[3,66,128]{2,1,0:T(8,128)(2,1)S(1)} %pad_maximum_fusion), channel_id=1, source_target_pairs={{0,16},{16,32},{32,48},{48,0},{1,17},{17,33},{33,49},{49,1},{2,18}... | collective-permute-start | bytes 152072 | tf_op jit(solution)/shard_map/ppermute | solution.py:59
  19.9 6.0 %collective-permute-start.3 = (bf16[3,66,128]{2,1,0:T(8,128)(2,1)S(1)}, bf16[3,66,128]{2,1,0:T(8,128)(2,1)S(1)}, u32[]{:S(2)}, u32[]{:S(2)}) collective-permute-start(bf16[3,66,128]{2,1,0:T(8,128)(2,1)S(1)} %pad_maximum_fusion), channel_id=1, source_target_pairs={{0,48},{16,0},{32,16},{48,32},{1,49},{17,1},{33,17},{49,33},{2,50}... | collective-permute-start | bytes 152072 | tf_op jit(solution)/shard_map/ppermute | solution.py:59
  26.2 21.9 %collective-permute-start.4 = (bf16[3,264,128]{2,1,0:T(8,128)(2,1)S(1)}, bf16[3,264,128]{2,1,0:T(8,128)(2,1)S(1)}, u32[]{:S(2)}, u32[]{:S(2)}) collective-permute-start(bf16[3,264,128]{2,1,0:T(8,128)(2,1)S(1)} %reshape.183), channel_id=1, source_target_pairs={{0,256},{64,320},{128,384},{192,448},{256,0},{320,64},{384,128},{4... | collective-permute-start | bytes 608264 | tf_op jit(solution)/shard_map/ppermute | solution.py:59
  33.1 25.8 %collective-permute-start.5 = (bf16[3,264,128]{2,1,0:T(8,128)(2,1)S(1)}, bf16[3,264,128]{2,1,0:T(8,128)(2,1)S(1)}, u32[]{:S(2)}, u32[]{:S(2)}) collective-permute-start(bf16[3,264,128]{2,1,0:T(8,128)(2,1)S(1)} %reshape.183), channel_id=1, source_target_pairs={{0,192},{64,256},{128,320},{192,384},{256,448},{320,0},{384,64},{4... | collective-permute-start | bytes 608264 | tf_op jit(solution)/shard_map/ppermute | solution.py:59
  40.2 25.0 %collective-permute-start.6 = (bf16[3,264,128]{2,1,0:T(8,128)(2,1)S(1)}, bf16[3,264,128]{2,1,0:T(8,128)(2,1)S(1)}, u32[]{:S(2)}, u32[]{:S(2)}) collective-permute-start(bf16[3,264,128]{2,1,0:T(8,128)(2,1)S(1)} %reshape.183), channel_id=1, source_target_pairs={{0,128},{64,192},{128,256},{192,320},{256,384},{320,448},{384,0},{... | collective-permute-start | bytes 608264 | tf_op jit(solution)/shard_map/ppermute | solution.py:59
  42.2 26.1 %collective-permute-start.7 = (bf16[3,264,128]{2,1,0:T(8,128)(2,1)S(1)}, bf16[3,264,128]{2,1,0:T(8,128)(2,1)S(1)}, u32[]{:S(2)}, u32[]{:S(2)}) collective-permute-start(bf16[3,264,128]{2,1,0:T(8,128)(2,1)S(1)} %reshape.183), channel_id=1, source_target_pairs={{0,64},{64,128},{128,192},{192,256},{256,320},{320,384},{384,448},... | collective-permute-start | bytes 608264 | tf_op jit(solution)/shard_map/ppermute | solution.py:59
  44.7 23.6 %collective-permute-start.8 = (bf16[3,264,128]{2,1,0:T(8,128)(2,1)S(1)}, bf16[3,264,128]{2,1,0:T(8,128)(2,1)S(1)}, u32[]{:S(2)}, u32[]{:S(2)}) collective-permute-start(bf16[3,264,128]{2,1,0:T(8,128)(2,1)S(1)} %reshape.183), channel_id=1, source_target_pairs={{0,448},{64,0},{128,64},{192,128},{256,192},{320,256},{384,320},{4... | collective-permute-start | bytes 608264 | tf_op jit(solution)/shard_map/ppermute | solution.py:59
  48.1 20.2 %collective-permute-start.9 = (bf16[3,264,128]{2,1,0:T(8,128)(2,1)S(1)}, bf16[3,264,128]{2,1,0:T(8,128)(2,1)S(1)}, u32[]{:S(2)}, u32[]{:S(2)}) collective-permute-start(bf16[3,264,128]{2,1,0:T(8,128)(2,1)S(1)} %reshape.183), channel_id=1, source_target_pairs={{0,384},{64,448},{128,0},{192,64},{256,128},{320,192},{384,256},{4... | collective-permute-start | bytes 608264 | tf_op jit(solution)/shard_map/ppermute | solution.py:59
  58.9 17.7 %collective-permute-start.10 = (bf16[3,264,128]{2,1,0:T(8,128)(2,1)S(1)}, bf16[3,264,128]{2,1,0:T(8,128)(2,1)S(1)}, u32[]{:S(2)}, u32[]{:S(2)}) collective-permute-start(bf16[3,264,128]{2,1,0:T(8,128)(2,1)S(1)} %reshape.183), channel_id=1, source_target_pairs={{0,320},{64,384},{128,448},{192,0},{256,64},{320,128},{384,192},{4... | collective-permute-start | bytes 608264 | tf_op jit(solution)/shard_map/ppermute | solution.py:59
  76.9 4.0 %copy-start.1 = (s32[1024]{0:T(1024)S(1)}, s32[1024]{0:T(1024)}, u32[]{:S(2)}) copy-start(s32[1024]{0:T(1024)} %param.7) | copy-start | bytes 12292
  78.4 8.0 %collective-permute-start.11 = (bf16[3,2112,128]{2,1,0:T(8,128)(2,1)}, bf16[3,2112,128]{2,1,0:T(8,128)(2,1)}, u32[]{:S(2)}, u32[]{:S(2)}) collective-permute-start(bf16[3,2112,128]{2,1,0:T(8,128)(2,1)} %bitcast.14), channel_id=1, source_target_pairs={{0,8},{8,0},{1,9},{9,1},{2,10},{10,2},{3,11},{11,3},{4,12},{12,4},... | collective-permute-start | bytes 4866056 | tf_op jit(solution)/shard_map/ppermute | solution.py:46
  99.7 2.3 %copy-start = (bf16[1,1024,256]{1,2,0:T(8,128)(2,1)}, bf16[1,1024,256]{1,2,0:T(8,128)(2,1)S(1)}, u32[]{:S(2)}) copy-start(bf16[1,1024,256]{1,2,0:T(8,128)(2,1)S(1)} %get-tuple-element.17) | copy-start | bytes 1572868
  102.0 18.7 %all-to-all-start = ((bf16[8,2,128,128]{3,2,1,0:T(8,128)(2,1)}), bf16[8,2,128,128]{3,2,1,0:T(8,128)(2,1)S(1)}, u32[]{:S(2)}, u32[]{:S(2)}) async-start(bf16[8,2,128,128]{3,2,1,0:T(8,128)(2,1)} %broadcast_in_dim.115), calls=%async_computation | async-start | bytes 1048576 | tf_op jit(solution)/shard_map/all_to_all | solution.py:86
  120.7 11.7 %copy-start.2 = (f32[256]{0:T(256)S(1)}, f32[256]{0:T(256)}, u32[]{:S(2)}) copy-start(f32[256]{0:T(256)} %param.6) | copy-start | bytes 3076
  121.0 8.7 %collective-permute-start.13 = (bf16[2,128,128]{2,1,0:T(8,128)(2,1)S(1)}, bf16[2,128,128]{2,1,0:T(8,128)(2,1)S(1)}, u32[]{:S(2)}, u32[]{:S(2)}) collective-permute-start(bf16[2,128,128]{2,1,0:T(8,128)(2,1)S(1)} %get-tuple-element.10), channel_id=1, source_target_pairs={{0,128},{64,192},{128,256},{192,320},{256,384},{320,448},{1,129},{... | collective-permute-start | bytes 196616 | tf_op jit(solution)/shard_map/ppermute | solution.py:15
  125.8 6.2 %collective-permute-start.12 = (bf16[2,128,128]{2,1,0:T(8,128)(2,1)S(1)}, bf16[2,128,128]{2,1,0:T(8,128)(2,1)S(1)}, u32[]{:S(2)}, u32[]{:S(2)}) collective-permute-start(bf16[2,128,128]{2,1,0:T(8,128)(2,1)S(1)} %get-tuple-element.9), channel_id=1, source_target_pairs={{0,64},{64,128},{128,192},{192,256},{256,320},{320,384},{384,448},... | collective-permute-start | bytes 196616 | tf_op jit(solution)/shard_map/ppermute | solution.py:15
Sparse Core Ops, SparseCore 0:
  18.1 69.0 all-gather.1
